TPU v7x, 256 devices: a whole 4x4x8 slice. The times are simulated.
256 devices in a mesh: blk: 32 (over x, y, core), sub: 8 (over z).
Axes of the slice: x: 4, y: 4, z: 8, core: 2. Of those that a mesh axis runs over, the one named last changes fastest.
Arguments:
- block_vec: bfloat16 [64, 512, 512], P('blk', 'sub'), may hold values from -6 to 6
- left_factor: bfloat16 [8, 512, 512], replicated, may hold values from -0.25 to 0.25
- right_factor: bfloat16 [8, 512, 512], replicated, may hold values from -0.25 to 0.25
- pairs: int32 [32, 32, 2, 3], replicated, may hold values from 0 to 7, as said below
- pair_count: int32 [32, 32], replicated, may hold values from 1 to 2, as said below
- left_basis: bfloat16 [64, 512, 512], P('blk'), may hold values from -0.25 to 0.25
- left_dual: bfloat16 [64, 512, 512], P('blk'), may hold values from -0.25 to 0.25
- right_eigenvector_matrix: bfloat16 [64, 512, 512], P('blk'), may hold values from -0.25 to 0.25
- right_dual: bfloat16 [64, 512, 512], P('blk'), may hold values from -0.25 to 0.25
- left_rates: float32 [64, 512], P('blk', 'sub'), may hold values from 0.5 to 8
- right_rates: float32 [64, 512], P('blk'), may hold values from 0.5 to 8
Outputs:
- next_vec: float32 [64, 512, 512], P('blk', None, 'sub')
Inputs may be any that keep to these rules, and one draw needn't show every extreme that they name: `pairs`: entry [g, h, c, 0] is a source block index within group g, [g, h, c, 1] a target block index within group h (0 to 1), and [g, h, c, 2] a term index (0 to 7); where g equals h, source and target differ. For some target group h, pair_count[g, h] is 2 for every g.
All inputs are finite; a program needn't handle non-finite values.
Results may differ from a plain program's by a relative error of at most 0.023.
Values may be sent and summed in bfloat16 or wider, within the bound.
No kernel may reach another device: no remote copies, remote signals or barrier semaphores. Data moves between devices by JAX's collectives and lax.ppermute only.
A program may use at most 64 MiB of HBM per device.

v0:
```python
import jax
import jax.numpy as jnp
from jax import lax
from jax.sharding import PartitionSpec as P


def exchange(chunks, axis):
    n = chunks.shape[0]
    me = lax.axis_index(axis)
    out = jnp.zeros_like(chunks)
    own = lax.dynamic_index_in_dim(chunks, me, 0, keepdims=True)
    out = lax.dynamic_update_index_in_dim(out, own, me, 0)
    for k in range(1, n):
        send = lax.dynamic_index_in_dim(chunks, (me + k) % n, 0, keepdims=True)
        got = lax.ppermute(send, axis, [(j, (j + k) % n) for j in range(n)])
        out = lax.dynamic_update_index_in_dim(out, got, (me - k) % n, 0)
    return out


def scatter_sum(chunks, axis):
    n = chunks.shape[0]
    me = lax.axis_index(axis)
    total = lax.dynamic_index_in_dim(chunks, me, 0, keepdims=False).astype(jnp.float32)
    for k in range(1, n):
        send = lax.dynamic_index_in_dim(chunks, (me + k) % n, 0, keepdims=False)
        got = lax.ppermute(send, axis, [(j, (j + k) % n) for j in range(n)])
        total = total + got.astype(jnp.float32)
    return total


def local(
    block_vec,
    left_factor,
    right_factor,
    pairs,
    pair_count,
    left_basis,
    left_dual,
    right_eigenvector_matrix,
    right_dual,
    left_rates,
    right_rates,
):
    owner = lax.axis_index("blk")
    part = lax.axis_index("sub")
    groups = lax.axis_size("blk")
    pieces = lax.axis_size("sub")
    local_blocks = block_vec.shape[0]
    row_count = block_vec.shape[1]
    width_two = block_vec.shape[2]
    slots_per = pairs.shape[2]
    term_total = left_factor.shape[0]
    all_count = groups * local_blocks
    cols = width_two // pieces
    incoming = lax.dynamic_index_in_dim(pairs, owner, 1, keepdims=False)
    counts = lax.dynamic_index_in_dim(pair_count, owner, 1, keepdims=False)
    live_mask = (jnp.arange(slots_per)[None, :] < counts[:, None]).astype(jnp.float32)
    target_term = incoming[..., 1] * term_total + incoming[..., 2]
    source = jnp.arange(groups, dtype=jnp.int32)[:, None] * local_blocks + incoming[..., 0]
    key_onehot = (
        target_term[..., None] == jnp.arange(local_blocks * term_total)[None, None, :]
    ).astype(jnp.float32) * live_mask[..., None]
    source_onehot = (source[..., None] == jnp.arange(all_count)[None, None, :]).astype(jnp.float32)
    weights = jnp.einsum("gqk,gqs->ks", key_onehot, source_onehot).astype(jnp.bfloat16)
    everything = lax.all_gather(block_vec, "blk", axis=0, tiled=True)
    pooled = jnp.einsum(
        "ks,srn->krn", weights, everything, preferred_element_type=jnp.float32
    ).astype(jnp.bfloat16)
    pooled = pooled.reshape(local_blocks, term_total, row_count, width_two)
    right_done = jnp.einsum(
        "ktrn,tmn->ktrm", pooled, right_factor, preferred_element_type=jnp.float32
    ).astype(jnp.bfloat16)
    left_part = lax.dynamic_slice_in_dim(left_factor, part * row_count, row_count, axis=2)
    rates_parts = exchange(jnp.broadcast_to(left_rates, (pieces,) + left_rates.shape), "sub")
    rates_full = jnp.moveaxis(rates_parts, 0, 1).reshape(local_blocks, width_two)
    partial = jnp.einsum(
        "tab,ktbc->kac", left_part, right_done, preferred_element_type=jnp.float32
    ).astype(jnp.bfloat16)
    dual_cols = jnp.einsum(
        "jab,jbc->jac", left_dual, partial, preferred_element_type=jnp.float32
    ).astype(jnp.bfloat16)
    mixed = jnp.einsum("jrn,jmn->jrm", dual_cols, right_dual, preferred_element_type=jnp.float32)
    scaled = (mixed / (rates_full[:, :, None] + right_rates[:, None, :])).astype(jnp.bfloat16)
    basis_rows = jnp.einsum(
        "jrm,jkm->jrk", scaled, right_eigenvector_matrix, preferred_element_type=jnp.float32
    ).astype(jnp.bfloat16)
    basis_rows = basis_rows.reshape(local_blocks, width_two, pieces, cols)
    spread = jnp.einsum(
        "jab,jbkc->kjac", left_basis, basis_rows, preferred_element_type=jnp.float32
    ).astype(jnp.bfloat16)
    return scatter_sum(spread, "sub")


def solution(mesh):
    placed = (
        P("blk", "sub", None),
        P(),
        P(),
        P(),
        P(),
        P("blk", None, None),
        P("blk", None, None),
        P("blk", None, None),
        P("blk", None, None),
        P("blk", "sub"),
        P("blk", None),
    )
    return jax.shard_map(
        local, mesh=mesh, in_specs=placed, out_specs=P("blk", None, "sub"), check_vma=False
    )
```

profile of v0, /device:TPU:24, one launch (start us, length us, event | category | flops | bytes accessed | tf_op | source)
XLA Modules:
  0.0 126.4 jit_solution(7733343149674585793)
XLA Ops:
  6.5 0.0 copy-start
  6.5 0.0 all-gather.2.cloned.1.call-start
  6.5 0.7 all-gather.2.cloned.1.call-update
  7.3 2.0 %collective-permute-start = (f32[1,2,64]{2,1,0:T(2,128)}, f32[1,2,64]{2,1,0:T(2,128)S(1)}, u32[]{:S(2)}, u32[]{:S(2)}) collective-permute-start(f32[1,2,64]{2,1,0:T(2,128)} %bitcast.125), channel_id=1, source_target_pairs={{0,1},{1,2},{2,3},{3,4},{4,5},{5,6},{6,7},{7,0},{8,9},{9,10},{10,1... | collective-permute-start | bytes 1544 | tf_op jit(solution)/shard_map/ppermute | solution.py:15
  9.3 3.3 %collective-permute-start.1 = (f32[1,2,64]{2,1,0:T(2,128)}, f32[1,2,64]{2,1,0:T(2,128)S(1)}, u32[]{:S(2)}, u32[]{:S(2)}) collective-permute-start(f32[1,2,64]{2,1,0:T(2,128)} %bitcast.126), channel_id=1, source_target_pairs={{0,2},{1,3},{2,4},{3,5},{4,6},{5,7},{6,0},{7,1},{8,10},{9,11},{10,... | collective-permute-start | bytes 1544 | tf_op jit(solution)/shard_map/ppermute | solution.py:15
  12.5 4.0 %collective-permute-start.2 = (f32[1,2,64]{2,1,0:T(2,128)}, f32[1,2,64]{2,1,0:T(2,128)S(1)}, u32[]{:S(2)}, u32[]{:S(2)}) collective-permute-start(f32[1,2,64]{2,1,0:T(2,128)} %bitcast.127), channel_id=1, source_target_pairs={{0,3},{1,4},{2,5},{3,6},{4,7},{5,0},{6,1},{7,2},{8,11},{9,12},{10,... | collective-permute-start | bytes 1544 | tf_op jit(solution)/shard_map/ppermute | solution.py:15
  16.6 0.5 collective-permute-start.3
  17.1 4.9 %collective-permute-start.4 = (f32[1,2,64]{2,1,0:T(2,128)}, f32[1,2,64]{2,1,0:T(2,128)S(1)}, u32[]{:S(2)}, u32[]{:S(2)}) collective-permute-start(f32[1,2,64]{2,1,0:T(2,128)} %bitcast.129), channel_id=1, source_target_pairs={{0,5},{1,6},{2,7},{3,0},{4,1},{5,2},{6,3},{7,4},{8,13},{9,14},{10,... | collective-permute-start | bytes 1544 | tf_op jit(solution)/shard_map/ppermute | solution.py:15
  22.1 1.1 constant_dynamic-slice_fusion
  23.1 0.1 copy.41
  23.3 0.9 dynamic-slice_reduce_fusion
  24.2 0.7 dynamic_update_slice.25
  25.0 0.0 collective-permute-done
  25.0 2.7 %collective-permute-start.5 = (f32[1,2,64]{2,1,0:T(2,128)}, f32[1,2,64]{2,1,0:T(2,128)S(1)}, u32[]{:S(2)}, u32[]{:S(2)}) collective-permute-start(f32[1,2,64]{2,1,0:T(2,128)} %bitcast.131), channel_id=1, source_target_pairs={{0,6},{1,7},{2,0},{3,1},{4,2},{5,3},{6,4},{7,5},{8,14},{9,15},{10,... | collective-permute-start | bytes 1544 | tf_op jit(solution)/shard_map/ppermute | solution.py:15
  27.7 0.0 collective-permute-done.1
  27.7 1.1 collective-permute-start.6
  28.8 0.0 collective-permute-done.2
  28.9 0.0 collective-permute-done.3
  28.9 0.0 collective-permute-done.4
  29.0 0.8 collective-permute-done.5
  29.7 1.8 %collective-permute-done.6 = f32[1,2,64]{2,1,0:T(2,128)S(1)} collective-permute-done((f32[1,2,64]{2,1,0:T(2,128)}, f32[1,2,64]{2,1,0:T(2,128)S(1)}, u32[]{:S(2)}, u32[]{:S(2)}) %collective-permute-start.6) | collective-permute-done | bytes 544 | tf_op jit(solution)/shard_map/ppermute | solution.py:15
  31.6 0.2 dynamic_update_slice.32
  31.8 0.1 add.220
  31.9 31.5 %all-gather.2.cloned.1.call-done = bf16[64,64,512]{2,1,0:T(8,128)(2,1)} async-done(((bf16[2,64,512]{2,1,0:T(8,128)(2,1)}), bf16[64,64,512]{2,1,0:T(8,128)(2,1)}) %all-gather.2.cloned.1.call-update) | async-done | bytes 4194320 | tf_op jit(solution)/shard_map/all_gather | solution.py:65
  63.4 6.7 %fusion.14 = bf16[2,8,64,512]{3,1,0,2:T(8,128)(2,1)S(1)} fusion(bf16[64,64,512]{2,1,0:T(8,128)(2,1)} %all-gather.2.cloned.1.call-done, s32[32,2]{0,1:T(2,128)S(1)} %get-tuple-element.13, bf16[32,2]{0,1:T(2,128)(2,1)S(1)} %compare_convert_fusion, s32[32,2]{0,1:T(2,128)S(1)} %get-tuple-element.12), kind=kOutput, calls=%fused_computation.13 | convolution fusion | flops 67770368 | bytes 5243520 | tf_op jit(solution)/shard_map/ks,srn->krn/dot_general | solution.py:66
  70.1 6.6 %bitcast_convert_fusion = bf16[2,512,512]{2,1,0:T(8,128)(2,1)} fusion(bf16[8,512,512]{2,1,0:T(8,128)(2,1)} %param.12, s32[]{:T(128)S(6)} %select_n.140, bf16[8,512,512]{2,1,0:T(8,128)(2,1)} %param.13, bf16[2,8,64,512]{3,1,0,2:T(8,128)(2,1)S(1)} %fusion.14), kind=kOutput, calls=%fused_computation.4 | convolution fusion | flops 1074790400 | bytes 7340036 | tf_op jit(solution)/shard_map/tab,ktbc->kac/dot_general | solution.py:76
  76.8 0.0 copy-done
  76.8 0.0 copy-start.4
  76.8 3.9 %fusion.10 = f32[2,512,512]{2,1,0:T(8,128)} fusion(bf16[2,512,512]{2,1,0:T(8,128)(2,1)S(1)} %copy-done, bf16[2,512,512]{2,1,0:T(8,128)(2,1)} %bitcast_convert_fusion, bf16[2,512,512]{2,1,0:T(8,128)(2,1)S(1)} %copy-done.2), kind=kOutput, calls=%fused_computation.11 | convolution fusion | flops 1074266112 | bytes 5242880 | tf_op jit(solution)/shard_map/jrn,jmn->jrm/dot_general | solution.py:82
  80.7 0.0 copy-done.4
  80.7 2.6 %convolution_convert_fusion.1 = bf16[2,512,512]{1,2,0:T(8,128)(2,1)S(1)} fusion(bf16[2,512,512]{2,1,0:T(8,128)(2,1)S(1)} %copy-done.3, f32[2,512,512]{2,1,0:T(8,128)} %fusion.10, f32[2,512]{1,0:T(2,128)S(1)} %copy-done.4, f32[2,512]{1,0:T(2,128)S(1)} %add.220), kind=kOutput, calls=%fused_computation.9 | convolution fusion | flops 538968064 | bytes 4202496 | tf_op jit(solution)/shard_map/jrm,jkm->jrk/dot_general | solution.py:84
  83.3 0.7 convolution_convert_fusion
  84.1 0.1 dynamic-slice_bitcast_fusion.6
  84.2 3.4 %collective-permute-start.13 = (bf16[2,512,64]{1,2,0:T(8,128)(2,1)S(1)}, bf16[2,512,64]{1,2,0:T(8,128)(2,1)S(1)}, u32[]{:S(2)}, u32[]{:S(2)}) collective-permute-start(bf16[2,512,64]{1,2,0:T(8,128)(2,1)S(1)} %get-tuple-element.10), channel_id=1, source_target_pairs={{0,7},{1,0},{2,1},{3,2},{4,3},{5,4},{6,5},{7,6},{8,15},{9,8},{10,9... | collective-permute-start | bytes 393224 | tf_op jit(solution)/shard_map/ppermute | solution.py:26
  87.6 2.2 %collective-permute-start.12 = (bf16[2,512,64]{1,2,0:T(8,128)(2,1)S(1)}, bf16[2,512,64]{1,2,0:T(8,128)(2,1)S(1)}, u32[]{:S(2)}, u32[]{:S(2)}) collective-permute-start(bf16[2,512,64]{1,2,0:T(8,128)(2,1)S(1)} %get-tuple-element.11), channel_id=1, source_target_pairs={{0,6},{1,7},{2,0},{3,1},{4,2},{5,3},{6,4},{7,5},{8,14},{9,15},{10,... | collective-permute-start | bytes 393224 | tf_op jit(solution)/shard_map/ppermute | solution.py:26
  89.7 1.2 collective-permute-start.11
  90.9 3.9 %collective-permute-start.10 = (bf16[2,512,64]{1,2,0:T(8,128)(2,1)S(1)}, bf16[2,512,64]{1,2,0:T(8,128)(2,1)S(1)}, u32[]{:S(2)}, u32[]{:S(2)}) collective-permute-start(bf16[2,512,64]{1,2,0:T(8,128)(2,1)S(1)} %get-tuple-element.7), channel_id=1, source_target_pairs={{0,4},{1,5},{2,6},{3,7},{4,0},{5,1},{6,2},{7,3},{8,12},{9,13},{10,... | collective-permute-start | bytes 393224 | tf_op jit(solution)/shard_map/ppermute | solution.py:26
  94.9 0.0 collective-permute-start.9
  94.9 0.0 collective-permute-done.13
  94.9 3.5 %collective-permute-start.8 = (bf16[2,512,64]{1,2,0:T(8,128)(2,1)S(1)}, bf16[2,512,64]{1,2,0:T(8,128)(2,1)S(1)}, u32[]{:S(2)}, u32[]{:S(2)}) collective-permute-start(bf16[2,512,64]{1,2,0:T(8,128)(2,1)S(1)} %get-tuple-element.9), channel_id=1, source_target_pairs={{0,2},{1,3},{2,4},{3,5},{4,6},{5,7},{6,0},{7,1},{8,10},{9,11},{10,... | collective-permute-start | bytes 393224 | tf_op jit(solution)/shard_map/ppermute | solution.py:26
  98.4 0.7 collective-permute-done.12
  99.1 0.8 collective-permute-start.7
  100.0 10.4 %collective-permute-done.11 = bf16[2,512,64]{1,2,0:T(8,128)(2,1)S(1)} collective-permute-done((bf16[2,512,64]{1,2,0:T(8,128)(2,1)S(1)}, bf16[2,512,64]{1,2,0:T(8,128)(2,1)S(1)}, u32[]{:S(2)}, u32[]{:S(2)}) %collective-permute-start.11) | collective-permute-done | bytes 131104 | tf_op jit(solution)/shard_map/ppermute | solution.py:26
  110.4 0.0 collective-permute-done.10
  110.4 1.2 collective-permute-done.9
  111.7 6.3 %collective-permute-done.8 = bf16[2,512,64]{1,2,0:T(8,128)(2,1)S(1)} collective-permute-done((bf16[2,512,64]{1,2,0:T(8,128)(2,1)S(1)}, bf16[2,512,64]{1,2,0:T(8,128)(2,1)S(1)}, u32[]{:S(2)}, u32[]{:S(2)}) %collective-permute-start.8) | collective-permute-done | bytes 131104 | tf_op jit(solution)/shard_map/ppermute | solution.py:26
  117.9 0.8 collective-permute-done.7
  118.7 0.8 fusion.33
  (16 shorter events, 0.2 us)
Async XLA Ops:
  6.5 70.2 %copy-start = (bf16[2,512,512]{2,1,0:T(8,128)(2,1)S(1)}, bf16[2,512,512]{2,1,0:T(8,128)(2,1)}, u32[]{:S(2)}) copy-start(bf16[2,512,512]{2,1,0:T(8,128)(2,1)} %param.19) | copy-start | bytes 3145732
  6.5 56.8 %all-gather.2.cloned.1.call-start = ((), (), s32[]{:S(2)}) async-start(), calls=%async_computation | async-start | bytes 4325376 | tf_op jit(solution)/shard_map/all_gather | solution.py:65
  7.3 17.7 %collective-permute-start = (f32[1,2,64]{2,1,0:T(2,128)}, f32[1,2,64]{2,1,0:T(2,128)S(1)}, u32[]{:S(2)}, u32[]{:S(2)}) collective-permute-start(f32[1,2,64]{2,1,0:T(2,128)} %bitcast.125), channel_id=1, source_target_pairs={{0,1},{1,2},{2,3},{3,4},{4,5},{5,6},{6,7},{7,0},{8,9},{9,10},{10,1... | collective-permute-start | bytes 1544 | tf_op jit(solution)/shard_map/ppermute | solution.py:15
  9.3 18.5 %collective-permute-start.1 = (f32[1,2,64]{2,1,0:T(2,128)}, f32[1,2,64]{2,1,0:T(2,128)S(1)}, u32[]{:S(2)}, u32[]{:S(2)}) collective-permute-start(f32[1,2,64]{2,1,0:T(2,128)} %bitcast.126), channel_id=1, source_target_pairs={{0,2},{1,3},{2,4},{3,5},{4,6},{5,7},{6,0},{7,1},{8,10},{9,11},{10,... | collective-permute-start | bytes 1544 | tf_op jit(solution)/shard_map/ppermute | solution.py:15
  12.5 16.3 %collective-permute-start.2 = (f32[1,2,64]{2,1,0:T(2,128)}, f32[1,2,64]{2,1,0:T(2,128)S(1)}, u32[]{:S(2)}, u32[]{:S(2)}) collective-permute-start(f32[1,2,64]{2,1,0:T(2,128)} %bitcast.127), channel_id=1, source_target_pairs={{0,3},{1,4},{2,5},{3,6},{4,7},{5,0},{6,1},{7,2},{8,11},{9,12},{10,... | collective-permute-start | bytes 1544 | tf_op jit(solution)/shard_map/ppermute | solution.py:15
  16.6 12.3 %collective-permute-start.3 = (f32[1,2,64]{2,1,0:T(2,128)}, f32[1,2,64]{2,1,0:T(2,128)S(1)}, u32[]{:S(2)}, u32[]{:S(2)}) collective-permute-start(f32[1,2,64]{2,1,0:T(2,128)} %bitcast.128), channel_id=1, source_target_pairs={{0,4},{1,5},{2,6},{3,7},{4,0},{5,1},{6,2},{7,3},{8,12},{9,13},{10,... | collective-permute-start | bytes 1544 | tf_op jit(solution)/shard_map/ppermute | solution.py:15
  17.1 11.8 %collective-permute-start.4 = (f32[1,2,64]{2,1,0:T(2,128)}, f32[1,2,64]{2,1,0:T(2,128)S(1)}, u32[]{:S(2)}, u32[]{:S(2)}) collective-permute-start(f32[1,2,64]{2,1,0:T(2,128)} %bitcast.129), channel_id=1, source_target_pairs={{0,5},{1,6},{2,7},{3,0},{4,1},{5,2},{6,3},{7,4},{8,13},{9,14},{10,... | collective-permute-start | bytes 1544 | tf_op jit(solution)/shard_map/ppermute | solution.py:15
  25.0 4.8 %collective-permute-start.5 = (f32[1,2,64]{2,1,0:T(2,128)}, f32[1,2,64]{2,1,0:T(2,128)S(1)}, u32[]{:S(2)}, u32[]{:S(2)}) collective-permute-start(f32[1,2,64]{2,1,0:T(2,128)} %bitcast.131), channel_id=1, source_target_pairs={{0,6},{1,7},{2,0},{3,1},{4,2},{5,3},{6,4},{7,5},{8,14},{9,15},{10,... | collective-permute-start | bytes 1544 | tf_op jit(solution)/shard_map/ppermute | solution.py:15
  27.7 3.9 %collective-permute-start.6 = (f32[1,2,64]{2,1,0:T(2,128)}, f32[1,2,64]{2,1,0:T(2,128)S(1)}, u32[]{:S(2)}, u32[]{:S(2)}) collective-permute-start(f32[1,2,64]{2,1,0:T(2,128)} %bitcast.132), channel_id=1, source_target_pairs={{0,7},{1,0},{2,1},{3,2},{4,3},{5,4},{6,5},{7,6},{8,15},{9,8},{10,9... | collective-permute-start | bytes 1544 | tf_op jit(solution)/shard_map/ppermute | solution.py:15
  70.1 6.7 %copy-start.2 = (bf16[2,512,512]{2,1,0:T(8,128)(2,1)S(1)}, bf16[2,512,512]{2,1,0:T(8,128)(2,1)}, u32[]{:S(2)}) copy-start(bf16[2,512,512]{2,1,0:T(8,128)(2,1)} %param.17) | copy-start | bytes 3145732
  76.8 3.9 %copy-start.3 = (bf16[2,512,512]{2,1,0:T(8,128)(2,1)S(1)}, bf16[2,512,512]{2,1,0:T(8,128)(2,1)}, u32[]{:S(2)}) copy-start(bf16[2,512,512]{2,1,0:T(8,128)(2,1)} %param.18) | copy-start | bytes 3145732
  76.8 3.9 %copy-start.4 = (f32[2,512]{1,0:T(2,128)S(1)}, f32[2,512]{1,0:T(2,128)}, u32[]{:S(2)}) copy-start(f32[2,512]{1,0:T(2,128)} %param.21) | copy-start | bytes 12292
  80.7 2.6 %copy-start.1 = (bf16[2,512,512]{2,1,0:T(8,128)(2,1)S(1)}, bf16[2,512,512]{2,1,0:T(8,128)(2,1)}, u32[]{:S(2)}) copy-start(bf16[2,512,512]{2,1,0:T(8,128)(2,1)} %param.16) | copy-start | bytes 3145732
  84.2 10.7 %collective-permute-start.13 = (bf16[2,512,64]{1,2,0:T(8,128)(2,1)S(1)}, bf16[2,512,64]{1,2,0:T(8,128)(2,1)S(1)}, u32[]{:S(2)}, u32[]{:S(2)}) collective-permute-start(bf16[2,512,64]{1,2,0:T(8,128)(2,1)S(1)} %get-tuple-element.10), channel_id=1, source_target_pairs={{0,7},{1,0},{2,1},{3,2},{4,3},{5,4},{6,5},{7,6},{8,15},{9,8},{10,9... | collective-permute-start | bytes 393224 | tf_op jit(solution)/shard_map/ppermute | solution.py:26
  87.6 11.6 %collective-permute-start.12 = (bf16[2,512,64]{1,2,0:T(8,128)(2,1)S(1)}, bf16[2,512,64]{1,2,0:T(8,128)(2,1)S(1)}, u32[]{:S(2)}, u32[]{:S(2)}) collective-permute-start(bf16[2,512,64]{1,2,0:T(8,128)(2,1)S(1)} %get-tuple-element.11), channel_id=1, source_target_pairs={{0,6},{1,7},{2,0},{3,1},{4,2},{5,3},{6,4},{7,5},{8,14},{9,15},{10,... | collective-permute-start | bytes 393224 | tf_op jit(solution)/shard_map/ppermute | solution.py:26
  89.7 20.7 %collective-permute-start.11 = (bf16[2,512,64]{1,2,0:T(8,128)(2,1)S(1)}, bf16[2,512,64]{1,2,0:T(8,128)(2,1)S(1)}, u32[]{:S(2)}, u32[]{:S(2)}) collective-permute-start(bf16[2,512,64]{1,2,0:T(8,128)(2,1)S(1)} %get-tuple-element.6), channel_id=1, source_target_pairs={{0,5},{1,6},{2,7},{3,0},{4,1},{5,2},{6,3},{7,4},{8,13},{9,14},{10,... | collective-permute-start | bytes 393224 | tf_op jit(solution)/shard_map/ppermute | solution.py:26
  90.9 19.5 %collective-permute-start.10 = (bf16[2,512,64]{1,2,0:T(8,128)(2,1)S(1)}, bf16[2,512,64]{1,2,0:T(8,128)(2,1)S(1)}, u32[]{:S(2)}, u32[]{:S(2)}) collective-permute-start(bf16[2,512,64]{1,2,0:T(8,128)(2,1)S(1)} %get-tuple-element.7), channel_id=1, source_target_pairs={{0,4},{1,5},{2,6},{3,7},{4,0},{5,1},{6,2},{7,3},{8,12},{9,13},{10,... | collective-permute-start | bytes 393224 | tf_op jit(solution)/shard_map/ppermute | solution.py:26
  94.9 16.8 %collective-permute-start.9 = (bf16[2,512,64]{1,2,0:T(8,128)(2,1)S(1)}, bf16[2,512,64]{1,2,0:T(8,128)(2,1)S(1)}, u32[]{:S(2)}, u32[]{:S(2)}) collective-permute-start(bf16[2,512,64]{1,2,0:T(8,128)(2,1)S(1)} %get-tuple-element.8), channel_id=1, source_target_pairs={{0,3},{1,4},{2,5},{3,6},{4,7},{5,0},{6,1},{7,2},{8,11},{9,12},{10,... | collective-permute-start | bytes 393224 | tf_op jit(solution)/shard_map/ppermute | solution.py:26
  94.9 23.1 %collective-permute-start.8 = (bf16[2,512,64]{1,2,0:T(8,128)(2,1)S(1)}, bf16[2,512,64]{1,2,0:T(8,128)(2,1)S(1)}, u32[]{:S(2)}, u32[]{:S(2)}) collective-permute-start(bf16[2,512,64]{1,2,0:T(8,128)(2,1)S(1)} %get-tuple-element.9), channel_id=1, source_target_pairs={{0,2},{1,3},{2,4},{3,5},{4,6},{5,7},{6,0},{7,1},{8,10},{9,11},{10,... | collective-permute-start | bytes 393224 | tf_op jit(solution)/shard_map/ppermute | solution.py:26
  99.1 19.6 %collective-permute-start.7 = (bf16[2,512,64]{1,2,0:T(8,128)(2,1)S(1)}, bf16[2,512,64]{1,2,0:T(8,128)(2,1)S(1)}, u32[]{:S(2)}, u32[]{:S(2)}) collective-permute-start(bf16[2,512,64]{1,2,0:T(8,128)(2,1)S(1)} %get-tuple-element.5), channel_id=1, source_target_pairs={{0,1},{1,2},{2,3},{3,4},{4,5},{5,6},{6,7},{7,0},{8,9},{9,10},{10,1... | collective-permute-start | bytes 393224 | tf_op jit(solution)/shard_map/ppermute | solution.py:26
Sparse Core Ops, SparseCore 0:
  9.9 53.4 all-gather.1
where the time goes:
time: 127 us; the launch traced here: 126 us
  waiting for transfers between devices  54.3 us (43%)
  starting transfers between devices  33.7 us (27%)
  matrix products  20.7 us (16%)
  between operations  13.6 us (11%)
  local copies, waits for them, and re-layouts  3.32 us (3%)
    all_gather x1, waiting for transfers between devices, local(): everything = lax.all_gather(block_vec, 'blk', axis=0, tiled=True)  31.5 us
    ppermute x7, waiting for transfers between devices, scatter_sum(): got = lax.ppermute(send, axis, [(j, (j + k) % n) for j in range(n)])  19.4 us
    ppermute x7, starting transfers between devices, exchange(): got = lax.ppermute(send, axis, [(j, (j + k) % n) for j in range(n)])  18.6 us
    ppermute x7, starting transfers between devices, scatter_sum(): got = lax.ppermute(send, axis, [(j, (j + k) % n) for j in range(n)])  15.1 us
    dot_general x1, matrix products, local(): jnp.einsum('ks,srn->krn', weights, everything, preferred_element_type=jnp...  6.75 us
    dot_general x1, matrix products, local(): jnp.einsum('tab,ktbc->kac', left_part, right_done, preferred_element_type...  6.65 us
    dot_general x1, matrix products, local(): jnp.einsum('jrn,jmn->jrm', dual_cols, right_dual, preferred_element_type=...  3.93 us
    ppermute x7, waiting for transfers between devices, exchange(): got = lax.ppermute(send, axis, [(j, (j + k) % n) for j in range(n)])  2.61 us
  transfers between devices with their start and end apart: 15, of which 8 were waited for; matrix products, arithmetic and copies ran while one was open for 3% of the time, Pallas kernels for 0%

commit v1 on v0

--- a/solution.py
+++ b/solution.py
@@ -60,11 +60,20 @@
     key_onehot = (
         target_term[..., None] == jnp.arange(local_blocks * term_total)[None, None, :]
     ).astype(jnp.float32) * live_mask[..., None]
-    source_onehot = (source[..., None] == jnp.arange(all_count)[None, None, :]).astype(jnp.float32)
-    weights = jnp.einsum("gqk,gqs->ks", key_onehot, source_onehot).astype(jnp.bfloat16)
-    everything = lax.all_gather(block_vec, "blk", axis=0, tiled=True)
-    pooled = jnp.einsum(
-        "ks,srn->krn", weights, everything, preferred_element_type=jnp.float32
+    core = owner % 2
+    half_index = jnp.arange(all_count // 2, dtype=jnp.int32)
+    mine_ids = ((half_index // local_blocks) * 2 + core) * local_blocks + half_index % local_blocks
+    other_ids = ((half_index // local_blocks) * 2 + 1 - core) * local_blocks + half_index % local_blocks
+    mine_onehot = (source[..., None] == mine_ids[None, None, :]).astype(jnp.float32)
+    other_onehot = (source[..., None] == other_ids[None, None, :]).astype(jnp.float32)
+    weights_mine = jnp.einsum("gqk,gqs->ks", key_onehot, mine_onehot).astype(jnp.bfloat16)
+    weights_other = jnp.einsum("gqk,gqs->ks", key_onehot, other_onehot).astype(jnp.bfloat16)
+    same_core = [[j for j in range(groups) if j % 2 == r] for r in range(2)]
+    half = lax.all_gather(block_vec, "blk", axis=0, tiled=True, axis_index_groups=same_core)
+    other = lax.ppermute(half, "blk", [(j, j ^ 1) for j in range(groups)])
+    pooled = (
+        jnp.einsum("ks,srn->krn", weights_mine, half, preferred_element_type=jnp.float32)
+        + jnp.einsum("ks,srn->krn", weights_other, other, preferred_element_type=jnp.float32)
     ).astype(jnp.bfloat16)
     pooled = pooled.reshape(local_blocks, term_total, row_count, width_two)
     right_done = jnp.einsum(

time: 127 us -> 142 us (1.12)
  waiting for transfers between devices: 54.3 us -> 68.2 us
  local copies, waits for them, and re-layouts: 3.32 us -> 5.28 us
    all_gather x1, waiting for transfers between devices: 31.5 us -> 54.8 us  [local(): lax.all_gather(block_vec, 'blk', axis=0, tiled=True, axis_index_groups=sa...]
    ppermute x7, waiting for transfers between devices: 19.4 us -> 10.6 us  [scatter_sum(): got = lax.ppermute(send, axis, [(j, (j + k) % n) for j in range(n)])]
    all_gather x0 -> x1, local copies, waits for them, and re-layouts: none -> 4.23 us  [local(): lax.all_gather(block_vec, 'blk', axis=0, tiled=True, axis_index_groups=sa...]
    ppermute x7, starting transfers between devices: 18.6 us -> 17.2 us  [exchange(): got = lax.ppermute(send, axis, [(j, (j + k) % n) for j in range(n)])]
    dot_general x1 -> x2, matrix products: 6.75 us -> 5.66 us  [the longest x1 2.83 us: local(): jnp.einsum('ks,srn->krn', weights_other, other, preferred_element_type=jn...]
  transfers between devices with their start and end apart: 15 -> 16, of which waited for: 8 -> 6; matrix products, arithmetic and copies ran while one was open for 3% -> 3% of each run, Pallas kernels for 0% -> 0%
where the time goes in v1:
time: 142 us; the launch traced here: 141 us
  waiting for transfers between devices  68.2 us (48%)
  starting transfers between devices  33.6 us (24%)
  matrix products  19.6 us (14%)
  between operations  13.7 us (10%)
  local copies, waits for them, and re-layouts  5.28 us (4%)
    all_gather x1, waiting for transfers between devices, local(): lax.all_gather(block_vec, 'blk', axis=0, tiled=True, axis_index_groups=sa...  54.8 us
    ppermute x7, starting transfers between devices, exchange(): got = lax.ppermute(send, axis, [(j, (j + k) % n) for j in range(n)])  17.2 us
    ppermute x7, starting transfers between devices, scatter_sum(): got = lax.ppermute(send, axis, [(j, (j + k) % n) for j in range(n)])  16.4 us
    ppermute x7, waiting for transfers between devices, scatter_sum(): got = lax.ppermute(send, axis, [(j, (j + k) % n) for j in range(n)])  10.6 us
    dot_general x1, matrix products, local(): jnp.einsum('tab,ktbc->kac', left_part, right_done, preferred_element_type...  6.67 us
    all_gather x1, local copies, waits for them, and re-layouts, local(): lax.all_gather(block_vec, 'blk', axis=0, tiled=True, axis_index_groups=sa...  4.23 us
    dot_general x1, matrix products, local(): jnp.einsum('jrn,jmn->jrm', dual_cols, right_dual, preferred_element_type=...  3.93 us
  transfers between devices with their start and end apart: 16, of which 6 were waited for; matrix products, arithmetic and copies ran while one was open for 3% of the time, Pallas kernels for 0%

profile of v1, /device:TPU:24, one launch (start us, length us, event | category | flops | bytes accessed | tf_op | source)
XLA Modules:
  0.0 141.1 jit_solution(7317838922021765416)
XLA Ops:
  6.5 0.7 all-gather.2.cloned.1.call-update
  7.3 54.8 %all-gather.2.cloned.1.call-done = bf16[32,64,512]{2,1,0:T(8,128)(2,1)} async-done(((bf16[2,64,512]{2,1,0:T(8,128)(2,1)}), bf16[32,64,512]{2,1,0:T(8,128)(2,1)}) %all-gather.2.cloned.1.call-update) | async-done | bytes 2097168 | tf_op jit(solution)/shard_map/all_gather | solution.py:72
  62.1 4.2 %copy.42 = bf16[32,64,512]{2,0,1:T(8,128)(2,1)} copy(bf16[32,64,512]{2,1,0:T(8,128)(2,1)} %all-gather.2.cloned.1.call-done) | data formatting | bytes 4194304 | tf_op jit(solution)/shard_map/all_gather | solution.py:72
  66.3 0.0 collective-permute-start
  66.3 1.6 %collective-permute-start.1 = (f32[1,2,64]{2,1,0:T(2,128)S(1)}, f32[1,2,64]{2,1,0:T(2,128)S(1)}, u32[]{:S(2)}, u32[]{:S(2)}) collective-permute-start(f32[1,2,64]{2,1,0:T(2,128)S(1)} %bitcast.138), channel_id=1, source_target_pairs={{0,1},{1,2},{2,3},{3,4},{4,5},{5,6},{6,7},{7,0},{8,9},{9,10},{10,1... | collective-permute-start | bytes 1544 | tf_op jit(solution)/shard_map/ppermute | solution.py:15
  67.9 2.5 %collective-permute-start.2 = (f32[1,2,64]{2,1,0:T(2,128)S(1)}, f32[1,2,64]{2,1,0:T(2,128)S(1)}, u32[]{:S(2)}, u32[]{:S(2)}) collective-permute-start(f32[1,2,64]{2,1,0:T(2,128)S(1)} %bitcast.139), channel_id=1, source_target_pairs={{0,2},{1,3},{2,4},{3,5},{4,6},{5,7},{6,0},{7,1},{8,10},{9,11},{10,... | collective-permute-start | bytes 1544 | tf_op jit(solution)/shard_map/ppermute | solution.py:15
  70.4 2.9 %collective-permute-start.3 = (f32[1,2,64]{2,1,0:T(2,128)S(1)}, f32[1,2,64]{2,1,0:T(2,128)S(1)}, u32[]{:S(2)}, u32[]{:S(2)}) collective-permute-start(f32[1,2,64]{2,1,0:T(2,128)S(1)} %bitcast.140), channel_id=1, source_target_pairs={{0,3},{1,4},{2,5},{3,6},{4,7},{5,0},{6,1},{7,2},{8,11},{9,12},{10,... | collective-permute-start | bytes 1544 | tf_op jit(solution)/shard_map/ppermute | solution.py:15
  73.4 2.0 %collective-permute-start.4 = (f32[1,2,64]{2,1,0:T(2,128)S(1)}, f32[1,2,64]{2,1,0:T(2,128)S(1)}, u32[]{:S(2)}, u32[]{:S(2)}) collective-permute-start(f32[1,2,64]{2,1,0:T(2,128)S(1)} %bitcast.141), channel_id=1, source_target_pairs={{0,4},{1,5},{2,6},{3,7},{4,0},{5,1},{6,2},{7,3},{8,12},{9,13},{10,... | collective-permute-start | bytes 1544 | tf_op jit(solution)/shard_map/ppermute | solution.py:15
  75.4 0.2 constant_dynamic-slice_fusion
  75.5 0.1 copy.41
  75.7 0.2 dynamic-slice_reduce_fusion
  76.0 0.0 collective-permute-done.1
  76.0 3.2 %collective-permute-start.5 = (f32[1,2,64]{2,1,0:T(2,128)S(1)}, f32[1,2,64]{2,1,0:T(2,128)S(1)}, u32[]{:S(2)}, u32[]{:S(2)}) collective-permute-start(f32[1,2,64]{2,1,0:T(2,128)S(1)} %bitcast.143), channel_id=1, source_target_pairs={{0,5},{1,6},{2,7},{3,0},{4,1},{5,2},{6,3},{7,4},{8,13},{9,14},{10,... | collective-permute-start | bytes 1544 | tf_op jit(solution)/shard_map/ppermute | solution.py:15
  79.3 0.0 collective-permute-done.2
  79.3 3.5 %collective-permute-start.6 = (f32[1,2,64]{2,1,0:T(2,128)S(1)}, f32[1,2,64]{2,1,0:T(2,128)S(1)}, u32[]{:S(2)}, u32[]{:S(2)}) collective-permute-start(f32[1,2,64]{2,1,0:T(2,128)S(1)} %bitcast.144), channel_id=1, source_target_pairs={{0,6},{1,7},{2,0},{3,1},{4,2},{5,3},{6,4},{7,5},{8,14},{9,15},{10,... | collective-permute-start | bytes 1544 | tf_op jit(solution)/shard_map/ppermute | solution.py:15
  82.8 0.0 collective-permute-done.3
  82.8 1.4 %collective-permute-start.7 = (f32[1,2,64]{2,1,0:T(2,128)S(1)}, f32[1,2,64]{2,1,0:T(2,128)S(1)}, u32[]{:S(2)}, u32[]{:S(2)}) collective-permute-start(f32[1,2,64]{2,1,0:T(2,128)S(1)} %bitcast.145), channel_id=1, source_target_pairs={{0,7},{1,0},{2,1},{3,2},{4,3},{5,4},{6,5},{7,6},{8,15},{9,8},{10,9... | collective-permute-start | bytes 1544 | tf_op jit(solution)/shard_map/ppermute | solution.py:15
  84.2 0.0 collective-permute-done.4
  84.3 0.0 collective-permute-done.5
  84.3 0.0 collective-permute-done.6
  84.4 2.0 %collective-permute-done.7 = f32[1,2,64]{2,1,0:T(2,128)S(1)} collective-permute-done((f32[1,2,64]{2,1,0:T(2,128)S(1)}, f32[1,2,64]{2,1,0:T(2,128)S(1)}, u32[]{:S(2)}, u32[]{:S(2)}) %collective-permute-start.7) | collective-permute-done | bytes 544 | tf_op jit(solution)/shard_map/ppermute | solution.py:15
  86.4 0.2 dynamic_update_slice.32
  86.6 0.1 add.291
  86.7 2.8 %fusion.23 = f32[16,64,512]{2,0,1:T(8,128)} fusion(s32[32]{0:T(128)S(1)} %get-tuple-element.15, s32[32,2]{0,1:T(2,128)S(1)} %get-tuple-element.13, bf16[32,2]{0,1:T(2,128)(2,1)S(1)} %compare_convert_fusion, s32[32,2]{0,1:T(2,128)S(1)} %get-tuple-element.12, bf16[32,64,512]{2,1,0:T(8,128)(2,1)S(1)} %copy-done.1), kind=kOutput, calls=%fused_computation.23 | convolution fusion | flops 33624064 | bytes 4195072 | tf_op jit(solution)/shard_map/ks,srn->krn/dot_general | solution.py:75
  89.5 0.0 collective-permute-done
  89.5 2.8 %fusion.9 = bf16[2,8,64,512]{3,1,0,2:T(8,128)(2,1)S(1)} fusion(f32[16,64,512]{2,0,1:T(8,128)} %fusion.23, bf16[32,64,512]{2,0,1:T(8,128)(2,1)} %collective-permute-done, s32[32]{0:T(128)S(1)} %get-tuple-element.14, s32[32,2]{0,1:T(2,128)S(1)} %get-tuple-element.13, bf16[32,2]{0,1:T(2,128)(2,1)S(1)} %compare_convert_fusion, s32[32,2]{0,1:T(2,128)S(1)} %get-tuple-element.12), kind=kOutput, calls=%fused_computation.11 | convolution fusion | flops 34672640 | bytes 5243648 | tf_op jit(solution)/shard_map/ks,srn->krn/dot_general | solution.py:76
  92.4 0.0 copy-start.6
  92.4 6.7 %bitcast_convert_fusion = bf16[2,512,512]{2,1,0:T(8,128)(2,1)} fusion(bf16[8,512,512]{2,1,0:T(8,128)(2,1)} %param.12, s32[]{:T(128)S(6)} %select_n.179, bf16[8,512,512]{2,1,0:T(8,128)(2,1)} %param.13, bf16[2,8,64,512]{3,1,0,2:T(8,128)(2,1)S(1)} %fusion.9), kind=kOutput, calls=%fused_computation.2 | convolution fusion | flops 1074790400 | bytes 7340036 | tf_op jit(solution)/shard_map/tab,ktbc->kac/dot_general | solution.py:85
  99.0 0.0 copy-start.8
  99.1 3.9 %fusion.5 = f32[2,512,512]{2,1,0:T(8,128)} fusion(bf16[2,512,512]{2,1,0:T(8,128)(2,1)S(1)} %copy-done, bf16[2,512,512]{2,1,0:T(8,128)(2,1)} %bitcast_convert_fusion, bf16[2,512,512]{2,1,0:T(8,128)(2,1)S(1)} %copy-done.6), kind=kOutput, calls=%fused_computation.9 | convolution fusion | flops 1074266112 | bytes 5242880 | tf_op jit(solution)/shard_map/jrn,jmn->jrm/dot_general | solution.py:91
  103.0 2.6 %convolution_convert_fusion.1 = bf16[2,512,512]{1,2,0:T(8,128)(2,1)S(1)} fusion(bf16[2,512,512]{2,1,0:T(8,128)(2,1)S(1)} %copy-done.7, f32[2,512,512]{2,1,0:T(8,128)} %fusion.5, f32[2,512]{1,0:T(2,128)S(1)} %copy-done.8, f32[2,512]{1,0:T(2,128)S(1)} %add.291), kind=kOutput, calls=%fused_computation.7 | convolution fusion | flops 538968064 | bytes 4202496 | tf_op jit(solution)/shard_map/jrm,jkm->jrk/dot_general | solution.py:93
  105.6 0.7 convolution_convert_fusion
  106.3 0.1 dynamic-slice_bitcast_fusion.6
  106.4 0.3 collective-permute-start.10
  106.7 5.6 %collective-permute-start.11 = (bf16[2,512,64]{1,2,0:T(8,128)(2,1)S(1)}, bf16[2,512,64]{1,2,0:T(8,128)(2,1)S(1)}, u32[]{:S(2)}, u32[]{:S(2)}) collective-permute-start(bf16[2,512,64]{1,2,0:T(8,128)(2,1)S(1)} %get-tuple-element.7), channel_id=1, source_target_pairs={{0,4},{1,5},{2,6},{3,7},{4,0},{5,1},{6,2},{7,3},{8,12},{9,13},{10,... | collective-permute-start | bytes 393224 | tf_op jit(solution)/shard_map/ppermute | solution.py:26
  112.3 0.3 collective-permute-start.12
  112.6 2.6 %collective-permute-start.13 = (bf16[2,512,64]{1,2,0:T(8,128)(2,1)S(1)}, bf16[2,512,64]{1,2,0:T(8,128)(2,1)S(1)}, u32[]{:S(2)}, u32[]{:S(2)}) collective-permute-start(bf16[2,512,64]{1,2,0:T(8,128)(2,1)S(1)} %get-tuple-element.11), channel_id=1, source_target_pairs={{0,6},{1,7},{2,0},{3,1},{4,2},{5,3},{6,4},{7,5},{8,14},{9,15},{10,... | collective-permute-start | bytes 393224 | tf_op jit(solution)/shard_map/ppermute | solution.py:26
  115.2 1.1 collective-permute-start.14
  116.3 1.7 %collective-permute-done.10 = bf16[2,512,64]{1,2,0:T(8,128)(2,1)S(1)} collective-permute-done((bf16[2,512,64]{1,2,0:T(8,128)(2,1)S(1)}, bf16[2,512,64]{1,2,0:T(8,128)(2,1)S(1)}, u32[]{:S(2)}, u32[]{:S(2)}) %collective-permute-start.10) | collective-permute-done | bytes 131104 | tf_op jit(solution)/shard_map/ppermute | solution.py:26
  118.0 3.0 %collective-permute-start.8 = (bf16[2,512,64]{1,2,0:T(8,128)(2,1)S(1)}, bf16[2,512,64]{1,2,0:T(8,128)(2,1)S(1)}, u32[]{:S(2)}, u32[]{:S(2)}) collective-permute-start(bf16[2,512,64]{1,2,0:T(8,128)(2,1)S(1)} %get-tuple-element.5), channel_id=1, source_target_pairs={{0,1},{1,2},{2,3},{3,4},{4,5},{5,6},{6,7},{7,0},{8,9},{9,10},{10,1... | collective-permute-start | bytes 393224 | tf_op jit(solution)/shard_map/ppermute | solution.py:26
  121.0 1.7 %collective-permute-done.11 = bf16[2,512,64]{1,2,0:T(8,128)(2,1)S(1)} collective-permute-done((bf16[2,512,64]{1,2,0:T(8,128)(2,1)S(1)}, bf16[2,512,64]{1,2,0:T(8,128)(2,1)S(1)}, u32[]{:S(2)}, u32[]{:S(2)}) %collective-permute-start.11) | collective-permute-done | bytes 131104 | tf_op jit(solution)/shard_map/ppermute | solution.py:26
  122.7 3.6 %collective-permute-start.9 = (bf16[2,512,64]{1,2,0:T(8,128)(2,1)S(1)}, bf16[2,512,64]{1,2,0:T(8,128)(2,1)S(1)}, u32[]{:S(2)}, u32[]{:S(2)}) collective-permute-start(bf16[2,512,64]{1,2,0:T(8,128)(2,1)S(1)} %get-tuple-element.9), channel_id=1, source_target_pairs={{0,2},{1,3},{2,4},{3,5},{4,6},{5,7},{6,0},{7,1},{8,10},{9,11},{10,... | collective-permute-start | bytes 393224 | tf_op jit(solution)/shard_map/ppermute | solution.py:26
  126.2 0.0 collective-permute-done.12
  126.2 5.0 %collective-permute-done.13 = bf16[2,512,64]{1,2,0:T(8,128)(2,1)S(1)} collective-permute-done((bf16[2,512,64]{1,2,0:T(8,128)(2,1)S(1)}, bf16[2,512,64]{1,2,0:T(8,128)(2,1)S(1)}, u32[]{:S(2)}, u32[]{:S(2)}) %collective-permute-start.13) | collective-permute-done | bytes 131104 | tf_op jit(solution)/shard_map/ppermute | solution.py:26
  131.2 2.2 %collective-permute-done.14 = bf16[2,512,64]{1,2,0:T(8,128)(2,1)S(1)} collective-permute-done((bf16[2,512,64]{1,2,0:T(8,128)(2,1)S(1)}, bf16[2,512,64]{1,2,0:T(8,128)(2,1)S(1)}, u32[]{:S(2)}, u32[]{:S(2)}) %collective-permute-start.14) | collective-permute-done | bytes 131104 | tf_op jit(solution)/shard_map/ppermute | solution.py:26
  133.5 0.0 collective-permute-done.8
  133.5 0.0 collective-permute-done.9
  133.5 0.8 fusion.29
  (29 shorter events, 0.3 us)
Async XLA Ops:
  6.5 92.5 %copy-start = (bf16[2,512,512]{2,1,0:T(8,128)(2,1)S(1)}, bf16[2,512,512]{2,1,0:T(8,128)(2,1)}, u32[]{:S(2)}) copy-start(bf16[2,512,512]{2,1,0:T(8,128)(2,1)} %param.19) | copy-start | bytes 3145732
  6.5 55.6 %all-gather.2.cloned.1.call-start = ((), (), s32[]{:S(2)}) async-start(), calls=%async_computation | async-start | bytes 2228224 | tf_op jit(solution)/shard_map/all_gather | solution.py:72
  7.3 59.1 %copy-start.5 = (f32[2,64]{1,0:T(2,128)S(1)}, f32[2,64]{1,0:T(2,128)}, u32[]{:S(2)}) copy-start(f32[2,64]{1,0:T(2,128)} %param.20) | copy-start | bytes 1540
  7.3 68.1 %copy-start.3 = (s32[32,32,2,3]{1,2,3,0:T(2,128)S(1)}, s32[32,32,2,3]{1,2,3,0:T(2,128)}, u32[]{:S(2)}) copy-start(s32[32,32,2,3]{1,2,3,0:T(2,128)} %param.14) | copy-start | bytes 73732
  7.3 68.4 %copy-start.4 = (s32[32,32]{1,0:T(8,128)S(1)}, s32[32,32]{1,0:T(8,128)}, u32[]{:S(2)}) copy-start(s32[32,32]{1,0:T(8,128)} %param.15) | copy-start | bytes 12292
  62.1 24.6 %copy-start.1 = (bf16[32,64,512]{2,1,0:T(8,128)(2,1)S(1)}, bf16[32,64,512]{2,1,0:T(8,128)(2,1)}, u32[]{:S(2)}) copy-start(bf16[32,64,512]{2,1,0:T(8,128)(2,1)} %all-gather.2.cloned.1.call-done) | copy-start | bytes 6291460
  66.3 23.2 %collective-permute-start = (bf16[32,64,512]{2,0,1:T(8,128)(2,1)}, bf16[32,64,512]{2,0,1:T(8,128)(2,1)}, u32[]{:S(2)}, u32[]{:S(2)}) collective-permute-start(bf16[32,64,512]{2,0,1:T(8,128)(2,1)} %copy.42), channel_id=1, source_target_pairs={{0,8},{8,0},{16,24},{24,16},{32,40},{40,32},{48,56},{56,48},{64,72... | collective-permute-start | bytes 6291464 | tf_op jit(solution)/shard_map/ppermute | solution.py:73
  66.3 9.7 %collective-permute-start.1 = (f32[1,2,64]{2,1,0:T(2,128)S(1)}, f32[1,2,64]{2,1,0:T(2,128)S(1)}, u32[]{:S(2)}, u32[]{:S(2)}) collective-permute-start(f32[1,2,64]{2,1,0:T(2,128)S(1)} %bitcast.138), channel_id=1, source_target_pairs={{0,1},{1,2},{2,3},{3,4},{4,5},{5,6},{6,7},{7,0},{8,9},{9,10},{10,1... | collective-permute-start | bytes 1544 | tf_op jit(solution)/shard_map/ppermute | solution.py:15
  67.9 11.4 %collective-permute-start.2 = (f32[1,2,64]{2,1,0:T(2,128)S(1)}, f32[1,2,64]{2,1,0:T(2,128)S(1)}, u32[]{:S(2)}, u32[]{:S(2)}) collective-permute-start(f32[1,2,64]{2,1,0:T(2,128)S(1)} %bitcast.139), channel_id=1, source_target_pairs={{0,2},{1,3},{2,4},{3,5},{4,6},{5,7},{6,0},{7,1},{8,10},{9,11},{10,... | collective-permute-start | bytes 1544 | tf_op jit(solution)/shard_map/ppermute | solution.py:15
  70.4 12.3 %collective-permute-start.3 = (f32[1,2,64]{2,1,0:T(2,128)S(1)}, f32[1,2,64]{2,1,0:T(2,128)S(1)}, u32[]{:S(2)}, u32[]{:S(2)}) collective-permute-start(f32[1,2,64]{2,1,0:T(2,128)S(1)} %bitcast.140), channel_id=1, source_target_pairs={{0,3},{1,4},{2,5},{3,6},{4,7},{5,0},{6,1},{7,2},{8,11},{9,12},{10,... | collective-permute-start | bytes 1544 | tf_op jit(solution)/shard_map/ppermute | solution.py:15
  73.4 10.9 %collective-permute-start.4 = (f32[1,2,64]{2,1,0:T(2,128)S(1)}, f32[1,2,64]{2,1,0:T(2,128)S(1)}, u32[]{:S(2)}, u32[]{:S(2)}) collective-permute-start(f32[1,2,64]{2,1,0:T(2,128)S(1)} %bitcast.141), channel_id=1, source_target_pairs={{0,4},{1,5},{2,6},{3,7},{4,0},{5,1},{6,2},{7,3},{8,12},{9,13},{10,... | collective-permute-start | bytes 1544 | tf_op jit(solution)/shard_map/ppermute | solution.py:15
  76.0 8.2 %collective-permute-start.5 = (f32[1,2,64]{2,1,0:T(2,128)S(1)}, f32[1,2,64]{2,1,0:T(2,128)S(1)}, u32[]{:S(2)}, u32[]{:S(2)}) collective-permute-start(f32[1,2,64]{2,1,0:T(2,128)S(1)} %bitcast.143), channel_id=1, source_target_pairs={{0,5},{1,6},{2,7},{3,0},{4,1},{5,2},{6,3},{7,4},{8,13},{9,14},{10,... | collective-permute-start | bytes 1544 | tf_op jit(solution)/shard_map/ppermute | solution.py:15
  79.3 5.0 %collective-permute-start.6 = (f32[1,2,64]{2,1,0:T(2,128)S(1)}, f32[1,2,64]{2,1,0:T(2,128)S(1)}, u32[]{:S(2)}, u32[]{:S(2)}) collective-permute-start(f32[1,2,64]{2,1,0:T(2,128)S(1)} %bitcast.144), channel_id=1, source_target_pairs={{0,6},{1,7},{2,0},{3,1},{4,2},{5,3},{6,4},{7,5},{8,14},{9,15},{10,... | collective-permute-start | bytes 1544 | tf_op jit(solution)/shard_map/ppermute | solution.py:15
  82.8 3.6 %collective-permute-start.7 = (f32[1,2,64]{2,1,0:T(2,128)S(1)}, f32[1,2,64]{2,1,0:T(2,128)S(1)}, u32[]{:S(2)}, u32[]{:S(2)}) collective-permute-start(f32[1,2,64]{2,1,0:T(2,128)S(1)} %bitcast.145), channel_id=1, source_target_pairs={{0,7},{1,0},{2,1},{3,2},{4,3},{5,4},{6,5},{7,6},{8,15},{9,8},{10,9... | collective-permute-start | bytes 1544 | tf_op jit(solution)/shard_map/ppermute | solution.py:15
  92.4 6.7 %copy-start.6 = (bf16[2,512,512]{2,1,0:T(8,128)(2,1)S(1)}, bf16[2,512,512]{2,1,0:T(8,128)(2,1)}, u32[]{:S(2)}) copy-start(bf16[2,512,512]{2,1,0:T(8,128)(2,1)} %param.17) | copy-start | bytes 3145732
  99.0 3.9 %copy-start.7 = (bf16[2,512,512]{2,1,0:T(8,128)(2,1)S(1)}, bf16[2,512,512]{2,1,0:T(8,128)(2,1)}, u32[]{:S(2)}) copy-start(bf16[2,512,512]{2,1,0:T(8,128)(2,1)} %param.18) | copy-start | bytes 3145732
  99.0 3.9 %copy-start.8 = (f32[2,512]{1,0:T(2,128)S(1)}, f32[2,512]{1,0:T(2,128)}, u32[]{:S(2)}) copy-start(f32[2,512]{1,0:T(2,128)} %param.21) | copy-start | bytes 12292
  103.0 2.6 %copy-start.2 = (bf16[2,512,512]{2,1,0:T(8,128)(2,1)S(1)}, bf16[2,512,512]{2,1,0:T(8,128)(2,1)}, u32[]{:S(2)}) copy-start(bf16[2,512,512]{2,1,0:T(8,128)(2,1)} %param.16) | copy-start | bytes 3145732
  106.4 11.6 %collective-permute-start.10 = (bf16[2,512,64]{1,2,0:T(8,128)(2,1)S(1)}, bf16[2,512,64]{1,2,0:T(8,128)(2,1)S(1)}, u32[]{:S(2)}, u32[]{:S(2)}) collective-permute-start(bf16[2,512,64]{1,2,0:T(8,128)(2,1)S(1)} %get-tuple-element.8), channel_id=1, source_target_pairs={{0,3},{1,4},{2,5},{3,6},{4,7},{5,0},{6,1},{7,2},{8,11},{9,12},{10,... | collective-permute-start | bytes 393224 | tf_op jit(solution)/shard_map/ppermute | solution.py:26
  106.7 15.9 %collective-permute-start.11 = (bf16[2,512,64]{1,2,0:T(8,128)(2,1)S(1)}, bf16[2,512,64]{1,2,0:T(8,128)(2,1)S(1)}, u32[]{:S(2)}, u32[]{:S(2)}) collective-permute-start(bf16[2,512,64]{1,2,0:T(8,128)(2,1)S(1)} %get-tuple-element.7), channel_id=1, source_target_pairs={{0,4},{1,5},{2,6},{3,7},{4,0},{5,1},{6,2},{7,3},{8,12},{9,13},{10,... | collective-permute-start | bytes 393224 | tf_op jit(solution)/shard_map/ppermute | solution.py:26
  112.3 13.9 %collective-permute-start.12 = (bf16[2,512,64]{1,2,0:T(8,128)(2,1)S(1)}, bf16[2,512,64]{1,2,0:T(8,128)(2,1)S(1)}, u32[]{:S(2)}, u32[]{:S(2)}) collective-permute-start(bf16[2,512,64]{1,2,0:T(8,128)(2,1)S(1)} %get-tuple-element.6), channel_id=1, source_target_pairs={{0,5},{1,6},{2,7},{3,0},{4,1},{5,2},{6,3},{7,4},{8,13},{9,14},{10,... | collective-permute-start | bytes 393224 | tf_op jit(solution)/shard_map/ppermute | solution.py:26
  112.6 18.6 %collective-permute-start.13 = (bf16[2,512,64]{1,2,0:T(8,128)(2,1)S(1)}, bf16[2,512,64]{1,2,0:T(8,128)(2,1)S(1)}, u32[]{:S(2)}, u32[]{:S(2)}) collective-permute-start(bf16[2,512,64]{1,2,0:T(8,128)(2,1)S(1)} %get-tuple-element.11), channel_id=1, source_target_pairs={{0,6},{1,7},{2,0},{3,1},{4,2},{5,3},{6,4},{7,5},{8,14},{9,15},{10,... | collective-permute-start | bytes 393224 | tf_op jit(solution)/shard_map/ppermute | solution.py:26
  115.2 18.2 %collective-permute-start.14 = (bf16[2,512,64]{1,2,0:T(8,128)(2,1)S(1)}, bf16[2,512,64]{1,2,0:T(8,128)(2,1)S(1)}, u32[]{:S(2)}, u32[]{:S(2)}) collective-permute-start(bf16[2,512,64]{1,2,0:T(8,128)(2,1)S(1)} %get-tuple-element.10), channel_id=1, source_target_pairs={{0,7},{1,0},{2,1},{3,2},{4,3},{5,4},{6,5},{7,6},{8,15},{9,8},{10,9... | collective-permute-start | bytes 393224 | tf_op jit(solution)/shard_map/ppermute | solution.py:26
  118.0 15.4 %collective-permute-start.8 = (bf16[2,512,64]{1,2,0:T(8,128)(2,1)S(1)}, bf16[2,512,64]{1,2,0:T(8,128)(2,1)S(1)}, u32[]{:S(2)}, u32[]{:S(2)}) collective-permute-start(bf16[2,512,64]{1,2,0:T(8,128)(2,1)S(1)} %get-tuple-element.5), channel_id=1, source_target_pairs={{0,1},{1,2},{2,3},{3,4},{4,5},{5,6},{6,7},{7,0},{8,9},{9,10},{10,1... | collective-permute-start | bytes 393224 | tf_op jit(solution)/shard_map/ppermute | solution.py:26
  122.7 10.8 %collective-permute-start.9 = (bf16[2,512,64]{1,2,0:T(8,128)(2,1)S(1)}, bf16[2,512,64]{1,2,0:T(8,128)(2,1)S(1)}, u32[]{:S(2)}, u32[]{:S(2)}) collective-permute-start(bf16[2,512,64]{1,2,0:T(8,128)(2,1)S(1)} %get-tuple-element.9), channel_id=1, source_target_pairs={{0,2},{1,3},{2,4},{3,5},{4,6},{5,7},{6,0},{7,1},{8,10},{9,11},{10,... | collective-permute-start | bytes 393224 | tf_op jit(solution)/shard_map/ppermute | solution.py:26
Sparse Core Ops, SparseCore 0:
  9.8 52.2 all-gather.1

commit v2 on v0

--- a/solution.py
+++ b/solution.py
@@ -60,11 +60,55 @@
     key_onehot = (
         target_term[..., None] == jnp.arange(local_blocks * term_total)[None, None, :]
     ).astype(jnp.float32) * live_mask[..., None]
-    source_onehot = (source[..., None] == jnp.arange(all_count)[None, None, :]).astype(jnp.float32)
+    ring = 4
+    core = owner % 2
+    here_x = owner // (2 * ring)
+    here_y = (owner // 2) % ring
+    offsets = jnp.arange(ring, dtype=jnp.int32)
+    plane_group = (((here_x + offsets[None, :]) % ring) * ring + (here_y + offsets[:, None]) % ring) * 2
+    side_group = plane_group[None] + jnp.stack([core, 1 - core])[:, None, None]
+    block_ids = (side_group[..., None] * local_blocks + jnp.arange(local_blocks)).reshape(-1)
+    source_onehot = (source[..., None] == block_ids[None, None, :]).astype(jnp.float32)
     weights = jnp.einsum("gqk,gqs->ks", key_onehot, source_onehot).astype(jnp.bfloat16)
-    everything = lax.all_gather(block_vec, "blk", axis=0, tiled=True)
-    pooled = jnp.einsum(
-        "ks,srn->krn", weights, everything, preferred_element_type=jnp.float32
+    weights = weights.reshape(local_blocks * term_total, 2, ring, ring, local_blocks)
+
+    def move(piece, dx, dy, sibling=False):
+        pairs_list = []
+        for b in range(groups):
+            bx, by, bc = b // (2 * ring), (b // 2) % ring, b % 2
+            if sibling:
+                dest = b ^ 1
+            else:
+                dest = (((bx + dx) % ring) * ring + (by + dy) % ring) * 2 + bc
+            pairs_list.append((b, dest))
+        return lax.ppermute(piece, "blk", pairs_list)
+
+    half_rows = row_count // 2
+    from_left = move(block_vec, 1, 0)
+    from_right = move(block_vec, -1, 0)
+    far = jnp.concatenate(
+        [move(from_left[:, :half_rows], 1, 0), move(from_right[:, half_rows:], -1, 0)], axis=1
+    )
+    x_row = jnp.stack([block_vec, from_right, far, from_left])
+    from_below = move(x_row, 0, 1)
+    from_above = move(x_row, 0, -1)
+    far_y = jnp.concatenate(
+        [move(from_below[:, :, :half_rows], 0, 1), move(from_above[:, :, half_rows:], 0, -1)], axis=2
+    )
+    plane = jnp.stack([x_row, from_above, far_y, from_below])
+    other = move(plane, 0, 0, sibling=True)
+
+    def pool(w, piece):
+        return jnp.einsum("kab,abrn->krn", w, piece, preferred_element_type=jnp.float32)
+
+    pooled = (
+        pool(weights[:, 0, 0], x_row)
+        + pool(weights[:, 0, 1], from_above)
+        + pool(weights[:, 0, 2], far_y)
+        + pool(weights[:, 0, 3], from_below)
+        + jnp.einsum(
+            "kyab,yabrn->krn", weights[:, 1], other, preferred_element_type=jnp.float32
+        )
     ).astype(jnp.bfloat16)
     pooled = pooled.reshape(local_blocks, term_total, row_count, width_two)
     right_done = jnp.einsum(

time: 127 us -> 115 us (0.906); the launches traced: 126 us -> 113 us
  waiting for transfers between devices: 54.3 us -> 37.3 us
  between operations: 13.6 us -> 0.68 us
  starting transfers between devices: 33.7 us -> 41.8 us
  other arithmetic: 0.85 us -> 6.55 us
  local copies, waits for them, and re-layouts: 3.32 us -> 5.77 us
    all_gather x1 -> x0, waiting for transfers between devices: 31.5 us -> none  [local(): everything = lax.all_gather(block_vec, 'blk', axis=0, tiled=True)]
    ppermute x0 -> x9, waiting for transfers between devices: none -> 19 us  [move(): return lax.ppermute(piece, 'blk', pairs_list)]
    ppermute x0 -> x9, starting transfers between devices: none -> 10.3 us  [move(): return lax.ppermute(piece, 'blk', pairs_list)]
    another operation x0 -> x5, other arithmetic: none -> 5.47 us  [the longest x2 4.16 us: local(): plane = jnp.stack([x_row, from_above, far_y, from_below])]
    ppermute x7, waiting for transfers between devices: 19.4 us -> 15.9 us  [scatter_sum(): got = lax.ppermute(send, axis, [(j, (j + k) % n) for j in range(n)])]
    ppermute x7, starting transfers between devices: 18.6 us -> 15.9 us  [exchange(): got = lax.ppermute(send, axis, [(j, (j + k) % n) for j in range(n)])]
    another operation x0 -> x4, local copies, waits for them, and re-layouts: none -> 1.72 us  [local(): x_row = jnp.stack([block_vec, from_right, far, from_left])]
    slice x0 -> x6, local copies, waits for them, and re-layouts: none -> 1.61 us  [the longest x1 0.79 us: local(): from_below[:, :, :half_rows]]
  transfers between devices with their start and end apart: 15 -> 23, of which waited for: 8 -> 12; matrix products, arithmetic and copies ran while one was open for 3% -> 12% of each run, Pallas kernels for 0% -> 0%
where the time goes in v2:
time: 115 us; the launch traced here: 113 us
  starting transfers between devices  41.8 us (36%)
  waiting for transfers between devices  37.3 us (32%)
  matrix products  20.8 us (18%)
  other arithmetic  6.55 us (6%)
  local copies, waits for them, and re-layouts  5.77 us (5%)
    ppermute x9, waiting for transfers between devices, move(): return lax.ppermute(piece, 'blk', pairs_list)  19 us
    ppermute x7, starting transfers between devices, exchange(): got = lax.ppermute(send, axis, [(j, (j + k) % n) for j in range(n)])  15.9 us
    ppermute x7, waiting for transfers between devices, scatter_sum(): got = lax.ppermute(send, axis, [(j, (j + k) % n) for j in range(n)])  15.9 us
    ppermute x7, starting transfers between devices, scatter_sum(): got = lax.ppermute(send, axis, [(j, (j + k) % n) for j in range(n)])  15.6 us
    ppermute x9, starting transfers between devices, move(): return lax.ppermute(piece, 'blk', pairs_list)  10.3 us
    dot_general x1, matrix products, local(): jnp.einsum('tab,ktbc->kac', left_part, right_done, preferred_element_type...  6.66 us
    another operation x2, other arithmetic, local(): plane = jnp.stack([x_row, from_above, far_y, from_below])  4.16 us
    dot_general x1, matrix products, local(): jnp.einsum('kyab,yabrn->krn', weights[:, 1], other, preferred_element_typ...  4.06 us
  transfers between devices with their start and end apart: 23, of which 12 were waited for; matrix products, arithmetic and copies ran while one was open for 12% of the time, Pallas kernels for 0%

profile of v2, /device:TPU:24, one launch (start us, length us, event | category | flops | bytes accessed | tf_op | source)
XLA Modules:
  0.0 113.0 jit_solution(13265101613773517573)
XLA Ops:
  0.0 2.8 %collective-permute-start = (bf16[2,64,512]{2,1,0:T(8,128)(2,1)}, bf16[2,64,512]{2,1,0:T(8,128)(2,1)S(1)}, u32[]{:S(2)}, u32[]{:S(2)}) collective-permute-start(bf16[2,64,512]{2,1,0:T(8,128)(2,1)} %param.11), channel_id=1, source_target_pairs={{0,192},{8,200},{16,208},{24,216},{32,224},{40,232},{48,240},{56,2... | collective-permute-start | bytes 393224 | tf_op jit(solution)/shard_map/ppermute | solution.py:84
  2.8 1.9 %collective-permute-start.9 = (f32[1,2,64]{2,1,0:T(2,128)}, f32[1,2,64]{2,1,0:T(2,128)S(1)}, u32[]{:S(2)}, u32[]{:S(2)}) collective-permute-start(f32[1,2,64]{2,1,0:T(2,128)} %bitcast.202), channel_id=1, source_target_pairs={{0,1},{1,2},{2,3},{3,4},{4,5},{5,6},{6,7},{7,0},{8,9},{9,10},{10,1... | collective-permute-start | bytes 1544 | tf_op jit(solution)/shard_map/ppermute | solution.py:15
  4.7 3.3 %collective-permute-start.10 = (f32[1,2,64]{2,1,0:T(2,128)}, f32[1,2,64]{2,1,0:T(2,128)S(1)}, u32[]{:S(2)}, u32[]{:S(2)}) collective-permute-start(f32[1,2,64]{2,1,0:T(2,128)} %bitcast.203), channel_id=1, source_target_pairs={{0,2},{1,3},{2,4},{3,5},{4,6},{5,7},{6,0},{7,1},{8,10},{9,11},{10,... | collective-permute-start | bytes 1544 | tf_op jit(solution)/shard_map/ppermute | solution.py:15
  8.0 4.0 %collective-permute-start.11 = (f32[1,2,64]{2,1,0:T(2,128)}, f32[1,2,64]{2,1,0:T(2,128)S(1)}, u32[]{:S(2)}, u32[]{:S(2)}) collective-permute-start(f32[1,2,64]{2,1,0:T(2,128)} %bitcast.204), channel_id=1, source_target_pairs={{0,3},{1,4},{2,5},{3,6},{4,7},{5,0},{6,1},{7,2},{8,11},{9,12},{10,... | collective-permute-start | bytes 1544 | tf_op jit(solution)/shard_map/ppermute | solution.py:15
  12.0 1.1 copy.95
  13.2 3.3 %collective-permute-start.3 = (bf16[2,32,512]{2,1,0:T(8,128)(2,1)S(1)}, bf16[2,32,512]{2,1,0:T(8,128)(2,1)S(1)}, u32[]{:S(2)}, u32[]{:S(2)}) collective-permute-start(bf16[2,32,512]{2,1,0:T(8,128)(2,1)S(1)} %slice.53), channel_id=1, source_target_pairs={{0,192},{8,200},{16,208},{24,216},{32,224},{40,232},{48,240},{56,2... | collective-permute-start | bytes 196616 | tf_op jit(solution)/shard_map/ppermute | solution.py:84
  17.0 1.4 %collective-permute-done.3 = bf16[2,32,512]{2,1,0:T(8,128)(2,1)S(1)} collective-permute-done((bf16[2,32,512]{2,1,0:T(8,128)(2,1)S(1)}, bf16[2,32,512]{2,1,0:T(8,128)(2,1)S(1)}, u32[]{:S(2)}, u32[]{:S(2)}) %collective-permute-start.3) | collective-permute-done | bytes 65568 | tf_op jit(solution)/shard_map/ppermute | solution.py:84
  18.4 3.7 %collective-permute-done.2 = bf16[2,32,512]{2,1,0:T(8,128)(2,1)S(1)} collective-permute-done((bf16[2,32,512]{2,1,0:T(8,128)(2,1)S(1)}, bf16[2,32,512]{2,1,0:T(8,128)(2,1)S(1)}, u32[]{:S(2)}, u32[]{:S(2)}) %collective-permute-start.2) | collective-permute-done | bytes 65568 | tf_op jit(solution)/shard_map/ppermute | solution.py:84
  22.3 1.2 %pad_maximum_fusion.1 = bf16[4,2,64,512]{3,0,1,2:T(4,128)(2,1)S(1)} fusion(bf16[1,2,64,512]{3,0,1,2:T(2,128)(2,1)S(1)} %copy.98, bf16[1,2,64,512]{3,0,1,2:T(2,128)(2,1)S(1)} %copy.97, bf16[1,2,64,512]{3,0,1,2:T(2,128)(2,1)S(1)} %copy.96, bf16[1,2,64,512]{3,0,1,2:T(2,128)(2,1)S(1)} %copy.95), kind=kLoop, calls=%fused_computation.26 | loop fusion | flops 2097152 | bytes 1048576 | tf_op jit(solution)/shard_map/stack | solution.py:92
  23.5 0.3 collective-permute-start.5
  23.8 1.8 %collective-permute-start.4 = (bf16[4,2,64,512]{3,0,1,2:T(4,128)(2,1)S(1)}, bf16[4,2,64,512]{3,0,1,2:T(4,128)(2,1)S(1)}, u32[]{:S(2)}, u32[]{:S(2)}) collective-permute-start(bf16[4,2,64,512]{3,0,1,2:T(4,128)(2,1)S(1)} %pad_maximum_fusion.1), channel_id=1, source_target_pairs={{0,48},{8,56},{16,0},{24,8},{32,16},{40,24},{48,32},{56,40},{64,11... | collective-permute-start | bytes 1572872 | tf_op jit(solution)/shard_map/ppermute | solution.py:84
  25.8 8.8 %collective-permute-done.5 = bf16[4,2,64,512]{3,0,1,2:T(4,128)(2,1)S(1)} collective-permute-done((bf16[4,2,64,512]{3,0,1,2:T(4,128)(2,1)S(1)}, bf16[4,2,64,512]{3,0,1,2:T(4,128)(2,1)S(1)}, u32[]{:S(2)}, u32[]{:S(2)}) %collective-permute-start.5) | collective-permute-done | bytes 524320 | tf_op jit(solution)/shard_map/ppermute | solution.py:84
  34.7 0.8 slice.56
  35.5 1.2 %collective-permute-start.6 = (bf16[4,2,32,512]{3,0,1,2:T(4,128)(2,1)}, bf16[4,2,32,512]{3,0,1,2:T(4,128)(2,1)S(1)}, u32[]{:S(2)}, u32[]{:S(2)}) collective-permute-start(bf16[4,2,32,512]{3,0,1,2:T(4,128)(2,1)} %slice.56), channel_id=1, source_target_pairs={{0,16},{8,24},{16,32},{24,40},{32,48},{40,56},{48,0},{56,8},{64,80... | collective-permute-start | bytes 786440 | tf_op jit(solution)/shard_map/ppermute | solution.py:84
  36.7 0.8 slice.57
  37.5 0.8 collective-permute-start.7
  38.4 1.2 %fusion.69 = bf16[1,4,2,64,512]{4,1,2,3,0:T(4,128)(2,1)S(1)} fusion(bf16[1,2,64,512]{3,0,1,2:T(2,128)(2,1)S(1)} %copy.98, bf16[1,2,64,512]{3,0,1,2:T(2,128)(2,1)S(1)} %copy.97, bf16[1,2,64,512]{3,0,1,2:T(2,128)(2,1)S(1)} %copy.96, bf16[1,2,64,512]{3,0,1,2:T(2,128)(2,1)S(1)} %copy.95), kind=kLoop, calls=%fused_computation.90 | loop fusion | flops 2097152 | bytes 1048576 | tf_op jit(solution)/shard_map/stack | solution.py:98
  39.6 2.5 %collective-permute-done.6 = bf16[4,2,32,512]{3,0,1,2:T(4,128)(2,1)S(1)} collective-permute-done((bf16[4,2,32,512]{3,0,1,2:T(4,128)(2,1)}, bf16[4,2,32,512]{3,0,1,2:T(4,128)(2,1)S(1)}, u32[]{:S(2)}, u32[]{:S(2)}) %collective-permute-start.6) | collective-permute-done | bytes 262176 | tf_op jit(solution)/shard_map/ppermute | solution.py:84
  42.1 0.5 collective-permute-start.12
  42.7 2.7 %collective-permute-done.7 = bf16[4,2,32,512]{3,0,1,2:T(4,128)(2,1)} collective-permute-done((bf16[4,2,32,512]{3,0,1,2:T(4,128)(2,1)}, bf16[4,2,32,512]{3,0,1,2:T(4,128)(2,1)}, u32[]{:S(2)}, u32[]{:S(2)}) %collective-permute-start.7) | collective-permute-done | bytes 262176 | tf_op jit(solution)/shard_map/ppermute | solution.py:84
  45.4 1.1 constant_dynamic-update-slice_fusion
  46.5 2.9 %pad_maximum_fusion = bf16[4,4,2,64,512]{4,1,2,3,0:T(4,128)(2,1)} fusion(bf16[1,4,2,64,512]{4,1,2,3,0:T(4,128)(2,1)S(1)} %bitcast.191, bf16[1,4,2,64,512]{4,1,2,3,0:T(4,128)(2,1)S(1)} %bitcast.193, bf16[1,4,2,64,512]{4,1,2,3,0:T(4,128)(2,1)S(1)} %bitcast.192, bf16[1,4,2,64,512]{4,1,2,3,0:T(4,128)(2,1)S(1)} %fusion.69), kind=kLoop, calls=%fused_computation.2 | loop fusion | flops 3145728 | bytes 4194304 | tf_op jit(solution)/shard_map/stack | solution.py:98
  50.8 2.3 %collective-permute-start.13 = (f32[1,2,64]{2,1,0:T(2,128)S(1)}, f32[1,2,64]{2,1,0:T(2,128)S(1)}, u32[]{:S(2)}, u32[]{:S(2)}) collective-permute-start(f32[1,2,64]{2,1,0:T(2,128)S(1)} %bitcast.207), channel_id=1, source_target_pairs={{0,5},{1,6},{2,7},{3,0},{4,1},{5,2},{6,3},{7,4},{8,13},{9,14},{10,... | collective-permute-start | bytes 1544 | tf_op jit(solution)/shard_map/ppermute | solution.py:15
  53.1 2.7 %collective-permute-start.14 = (f32[1,2,64]{2,1,0:T(2,128)S(1)}, f32[1,2,64]{2,1,0:T(2,128)S(1)}, u32[]{:S(2)}, u32[]{:S(2)}) collective-permute-start(f32[1,2,64]{2,1,0:T(2,128)S(1)} %bitcast.208), channel_id=1, source_target_pairs={{0,6},{1,7},{2,0},{3,1},{4,2},{5,3},{6,4},{7,5},{8,14},{9,15},{10,... | collective-permute-start | bytes 1544 | tf_op jit(solution)/shard_map/ppermute | solution.py:15
  55.9 1.1 collective-permute-start.15
  57.1 0.6 collective-permute-done.14
  57.7 1.8 %collective-permute-done.15 = f32[1,2,64]{2,1,0:T(2,128)S(1)} collective-permute-done((f32[1,2,64]{2,1,0:T(2,128)S(1)}, f32[1,2,64]{2,1,0:T(2,128)S(1)}, u32[]{:S(2)}, u32[]{:S(2)}) %collective-permute-start.15) | collective-permute-done | bytes 544 | tf_op jit(solution)/shard_map/ppermute | solution.py:15
  59.9 0.6 fusion.47
  60.5 0.6 fusion.41
  61.1 0.6 fusion.45
  61.7 0.6 fusion.43
  62.4 4.1 %fusion.15 = bf16[2,8,64,512]{3,1,0,2:T(8,128)(2,1)S(1)} fusion(bf16[4,4,2,64,512]{4,1,2,3,0:T(4,128)(2,1)} %collective-permute-done.8, f32[16,64,512,1]{2,0,3,1:T(8,128)S(1)} %fusion.41, f32[16,64,512,1]{2,0,3,1:T(8,128)S(1)} %fusion.43, f32[16,64,512,1]{2,0,3,1:T(8,128)S(1)} %fusion.45, f32[16,64,512,1]{2,0,3,1:T(8,128)S(1)} %fusion.47, ...), kind=kOutput, calls=%fused_computation.20 | convolution fusion | flops 36175872 | bytes 11535360 | tf_op jit(solution)/shard_map/kyab,yabrn->krn/dot_general | solution.py:109
  66.4 6.7 %bitcast_convert_fusion = bf16[2,512,512]{2,1,0:T(8,128)(2,1)} fusion(bf16[8,512,512]{2,1,0:T(8,128)(2,1)} %param.12, s32[]{:T(128)S(6)} %select_n.183, bf16[8,512,512]{2,1,0:T(8,128)(2,1)} %param.13, bf16[2,8,64,512]{3,1,0,2:T(8,128)(2,1)S(1)} %fusion.15), kind=kOutput, calls=%fused_computation.5 | convolution fusion | flops 1074790400 | bytes 7340036 | tf_op jit(solution)/shard_map/tab,ktbc->kac/dot_general | solution.py:120
  73.1 3.9 %fusion.8 = f32[2,512,512]{2,1,0:T(8,128)} fusion(bf16[2,512,512]{2,1,0:T(8,128)(2,1)S(1)} %copy-done, bf16[2,512,512]{2,1,0:T(8,128)(2,1)} %bitcast_convert_fusion, bf16[2,512,512]{2,1,0:T(8,128)(2,1)S(1)} %copy-done.7), kind=kOutput, calls=%fused_computation.16 | convolution fusion | flops 1074266112 | bytes 5242880 | tf_op jit(solution)/shard_map/jrn,jmn->jrm/dot_general | solution.py:126
  77.0 2.8 %convolution_convert_fusion.1 = bf16[2,512,512]{1,2,0:T(8,128)(2,1)S(1)} fusion(bf16[2,512,512]{2,1,0:T(8,128)(2,1)} %param.18, f32[2,512,512]{2,1,0:T(8,128)} %fusion.8, f32[2,512]{1,0:T(2,128)S(1)} %copy-done.8, f32[2,512]{1,0:T(2,128)S(1)} %add.360), kind=kOutput, calls=%fused_computation.14 | convolution fusion | flops 538968064 | bytes 4202496 | tf_op jit(solution)/shard_map/jrm,jkm->jrk/dot_general | solution.py:128
  79.8 0.7 convolution_convert_fusion
  80.7 2.3 %collective-permute-start.22 = (bf16[2,512,64]{1,2,0:T(8,128)(2,1)S(1)}, bf16[2,512,64]{1,2,0:T(8,128)(2,1)S(1)}, u32[]{:S(2)}, u32[]{:S(2)}) collective-permute-start(bf16[2,512,64]{1,2,0:T(8,128)(2,1)S(1)} %get-tuple-element.10), channel_id=1, source_target_pairs={{0,7},{1,0},{2,1},{3,2},{4,3},{5,4},{6,5},{7,6},{8,15},{9,8},{10,9... | collective-permute-start | bytes 393224 | tf_op jit(solution)/shard_map/ppermute | solution.py:26
  83.0 3.6 %collective-permute-start.20 = (bf16[2,512,64]{1,2,0:T(8,128)(2,1)S(1)}, bf16[2,512,64]{1,2,0:T(8,128)(2,1)S(1)}, u32[]{:S(2)}, u32[]{:S(2)}) collective-permute-start(bf16[2,512,64]{1,2,0:T(8,128)(2,1)S(1)} %get-tuple-element.6), channel_id=1, source_target_pairs={{0,5},{1,6},{2,7},{3,0},{4,1},{5,2},{6,3},{7,4},{8,13},{9,14},{10,... | collective-permute-start | bytes 393224 | tf_op jit(solution)/shard_map/ppermute | solution.py:26
  86.6 2.7 %collective-permute-start.19 = (bf16[2,512,64]{1,2,0:T(8,128)(2,1)S(1)}, bf16[2,512,64]{1,2,0:T(8,128)(2,1)S(1)}, u32[]{:S(2)}, u32[]{:S(2)}) collective-permute-start(bf16[2,512,64]{1,2,0:T(8,128)(2,1)S(1)} %get-tuple-element.7), channel_id=1, source_target_pairs={{0,4},{1,5},{2,6},{3,7},{4,0},{5,1},{6,2},{7,3},{8,12},{9,13},{10,... | collective-permute-start | bytes 393224 | tf_op jit(solution)/shard_map/ppermute | solution.py:26
  89.3 0.7 collective-permute-start.18
  90.0 4.1 %collective-permute-start.17 = (bf16[2,512,64]{1,2,0:T(8,128)(2,1)S(1)}, bf16[2,512,64]{1,2,0:T(8,128)(2,1)S(1)}, u32[]{:S(2)}, u32[]{:S(2)}) collective-permute-start(bf16[2,512,64]{1,2,0:T(8,128)(2,1)S(1)} %get-tuple-element.9), channel_id=1, source_target_pairs={{0,2},{1,3},{2,4},{3,5},{4,6},{5,7},{6,0},{7,1},{8,10},{9,11},{10,... | collective-permute-start | bytes 393224 | tf_op jit(solution)/shard_map/ppermute | solution.py:26
  94.2 2.1 %collective-permute-start.16 = (bf16[2,512,64]{1,2,0:T(8,128)(2,1)S(1)}, bf16[2,512,64]{1,2,0:T(8,128)(2,1)S(1)}, u32[]{:S(2)}, u32[]{:S(2)}) collective-permute-start(bf16[2,512,64]{1,2,0:T(8,128)(2,1)S(1)} %get-tuple-element.5), channel_id=1, source_target_pairs={{0,1},{1,2},{2,3},{3,4},{4,5},{5,6},{6,7},{7,0},{8,9},{9,10},{10,1... | collective-permute-start | bytes 393224 | tf_op jit(solution)/shard_map/ppermute | solution.py:26
  96.3 2.6 %collective-permute-done.20 = bf16[2,512,64]{1,2,0:T(8,128)(2,1)S(1)} collective-permute-done((bf16[2,512,64]{1,2,0:T(8,128)(2,1)S(1)}, bf16[2,512,64]{1,2,0:T(8,128)(2,1)S(1)}, u32[]{:S(2)}, u32[]{:S(2)}) %collective-permute-start.20) | collective-permute-done | bytes 131104 | tf_op jit(solution)/shard_map/ppermute | solution.py:26
  98.9 1.9 %collective-permute-done.19 = bf16[2,512,64]{1,2,0:T(8,128)(2,1)S(1)} collective-permute-done((bf16[2,512,64]{1,2,0:T(8,128)(2,1)S(1)}, bf16[2,512,64]{1,2,0:T(8,128)(2,1)S(1)}, u32[]{:S(2)}, u32[]{:S(2)}) %collective-permute-start.19) | collective-permute-done | bytes 131104 | tf_op jit(solution)/shard_map/ppermute | solution.py:26
  100.8 6.2 %collective-permute-done.18 = bf16[2,512,64]{1,2,0:T(8,128)(2,1)S(1)} collective-permute-done((bf16[2,512,64]{1,2,0:T(8,128)(2,1)S(1)}, bf16[2,512,64]{1,2,0:T(8,128)(2,1)S(1)}, u32[]{:S(2)}, u32[]{:S(2)}) %collective-permute-start.18) | collective-permute-done | bytes 131104 | tf_op jit(solution)/shard_map/ppermute | solution.py:26
  107.0 4.6 %collective-permute-done.17 = bf16[2,512,64]{1,2,0:T(8,128)(2,1)S(1)} collective-permute-done((bf16[2,512,64]{1,2,0:T(8,128)(2,1)S(1)}, bf16[2,512,64]{1,2,0:T(8,128)(2,1)S(1)}, u32[]{:S(2)}, u32[]{:S(2)}) %collective-permute-start.17) | collective-permute-done | bytes 131104 | tf_op jit(solution)/shard_map/ppermute | solution.py:26
  111.6 0.5 collective-permute-done.16
  112.1 0.8 fusion.32
  (67 shorter events, 2.7 us)
Async XLA Ops:
  0.0 73.1 %copy-start = (bf16[2,512,512]{2,1,0:T(8,128)(2,1)S(1)}, bf16[2,512,512]{2,1,0:T(8,128)(2,1)}, u32[]{:S(2)}) copy-start(bf16[2,512,512]{2,1,0:T(8,128)(2,1)} %param.19) | copy-start | bytes 3145732
  0.0 13.1 %collective-permute-start = (bf16[2,64,512]{2,1,0:T(8,128)(2,1)}, bf16[2,64,512]{2,1,0:T(8,128)(2,1)S(1)}, u32[]{:S(2)}, u32[]{:S(2)}) collective-permute-start(bf16[2,64,512]{2,1,0:T(8,128)(2,1)} %param.11), channel_id=1, source_target_pairs={{0,192},{8,200},{16,208},{24,216},{32,224},{40,232},{48,240},{56,2... | collective-permute-start | bytes 393224 | tf_op jit(solution)/shard_map/ppermute | solution.py:84
  2.8 13.7 %collective-permute-start.1 = (bf16[2,64,512]{2,1,0:T(8,128)(2,1)}, bf16[2,64,512]{2,1,0:T(8,128)(2,1)S(1)}, u32[]{:S(2)}, u32[]{:S(2)}) collective-permute-start(bf16[2,64,512]{2,1,0:T(8,128)(2,1)} %param.11), channel_id=1, source_target_pairs={{0,64},{8,72},{16,80},{24,88},{32,96},{40,104},{48,112},{56,120},{... | collective-permute-start | bytes 393224 | tf_op jit(solution)/shard_map/ppermute | solution.py:84
  2.8 48.0 %collective-permute-start.9 = (f32[1,2,64]{2,1,0:T(2,128)}, f32[1,2,64]{2,1,0:T(2,128)S(1)}, u32[]{:S(2)}, u32[]{:S(2)}) collective-permute-start(f32[1,2,64]{2,1,0:T(2,128)} %bitcast.202), channel_id=1, source_target_pairs={{0,1},{1,2},{2,3},{3,4},{4,5},{5,6},{6,7},{7,0},{8,9},{9,10},{10,1... | collective-permute-start | bytes 1544 | tf_op jit(solution)/shard_map/ppermute | solution.py:15
  4.7 48.4 %collective-permute-start.10 = (f32[1,2,64]{2,1,0:T(2,128)}, f32[1,2,64]{2,1,0:T(2,128)S(1)}, u32[]{:S(2)}, u32[]{:S(2)}) collective-permute-start(f32[1,2,64]{2,1,0:T(2,128)} %bitcast.203), channel_id=1, source_target_pairs={{0,2},{1,3},{2,4},{3,5},{4,6},{5,7},{6,0},{7,1},{8,10},{9,11},{10,... | collective-permute-start | bytes 1544 | tf_op jit(solution)/shard_map/ppermute | solution.py:15
  8.0 47.9 %collective-permute-start.11 = (f32[1,2,64]{2,1,0:T(2,128)}, f32[1,2,64]{2,1,0:T(2,128)S(1)}, u32[]{:S(2)}, u32[]{:S(2)}) collective-permute-start(f32[1,2,64]{2,1,0:T(2,128)} %bitcast.204), channel_id=1, source_target_pairs={{0,3},{1,4},{2,5},{3,6},{4,7},{5,0},{6,1},{7,2},{8,11},{9,12},{10,... | collective-permute-start | bytes 1544 | tf_op jit(solution)/shard_map/ppermute | solution.py:15
  13.2 5.2 %collective-permute-start.3 = (bf16[2,32,512]{2,1,0:T(8,128)(2,1)S(1)}, bf16[2,32,512]{2,1,0:T(8,128)(2,1)S(1)}, u32[]{:S(2)}, u32[]{:S(2)}) collective-permute-start(bf16[2,32,512]{2,1,0:T(8,128)(2,1)S(1)} %slice.53), channel_id=1, source_target_pairs={{0,192},{8,200},{16,208},{24,216},{32,224},{40,232},{48,240},{56,2... | collective-permute-start | bytes 196616 | tf_op jit(solution)/shard_map/ppermute | solution.py:84
  16.5 5.6 %collective-permute-start.2 = (bf16[2,32,512]{2,1,0:T(8,128)(2,1)S(1)}, bf16[2,32,512]{2,1,0:T(8,128)(2,1)S(1)}, u32[]{:S(2)}, u32[]{:S(2)}) collective-permute-start(bf16[2,32,512]{2,1,0:T(8,128)(2,1)S(1)} %slice.52), channel_id=1, source_target_pairs={{0,64},{8,72},{16,80},{24,88},{32,96},{40,104},{48,112},{56,120},{... | collective-permute-start | bytes 196616 | tf_op jit(solution)/shard_map/ppermute | solution.py:84
  22.3 19.8 %copy-start.6 = (f32[2,64]{1,0:T(2,128)S(1)}, f32[2,64]{1,0:T(2,128)}, u32[]{:S(2)}) copy-start(f32[2,64]{1,0:T(2,128)} %param.20) | copy-start | bytes 1540
  23.5 13.2 %copy-start.1 = (bf16[4,2,64,512]{3,0,1,2:T(4,128)(2,1)}, bf16[4,2,64,512]{3,0,1,2:T(4,128)(2,1)S(1)}, u32[]{:S(2)}) copy-start(bf16[4,2,64,512]{3,0,1,2:T(4,128)(2,1)S(1)} %pad_maximum_fusion.1) | copy-start | bytes 1572868
  23.5 11.2 %collective-permute-start.5 = (bf16[4,2,64,512]{3,0,1,2:T(4,128)(2,1)S(1)}, bf16[4,2,64,512]{3,0,1,2:T(4,128)(2,1)S(1)}, u32[]{:S(2)}, u32[]{:S(2)}) collective-permute-start(bf16[4,2,64,512]{3,0,1,2:T(4,128)(2,1)S(1)} %pad_maximum_fusion.1), channel_id=1, source_target_pairs={{0,16},{8,24},{16,32},{24,40},{32,48},{40,56},{48,0},{56,8},{64,80... | collective-permute-start | bytes 1572872 | tf_op jit(solution)/shard_map/ppermute | solution.py:84
  23.8 12.9 %collective-permute-start.4 = (bf16[4,2,64,512]{3,0,1,2:T(4,128)(2,1)S(1)}, bf16[4,2,64,512]{3,0,1,2:T(4,128)(2,1)S(1)}, u32[]{:S(2)}, u32[]{:S(2)}) collective-permute-start(bf16[4,2,64,512]{3,0,1,2:T(4,128)(2,1)S(1)} %pad_maximum_fusion.1), channel_id=1, source_target_pairs={{0,48},{8,56},{16,0},{24,8},{32,16},{40,24},{48,32},{56,40},{64,11... | collective-permute-start | bytes 1572872 | tf_op jit(solution)/shard_map/ppermute | solution.py:84
  35.5 6.6 %collective-permute-start.6 = (bf16[4,2,32,512]{3,0,1,2:T(4,128)(2,1)}, bf16[4,2,32,512]{3,0,1,2:T(4,128)(2,1)S(1)}, u32[]{:S(2)}, u32[]{:S(2)}) collective-permute-start(bf16[4,2,32,512]{3,0,1,2:T(4,128)(2,1)} %slice.56), channel_id=1, source_target_pairs={{0,16},{8,24},{16,32},{24,40},{32,48},{40,56},{48,0},{56,8},{64,80... | collective-permute-start | bytes 786440 | tf_op jit(solution)/shard_map/ppermute | solution.py:84
  37.5 7.9 %collective-permute-start.7 = (bf16[4,2,32,512]{3,0,1,2:T(4,128)(2,1)}, bf16[4,2,32,512]{3,0,1,2:T(4,128)(2,1)}, u32[]{:S(2)}, u32[]{:S(2)}) collective-permute-start(bf16[4,2,32,512]{3,0,1,2:T(4,128)(2,1)} %slice.57), channel_id=1, source_target_pairs={{0,48},{8,56},{16,0},{24,8},{32,16},{40,24},{48,32},{56,40},{64,11... | collective-permute-start | bytes 786440 | tf_op jit(solution)/shard_map/ppermute | solution.py:84
  42.1 14.9 %collective-permute-start.12 = (f32[1,2,64]{2,1,0:T(2,128)S(1)}, f32[1,2,64]{2,1,0:T(2,128)S(1)}, u32[]{:S(2)}, u32[]{:S(2)}) collective-permute-start(f32[1,2,64]{2,1,0:T(2,128)S(1)} %bitcast.205), channel_id=1, source_target_pairs={{0,4},{1,5},{2,6},{3,7},{4,0},{5,1},{6,2},{7,3},{8,12},{9,13},{10,... | collective-permute-start | bytes 1544 | tf_op jit(solution)/shard_map/ppermute | solution.py:15
  46.5 3.0 %copy-start.4 = (s32[32,32,2,3]{1,2,3,0:T(2,128)S(1)}, s32[32,32,2,3]{1,2,3,0:T(2,128)}, u32[]{:S(2)}) copy-start(s32[32,32,2,3]{1,2,3,0:T(2,128)} %param.14) | copy-start | bytes 73732
  46.5 3.6 %copy-start.5 = (s32[32,32]{1,0:T(8,128)S(1)}, s32[32,32]{1,0:T(8,128)}, u32[]{:S(2)}) copy-start(s32[32,32]{1,0:T(8,128)} %param.15) | copy-start | bytes 12292
  46.5 13.4 %copy-start.2 = (bf16[4,2,64,512]{3,0,1,2:T(4,128)(2,1)S(1)}, bf16[4,2,64,512]{3,0,1,2:T(4,128)(2,1)}, u32[]{:S(2)}) copy-start(bf16[4,2,64,512]{3,0,1,2:T(4,128)(2,1)} %copy-done.1) | copy-start | bytes 1572868
  49.4 12.9 %collective-permute-start.8 = (bf16[4,4,2,64,512]{4,1,2,3,0:T(4,128)(2,1)}, bf16[4,4,2,64,512]{4,1,2,3,0:T(4,128)(2,1)}, u32[]{:S(2)}, u32[]{:S(2)}) collective-permute-start(bf16[4,4,2,64,512]{4,1,2,3,0:T(4,128)(2,1)} %pad_maximum_fusion), channel_id=1, source_target_pairs={{0,8},{8,0},{16,24},{24,16},{32,40},{40,32},{48,56},{56,48},{64,72... | collective-permute-start | bytes 6291464 | tf_op jit(solution)/shard_map/ppermute | solution.py:84
  50.8 6.3 %collective-permute-start.13 = (f32[1,2,64]{2,1,0:T(2,128)S(1)}, f32[1,2,64]{2,1,0:T(2,128)S(1)}, u32[]{:S(2)}, u32[]{:S(2)}) collective-permute-start(f32[1,2,64]{2,1,0:T(2,128)S(1)} %bitcast.207), channel_id=1, source_target_pairs={{0,5},{1,6},{2,7},{3,0},{4,1},{5,2},{6,3},{7,4},{8,13},{9,14},{10,... | collective-permute-start | bytes 1544 | tf_op jit(solution)/shard_map/ppermute | solution.py:15
  53.1 4.5 %collective-permute-start.14 = (f32[1,2,64]{2,1,0:T(2,128)S(1)}, f32[1,2,64]{2,1,0:T(2,128)S(1)}, u32[]{:S(2)}, u32[]{:S(2)}) collective-permute-start(f32[1,2,64]{2,1,0:T(2,128)S(1)} %bitcast.208), channel_id=1, source_target_pairs={{0,6},{1,7},{2,0},{3,1},{4,2},{5,3},{6,4},{7,5},{8,14},{9,15},{10,... | collective-permute-start | bytes 1544 | tf_op jit(solution)/shard_map/ppermute | solution.py:15
  55.9 3.6 %collective-permute-start.15 = (f32[1,2,64]{2,1,0:T(2,128)S(1)}, f32[1,2,64]{2,1,0:T(2,128)S(1)}, u32[]{:S(2)}, u32[]{:S(2)}) collective-permute-start(f32[1,2,64]{2,1,0:T(2,128)S(1)} %bitcast.209), channel_id=1, source_target_pairs={{0,7},{1,0},{2,1},{3,2},{4,3},{5,4},{6,5},{7,6},{8,15},{9,8},{10,9... | collective-permute-start | bytes 1544 | tf_op jit(solution)/shard_map/ppermute | solution.py:15
  66.4 6.7 %copy-start.7 = (bf16[2,512,512]{2,1,0:T(8,128)(2,1)S(1)}, bf16[2,512,512]{2,1,0:T(8,128)(2,1)}, u32[]{:S(2)}) copy-start(bf16[2,512,512]{2,1,0:T(8,128)(2,1)} %param.17) | copy-start | bytes 3145732
  73.1 3.9 %copy-start.8 = (f32[2,512]{1,0:T(2,128)S(1)}, f32[2,512]{1,0:T(2,128)}, u32[]{:S(2)}) copy-start(f32[2,512]{1,0:T(2,128)} %param.21) | copy-start | bytes 12292
  77.0 2.8 %copy-start.3 = (bf16[2,512,512]{2,1,0:T(8,128)(2,1)S(1)}, bf16[2,512,512]{2,1,0:T(8,128)(2,1)}, u32[]{:S(2)}) copy-start(bf16[2,512,512]{2,1,0:T(8,128)(2,1)} %param.16) | copy-start | bytes 3145732
  80.7 9.4 %collective-permute-start.22 = (bf16[2,512,64]{1,2,0:T(8,128)(2,1)S(1)}, bf16[2,512,64]{1,2,0:T(8,128)(2,1)S(1)}, u32[]{:S(2)}, u32[]{:S(2)}) collective-permute-start(bf16[2,512,64]{1,2,0:T(8,128)(2,1)S(1)} %get-tuple-element.10), channel_id=1, source_target_pairs={{0,7},{1,0},{2,1},{3,2},{4,3},{5,4},{6,5},{7,6},{8,15},{9,8},{10,9... | collective-permute-start | bytes 393224 | tf_op jit(solution)/shard_map/ppermute | solution.py:26
  82.9 11.2 %collective-permute-start.21 = (bf16[2,512,64]{1,2,0:T(8,128)(2,1)S(1)}, bf16[2,512,64]{1,2,0:T(8,128)(2,1)S(1)}, u32[]{:S(2)}, u32[]{:S(2)}) collective-permute-start(bf16[2,512,64]{1,2,0:T(8,128)(2,1)S(1)} %get-tuple-element.11), channel_id=1, source_target_pairs={{0,6},{1,7},{2,0},{3,1},{4,2},{5,3},{6,4},{7,5},{8,14},{9,15},{10,... | collective-permute-start | bytes 393224 | tf_op jit(solution)/shard_map/ppermute | solution.py:26
  83.0 16.0 %collective-permute-start.20 = (bf16[2,512,64]{1,2,0:T(8,128)(2,1)S(1)}, bf16[2,512,64]{1,2,0:T(8,128)(2,1)S(1)}, u32[]{:S(2)}, u32[]{:S(2)}) collective-permute-start(bf16[2,512,64]{1,2,0:T(8,128)(2,1)S(1)} %get-tuple-element.6), channel_id=1, source_target_pairs={{0,5},{1,6},{2,7},{3,0},{4,1},{5,2},{6,3},{7,4},{8,13},{9,14},{10,... | collective-permute-start | bytes 393224 | tf_op jit(solution)/shard_map/ppermute | solution.py:26
  86.6 14.2 %collective-permute-start.19 = (bf16[2,512,64]{1,2,0:T(8,128)(2,1)S(1)}, bf16[2,512,64]{1,2,0:T(8,128)(2,1)S(1)}, u32[]{:S(2)}, u32[]{:S(2)}) collective-permute-start(bf16[2,512,64]{1,2,0:T(8,128)(2,1)S(1)} %get-tuple-element.7), channel_id=1, source_target_pairs={{0,4},{1,5},{2,6},{3,7},{4,0},{5,1},{6,2},{7,3},{8,12},{9,13},{10,... | collective-permute-start | bytes 393224 | tf_op jit(solution)/shard_map/ppermute | solution.py:26
  89.3 17.8 %collective-permute-start.18 = (bf16[2,512,64]{1,2,0:T(8,128)(2,1)S(1)}, bf16[2,512,64]{1,2,0:T(8,128)(2,1)S(1)}, u32[]{:S(2)}, u32[]{:S(2)}) collective-permute-start(bf16[2,512,64]{1,2,0:T(8,128)(2,1)S(1)} %get-tuple-element.8), channel_id=1, source_target_pairs={{0,3},{1,4},{2,5},{3,6},{4,7},{5,0},{6,1},{7,2},{8,11},{9,12},{10,... | collective-permute-start | bytes 393224 | tf_op jit(solution)/shard_map/ppermute | solution.py:26
  90.0 21.6 %collective-permute-start.17 = (bf16[2,512,64]{1,2,0:T(8,128)(2,1)S(1)}, bf16[2,512,64]{1,2,0:T(8,128)(2,1)S(1)}, u32[]{:S(2)}, u32[]{:S(2)}) collective-permute-start(bf16[2,512,64]{1,2,0:T(8,128)(2,1)S(1)} %get-tuple-element.9), channel_id=1, source_target_pairs={{0,2},{1,3},{2,4},{3,5},{4,6},{5,7},{6,0},{7,1},{8,10},{9,11},{10,... | collective-permute-start | bytes 393224 | tf_op jit(solution)/shard_map/ppermute | solution.py:26
  94.2 18.0 %collective-permute-start.16 = (bf16[2,512,64]{1,2,0:T(8,128)(2,1)S(1)}, bf16[2,512,64]{1,2,0:T(8,128)(2,1)S(1)}, u32[]{:S(2)}, u32[]{:S(2)}) collective-permute-start(bf16[2,512,64]{1,2,0:T(8,128)(2,1)S(1)} %get-tuple-element.5), channel_id=1, source_target_pairs={{0,1},{1,2},{2,3},{3,4},{4,5},{5,6},{6,7},{7,0},{8,9},{9,10},{10,1... | collective-permute-start | bytes 393224 | tf_op jit(solution)/shard_map/ppermute | solution.py:26

commit v3 on v2

--- a/solution.py
+++ b/solution.py
@@ -2,19 +2,6 @@
 import jax.numpy as jnp
 from jax import lax
 from jax.sharding import PartitionSpec as P
-
-
-def exchange(chunks, axis):
-    n = chunks.shape[0]
-    me = lax.axis_index(axis)
-    out = jnp.zeros_like(chunks)
-    own = lax.dynamic_index_in_dim(chunks, me, 0, keepdims=True)
-    out = lax.dynamic_update_index_in_dim(out, own, me, 0)
-    for k in range(1, n):
-        send = lax.dynamic_index_in_dim(chunks, (me + k) % n, 0, keepdims=True)
-        got = lax.ppermute(send, axis, [(j, (j + k) % n) for j in range(n)])
-        out = lax.dynamic_update_index_in_dim(out, got, (me - k) % n, 0)
-    return out
 
 
 def scatter_sum(chunks, axis):
@@ -83,20 +70,23 @@
             pairs_list.append((b, dest))
         return lax.ppermute(piece, "blk", pairs_list)
 
-    half_rows = row_count // 2
+    half_blocks = local_blocks // 2
     from_left = move(block_vec, 1, 0)
     from_right = move(block_vec, -1, 0)
     far = jnp.concatenate(
-        [move(from_left[:, :half_rows], 1, 0), move(from_right[:, half_rows:], -1, 0)], axis=1
+        [move(from_left[:half_blocks], 1, 0), move(from_right[half_blocks:], -1, 0)], axis=0
     )
     x_row = jnp.stack([block_vec, from_right, far, from_left])
+    side_x = move(x_row, 0, 0, sibling=True)
     from_below = move(x_row, 0, 1)
     from_above = move(x_row, 0, -1)
+    side_above = move(from_above, 0, 0, sibling=True)
+    side_below = move(from_below, 0, 0, sibling=True)
+    half_ring = ring // 2
     far_y = jnp.concatenate(
-        [move(from_below[:, :, :half_rows], 0, 1), move(from_above[:, :, half_rows:], 0, -1)], axis=2
+        [move(from_below[:half_ring], 0, 1), move(from_above[half_ring:], 0, -1)], axis=0
     )
-    plane = jnp.stack([x_row, from_above, far_y, from_below])
-    other = move(plane, 0, 0, sibling=True)
+    side_far = move(far_y, 0, 0, sibling=True)
 
     def pool(w, piece):
         return jnp.einsum("kab,abrn->krn", w, piece, preferred_element_type=jnp.float32)
@@ -106,16 +96,24 @@
         + pool(weights[:, 0, 1], from_above)
         + pool(weights[:, 0, 2], far_y)
         + pool(weights[:, 0, 3], from_below)
-        + jnp.einsum(
-            "kyab,yabrn->krn", weights[:, 1], other, preferred_element_type=jnp.float32
-        )
+        + pool(weights[:, 1, 0], side_x)
+        + pool(weights[:, 1, 1], side_above)
+        + pool(weights[:, 1, 2], side_far)
+        + pool(weights[:, 1, 3], side_below)
     ).astype(jnp.bfloat16)
     pooled = pooled.reshape(local_blocks, term_total, row_count, width_two)
     right_done = jnp.einsum(
         "ktrn,tmn->ktrm", pooled, right_factor, preferred_element_type=jnp.float32
     ).astype(jnp.bfloat16)
     left_part = lax.dynamic_slice_in_dim(left_factor, part * row_count, row_count, axis=2)
-    rates_parts = exchange(jnp.broadcast_to(left_rates, (pieces,) + left_rates.shape), "sub")
+    rates_run = left_rates[None]
+    step = 1
+    while step < pieces:
+        came = lax.ppermute(rates_run, "sub", [(j, (j + step) % pieces) for j in range(pieces)])
+        rates_run = jnp.concatenate([came, rates_run], axis=0)
+        step *= 2
+    rates_twice = jnp.concatenate([rates_run, rates_run], axis=0)
+    rates_parts = lax.dynamic_slice_in_dim(rates_twice, (pieces - 1 - part) % pieces, pieces, axis=0)
     rates_full = jnp.moveaxis(rates_parts, 0, 1).reshape(local_blocks, width_two)
     partial = jnp.einsum(
         "tab,ktbc->kac", left_part, right_done, preferred_element_type=jnp.float32

time: 115 us -> 107 us (0.930)
  starting transfers between devices: 41.8 us -> 34.7 us
  waiting for transfers between devices: 37.3 us -> 40.2 us
  matrix products: 20.8 us -> 19 us
  other arithmetic: 6.55 us -> 5.23 us
    ppermute x7 -> x3, starting transfers between devices: 15.9 us -> 6.97 us  [local(): lax.ppermute(rates_run, 'sub', [(j, (j + step) % pieces) for j in range(p...]
    ppermute x7 -> x3, waiting for transfers between devices: 2.44 us -> 9.79 us  [local(): lax.ppermute(rates_run, 'sub', [(j, (j + step) % pieces) for j in range(p...]
    ppermute x9 -> x12, waiting for transfers between devices: 19 us -> 14.8 us  [move(): return lax.ppermute(piece, 'blk', pairs_list)]
    another operation x2 -> x0, other arithmetic: 4.16 us -> none  [local(): plane = jnp.stack([x_row, from_above, far_y, from_below])]
    dot_general x1 -> x0, matrix products: 4.06 us -> none  [local(): jnp.einsum('kyab,yabrn->krn', weights[:, 1], other, preferred_element_typ...]
    dot_general x4 -> x8, matrix products: 2.46 us -> 5.76 us  [pool(): jnp.einsum('kab,abrn->krn', w, piece, preferred_element_type=jnp.float32)]
    concatenate x0 -> x3, other arithmetic: none -> 1.91 us  [the longest x2 1.37 us: local(): rates_run = jnp.concatenate([came, rates_run], axis=0)]
    ppermute x9 -> x12, starting transfers between devices: 10.3 us -> 11.7 us  [move(): return lax.ppermute(piece, 'blk', pairs_list)]
  transfers between devices with their start and end apart: 23 -> 22, of which waited for: 12 -> 13; matrix products, arithmetic and copies ran while one was open for 12% -> 12% of each run, Pallas kernels for 0% -> 0%
where the time goes in v3:
time: 107 us; the launch traced here: 105 us
  waiting for transfers between devices  40.2 us (38%)
  starting transfers between devices  34.7 us (32%)
  matrix products  19 us (18%)
  local copies, waits for them, and re-layouts  5.46 us (5%)
  other arithmetic  5.23 us (5%)
    ppermute x7, starting transfers between devices, scatter_sum(): got = lax.ppermute(send, axis, [(j, (j + k) % n) for j in range(n)])  16.1 us
    ppermute x7, waiting for transfers between devices, scatter_sum(): got = lax.ppermute(send, axis, [(j, (j + k) % n) for j in range(n)])  15.7 us
    ppermute x12, waiting for transfers between devices, move(): return lax.ppermute(piece, 'blk', pairs_list)  14.8 us
    ppermute x12, starting transfers between devices, move(): return lax.ppermute(piece, 'blk', pairs_list)  11.7 us
    ppermute x3, waiting for transfers between devices, local(): lax.ppermute(rates_run, 'sub', [(j, (j + step) % pieces) for j in range(p...  9.79 us
    ppermute x3, starting transfers between devices, local(): lax.ppermute(rates_run, 'sub', [(j, (j + step) % pieces) for j in range(p...  6.97 us
    dot_general x1, matrix products, local(): jnp.einsum('tab,ktbc->kac', left_part, right_done, preferred_element_type...  6.71 us
    dot_general x8, matrix products, pool(): jnp.einsum('kab,abrn->krn', w, piece, preferred_element_type=jnp.float32)  5.76 us
  transfers between devices with their start and end apart: 22, of which 13 were waited for; matrix products, arithmetic and copies ran while one was open for 12% of the time, Pallas kernels for 0%

profile of v3, /device:TPU:24, one launch (start us, length us, event | category | flops | bytes accessed | tf_op | source)
XLA Modules:
  0.0 105.1 jit_solution(13423985698155942272)
XLA Ops:
  0.0 1.5 %collective-permute-start.1 = (bf16[2,64,512]{2,1,0:T(8,128)(2,1)}, bf16[2,64,512]{2,1,0:T(8,128)(2,1)S(1)}, u32[]{:S(2)}, u32[]{:S(2)}) collective-permute-start(bf16[2,64,512]{2,1,0:T(8,128)(2,1)} %param.11), channel_id=1, source_target_pairs={{0,64},{8,72},{16,80},{24,88},{32,96},{40,104},{48,112},{56,120},{... | collective-permute-start | bytes 393224 | tf_op jit(solution)/shard_map/ppermute | solution.py:71
  1.5 1.7 %collective-permute-start = (bf16[2,64,512]{2,1,0:T(8,128)(2,1)}, bf16[2,64,512]{2,1,0:T(8,128)(2,1)S(1)}, u32[]{:S(2)}, u32[]{:S(2)}) collective-permute-start(bf16[2,64,512]{2,1,0:T(8,128)(2,1)} %param.11), channel_id=1, source_target_pairs={{0,192},{8,200},{16,208},{24,216},{32,224},{40,232},{48,240},{56,2... | collective-permute-start | bytes 393224 | tf_op jit(solution)/shard_map/ppermute | solution.py:71
  3.2 1.9 %collective-permute-start.12 = (f32[1,2,64]{2,1,0:T(2,128)}, f32[1,2,64]{2,1,0:T(2,128)S(1)}, u32[]{:S(2)}, u32[]{:S(2)}) collective-permute-start(f32[1,2,64]{2,1,0:T(2,128)} %bitcast.223), channel_id=1, source_target_pairs={{0,1},{1,2},{2,3},{3,4},{4,5},{5,6},{6,7},{7,0},{8,9},{9,10},{10,1... | collective-permute-start | bytes 1544 | tf_op jit(solution)/shard_map/ppermute | solution.py:112
  5.6 1.1 %constant_dynamic-slice_fusion = s32[32,1,2,3]{1,2,3,0:T(2,128)S(1)} fusion(s32[32,32,2,3]{1,2,3,0:T(2,128)} %param.14, s32[]{:T(128)S(6)} %select_n.109), kind=kLoop, calls=%fused_computation.63 | loop fusion | bytes 1540 | tf_op jit(solution)/shard_map/jit(dynamic_index_in_dim)/dynamic_slice | solution.py:42
  6.8 0.9 dynamic-slice_reduce_fusion
  8.1 2.8 %collective-permute-done.12 = f32[1,2,64]{2,1,0:T(2,128)S(1)} collective-permute-done((f32[1,2,64]{2,1,0:T(2,128)}, f32[1,2,64]{2,1,0:T(2,128)S(1)}, u32[]{:S(2)}, u32[]{:S(2)}) %collective-permute-start.12) | collective-permute-done | bytes 544 | tf_op jit(solution)/shard_map/ppermute | solution.py:112
  10.9 0.7 pad_maximum_fusion.3
  11.5 0.5 collective-permute-start.13
  12.0 5.2 %collective-permute-done.13 = f32[2,2,64]{2,1,0:T(2,128)S(1)} collective-permute-done((f32[2,2,64]{2,1,0:T(2,128)S(1)}, f32[2,2,64]{2,1,0:T(2,128)S(1)}, u32[]{:S(2)}, u32[]{:S(2)}) %collective-permute-start.13) | collective-permute-done | bytes 1056 | tf_op jit(solution)/shard_map/ppermute | solution.py:112
  17.2 0.7 pad_maximum_fusion.2
  17.9 4.6 %collective-permute-start.14 = (f32[4,2,64]{2,1,0:T(2,128)S(1)}, f32[4,2,64]{2,1,0:T(2,128)S(1)}, u32[]{:S(2)}, u32[]{:S(2)}) collective-permute-start(f32[4,2,64]{2,1,0:T(2,128)S(1)} %pad_maximum_fusion.2), channel_id=1, source_target_pairs={{0,4},{1,5},{2,6},{3,7},{4,0},{5,1},{6,2},{7,3},{8,12},{9,13},{10,... | collective-permute-start | bytes 6152 | tf_op jit(solution)/shard_map/ppermute | solution.py:112
  22.5 1.1 %copy.87 = bf16[1,2,64,512]{3,0,1,2:T(2,128)(2,1)S(1)} copy(bf16[1,2,64,512]{3,2,1,0:T(8,128)(2,1)} %bitcast.221) | data formatting | bytes 262144 | tf_op jit(solution)/shard_map/stack | solution.py:79
  23.6 1.8 %collective-permute-done.14 = f32[4,2,64]{2,1,0:T(2,128)S(1)} collective-permute-done((f32[4,2,64]{2,1,0:T(2,128)S(1)}, f32[4,2,64]{2,1,0:T(2,128)S(1)}, u32[]{:S(2)}, u32[]{:S(2)}) %collective-permute-start.14) | collective-permute-done | bytes 2080 | tf_op jit(solution)/shard_map/ppermute | solution.py:112
  25.4 0.7 constant_dynamic-update-slice_fusion.4
  26.5 3.0 %collective-permute-start.3 = (bf16[1,64,512]{2,1,0:T(8,128)(2,1)S(1)}, bf16[1,64,512]{2,1,0:T(8,128)(2,1)S(1)}, u32[]{:S(2)}, u32[]{:S(2)}) collective-permute-start(bf16[1,64,512]{2,1,0:T(8,128)(2,1)S(1)} %slice.65), channel_id=1, source_target_pairs={{0,192},{8,200},{16,208},{24,216},{32,224},{40,232},{48,240},{56,2... | collective-permute-start | bytes 196616 | tf_op jit(solution)/shard_map/ppermute | solution.py:71
  30.0 1.7 %collective-permute-done.2 = bf16[1,64,512]{2,1,0:T(8,128)(2,1)S(1)} collective-permute-done((bf16[1,64,512]{2,1,0:T(8,128)(2,1)S(1)}, bf16[1,64,512]{2,1,0:T(8,128)(2,1)S(1)}, u32[]{:S(2)}, u32[]{:S(2)}) %collective-permute-start.2) | collective-permute-done | bytes 65568 | tf_op jit(solution)/shard_map/ppermute | solution.py:71
  32.0 1.2 %pad_maximum_fusion = bf16[4,2,64,512]{3,0,1,2:T(4,128)(2,1)S(1)} fusion(bf16[1,2,64,512]{3,0,1,2:T(2,128)(2,1)S(1)} %copy.90, bf16[1,2,64,512]{3,0,1,2:T(2,128)(2,1)S(1)} %copy.89, bf16[1,2,64,512]{3,0,1,2:T(2,128)(2,1)S(1)} %copy.88, bf16[1,2,64,512]{3,0,1,2:T(2,128)(2,1)S(1)} %copy.87), kind=kLoop, calls=%fused_computation.24 | loop fusion | flops 2097152 | bytes 1048576 | tf_op jit(solution)/shard_map/stack | solution.py:79
  33.5 1.8 %collective-permute-start.4 = (bf16[4,2,64,512]{3,0,1,2:T(4,128)(2,1)S(1)}, bf16[4,2,64,512]{3,0,1,2:T(4,128)(2,1)S(1)}, u32[]{:S(2)}, u32[]{:S(2)}) collective-permute-start(bf16[4,2,64,512]{3,0,1,2:T(4,128)(2,1)S(1)} %pad_maximum_fusion), channel_id=1, source_target_pairs={{0,48},{8,56},{16,0},{24,8},{32,16},{40,24},{48,32},{56,40},{64,11... | collective-permute-start | bytes 1572872 | tf_op jit(solution)/shard_map/ppermute | solution.py:71
  35.4 0.6 fusion.46
  36.0 9.2 %collective-permute-done.5 = bf16[4,2,64,512]{3,0,1,2:T(4,128)(2,1)S(1)} collective-permute-done((bf16[4,2,64,512]{3,0,1,2:T(4,128)(2,1)S(1)}, bf16[4,2,64,512]{3,0,1,2:T(4,128)(2,1)S(1)}, u32[]{:S(2)}, u32[]{:S(2)}) %collective-permute-start.5) | collective-permute-done | bytes 524320 | tf_op jit(solution)/shard_map/ppermute | solution.py:71
  46.2 1.9 %collective-permute-start.7 = (bf16[2,2,64,512]{3,0,1,2:T(2,128)(2,1)S(1)}, bf16[2,2,64,512]{3,0,1,2:T(2,128)(2,1)S(1)}, u32[]{:S(2)}, u32[]{:S(2)}) collective-permute-start(bf16[2,2,64,512]{3,0,1,2:T(2,128)(2,1)S(1)} %slice.69), channel_id=1, source_target_pairs={{0,48},{8,56},{16,0},{24,8},{32,16},{40,24},{48,32},{56,40},{64,11... | collective-permute-start | bytes 786440 | tf_op jit(solution)/shard_map/ppermute | solution.py:71
  48.1 0.5 collective-permute-start.11
  48.6 0.6 fusion.40
  49.2 0.6 fusion.44
  49.9 0.6 fusion.38
  50.5 1.4 %collective-permute-done.6 = bf16[2,2,64,512]{3,0,1,2:T(2,128)(2,1)S(1)} collective-permute-done((bf16[2,2,64,512]{3,0,1,2:T(2,128)(2,1)S(1)}, bf16[2,2,64,512]{3,0,1,2:T(2,128)(2,1)S(1)}, u32[]{:S(2)}, u32[]{:S(2)}) %collective-permute-start.6) | collective-permute-done | bytes 262176 | tf_op jit(solution)/shard_map/ppermute | solution.py:71
  51.9 2.1 %collective-permute-done.7 = bf16[2,2,64,512]{3,0,1,2:T(2,128)(2,1)S(1)} collective-permute-done((bf16[2,2,64,512]{3,0,1,2:T(2,128)(2,1)S(1)}, bf16[2,2,64,512]{3,0,1,2:T(2,128)(2,1)S(1)}, u32[]{:S(2)}, u32[]{:S(2)}) %collective-permute-start.7) | collective-permute-done | bytes 262176 | tf_op jit(solution)/shard_map/ppermute | solution.py:71
  54.0 0.5 pad_maximum_fusion.1
  54.7 1.0 fusion.42
  55.7 0.6 fusion.36
  56.6 0.6 fusion.34
  57.2 1.1 %fusion.9 = bf16[2,8,64,512]{3,1,0,2:T(8,128)(2,1)S(1)} fusion(bf16[4,2,64,512]{3,0,1,2:T(4,128)(2,1)S(1)} %collective-permute-done.11, f32[16,64,512,1]{2,0,3,1:T(8,128)S(1)} %fusion.34, f32[16,64,512,1]{2,0,3,1:T(8,128)S(1)} %fusion.36, f32[16,64,512,1]{2,0,3,1:T(8,128)S(1)} %fusion.38, f32[16,64,512,1]{2,0,3,1:T(8,128)S(1)} %fusion.40, ...), kind=kOutput, calls=%fused_computation.17 | convolution fusion | flops 12582912 | bytes 16253184 | tf_op jit(solution)/shard_map/kab,abrn->krn/dot_general | solution.py:92
  58.3 6.7 %bitcast_convert_fusion = bf16[2,512,512]{2,1,0:T(8,128)(2,1)} fusion(bf16[8,512,512]{2,1,0:T(8,128)(2,1)} %param.12, s32[]{:T(128)S(6)} %select_n.116, bf16[8,512,512]{2,1,0:T(8,128)(2,1)} %param.13, bf16[2,8,64,512]{3,1,0,2:T(8,128)(2,1)S(1)} %fusion.9), kind=kOutput, calls=%fused_computation.2 | convolution fusion | flops 1074790400 | bytes 7340036 | tf_op jit(solution)/shard_map/tab,ktbc->kac/dot_general | solution.py:118
  65.0 3.6 %divide_convert_fusion = bf16[2,512,512]{2,1,0:T(8,128)(2,1)} fusion(bf16[2,512,512]{2,1,0:T(8,128)(2,1)S(1)} %copy-done, bf16[2,512,512]{2,1,0:T(8,128)(2,1)} %bitcast_convert_fusion, bf16[2,512,512]{2,1,0:T(8,128)(2,1)S(1)} %copy-done.3, f32[2,512]{1,0:T(2,128)S(1)} %copy-done.5, f32[2,512]{1,0:T(2,128)S(1)} %add.291), kind=kOutput, calls=%fused_computation.11 | convolution fusion | flops 1075838976 | bytes 4202496 | tf_op jit(solution)/shard_map/jrn,jmn->jrm/dot_general | solution.py:124
  68.6 2.1 %convolution_convert_fusion.1 = bf16[2,512,512]{1,2,0:T(8,128)(2,1)S(1)} fusion(bf16[2,512,512]{2,1,0:T(8,128)(2,1)} %divide_convert_fusion, bf16[2,512,512]{2,1,0:T(8,128)(2,1)S(1)} %copy-done.4), kind=kOutput, calls=%fused_computation.14 | convolution fusion | flops 537395200 | bytes 3145728 | tf_op jit(solution)/shard_map/jrm,jkm->jrk/dot_general | solution.py:126
  70.7 0.7 convolution_convert_fusion
  71.8 2.1 %collective-permute-start.16 = (bf16[2,512,64]{1,2,0:T(8,128)(2,1)S(1)}, bf16[2,512,64]{1,2,0:T(8,128)(2,1)S(1)}, u32[]{:S(2)}, u32[]{:S(2)}) collective-permute-start(bf16[2,512,64]{1,2,0:T(8,128)(2,1)S(1)} %get-tuple-element.9), channel_id=1, source_target_pairs={{0,2},{1,3},{2,4},{3,5},{4,6},{5,7},{6,0},{7,1},{8,10},{9,11},{10,... | collective-permute-start | bytes 393224 | tf_op jit(solution)/shard_map/ppermute | solution.py:13
  73.9 3.0 %collective-permute-start.17 = (bf16[2,512,64]{1,2,0:T(8,128)(2,1)S(1)}, bf16[2,512,64]{1,2,0:T(8,128)(2,1)S(1)}, u32[]{:S(2)}, u32[]{:S(2)}) collective-permute-start(bf16[2,512,64]{1,2,0:T(8,128)(2,1)S(1)} %get-tuple-element.8), channel_id=1, source_target_pairs={{0,3},{1,4},{2,5},{3,6},{4,7},{5,0},{6,1},{7,2},{8,11},{9,12},{10,... | collective-permute-start | bytes 393224 | tf_op jit(solution)/shard_map/ppermute | solution.py:13
  77.0 2.0 %collective-permute-start.18 = (bf16[2,512,64]{1,2,0:T(8,128)(2,1)S(1)}, bf16[2,512,64]{1,2,0:T(8,128)(2,1)S(1)}, u32[]{:S(2)}, u32[]{:S(2)}) collective-permute-start(bf16[2,512,64]{1,2,0:T(8,128)(2,1)S(1)} %get-tuple-element.7), channel_id=1, source_target_pairs={{0,4},{1,5},{2,6},{3,7},{4,0},{5,1},{6,2},{7,3},{8,12},{9,13},{10,... | collective-permute-start | bytes 393224 | tf_op jit(solution)/shard_map/ppermute | solution.py:13
  79.0 3.0 %collective-permute-start.19 = (bf16[2,512,64]{1,2,0:T(8,128)(2,1)S(1)}, bf16[2,512,64]{1,2,0:T(8,128)(2,1)S(1)}, u32[]{:S(2)}, u32[]{:S(2)}) collective-permute-start(bf16[2,512,64]{1,2,0:T(8,128)(2,1)S(1)} %get-tuple-element.6), channel_id=1, source_target_pairs={{0,5},{1,6},{2,7},{3,0},{4,1},{5,2},{6,3},{7,4},{8,13},{9,14},{10,... | collective-permute-start | bytes 393224 | tf_op jit(solution)/shard_map/ppermute | solution.py:13
  82.0 3.7 %collective-permute-start.20 = (bf16[2,512,64]{1,2,0:T(8,128)(2,1)S(1)}, bf16[2,512,64]{1,2,0:T(8,128)(2,1)S(1)}, u32[]{:S(2)}, u32[]{:S(2)}) collective-permute-start(bf16[2,512,64]{1,2,0:T(8,128)(2,1)S(1)} %get-tuple-element.11), channel_id=1, source_target_pairs={{0,6},{1,7},{2,0},{3,1},{4,2},{5,3},{6,4},{7,5},{8,14},{9,15},{10,... | collective-permute-start | bytes 393224 | tf_op jit(solution)/shard_map/ppermute | solution.py:13
  85.7 1.9 %collective-permute-start.21 = (bf16[2,512,64]{1,2,0:T(8,128)(2,1)S(1)}, bf16[2,512,64]{1,2,0:T(8,128)(2,1)}, u32[]{:S(2)}, u32[]{:S(2)}) collective-permute-start(bf16[2,512,64]{1,2,0:T(8,128)(2,1)S(1)} %get-tuple-element.10), channel_id=1, source_target_pairs={{0,7},{1,0},{2,1},{3,2},{4,3},{5,4},{6,5},{7,6},{8,15},{9,8},{10,9... | collective-permute-start | bytes 393224 | tf_op jit(solution)/shard_map/ppermute | solution.py:13
  87.6 3.4 %collective-permute-done.17 = bf16[2,512,64]{1,2,0:T(8,128)(2,1)S(1)} collective-permute-done((bf16[2,512,64]{1,2,0:T(8,128)(2,1)S(1)}, bf16[2,512,64]{1,2,0:T(8,128)(2,1)S(1)}, u32[]{:S(2)}, u32[]{:S(2)}) %collective-permute-start.17) | collective-permute-done | bytes 131104 | tf_op jit(solution)/shard_map/ppermute | solution.py:13
  91.0 2.9 %collective-permute-done.18 = bf16[2,512,64]{1,2,0:T(8,128)(2,1)S(1)} collective-permute-done((bf16[2,512,64]{1,2,0:T(8,128)(2,1)S(1)}, bf16[2,512,64]{1,2,0:T(8,128)(2,1)S(1)}, u32[]{:S(2)}, u32[]{:S(2)}) %collective-permute-start.18) | collective-permute-done | bytes 131104 | tf_op jit(solution)/shard_map/ppermute | solution.py:13
  94.0 3.6 %collective-permute-done.19 = bf16[2,512,64]{1,2,0:T(8,128)(2,1)S(1)} collective-permute-done((bf16[2,512,64]{1,2,0:T(8,128)(2,1)S(1)}, bf16[2,512,64]{1,2,0:T(8,128)(2,1)S(1)}, u32[]{:S(2)}, u32[]{:S(2)}) %collective-permute-start.19) | collective-permute-done | bytes 131104 | tf_op jit(solution)/shard_map/ppermute | solution.py:13
  97.6 5.1 %collective-permute-done.20 = bf16[2,512,64]{1,2,0:T(8,128)(2,1)S(1)} collective-permute-done((bf16[2,512,64]{1,2,0:T(8,128)(2,1)S(1)}, bf16[2,512,64]{1,2,0:T(8,128)(2,1)S(1)}, u32[]{:S(2)}, u32[]{:S(2)}) %collective-permute-start.20) | collective-permute-done | bytes 131104 | tf_op jit(solution)/shard_map/ppermute | solution.py:13
  102.6 0.7 collective-permute-done.21
  103.3 1.8 %fusion.24 = f32[2,512,64]{1,2,0:T(8,128)} fusion(bf16[2,512,64]{1,2,0:T(8,128)(2,1)} %collective-permute-done.21, bf16[2,512,64]{1,2,0:T(8,128)(2,1)S(1)} %collective-permute-done.20, bf16[2,512,64]{1,2,0:T(8,128)(2,1)S(1)} %collective-permute-done.19, bf16[2,512,64]{1,2,0:T(8,128)(2,1)S(1)} %collective-permute-done.18, ...), kind=kLoop, calls=%fused_computation.32 | loop fusion | flops 983040 | bytes 1310724 | tf_op jit(solution)/shard_map/add | solution.py:14
  (61 shorter events, 4.1 us)
Async XLA Ops:
  0.0 65.0 %copy-start = (bf16[2,512,512]{2,1,0:T(8,128)(2,1)S(1)}, bf16[2,512,512]{2,1,0:T(8,128)(2,1)}, u32[]{:S(2)}) copy-start(bf16[2,512,512]{2,1,0:T(8,128)(2,1)} %param.19) | copy-start | bytes 3145732
  0.0 26.2 %collective-permute-start.1 = (bf16[2,64,512]{2,1,0:T(8,128)(2,1)}, bf16[2,64,512]{2,1,0:T(8,128)(2,1)S(1)}, u32[]{:S(2)}, u32[]{:S(2)}) collective-permute-start(bf16[2,64,512]{2,1,0:T(8,128)(2,1)} %param.11), channel_id=1, source_target_pairs={{0,64},{8,72},{16,80},{24,88},{32,96},{40,104},{48,112},{56,120},{... | collective-permute-start | bytes 393224 | tf_op jit(solution)/shard_map/ppermute | solution.py:71
  1.5 25.0 %collective-permute-start = (bf16[2,64,512]{2,1,0:T(8,128)(2,1)}, bf16[2,64,512]{2,1,0:T(8,128)(2,1)S(1)}, u32[]{:S(2)}, u32[]{:S(2)}) collective-permute-start(bf16[2,64,512]{2,1,0:T(8,128)(2,1)} %param.11), channel_id=1, source_target_pairs={{0,192},{8,200},{16,208},{24,216},{32,224},{40,232},{48,240},{56,2... | collective-permute-start | bytes 393224 | tf_op jit(solution)/shard_map/ppermute | solution.py:71
  3.2 7.6 %collective-permute-start.12 = (f32[1,2,64]{2,1,0:T(2,128)}, f32[1,2,64]{2,1,0:T(2,128)S(1)}, u32[]{:S(2)}, u32[]{:S(2)}) collective-permute-start(f32[1,2,64]{2,1,0:T(2,128)} %bitcast.223), channel_id=1, source_target_pairs={{0,1},{1,2},{2,3},{3,4},{4,5},{5,6},{6,7},{7,0},{8,9},{9,10},{10,1... | collective-permute-start | bytes 1544 | tf_op jit(solution)/shard_map/ppermute | solution.py:112
  6.7 28.6 %copy-start.2 = (f32[2,64]{1,0:T(2,128)S(1)}, f32[2,64]{1,0:T(2,128)}, u32[]{:S(2)}) copy-start(f32[2,64]{1,0:T(2,128)} %param.20) | copy-start | bytes 1540
  11.5 5.7 %collective-permute-start.13 = (f32[2,2,64]{2,1,0:T(2,128)S(1)}, f32[2,2,64]{2,1,0:T(2,128)S(1)}, u32[]{:S(2)}, u32[]{:S(2)}) collective-permute-start(f32[2,2,64]{2,1,0:T(2,128)S(1)} %pad_maximum_fusion.3), channel_id=1, source_target_pairs={{0,2},{1,3},{2,4},{3,5},{4,6},{5,7},{6,0},{7,1},{8,10},{9,11},{10,... | collective-permute-start | bytes 3080 | tf_op jit(solution)/shard_map/ppermute | solution.py:112
  17.9 7.5 %collective-permute-start.14 = (f32[4,2,64]{2,1,0:T(2,128)S(1)}, f32[4,2,64]{2,1,0:T(2,128)S(1)}, u32[]{:S(2)}, u32[]{:S(2)}) collective-permute-start(f32[4,2,64]{2,1,0:T(2,128)S(1)} %pad_maximum_fusion.2), channel_id=1, source_target_pairs={{0,4},{1,5},{2,6},{3,7},{4,0},{5,1},{6,2},{7,3},{8,12},{9,13},{10,... | collective-permute-start | bytes 6152 | tf_op jit(solution)/shard_map/ppermute | solution.py:112
  26.2 5.6 %collective-permute-start.2 = (bf16[1,64,512]{2,1,0:T(8,128)(2,1)S(1)}, bf16[1,64,512]{2,1,0:T(8,128)(2,1)S(1)}, u32[]{:S(2)}, u32[]{:S(2)}) collective-permute-start(bf16[1,64,512]{2,1,0:T(8,128)(2,1)S(1)} %slice.64), channel_id=1, source_target_pairs={{0,64},{8,72},{16,80},{24,88},{32,96},{40,104},{48,112},{56,120},{... | collective-permute-start | bytes 196616 | tf_op jit(solution)/shard_map/ppermute | solution.py:71
  26.5 5.2 %collective-permute-start.3 = (bf16[1,64,512]{2,1,0:T(8,128)(2,1)S(1)}, bf16[1,64,512]{2,1,0:T(8,128)(2,1)S(1)}, u32[]{:S(2)}, u32[]{:S(2)}) collective-permute-start(bf16[1,64,512]{2,1,0:T(8,128)(2,1)S(1)} %slice.65), channel_id=1, source_target_pairs={{0,192},{8,200},{16,208},{24,216},{32,224},{40,232},{48,240},{56,2... | collective-permute-start | bytes 196616 | tf_op jit(solution)/shard_map/ppermute | solution.py:71
  33.2 12.1 %collective-permute-start.5 = (bf16[4,2,64,512]{3,0,1,2:T(4,128)(2,1)S(1)}, bf16[4,2,64,512]{3,0,1,2:T(4,128)(2,1)S(1)}, u32[]{:S(2)}, u32[]{:S(2)}) collective-permute-start(bf16[4,2,64,512]{3,0,1,2:T(4,128)(2,1)S(1)} %pad_maximum_fusion), channel_id=1, source_target_pairs={{0,16},{8,24},{16,32},{24,40},{32,48},{40,56},{48,0},{56,8},{64,80... | collective-permute-start | bytes 1572872 | tf_op jit(solution)/shard_map/ppermute | solution.py:71
  33.5 12.4 %collective-permute-start.4 = (bf16[4,2,64,512]{3,0,1,2:T(4,128)(2,1)S(1)}, bf16[4,2,64,512]{3,0,1,2:T(4,128)(2,1)S(1)}, u32[]{:S(2)}, u32[]{:S(2)}) collective-permute-start(bf16[4,2,64,512]{3,0,1,2:T(4,128)(2,1)S(1)} %pad_maximum_fusion), channel_id=1, source_target_pairs={{0,48},{8,56},{16,0},{24,8},{32,16},{40,24},{48,32},{56,40},{64,11... | collective-permute-start | bytes 1572872 | tf_op jit(solution)/shard_map/ppermute | solution.py:71
  35.4 14.5 %collective-permute-start.8 = (bf16[4,2,64,512]{3,0,1,2:T(4,128)(2,1)S(1)}, bf16[4,2,64,512]{3,0,1,2:T(4,128)(2,1)S(1)}, u32[]{:S(2)}, u32[]{:S(2)}) collective-permute-start(bf16[4,2,64,512]{3,0,1,2:T(4,128)(2,1)S(1)} %pad_maximum_fusion), channel_id=1, source_target_pairs={{0,8},{8,0},{16,24},{24,16},{32,40},{40,32},{48,56},{56,48},{64,72... | collective-permute-start | bytes 1572872 | tf_op jit(solution)/shard_map/ppermute | solution.py:71
  45.4 6.4 %collective-permute-start.6 = (bf16[2,2,64,512]{3,0,1,2:T(2,128)(2,1)S(1)}, bf16[2,2,64,512]{3,0,1,2:T(2,128)(2,1)S(1)}, u32[]{:S(2)}, u32[]{:S(2)}) collective-permute-start(bf16[2,2,64,512]{3,0,1,2:T(2,128)(2,1)S(1)} %slice.68), channel_id=1, source_target_pairs={{0,16},{8,24},{16,32},{24,40},{32,48},{40,56},{48,0},{56,8},{64,80... | collective-permute-start | bytes 786440 | tf_op jit(solution)/shard_map/ppermute | solution.py:71
  46.2 7.8 %collective-permute-start.7 = (bf16[2,2,64,512]{3,0,1,2:T(2,128)(2,1)S(1)}, bf16[2,2,64,512]{3,0,1,2:T(2,128)(2,1)S(1)}, u32[]{:S(2)}, u32[]{:S(2)}) collective-permute-start(bf16[2,2,64,512]{3,0,1,2:T(2,128)(2,1)S(1)} %slice.69), channel_id=1, source_target_pairs={{0,48},{8,56},{16,0},{24,8},{32,16},{40,24},{48,32},{56,40},{64,11... | collective-permute-start | bytes 786440 | tf_op jit(solution)/shard_map/ppermute | solution.py:71
  48.1 7.6 %collective-permute-start.9 = (bf16[4,2,64,512]{3,0,1,2:T(4,128)(2,1)S(1)}, bf16[4,2,64,512]{3,0,1,2:T(4,128)(2,1)S(1)}, u32[]{:S(2)}, u32[]{:S(2)}) collective-permute-start(bf16[4,2,64,512]{3,0,1,2:T(4,128)(2,1)S(1)} %collective-permute-done.4), channel_id=1, source_target_pairs={{0,8},{8,0},{16,24},{24,16},{32,40},{40,32},{48,56},{56,48},{64,72... | collective-permute-start | bytes 1572872 | tf_op jit(solution)/shard_map/ppermute | solution.py:71
  48.1 9.1 %collective-permute-start.11 = (bf16[4,2,64,512]{3,0,1,2:T(4,128)(2,1)S(1)}, bf16[4,2,64,512]{3,0,1,2:T(4,128)(2,1)S(1)}, u32[]{:S(2)}, u32[]{:S(2)}) collective-permute-start(bf16[4,2,64,512]{3,0,1,2:T(4,128)(2,1)S(1)} %collective-permute-done.5), channel_id=1, source_target_pairs={{0,8},{8,0},{16,24},{24,16},{32,40},{40,32},{48,56},{56,48},{64,72... | collective-permute-start | bytes 1572872 | tf_op jit(solution)/shard_map/ppermute | solution.py:71
  54.6 2.0 %collective-permute-start.10 = (bf16[4,2,64,512]{3,0,1,2:T(4,128)(2,1)S(1)}, bf16[4,2,64,512]{3,0,1,2:T(4,128)(2,1)S(1)}, u32[]{:S(2)}, u32[]{:S(2)}) collective-permute-start(bf16[4,2,64,512]{3,0,1,2:T(4,128)(2,1)S(1)} %pad_maximum_fusion.1), channel_id=1, source_target_pairs={{0,8},{8,0},{16,24},{24,16},{32,40},{40,32},{48,56},{56,48},{64,72... | collective-permute-start | bytes 1572872 | tf_op jit(solution)/shard_map/ppermute | solution.py:71
  58.3 6.7 %copy-start.3 = (bf16[2,512,512]{2,1,0:T(8,128)(2,1)S(1)}, bf16[2,512,512]{2,1,0:T(8,128)(2,1)}, u32[]{:S(2)}) copy-start(bf16[2,512,512]{2,1,0:T(8,128)(2,1)} %param.17) | copy-start | bytes 3145732
  58.3 6.7 %copy-start.5 = (f32[2,512]{1,0:T(2,128)S(1)}, f32[2,512]{1,0:T(2,128)}, u32[]{:S(2)}) copy-start(f32[2,512]{1,0:T(2,128)} %param.21) | copy-start | bytes 12292
  65.0 3.6 %copy-start.4 = (bf16[2,512,512]{2,1,0:T(8,128)(2,1)S(1)}, bf16[2,512,512]{2,1,0:T(8,128)(2,1)}, u32[]{:S(2)}) copy-start(bf16[2,512,512]{2,1,0:T(8,128)(2,1)} %param.18) | copy-start | bytes 3145732
  68.6 2.1 %copy-start.1 = (bf16[2,512,512]{2,1,0:T(8,128)(2,1)S(1)}, bf16[2,512,512]{2,1,0:T(8,128)(2,1)}, u32[]{:S(2)}) copy-start(bf16[2,512,512]{2,1,0:T(8,128)(2,1)} %param.16) | copy-start | bytes 3145732
  71.5 10.5 %collective-permute-start.15 = (bf16[2,512,64]{1,2,0:T(8,128)(2,1)S(1)}, bf16[2,512,64]{1,2,0:T(8,128)(2,1)S(1)}, u32[]{:S(2)}, u32[]{:S(2)}) collective-permute-start(bf16[2,512,64]{1,2,0:T(8,128)(2,1)S(1)} %get-tuple-element.5), channel_id=1, source_target_pairs={{0,1},{1,2},{2,3},{3,4},{4,5},{5,6},{6,7},{7,0},{8,9},{9,10},{10,1... | collective-permute-start | bytes 393224 | tf_op jit(solution)/shard_map/ppermute | solution.py:13
  71.8 13.8 %collective-permute-start.16 = (bf16[2,512,64]{1,2,0:T(8,128)(2,1)S(1)}, bf16[2,512,64]{1,2,0:T(8,128)(2,1)S(1)}, u32[]{:S(2)}, u32[]{:S(2)}) collective-permute-start(bf16[2,512,64]{1,2,0:T(8,128)(2,1)S(1)} %get-tuple-element.9), channel_id=1, source_target_pairs={{0,2},{1,3},{2,4},{3,5},{4,6},{5,7},{6,0},{7,1},{8,10},{9,11},{10,... | collective-permute-start | bytes 393224 | tf_op jit(solution)/shard_map/ppermute | solution.py:13
  73.9 17.1 %collective-permute-start.17 = (bf16[2,512,64]{1,2,0:T(8,128)(2,1)S(1)}, bf16[2,512,64]{1,2,0:T(8,128)(2,1)S(1)}, u32[]{:S(2)}, u32[]{:S(2)}) collective-permute-start(bf16[2,512,64]{1,2,0:T(8,128)(2,1)S(1)} %get-tuple-element.8), channel_id=1, source_target_pairs={{0,3},{1,4},{2,5},{3,6},{4,7},{5,0},{6,1},{7,2},{8,11},{9,12},{10,... | collective-permute-start | bytes 393224 | tf_op jit(solution)/shard_map/ppermute | solution.py:13
  77.0 17.0 %collective-permute-start.18 = (bf16[2,512,64]{1,2,0:T(8,128)(2,1)S(1)}, bf16[2,512,64]{1,2,0:T(8,128)(2,1)S(1)}, u32[]{:S(2)}, u32[]{:S(2)}) collective-permute-start(bf16[2,512,64]{1,2,0:T(8,128)(2,1)S(1)} %get-tuple-element.7), channel_id=1, source_target_pairs={{0,4},{1,5},{2,6},{3,7},{4,0},{5,1},{6,2},{7,3},{8,12},{9,13},{10,... | collective-permute-start | bytes 393224 | tf_op jit(solution)/shard_map/ppermute | solution.py:13
  79.0 18.5 %collective-permute-start.19 = (bf16[2,512,64]{1,2,0:T(8,128)(2,1)S(1)}, bf16[2,512,64]{1,2,0:T(8,128)(2,1)S(1)}, u32[]{:S(2)}, u32[]{:S(2)}) collective-permute-start(bf16[2,512,64]{1,2,0:T(8,128)(2,1)S(1)} %get-tuple-element.6), channel_id=1, source_target_pairs={{0,5},{1,6},{2,7},{3,0},{4,1},{5,2},{6,3},{7,4},{8,13},{9,14},{10,... | collective-permute-start | bytes 393224 | tf_op jit(solution)/shard_map/ppermute | solution.py:13
  82.0 20.6 %collective-permute-start.20 = (bf16[2,512,64]{1,2,0:T(8,128)(2,1)S(1)}, bf16[2,512,64]{1,2,0:T(8,128)(2,1)S(1)}, u32[]{:S(2)}, u32[]{:S(2)}) collective-permute-start(bf16[2,512,64]{1,2,0:T(8,128)(2,1)S(1)} %get-tuple-element.11), channel_id=1, source_target_pairs={{0,6},{1,7},{2,0},{3,1},{4,2},{5,3},{6,4},{7,5},{8,14},{9,15},{10,... | collective-permute-start | bytes 393224 | tf_op jit(solution)/shard_map/ppermute | solution.py:13
  85.7 17.6 %collective-permute-start.21 = (bf16[2,512,64]{1,2,0:T(8,128)(2,1)S(1)}, bf16[2,512,64]{1,2,0:T(8,128)(2,1)}, u32[]{:S(2)}, u32[]{:S(2)}) collective-permute-start(bf16[2,512,64]{1,2,0:T(8,128)(2,1)S(1)} %get-tuple-element.10), channel_id=1, source_target_pairs={{0,7},{1,0},{2,1},{3,2},{4,3},{5,4},{6,5},{7,6},{8,15},{9,8},{10,9... | collective-permute-start | bytes 393224 | tf_op jit(solution)/shard_map/ppermute | solution.py:13

commit v4 on v3

--- a/solution.py
+++ b/solution.py
@@ -106,7 +106,7 @@
         "ktrn,tmn->ktrm", pooled, right_factor, preferred_element_type=jnp.float32
     ).astype(jnp.bfloat16)
     left_part = lax.dynamic_slice_in_dim(left_factor, part * row_count, row_count, axis=2)
-    rates_run = left_rates[None]
+    rates_run, pooled = lax.optimization_barrier((left_rates[None], pooled))
     step = 1
     while step < pieces:
         came = lax.ppermute(rates_run, "sub", [(j, (j + step) % pieces) for j in range(pieces)])

time: 107 us -> 102 us (0.953)
  starting transfers between devices: 34.7 us -> 26.7 us
  waiting for transfers between devices: 40.2 us -> 46.6 us
  other arithmetic: 5.23 us -> 3.86 us
    ppermute x7, starting transfers between devices: 16.1 us -> 8.38 us  [scatter_sum(): got = lax.ppermute(send, axis, [(j, (j + k) % n) for j in range(n)])]
    ppermute x7, waiting for transfers between devices: 15.7 us -> 20.2 us  [scatter_sum(): got = lax.ppermute(send, axis, [(j, (j + k) % n) for j in range(n)])]
    concatenate x2, other arithmetic: 1.37 us -> 0.01 us  [local(): rates_run = jnp.concatenate([came, rates_run], axis=0)]
    ppermute x3, waiting for transfers between devices: 9.79 us -> 11.1 us  [local(): lax.ppermute(rates_run, 'sub', [(j, (j + step) % pieces) for j in range(p...]
  transfers between devices with their start and end apart: 22 -> 22, of which waited for: 13 -> 14; matrix products, arithmetic and copies ran while one was open for 12% -> 16% of each run, Pallas kernels for 0% -> 0%
where the time goes in v4:
time: 102 us; the launch traced here: 101 us
  waiting for transfers between devices  46.6 us (46%)
  starting transfers between devices  26.7 us (26%)
  matrix products  18.8 us (18%)
  local copies, waits for them, and re-layouts  4.79 us (5%)
  other arithmetic  3.86 us (4%)
    ppermute x7, waiting for transfers between devices, scatter_sum(): got = lax.ppermute(send, axis, [(j, (j + k) % n) for j in range(n)])  20.2 us
    ppermute x12, waiting for transfers between devices, move(): return lax.ppermute(piece, 'blk', pairs_list)  15.3 us
    ppermute x12, starting transfers between devices, move(): return lax.ppermute(piece, 'blk', pairs_list)  11.5 us
    ppermute x3, waiting for transfers between devices, local(): lax.ppermute(rates_run, 'sub', [(j, (j + step) % pieces) for j in range(p...  11.1 us
    ppermute x7, starting transfers between devices, scatter_sum(): got = lax.ppermute(send, axis, [(j, (j + k) % n) for j in range(n)])  8.38 us
    ppermute x3, starting transfers between devices, local(): lax.ppermute(rates_run, 'sub', [(j, (j + step) % pieces) for j in range(p...  6.8 us
    dot_general x1, matrix products, local(): jnp.einsum('tab,ktbc->kac', left_part, right_done, preferred_element_type...  6.58 us
    dot_general x8, matrix products, pool(): jnp.einsum('kab,abrn->krn', w, piece, preferred_element_type=jnp.float32)  5.7 us
  transfers between devices with their start and end apart: 22, of which 14 were waited for; matrix products, arithmetic and copies ran while one was open for 16% of the time, Pallas kernels for 0%

profile of v4, /device:TPU:24, one launch (start us, length us, event | category | flops | bytes accessed | tf_op | source)
XLA Modules:
  0.0 101.1 jit_solution(1035376664678027264)
XLA Ops:
  0.0 1.5 %collective-permute-start.1 = (bf16[2,64,512]{2,1,0:T(8,128)(2,1)}, bf16[2,64,512]{2,1,0:T(8,128)(2,1)S(1)}, u32[]{:S(2)}, u32[]{:S(2)}) collective-permute-start(bf16[2,64,512]{2,1,0:T(8,128)(2,1)} %param.11), channel_id=1, source_target_pairs={{0,64},{8,72},{16,80},{24,88},{32,96},{40,104},{48,112},{56,120},{... | collective-permute-start | bytes 393224 | tf_op jit(solution)/shard_map/ppermute | solution.py:71
  1.5 1.7 %collective-permute-start = (bf16[2,64,512]{2,1,0:T(8,128)(2,1)}, bf16[2,64,512]{2,1,0:T(8,128)(2,1)S(1)}, u32[]{:S(2)}, u32[]{:S(2)}) collective-permute-start(bf16[2,64,512]{2,1,0:T(8,128)(2,1)} %param.11), channel_id=1, source_target_pairs={{0,192},{8,200},{16,208},{24,216},{32,224},{40,232},{48,240},{56,2... | collective-permute-start | bytes 393224 | tf_op jit(solution)/shard_map/ppermute | solution.py:71
  3.6 1.1 %constant_dynamic-slice_fusion = s32[32,1,2,3]{1,2,3,0:T(2,128)S(1)} fusion(s32[32,32,2,3]{1,2,3,0:T(2,128)} %param.14, s32[]{:T(128)S(6)} %select_n.109), kind=kLoop, calls=%fused_computation.63 | loop fusion | bytes 1540 | tf_op jit(solution)/shard_map/jit(dynamic_index_in_dim)/dynamic_slice | solution.py:42
  4.7 0.9 dynamic-slice_reduce_fusion
  5.7 1.0 collective-permute-done.1
  7.0 3.0 %collective-permute-start.3 = (bf16[1,64,512]{2,1,0:T(8,128)(2,1)S(1)}, bf16[1,64,512]{2,1,0:T(8,128)(2,1)S(1)}, u32[]{:S(2)}, u32[]{:S(2)}) collective-permute-start(bf16[1,64,512]{2,1,0:T(8,128)(2,1)S(1)} %slice.65), channel_id=1, source_target_pairs={{0,192},{8,200},{16,208},{24,216},{32,224},{40,232},{48,240},{56,2... | collective-permute-start | bytes 196616 | tf_op jit(solution)/shard_map/ppermute | solution.py:71
  10.1 1.1 %copy.87 = bf16[1,2,64,512]{3,0,1,2:T(2,128)(2,1)S(1)} copy(bf16[1,2,64,512]{3,2,1,0:T(8,128)(2,1)} %bitcast.219) | data formatting | bytes 262144 | tf_op jit(solution)/shard_map/stack | solution.py:79
  11.6 0.5 collective-permute-done.2
  12.4 1.2 %pad_maximum_fusion = bf16[4,2,64,512]{3,0,1,2:T(4,128)(2,1)S(1)} fusion(bf16[1,2,64,512]{3,0,1,2:T(2,128)(2,1)S(1)} %copy.90, bf16[1,2,64,512]{3,0,1,2:T(2,128)(2,1)S(1)} %copy.89, bf16[1,2,64,512]{3,0,1,2:T(2,128)(2,1)S(1)} %copy.88, bf16[1,2,64,512]{3,0,1,2:T(2,128)(2,1)S(1)} %copy.87), kind=kLoop, calls=%fused_computation.24 | loop fusion | flops 2097152 | bytes 1048576 | tf_op jit(solution)/shard_map/stack | solution.py:79
  13.6 1.8 %collective-permute-start.5 = (bf16[4,2,64,512]{3,0,1,2:T(4,128)(2,1)S(1)}, bf16[4,2,64,512]{3,0,1,2:T(4,128)(2,1)S(1)}, u32[]{:S(2)}, u32[]{:S(2)}) collective-permute-start(bf16[4,2,64,512]{3,0,1,2:T(4,128)(2,1)S(1)} %pad_maximum_fusion), channel_id=1, source_target_pairs={{0,16},{8,24},{16,32},{24,40},{32,48},{40,56},{48,0},{56,8},{64,80... | collective-permute-start | bytes 1572872 | tf_op jit(solution)/shard_map/ppermute | solution.py:71
  15.4 0.3 collective-permute-start.4
  16.1 0.6 fusion.46
  16.7 8.8 %collective-permute-done.5 = bf16[4,2,64,512]{3,0,1,2:T(4,128)(2,1)S(1)} collective-permute-done((bf16[4,2,64,512]{3,0,1,2:T(4,128)(2,1)S(1)}, bf16[4,2,64,512]{3,0,1,2:T(4,128)(2,1)S(1)}, u32[]{:S(2)}, u32[]{:S(2)}) %collective-permute-start.5) | collective-permute-done | bytes 524320 | tf_op jit(solution)/shard_map/ppermute | solution.py:71
  25.7 1.6 %collective-permute-start.6 = (bf16[2,2,64,512]{3,0,1,2:T(2,128)(2,1)S(1)}, bf16[2,2,64,512]{3,0,1,2:T(2,128)(2,1)S(1)}, u32[]{:S(2)}, u32[]{:S(2)}) collective-permute-start(bf16[2,2,64,512]{3,0,1,2:T(2,128)(2,1)S(1)} %slice.68), channel_id=1, source_target_pairs={{0,16},{8,24},{16,32},{24,40},{32,48},{40,56},{48,0},{56,8},{64,80... | collective-permute-start | bytes 786440 | tf_op jit(solution)/shard_map/ppermute | solution.py:71
  27.3 0.3 slice.69
  27.6 0.6 collective-permute-start.7
  28.2 0.5 collective-permute-start.11
  28.7 0.6 fusion.40
  29.3 0.6 fusion.44
  29.9 0.6 fusion.38
  30.5 1.6 %collective-permute-done.6 = bf16[2,2,64,512]{3,0,1,2:T(2,128)(2,1)S(1)} collective-permute-done((bf16[2,2,64,512]{3,0,1,2:T(2,128)(2,1)S(1)}, bf16[2,2,64,512]{3,0,1,2:T(2,128)(2,1)S(1)}, u32[]{:S(2)}, u32[]{:S(2)}) %collective-permute-start.6) | collective-permute-done | bytes 262176 | tf_op jit(solution)/shard_map/ppermute | solution.py:71
  32.1 3.1 %collective-permute-done.7 = bf16[2,2,64,512]{3,0,1,2:T(2,128)(2,1)S(1)} collective-permute-done((bf16[2,2,64,512]{3,0,1,2:T(2,128)(2,1)S(1)}, bf16[2,2,64,512]{3,0,1,2:T(2,128)(2,1)S(1)}, u32[]{:S(2)}, u32[]{:S(2)}) %collective-permute-start.7) | collective-permute-done | bytes 262176 | tf_op jit(solution)/shard_map/ppermute | solution.py:71
  35.2 0.5 pad_maximum_fusion.1
  35.9 1.0 fusion.42
  36.9 0.6 fusion.36
  37.5 0.3 collective-permute-done.10
  37.8 0.6 fusion.34
  38.4 1.1 %fusion.9 = bf16[2,8,64,512]{3,1,0,2:T(8,128)(2,1)S(1)} fusion(bf16[4,2,64,512]{3,0,1,2:T(4,128)(2,1)S(1)} %collective-permute-done.11, f32[16,64,512,1]{2,0,3,1:T(8,128)S(1)} %fusion.34, f32[16,64,512,1]{2,0,3,1:T(8,128)S(1)} %fusion.36, f32[16,64,512,1]{2,0,3,1:T(8,128)S(1)} %fusion.38, f32[16,64,512,1]{2,0,3,1:T(8,128)S(1)} %fusion.40, ...), kind=kOutput, calls=%fused_computation.17 | convolution fusion | flops 12582912 | bytes 16253184 | tf_op jit(solution)/shard_map/kab,abrn->krn/dot_general | solution.py:92
  39.5 1.9 %collective-permute-start.12 = (f32[1,2,64]{2,1,0:T(2,128)S(1)}, f32[1,2,64]{2,1,0:T(2,128)S(1)}, u32[]{:S(2)}, u32[]{:S(2)}) collective-permute-start(f32[1,2,64]{2,1,0:T(2,128)S(1)} %bitcast.221), channel_id=1, source_target_pairs={{0,1},{1,2},{2,3},{3,4},{4,5},{5,6},{6,7},{7,0},{8,9},{9,10},{10,1... | collective-permute-start | bytes 1544 | tf_op jit(solution)/shard_map/ppermute | solution.py:112
  41.4 5.5 %collective-permute-done.12 = f32[1,2,64]{2,1,0:T(2,128)S(1)} collective-permute-done((f32[1,2,64]{2,1,0:T(2,128)S(1)}, f32[1,2,64]{2,1,0:T(2,128)S(1)}, u32[]{:S(2)}, u32[]{:S(2)}) %collective-permute-start.12) | collective-permute-done | bytes 544 | tf_op jit(solution)/shard_map/ppermute | solution.py:112
  47.0 5.6 %collective-permute-done.13 = f32[2,2,64]{2,1,0:T(2,128)S(1)} collective-permute-done((f32[2,2,64]{2,1,0:T(2,128)S(1)}, f32[2,2,64]{2,1,0:T(2,128)S(1)}, u32[]{:S(2)}, u32[]{:S(2)}) %collective-permute-start.13) | collective-permute-done | bytes 1056 | tf_op jit(solution)/shard_map/ppermute | solution.py:112
  52.6 4.9 %collective-permute-start.14 = (f32[4,2,64]{2,1,0:T(2,128)S(1)}, f32[4,2,64]{2,1,0:T(2,128)S(1)}, u32[]{:S(2)}, u32[]{:S(2)}) collective-permute-start(f32[4,2,64]{2,1,0:T(2,128)S(1)} %pad_maximum_fusion.2), channel_id=1, source_target_pairs={{0,4},{1,5},{2,6},{3,7},{4,0},{5,1},{6,2},{7,3},{8,12},{9,13},{10,... | collective-permute-start | bytes 6152 | tf_op jit(solution)/shard_map/ppermute | solution.py:112
  57.5 6.6 %bitcast_convert_fusion = bf16[2,512,512]{2,1,0:T(8,128)(2,1)} fusion(bf16[8,512,512]{2,1,0:T(8,128)(2,1)} %param.12, s32[]{:T(128)S(6)} %select_n.116, bf16[8,512,512]{2,1,0:T(8,128)(2,1)} %param.13, bf16[2,8,64,512]{3,1,0,2:T(8,128)(2,1)S(1)} %fusion.9), kind=kOutput, calls=%fused_computation.2 | convolution fusion | flops 1074790400 | bytes 7340036 | tf_op jit(solution)/shard_map/tab,ktbc->kac/dot_general | solution.py:118
  64.3 3.6 %divide_convert_fusion = bf16[2,512,512]{2,1,0:T(8,128)(2,1)} fusion(bf16[2,512,512]{2,1,0:T(8,128)(2,1)S(1)} %copy-done, bf16[2,512,512]{2,1,0:T(8,128)(2,1)} %bitcast_convert_fusion, bf16[2,512,512]{2,1,0:T(8,128)(2,1)S(1)} %copy-done.3, f32[2,512]{1,0:T(2,128)S(1)} %copy-done.5, f32[2,512]{1,0:T(2,128)S(1)} %add.291), kind=kOutput, calls=%fused_computation.11 | convolution fusion | flops 1075838976 | bytes 4202496 | tf_op jit(solution)/shard_map/jrn,jmn->jrm/dot_general | solution.py:124
  67.9 2.1 %convolution_convert_fusion.1 = bf16[2,512,512]{1,2,0:T(8,128)(2,1)S(1)} fusion(bf16[2,512,512]{2,1,0:T(8,128)(2,1)} %divide_convert_fusion, bf16[2,512,512]{2,1,0:T(8,128)(2,1)S(1)} %copy-done.4), kind=kOutput, calls=%fused_computation.14 | convolution fusion | flops 537395200 | bytes 3145728 | tf_op jit(solution)/shard_map/jrm,jkm->jrk/dot_general | solution.py:126
  70.0 0.7 convolution_convert_fusion
  71.0 2.6 %collective-permute-start.17 = (bf16[2,512,64]{1,2,0:T(8,128)(2,1)S(1)}, bf16[2,512,64]{1,2,0:T(8,128)(2,1)S(1)}, u32[]{:S(2)}, u32[]{:S(2)}) collective-permute-start(bf16[2,512,64]{1,2,0:T(8,128)(2,1)S(1)} %get-tuple-element.10), channel_id=1, source_target_pairs={{0,3},{1,4},{2,5},{3,6},{4,7},{5,0},{6,1},{7,2},{8,11},{9,12},{10,... | collective-permute-start | bytes 393224 | tf_op jit(solution)/shard_map/ppermute | solution.py:13
  73.6 3.8 %collective-permute-start.18 = (bf16[2,512,64]{1,2,0:T(8,128)(2,1)S(1)}, bf16[2,512,64]{1,2,0:T(8,128)(2,1)S(1)}, u32[]{:S(2)}, u32[]{:S(2)}) collective-permute-start(bf16[2,512,64]{1,2,0:T(8,128)(2,1)S(1)} %get-tuple-element.9), channel_id=1, source_target_pairs={{0,4},{1,5},{2,6},{3,7},{4,0},{5,1},{6,2},{7,3},{8,12},{9,13},{10,... | collective-permute-start | bytes 393224 | tf_op jit(solution)/shard_map/ppermute | solution.py:13
  77.4 0.9 collective-permute-start.19
  78.3 2.9 %collective-permute-done.15 = bf16[2,512,64]{1,2,0:T(8,128)(2,1)S(1)} collective-permute-done((bf16[2,512,64]{1,2,0:T(8,128)(2,1)S(1)}, bf16[2,512,64]{1,2,0:T(8,128)(2,1)S(1)}, u32[]{:S(2)}, u32[]{:S(2)}) %collective-permute-start.15) | collective-permute-done | bytes 131104 | tf_op jit(solution)/shard_map/ppermute | solution.py:13
  81.2 0.4 collective-permute-start.20
  81.5 6.2 %collective-permute-done.16 = bf16[2,512,64]{1,2,0:T(8,128)(2,1)S(1)} collective-permute-done((bf16[2,512,64]{1,2,0:T(8,128)(2,1)S(1)}, bf16[2,512,64]{1,2,0:T(8,128)(2,1)S(1)}, u32[]{:S(2)}, u32[]{:S(2)}) %collective-permute-start.16) | collective-permute-done | bytes 131104 | tf_op jit(solution)/shard_map/ppermute | solution.py:13
  87.7 0.6 collective-permute-start.21
  88.2 2.7 %collective-permute-done.17 = bf16[2,512,64]{1,2,0:T(8,128)(2,1)S(1)} collective-permute-done((bf16[2,512,64]{1,2,0:T(8,128)(2,1)S(1)}, bf16[2,512,64]{1,2,0:T(8,128)(2,1)S(1)}, u32[]{:S(2)}, u32[]{:S(2)}) %collective-permute-start.17) | collective-permute-done | bytes 131104 | tf_op jit(solution)/shard_map/ppermute | solution.py:13
  90.9 0.8 collective-permute-done.19
  91.7 5.9 %collective-permute-done.20 = bf16[2,512,64]{1,2,0:T(8,128)(2,1)S(1)} collective-permute-done((bf16[2,512,64]{1,2,0:T(8,128)(2,1)S(1)}, bf16[2,512,64]{1,2,0:T(8,128)(2,1)S(1)}, u32[]{:S(2)}, u32[]{:S(2)}) %collective-permute-start.20) | collective-permute-done | bytes 131104 | tf_op jit(solution)/shard_map/ppermute | solution.py:13
  97.6 1.8 %collective-permute-done.21 = bf16[2,512,64]{1,2,0:T(8,128)(2,1)} collective-permute-done((bf16[2,512,64]{1,2,0:T(8,128)(2,1)S(1)}, bf16[2,512,64]{1,2,0:T(8,128)(2,1)}, u32[]{:S(2)}, u32[]{:S(2)}) %collective-permute-start.21) | collective-permute-done | bytes 131104 | tf_op jit(solution)/shard_map/ppermute | solution.py:13
  99.4 1.7 %fusion.24 = f32[2,512,64]{1,2,0:T(8,128)} fusion(bf16[2,512,64]{1,2,0:T(8,128)(2,1)} %collective-permute-done.21, bf16[2,512,64]{1,2,0:T(8,128)(2,1)S(1)} %collective-permute-done.20, bf16[2,512,64]{1,2,0:T(8,128)(2,1)S(1)} %collective-permute-done.19, bf16[2,512,64]{1,2,0:T(8,128)(2,1)S(1)} %collective-permute-done.18, ...), kind=kLoop, calls=%fused_computation.32 | loop fusion | flops 983040 | bytes 1310724 | tf_op jit(solution)/shard_map/add | solution.py:14
  (61 shorter events, 2.6 us)
Async XLA Ops:
  0.0 64.3 %copy-start = (bf16[2,512,512]{2,1,0:T(8,128)(2,1)S(1)}, bf16[2,512,512]{2,1,0:T(8,128)(2,1)}, u32[]{:S(2)}) copy-start(bf16[2,512,512]{2,1,0:T(8,128)(2,1)} %param.19) | copy-start | bytes 3145732
  0.0 6.7 %collective-permute-start.1 = (bf16[2,64,512]{2,1,0:T(8,128)(2,1)}, bf16[2,64,512]{2,1,0:T(8,128)(2,1)S(1)}, u32[]{:S(2)}, u32[]{:S(2)}) collective-permute-start(bf16[2,64,512]{2,1,0:T(8,128)(2,1)} %param.11), channel_id=1, source_target_pairs={{0,64},{8,72},{16,80},{24,88},{32,96},{40,104},{48,112},{56,120},{... | collective-permute-start | bytes 393224 | tf_op jit(solution)/shard_map/ppermute | solution.py:71
  1.5 5.5 %collective-permute-start = (bf16[2,64,512]{2,1,0:T(8,128)(2,1)}, bf16[2,64,512]{2,1,0:T(8,128)(2,1)S(1)}, u32[]{:S(2)}, u32[]{:S(2)}) collective-permute-start(bf16[2,64,512]{2,1,0:T(8,128)(2,1)} %param.11), channel_id=1, source_target_pairs={{0,192},{8,200},{16,208},{24,216},{32,224},{40,232},{48,240},{56,2... | collective-permute-start | bytes 393224 | tf_op jit(solution)/shard_map/ppermute | solution.py:71
  6.7 5.5 %collective-permute-start.2 = (bf16[1,64,512]{2,1,0:T(8,128)(2,1)S(1)}, bf16[1,64,512]{2,1,0:T(8,128)(2,1)S(1)}, u32[]{:S(2)}, u32[]{:S(2)}) collective-permute-start(bf16[1,64,512]{2,1,0:T(8,128)(2,1)S(1)} %slice.64), channel_id=1, source_target_pairs={{0,64},{8,72},{16,80},{24,88},{32,96},{40,104},{48,112},{56,120},{... | collective-permute-start | bytes 196616 | tf_op jit(solution)/shard_map/ppermute | solution.py:71
  7.0 5.2 %collective-permute-start.3 = (bf16[1,64,512]{2,1,0:T(8,128)(2,1)S(1)}, bf16[1,64,512]{2,1,0:T(8,128)(2,1)S(1)}, u32[]{:S(2)}, u32[]{:S(2)}) collective-permute-start(bf16[1,64,512]{2,1,0:T(8,128)(2,1)S(1)} %slice.65), channel_id=1, source_target_pairs={{0,192},{8,200},{16,208},{24,216},{32,224},{40,232},{48,240},{56,2... | collective-permute-start | bytes 196616 | tf_op jit(solution)/shard_map/ppermute | solution.py:71
  13.6 11.9 %collective-permute-start.5 = (bf16[4,2,64,512]{3,0,1,2:T(4,128)(2,1)S(1)}, bf16[4,2,64,512]{3,0,1,2:T(4,128)(2,1)S(1)}, u32[]{:S(2)}, u32[]{:S(2)}) collective-permute-start(bf16[4,2,64,512]{3,0,1,2:T(4,128)(2,1)S(1)} %pad_maximum_fusion), channel_id=1, source_target_pairs={{0,16},{8,24},{16,32},{24,40},{32,48},{40,56},{48,0},{56,8},{64,80... | collective-permute-start | bytes 1572872 | tf_op jit(solution)/shard_map/ppermute | solution.py:71
  15.4 11.9 %collective-permute-start.4 = (bf16[4,2,64,512]{3,0,1,2:T(4,128)(2,1)S(1)}, bf16[4,2,64,512]{3,0,1,2:T(4,128)(2,1)S(1)}, u32[]{:S(2)}, u32[]{:S(2)}) collective-permute-start(bf16[4,2,64,512]{3,0,1,2:T(4,128)(2,1)S(1)} %pad_maximum_fusion), channel_id=1, source_target_pairs={{0,48},{8,56},{16,0},{24,8},{32,16},{40,24},{48,32},{56,40},{64,11... | collective-permute-start | bytes 1572872 | tf_op jit(solution)/shard_map/ppermute | solution.py:71
  16.0 13.9 %collective-permute-start.8 = (bf16[4,2,64,512]{3,0,1,2:T(4,128)(2,1)S(1)}, bf16[4,2,64,512]{3,0,1,2:T(4,128)(2,1)S(1)}, u32[]{:S(2)}, u32[]{:S(2)}) collective-permute-start(bf16[4,2,64,512]{3,0,1,2:T(4,128)(2,1)S(1)} %pad_maximum_fusion), channel_id=1, source_target_pairs={{0,8},{8,0},{16,24},{24,16},{32,40},{40,32},{48,56},{56,48},{64,72... | collective-permute-start | bytes 1572872 | tf_op jit(solution)/shard_map/ppermute | solution.py:71
  25.7 6.4 %collective-permute-start.6 = (bf16[2,2,64,512]{3,0,1,2:T(2,128)(2,1)S(1)}, bf16[2,2,64,512]{3,0,1,2:T(2,128)(2,1)S(1)}, u32[]{:S(2)}, u32[]{:S(2)}) collective-permute-start(bf16[2,2,64,512]{3,0,1,2:T(2,128)(2,1)S(1)} %slice.68), channel_id=1, source_target_pairs={{0,16},{8,24},{16,32},{24,40},{32,48},{40,56},{48,0},{56,8},{64,80... | collective-permute-start | bytes 786440 | tf_op jit(solution)/shard_map/ppermute | solution.py:71
  27.6 7.7 %collective-permute-start.7 = (bf16[2,2,64,512]{3,0,1,2:T(2,128)(2,1)S(1)}, bf16[2,2,64,512]{3,0,1,2:T(2,128)(2,1)S(1)}, u32[]{:S(2)}, u32[]{:S(2)}) collective-permute-start(bf16[2,2,64,512]{3,0,1,2:T(2,128)(2,1)S(1)} %slice.69), channel_id=1, source_target_pairs={{0,48},{8,56},{16,0},{24,8},{32,16},{40,24},{48,32},{56,40},{64,11... | collective-permute-start | bytes 786440 | tf_op jit(solution)/shard_map/ppermute | solution.py:71
  28.2 8.7 %collective-permute-start.9 = (bf16[4,2,64,512]{3,0,1,2:T(4,128)(2,1)S(1)}, bf16[4,2,64,512]{3,0,1,2:T(4,128)(2,1)S(1)}, u32[]{:S(2)}, u32[]{:S(2)}) collective-permute-start(bf16[4,2,64,512]{3,0,1,2:T(4,128)(2,1)S(1)} %collective-permute-done.4), channel_id=1, source_target_pairs={{0,8},{8,0},{16,24},{24,16},{32,40},{40,32},{48,56},{56,48},{64,72... | collective-permute-start | bytes 1572872 | tf_op jit(solution)/shard_map/ppermute | solution.py:71
  28.2 10.2 %collective-permute-start.11 = (bf16[4,2,64,512]{3,0,1,2:T(4,128)(2,1)S(1)}, bf16[4,2,64,512]{3,0,1,2:T(4,128)(2,1)S(1)}, u32[]{:S(2)}, u32[]{:S(2)}) collective-permute-start(bf16[4,2,64,512]{3,0,1,2:T(4,128)(2,1)S(1)} %collective-permute-done.5), channel_id=1, source_target_pairs={{0,8},{8,0},{16,24},{24,16},{32,40},{40,32},{48,56},{56,48},{64,72... | collective-permute-start | bytes 1572872 | tf_op jit(solution)/shard_map/ppermute | solution.py:71
  35.8 2.0 %collective-permute-start.10 = (bf16[4,2,64,512]{3,0,1,2:T(4,128)(2,1)S(1)}, bf16[4,2,64,512]{3,0,1,2:T(4,128)(2,1)S(1)}, u32[]{:S(2)}, u32[]{:S(2)}) collective-permute-start(bf16[4,2,64,512]{3,0,1,2:T(4,128)(2,1)S(1)} %pad_maximum_fusion.1), channel_id=1, source_target_pairs={{0,8},{8,0},{16,24},{24,16},{32,40},{40,32},{48,56},{56,48},{64,72... | collective-permute-start | bytes 1572872 | tf_op jit(solution)/shard_map/ppermute | solution.py:71
  38.4 1.1 %copy-start.2 = (f32[2,64]{1,0:T(2,128)S(1)}, f32[2,64]{1,0:T(2,128)}, u32[]{:S(2)}) copy-start(f32[2,64]{1,0:T(2,128)} %param.20) | copy-start | bytes 1540
  39.5 7.4 %collective-permute-start.12 = (f32[1,2,64]{2,1,0:T(2,128)S(1)}, f32[1,2,64]{2,1,0:T(2,128)S(1)}, u32[]{:S(2)}, u32[]{:S(2)}) collective-permute-start(f32[1,2,64]{2,1,0:T(2,128)S(1)} %bitcast.221), channel_id=1, source_target_pairs={{0,1},{1,2},{2,3},{3,4},{4,5},{5,6},{6,7},{7,0},{8,9},{9,10},{10,1... | collective-permute-start | bytes 1544 | tf_op jit(solution)/shard_map/ppermute | solution.py:112
  46.9 5.7 %collective-permute-start.13 = (f32[2,2,64]{2,1,0:T(2,128)S(1)}, f32[2,2,64]{2,1,0:T(2,128)S(1)}, u32[]{:S(2)}, u32[]{:S(2)}) collective-permute-start(f32[2,2,64]{2,1,0:T(2,128)S(1)} %pad_maximum_fusion.3), channel_id=1, source_target_pairs={{0,2},{1,3},{2,4},{3,5},{4,6},{5,7},{6,0},{7,1},{8,10},{9,11},{10,... | collective-permute-start | bytes 3080 | tf_op jit(solution)/shard_map/ppermute | solution.py:112
  52.6 11.7 %copy-start.3 = (bf16[2,512,512]{2,1,0:T(8,128)(2,1)S(1)}, bf16[2,512,512]{2,1,0:T(8,128)(2,1)}, u32[]{:S(2)}) copy-start(bf16[2,512,512]{2,1,0:T(8,128)(2,1)} %param.17) | copy-start | bytes 3145732
  52.6 11.7 %copy-start.5 = (f32[2,512]{1,0:T(2,128)S(1)}, f32[2,512]{1,0:T(2,128)}, u32[]{:S(2)}) copy-start(f32[2,512]{1,0:T(2,128)} %param.21) | copy-start | bytes 12292
  52.6 11.5 %collective-permute-start.14 = (f32[4,2,64]{2,1,0:T(2,128)S(1)}, f32[4,2,64]{2,1,0:T(2,128)S(1)}, u32[]{:S(2)}, u32[]{:S(2)}) collective-permute-start(f32[4,2,64]{2,1,0:T(2,128)S(1)} %pad_maximum_fusion.2), channel_id=1, source_target_pairs={{0,4},{1,5},{2,6},{3,7},{4,0},{5,1},{6,2},{7,3},{8,12},{9,13},{10,... | collective-permute-start | bytes 6152 | tf_op jit(solution)/shard_map/ppermute | solution.py:112
  64.3 3.6 %copy-start.4 = (bf16[2,512,512]{2,1,0:T(8,128)(2,1)S(1)}, bf16[2,512,512]{2,1,0:T(8,128)(2,1)}, u32[]{:S(2)}) copy-start(bf16[2,512,512]{2,1,0:T(8,128)(2,1)} %param.18) | copy-start | bytes 3145732
  67.9 2.1 %copy-start.1 = (bf16[2,512,512]{2,1,0:T(8,128)(2,1)S(1)}, bf16[2,512,512]{2,1,0:T(8,128)(2,1)}, u32[]{:S(2)}) copy-start(bf16[2,512,512]{2,1,0:T(8,128)(2,1)} %param.16) | copy-start | bytes 3145732
  70.8 10.4 %collective-permute-start.15 = (bf16[2,512,64]{1,2,0:T(8,128)(2,1)S(1)}, bf16[2,512,64]{1,2,0:T(8,128)(2,1)S(1)}, u32[]{:S(2)}, u32[]{:S(2)}) collective-permute-start(bf16[2,512,64]{1,2,0:T(8,128)(2,1)S(1)} %get-tuple-element.7), channel_id=1, source_target_pairs={{0,1},{1,2},{2,3},{3,4},{4,5},{5,6},{6,7},{7,0},{8,9},{9,10},{10,1... | collective-permute-start | bytes 393224 | tf_op jit(solution)/shard_map/ppermute | solution.py:13
  70.9 16.8 %collective-permute-start.16 = (bf16[2,512,64]{1,2,0:T(8,128)(2,1)S(1)}, bf16[2,512,64]{1,2,0:T(8,128)(2,1)S(1)}, u32[]{:S(2)}, u32[]{:S(2)}) collective-permute-start(bf16[2,512,64]{1,2,0:T(8,128)(2,1)S(1)} %get-tuple-element.11), channel_id=1, source_target_pairs={{0,2},{1,3},{2,4},{3,5},{4,6},{5,7},{6,0},{7,1},{8,10},{9,11},{10,... | collective-permute-start | bytes 393224 | tf_op jit(solution)/shard_map/ppermute | solution.py:13
  71.0 19.9 %collective-permute-start.17 = (bf16[2,512,64]{1,2,0:T(8,128)(2,1)S(1)}, bf16[2,512,64]{1,2,0:T(8,128)(2,1)S(1)}, u32[]{:S(2)}, u32[]{:S(2)}) collective-permute-start(bf16[2,512,64]{1,2,0:T(8,128)(2,1)S(1)} %get-tuple-element.10), channel_id=1, source_target_pairs={{0,3},{1,4},{2,5},{3,6},{4,7},{5,0},{6,1},{7,2},{8,11},{9,12},{10,... | collective-permute-start | bytes 393224 | tf_op jit(solution)/shard_map/ppermute | solution.py:13
  73.6 17.3 %collective-permute-start.18 = (bf16[2,512,64]{1,2,0:T(8,128)(2,1)S(1)}, bf16[2,512,64]{1,2,0:T(8,128)(2,1)S(1)}, u32[]{:S(2)}, u32[]{:S(2)}) collective-permute-start(bf16[2,512,64]{1,2,0:T(8,128)(2,1)S(1)} %get-tuple-element.9), channel_id=1, source_target_pairs={{0,4},{1,5},{2,6},{3,7},{4,0},{5,1},{6,2},{7,3},{8,12},{9,13},{10,... | collective-permute-start | bytes 393224 | tf_op jit(solution)/shard_map/ppermute | solution.py:13
  77.4 14.3 %collective-permute-start.19 = (bf16[2,512,64]{1,2,0:T(8,128)(2,1)S(1)}, bf16[2,512,64]{1,2,0:T(8,128)(2,1)S(1)}, u32[]{:S(2)}, u32[]{:S(2)}) collective-permute-start(bf16[2,512,64]{1,2,0:T(8,128)(2,1)S(1)} %get-tuple-element.8), channel_id=1, source_target_pairs={{0,5},{1,6},{2,7},{3,0},{4,1},{5,2},{6,3},{7,4},{8,13},{9,14},{10,... | collective-permute-start | bytes 393224 | tf_op jit(solution)/shard_map/ppermute | solution.py:13
  81.2 16.4 %collective-permute-start.20 = (bf16[2,512,64]{1,2,0:T(8,128)(2,1)S(1)}, bf16[2,512,64]{1,2,0:T(8,128)(2,1)S(1)}, u32[]{:S(2)}, u32[]{:S(2)}) collective-permute-start(bf16[2,512,64]{1,2,0:T(8,128)(2,1)S(1)} %get-tuple-element.13), channel_id=1, source_target_pairs={{0,6},{1,7},{2,0},{3,1},{4,2},{5,3},{6,4},{7,5},{8,14},{9,15},{10,... | collective-permute-start | bytes 393224 | tf_op jit(solution)/shard_map/ppermute | solution.py:13
  87.7 11.7 %collective-permute-start.21 = (bf16[2,512,64]{1,2,0:T(8,128)(2,1)S(1)}, bf16[2,512,64]{1,2,0:T(8,128)(2,1)}, u32[]{:S(2)}, u32[]{:S(2)}) collective-permute-start(bf16[2,512,64]{1,2,0:T(8,128)(2,1)S(1)} %get-tuple-element.12), channel_id=1, source_target_pairs={{0,7},{1,0},{2,1},{3,2},{4,3},{5,4},{6,5},{7,6},{8,15},{9,8},{10,9... | collective-permute-start | bytes 393224 | tf_op jit(solution)/shard_map/ppermute | solution.py:13

commit v5 on v4

--- a/solution.py
+++ b/solution.py
@@ -80,6 +80,9 @@
     side_x = move(x_row, 0, 0, sibling=True)
     from_below = move(x_row, 0, 1)
     from_above = move(x_row, 0, -1)
+    rates_seed, from_above, from_below = lax.optimization_barrier(
+        (left_rates[None], from_above, from_below)
+    )
     side_above = move(from_above, 0, 0, sibling=True)
     side_below = move(from_below, 0, 0, sibling=True)
     half_ring = ring // 2
@@ -106,14 +109,11 @@
         "ktrn,tmn->ktrm", pooled, right_factor, preferred_element_type=jnp.float32
     ).astype(jnp.bfloat16)
     left_part = lax.dynamic_slice_in_dim(left_factor, part * row_count, row_count, axis=2)
-    rates_run, pooled = lax.optimization_barrier((left_rates[None], pooled))
-    step = 1
-    while step < pieces:
-        came = lax.ppermute(rates_run, "sub", [(j, (j + step) % pieces) for j in range(pieces)])
-        rates_run = jnp.concatenate([came, rates_run], axis=0)
-        step *= 2
-    rates_twice = jnp.concatenate([rates_run, rates_run], axis=0)
-    rates_parts = lax.dynamic_slice_in_dim(rates_twice, (pieces - 1 - part) % pieces, pieces, axis=0)
+    rates_parts = jnp.zeros((pieces,) + left_rates.shape, left_rates.dtype)
+    rates_parts = lax.dynamic_update_index_in_dim(rates_parts, rates_seed, part, 0)
+    for k in range(1, pieces):
+        came = lax.ppermute(rates_seed, "sub", [(j, (j + k) % pieces) for j in range(pieces)])
+        rates_parts = lax.dynamic_update_index_in_dim(rates_parts, came, (part - k) % pieces, 0)
     rates_full = jnp.moveaxis(rates_parts, 0, 1).reshape(local_blocks, width_two)
     partial = jnp.einsum(
         "tab,ktbc->kac", left_part, right_done, preferred_element_type=jnp.float32

time: 102 us -> 128 us (1.25)
  the two profiles are of different devices: /device:TPU:24 before, /device:TPU:1 now
where the time goes in v5:
time: 128 us
  starting transfers between devices  54.4 us (42%)
  matrix products  31.8 us (25%)
  waiting for transfers between devices  27.9 us (22%)
  local copies, waits for them, and re-layouts  8.47 us (7%)
  other arithmetic  4.74 us (4%)
    ppermute x12, starting transfers between devices, move(): return lax.ppermute(piece, 'blk', pairs_list)  24 us
    ppermute x7, waiting for transfers between devices, scatter_sum(): got = lax.ppermute(send, axis, [(j, (j + k) % n) for j in range(n)])  19.6 us
    dot_general x8, matrix products, pool(): jnp.einsum('kab,abrn->krn', w, piece, preferred_element_type=jnp.float32)  17.4 us
    ppermute x7, starting transfers between devices, local(): lax.ppermute(rates_seed, 'sub', [(j, (j + k) % pieces) for j in range(pie...  16.6 us
    ppermute x7, starting transfers between devices, scatter_sum(): got = lax.ppermute(send, axis, [(j, (j + k) % n) for j in range(n)])  13.9 us
    ppermute x12, waiting for transfers between devices, move(): return lax.ppermute(piece, 'blk', pairs_list)  8.32 us
    dot_general x1, matrix products, local(): jnp.einsum('tab,ktbc->kac', left_part, right_done, preferred_element_type...  6.92 us
    dot_general x1, matrix products, local(): jnp.einsum('jrn,jmn->jrm', dual_cols, right_dual, preferred_element_type=...  3.94 us
  transfers between devices with their start and end apart: 26, of which 8 were waited for; matrix products, arithmetic and copies ran while one was open for 19% of the time, Pallas kernels for 0%

profile of v5, /device:TPU:1, one launch (start us, length us, event | category | flops | bytes accessed | tf_op | source)
XLA Modules:
  0.0 127.7 jit_solution(11262720781879331337)
XLA Ops:
  0.0 2.0 %collective-permute-start.1 = (bf16[2,64,512]{2,1,0:T(8,128)(2,1)}, bf16[2,64,512]{2,1,0:T(8,128)(2,1)S(1)}, u32[]{:S(2)}, u32[]{:S(2)}) collective-permute-start(bf16[2,64,512]{2,1,0:T(8,128)(2,1)} %param.11), channel_id=1, source_target_pairs={{0,64},{8,72},{16,80},{24,88},{32,96},{40,104},{48,112},{56,120},{... | collective-permute-start | bytes 393224 | tf_op jit(solution)/shard_map/ppermute | solution.py:71
  2.0 1.4 %collective-permute-start = (bf16[2,64,512]{2,1,0:T(8,128)(2,1)}, bf16[2,64,512]{2,1,0:T(8,128)(2,1)S(1)}, u32[]{:S(2)}, u32[]{:S(2)}) collective-permute-start(bf16[2,64,512]{2,1,0:T(8,128)(2,1)} %param.11), channel_id=1, source_target_pairs={{0,192},{8,200},{16,208},{24,216},{32,224},{40,232},{48,240},{56,2... | collective-permute-start | bytes 393224 | tf_op jit(solution)/shard_map/ppermute | solution.py:71
  3.4 1.1 copy.101
  5.0 1.1 constant_dynamic-slice_fusion
  6.2 0.9 dynamic-slice_reduce_fusion
  7.1 1.5 %collective-permute-start.3 = (bf16[1,64,512]{2,1,0:T(8,128)(2,1)S(1)}, bf16[1,64,512]{2,1,0:T(8,128)(2,1)S(1)}, u32[]{:S(2)}, u32[]{:S(2)}) collective-permute-start(bf16[1,64,512]{2,1,0:T(8,128)(2,1)S(1)} %slice.65), channel_id=1, source_target_pairs={{0,192},{8,200},{16,208},{24,216},{32,224},{40,232},{48,240},{56,2... | collective-permute-start | bytes 196616 | tf_op jit(solution)/shard_map/ppermute | solution.py:71
  9.4 0.9 collective-permute-done.3
  10.3 2.7 %collective-permute-done.2 = bf16[1,64,512]{2,1,0:T(8,128)(2,1)S(1)} collective-permute-done((bf16[1,64,512]{2,1,0:T(8,128)(2,1)S(1)}, bf16[1,64,512]{2,1,0:T(8,128)(2,1)S(1)}, u32[]{:S(2)}, u32[]{:S(2)}) %collective-permute-start.2) | collective-permute-done | bytes 65568 | tf_op jit(solution)/shard_map/ppermute | solution.py:71
  13.3 2.0 %pad_maximum_fusion = bf16[4,2,64,512]{3,0,1,2:T(4,128)(2,1)} fusion(bf16[1,2,64,512]{3,0,1,2:T(2,128)(2,1)S(1)} %copy.104, bf16[1,2,64,512]{3,0,1,2:T(2,128)(2,1)S(1)} %copy.103, bf16[1,2,64,512]{3,0,1,2:T(2,128)(2,1)S(1)} %copy.102, bf16[1,2,64,512]{3,0,1,2:T(2,128)(2,1)S(1)} %copy.101), kind=kLoop, calls=%fused_computation.26 | loop fusion | flops 2097152 | bytes 1048576 | tf_op jit(solution)/shard_map/stack | solution.py:79
  15.3 2.8 %collective-permute-start.4 = (bf16[4,2,64,512]{3,0,1,2:T(4,128)(2,1)}, bf16[4,2,64,512]{3,0,1,2:T(4,128)(2,1)}, u32[]{:S(2)}, u32[]{:S(2)}) collective-permute-start(bf16[4,2,64,512]{3,0,1,2:T(4,128)(2,1)} %pad_maximum_fusion), channel_id=1, source_target_pairs={{0,48},{8,56},{16,0},{24,8},{32,16},{40,24},{48,32},{56,40},{64,11... | collective-permute-start | bytes 1572872 | tf_op jit(solution)/shard_map/ppermute | solution.py:71
  18.4 4.6 %collective-permute-start.8 = (bf16[4,2,64,512]{3,0,1,2:T(4,128)(2,1)}, bf16[4,2,64,512]{3,0,1,2:T(4,128)(2,1)S(1)}, u32[]{:S(2)}, u32[]{:S(2)}) collective-permute-start(bf16[4,2,64,512]{3,0,1,2:T(4,128)(2,1)} %pad_maximum_fusion), channel_id=1, source_target_pairs={{0,8},{8,0},{16,24},{24,16},{32,40},{40,32},{48,56},{56,48},{64,72... | collective-permute-start | bytes 1572872 | tf_op jit(solution)/shard_map/ppermute | solution.py:71
  23.0 1.6 %fusion.48 = f32[16,64,512,1]{2,0,3,1:T(8,128)S(1)} fusion(bf16[4,2,64,512]{3,0,1,2:T(4,128)(2,1)} %pad_maximum_fusion, bf16[16,1,1,4,2]{0,4,3,2,1:T(2,128)(2,1)S(1)} %get-tuple-element.25), kind=kOutput, calls=%fused_computation.73 | convolution fusion | flops 8388608 | bytes 2621696 | tf_op jit(solution)/shard_map/kab,abrn->krn/dot_general | solution.py:95
  24.7 1.5 %collective-permute-done.4 = bf16[4,2,64,512]{3,0,1,2:T(4,128)(2,1)} collective-permute-done((bf16[4,2,64,512]{3,0,1,2:T(4,128)(2,1)}, bf16[4,2,64,512]{3,0,1,2:T(4,128)(2,1)}, u32[]{:S(2)}, u32[]{:S(2)}) %collective-permute-start.4) | collective-permute-done | bytes 524320 | tf_op jit(solution)/shard_map/ppermute | solution.py:71
  26.2 3.1 %collective-permute-done.5 = bf16[4,2,64,512]{3,0,1,2:T(4,128)(2,1)} collective-permute-done((bf16[4,2,64,512]{3,0,1,2:T(4,128)(2,1)}, bf16[4,2,64,512]{3,0,1,2:T(4,128)(2,1)}, u32[]{:S(2)}, u32[]{:S(2)}) %collective-permute-start.5) | collective-permute-done | bytes 524320 | tf_op jit(solution)/shard_map/ppermute | solution.py:71
  29.3 1.6 %collective-permute-start.12 = (f32[1,2,64]{2,1,0:T(2,128)S(1)}, f32[1,2,64]{2,1,0:T(2,128)S(1)}, u32[]{:S(2)}, u32[]{:S(2)}) collective-permute-start(f32[1,2,64]{2,1,0:T(2,128)S(1)} %bitcast.229), channel_id=1, source_target_pairs={{0,1},{1,2},{2,3},{3,4},{4,5},{5,6},{6,7},{7,0},{8,9},{9,10},{10,1... | collective-permute-start | bytes 1544 | tf_op jit(solution)/shard_map/ppermute | solution.py:115
  30.9 3.0 %collective-permute-start.13 = (f32[1,2,64]{2,1,0:T(2,128)S(1)}, f32[1,2,64]{2,1,0:T(2,128)S(1)}, u32[]{:S(2)}, u32[]{:S(2)}) collective-permute-start(f32[1,2,64]{2,1,0:T(2,128)S(1)} %bitcast.230), channel_id=1, source_target_pairs={{0,2},{1,3},{2,4},{3,5},{4,6},{5,7},{6,0},{7,1},{8,10},{9,11},{10,... | collective-permute-start | bytes 1544 | tf_op jit(solution)/shard_map/ppermute | solution.py:115
  33.9 3.8 %collective-permute-start.14 = (f32[1,2,64]{2,1,0:T(2,128)S(1)}, f32[1,2,64]{2,1,0:T(2,128)S(1)}, u32[]{:S(2)}, u32[]{:S(2)}) collective-permute-start(f32[1,2,64]{2,1,0:T(2,128)S(1)} %bitcast.231), channel_id=1, source_target_pairs={{0,3},{1,4},{2,5},{3,6},{4,7},{5,0},{6,1},{7,2},{8,11},{9,12},{10,... | collective-permute-start | bytes 1544 | tf_op jit(solution)/shard_map/ppermute | solution.py:115
  37.7 5.6 %collective-permute-start.9 = (bf16[4,2,64,512]{3,0,1,2:T(4,128)(2,1)}, bf16[4,2,64,512]{3,0,1,2:T(4,128)(2,1)}, u32[]{:S(2)}, u32[]{:S(2)}) collective-permute-start(bf16[4,2,64,512]{3,0,1,2:T(4,128)(2,1)} %collective-permute-done.4), channel_id=1, source_target_pairs={{0,8},{8,0},{16,24},{24,16},{32,40},{40,32},{48,56},{56,48},{64,72... | collective-permute-start | bytes 1572872 | tf_op jit(solution)/shard_map/ppermute | solution.py:71
  43.3 3.0 %fusion.46 = f32[16,64,512,1]{2,0,3,1:T(8,128)} fusion(bf16[4,2,64,512]{3,0,1,2:T(4,128)(2,1)} %collective-permute-done.4, bf16[16,1,1,4,2]{0,4,3,2,1:T(2,128)(2,1)S(1)} %get-tuple-element.24), kind=kOutput, calls=%fused_computation.71 | convolution fusion | flops 8388608 | bytes 2621696 | tf_op jit(solution)/shard_map/kab,abrn->krn/dot_general | solution.py:95
  46.3 3.0 %fusion.42 = f32[16,64,512,1]{2,0,3,1:T(8,128)} fusion(bf16[4,2,64,512]{3,0,1,2:T(4,128)(2,1)} %collective-permute-done.5, bf16[16,1,1,4,2]{0,4,3,2,1:T(2,128)(2,1)S(1)} %get-tuple-element.22), kind=kOutput, calls=%fused_computation.67 | convolution fusion | flops 8388608 | bytes 2621696 | tf_op jit(solution)/shard_map/kab,abrn->krn/dot_general | solution.py:95
  49.3 2.0 %slice.54 = bf16[2,2,64,512]{3,0,1,2:T(2,128)(2,1)} slice(bf16[4,2,64,512]{3,0,1,2:T(4,128)(2,1)} %collective-permute-done.4), slice={[2:4], [0:2], [0:64], [0:512]} | slice | bytes 524288 | tf_op jit(solution)/shard_map/slice | solution.py:90
  51.3 1.9 %slice.53 = bf16[2,2,64,512]{3,0,1,2:T(2,128)(2,1)} slice(bf16[4,2,64,512]{3,0,1,2:T(4,128)(2,1)} %collective-permute-done.5), slice={[0:2], [0:2], [0:64], [0:512]} | slice | bytes 524288 | tf_op jit(solution)/shard_map/slice | solution.py:90
  53.5 1.5 %collective-permute-start.6 = (bf16[2,2,64,512]{3,0,1,2:T(2,128)(2,1)}, bf16[2,2,64,512]{3,0,1,2:T(2,128)(2,1)}, u32[]{:S(2)}, u32[]{:S(2)}) collective-permute-start(bf16[2,2,64,512]{3,0,1,2:T(2,128)(2,1)} %slice.53), channel_id=1, source_target_pairs={{0,16},{8,24},{16,32},{24,40},{32,48},{40,56},{48,0},{56,8},{64,80... | collective-permute-start | bytes 786440 | tf_op jit(solution)/shard_map/ppermute | solution.py:71
  55.0 2.0 %fusion.40 = f32[16,64,512,1]{2,0,3,1:T(8,128)} fusion(bf16[4,2,64,512]{3,0,1,2:T(4,128)(2,1)S(1)} %collective-permute-done.8, bf16[16,1,1,4,2]{0,4,3,2,1:T(2,128)(2,1)S(1)} %get-tuple-element.21), kind=kOutput, calls=%fused_computation.65 | convolution fusion | flops 8388608 | bytes 2621696 | tf_op jit(solution)/shard_map/kab,abrn->krn/dot_general | solution.py:95
  57.0 4.7 %collective-permute-start.16 = (f32[1,2,64]{2,1,0:T(2,128)S(1)}, f32[1,2,64]{2,1,0:T(2,128)S(1)}, u32[]{:S(2)}, u32[]{:S(2)}) collective-permute-start(f32[1,2,64]{2,1,0:T(2,128)S(1)} %bitcast.233), channel_id=1, source_target_pairs={{0,5},{1,6},{2,7},{3,0},{4,1},{5,2},{6,3},{7,4},{8,13},{9,14},{10,... | collective-permute-start | bytes 1544 | tf_op jit(solution)/shard_map/ppermute | solution.py:115
  61.7 2.5 %collective-permute-start.17 = (f32[1,2,64]{2,1,0:T(2,128)S(1)}, f32[1,2,64]{2,1,0:T(2,128)S(1)}, u32[]{:S(2)}, u32[]{:S(2)}) collective-permute-start(f32[1,2,64]{2,1,0:T(2,128)S(1)} %bitcast.235), channel_id=1, source_target_pairs={{0,6},{1,7},{2,0},{3,1},{4,2},{5,3},{6,4},{7,5},{8,14},{9,15},{10,... | collective-permute-start | bytes 1544 | tf_op jit(solution)/shard_map/ppermute | solution.py:115
  64.2 0.8 collective-permute-start.18
  65.1 2.3 %collective-permute-start.11 = (bf16[4,2,64,512]{3,0,1,2:T(4,128)(2,1)}, bf16[4,2,64,512]{3,0,1,2:T(4,128)(2,1)}, u32[]{:S(2)}, u32[]{:S(2)}) collective-permute-start(bf16[4,2,64,512]{3,0,1,2:T(4,128)(2,1)} %collective-permute-done.5), channel_id=1, source_target_pairs={{0,8},{8,0},{16,24},{24,16},{32,40},{40,32},{48,56},{56,48},{64,72... | collective-permute-start | bytes 1572872 | tf_op jit(solution)/shard_map/ppermute | solution.py:71
  67.6 1.5 %pad_maximum_fusion.1 = bf16[4,2,64,512]{3,0,1,2:T(4,128)(2,1)S(1)} fusion(bf16[2,2,64,512]{3,0,1,2:T(2,128)(2,1)S(1)} %collective-permute-done.7, bf16[2,2,64,512]{3,0,1,2:T(2,128)(2,1)} %collective-permute-done.6), kind=kLoop, calls=%fused_computation.27 | loop fusion | flops 1048576 | bytes 1048576 | tf_op jit(solution)/shard_map/concatenate | solution.py:89
  69.1 2.1 %collective-permute-start.10 = (bf16[4,2,64,512]{3,0,1,2:T(4,128)(2,1)S(1)}, bf16[4,2,64,512]{3,0,1,2:T(4,128)(2,1)S(1)}, u32[]{:S(2)}, u32[]{:S(2)}) collective-permute-start(bf16[4,2,64,512]{3,0,1,2:T(4,128)(2,1)S(1)} %pad_maximum_fusion.1), channel_id=1, source_target_pairs={{0,8},{8,0},{16,24},{24,16},{32,40},{40,32},{48,56},{56,48},{64,72... | collective-permute-start | bytes 1572872 | tf_op jit(solution)/shard_map/ppermute | solution.py:71
  71.2 2.1 %fusion.44 = f32[16,64,512,1]{2,0,3,1:T(8,128)S(1)} fusion(bf16[16,1,1,4,2]{0,4,3,2,1:T(2,128)(2,1)S(1)} %get-tuple-element.23, bf16[2,2,64,512]{3,0,1,2:T(2,128)(2,1)S(1)} %collective-permute-done.7, bf16[2,2,64,512]{3,0,1,2:T(2,128)(2,1)} %collective-permute-done.6), kind=kOutput, calls=%fused_computation.69 | convolution fusion | flops 9437184 | bytes 2621696 | tf_op jit(solution)/shard_map/kab,abrn->krn/dot_general | solution.py:95
  73.3 1.8 %fusion.38 = f32[16,64,512,1]{2,0,3,1:T(8,128)S(1)} fusion(bf16[4,2,64,512]{3,0,1,2:T(4,128)(2,1)} %collective-permute-done.9, bf16[16,1,1,4,2]{0,4,3,2,1:T(2,128)(2,1)S(1)} %get-tuple-element.20), kind=kOutput, calls=%fused_computation.63 | convolution fusion | flops 8388608 | bytes 2621696 | tf_op jit(solution)/shard_map/kab,abrn->krn/dot_general | solution.py:95
  75.8 3.2 %fusion.10 = bf16[2,8,64,512]{3,1,0,2:T(8,128)(2,1)} fusion(bf16[4,2,64,512]{3,0,1,2:T(4,128)(2,1)} %collective-permute-done.11, f32[16,64,512,1]{2,0,3,1:T(8,128)S(1)} %fusion.36, f32[16,64,512,1]{2,0,3,1:T(8,128)S(1)} %fusion.38, f32[16,64,512,1]{2,0,3,1:T(8,128)S(1)} %copy-done.3, f32[16,64,512,1]{2,0,3,1:T(8,128)S(1)} %copy-done.2, ...), kind=kOutput, calls=%fused_computation.18 | convolution fusion | flops 12582912 | bytes 16253184 | tf_op jit(solution)/shard_map/kab,abrn->krn/dot_general | solution.py:95
  79.0 6.9 %bitcast_convert_fusion = bf16[2,512,512]{2,1,0:T(8,128)(2,1)} fusion(bf16[8,512,512]{2,1,0:T(8,128)(2,1)} %param.12, s32[]{:T(128)S(6)} %select_n.160, bf16[8,512,512]{2,1,0:T(8,128)(2,1)} %param.13, bf16[2,8,64,512]{3,1,0,2:T(8,128)(2,1)} %fusion.10), kind=kOutput, calls=%fused_computation.2 | convolution fusion | flops 1074790400 | bytes 7340036 | tf_op jit(solution)/shard_map/tab,ktbc->kac/dot_general | solution.py:118
  86.0 3.9 %fusion.6 = f32[2,512,512]{2,1,0:T(8,128)} fusion(bf16[2,512,512]{2,1,0:T(8,128)(2,1)S(1)} %copy-done, bf16[2,512,512]{2,1,0:T(8,128)(2,1)} %bitcast_convert_fusion, bf16[2,512,512]{2,1,0:T(8,128)(2,1)S(1)} %copy-done.6), kind=kOutput, calls=%fused_computation.16 | convolution fusion | flops 1074266112 | bytes 5242880 | tf_op jit(solution)/shard_map/jrn,jmn->jrm/dot_general | solution.py:124
  89.9 2.6 %convolution_convert_fusion.1 = bf16[2,512,512]{1,2,0:T(8,128)(2,1)S(1)} fusion(bf16[2,512,512]{2,1,0:T(8,128)(2,1)S(1)} %copy-done.7, f32[2,512,512]{2,1,0:T(8,128)} %fusion.6, f32[2,512]{1,0:T(2,128)S(1)} %copy-done.8, f32[2,512]{1,0:T(2,128)S(1)} %add.349), kind=kOutput, calls=%fused_computation.14 | convolution fusion | flops 538968064 | bytes 4202496 | tf_op jit(solution)/shard_map/jrm,jkm->jrk/dot_general | solution.py:126
  92.6 0.7 convolution_convert_fusion
  93.4 2.3 %collective-permute-start.25 = (bf16[2,512,64]{1,2,0:T(8,128)(2,1)S(1)}, bf16[2,512,64]{1,2,0:T(8,128)(2,1)S(1)}, u32[]{:S(2)}, u32[]{:S(2)}) collective-permute-start(bf16[2,512,64]{1,2,0:T(8,128)(2,1)S(1)} %get-tuple-element.16), channel_id=1, source_target_pairs={{0,7},{1,0},{2,1},{3,2},{4,3},{5,4},{6,5},{7,6},{8,15},{9,8},{10,9... | collective-permute-start | bytes 393224 | tf_op jit(solution)/shard_map/ppermute | solution.py:13
  95.7 1.4 %collective-permute-start.24 = (bf16[2,512,64]{1,2,0:T(8,128)(2,1)S(1)}, bf16[2,512,64]{1,2,0:T(8,128)(2,1)S(1)}, u32[]{:S(2)}, u32[]{:S(2)}) collective-permute-start(bf16[2,512,64]{1,2,0:T(8,128)(2,1)S(1)} %get-tuple-element.17), channel_id=1, source_target_pairs={{0,6},{1,7},{2,0},{3,1},{4,2},{5,3},{6,4},{7,5},{8,14},{9,15},{10,... | collective-permute-start | bytes 393224 | tf_op jit(solution)/shard_map/ppermute | solution.py:13
  97.1 3.4 %collective-permute-start.23 = (bf16[2,512,64]{1,2,0:T(8,128)(2,1)S(1)}, bf16[2,512,64]{1,2,0:T(8,128)(2,1)S(1)}, u32[]{:S(2)}, u32[]{:S(2)}) collective-permute-start(bf16[2,512,64]{1,2,0:T(8,128)(2,1)S(1)} %get-tuple-element.12), channel_id=1, source_target_pairs={{0,5},{1,6},{2,7},{3,0},{4,1},{5,2},{6,3},{7,4},{8,13},{9,14},{10,... | collective-permute-start | bytes 393224 | tf_op jit(solution)/shard_map/ppermute | solution.py:13
  100.5 0.6 collective-permute-start.22
  101.2 2.5 %collective-permute-start.21 = (bf16[2,512,64]{1,2,0:T(8,128)(2,1)S(1)}, bf16[2,512,64]{1,2,0:T(8,128)(2,1)S(1)}, u32[]{:S(2)}, u32[]{:S(2)}) collective-permute-start(bf16[2,512,64]{1,2,0:T(8,128)(2,1)S(1)} %get-tuple-element.14), channel_id=1, source_target_pairs={{0,3},{1,4},{2,5},{3,6},{4,7},{5,0},{6,1},{7,2},{8,11},{9,12},{10,... | collective-permute-start | bytes 393224 | tf_op jit(solution)/shard_map/ppermute | solution.py:13
  103.7 3.6 %collective-permute-start.20 = (bf16[2,512,64]{1,2,0:T(8,128)(2,1)S(1)}, bf16[2,512,64]{1,2,0:T(8,128)(2,1)S(1)}, u32[]{:S(2)}, u32[]{:S(2)}) collective-permute-start(bf16[2,512,64]{1,2,0:T(8,128)(2,1)S(1)} %get-tuple-element.15), channel_id=1, source_target_pairs={{0,2},{1,3},{2,4},{3,5},{4,6},{5,7},{6,0},{7,1},{8,10},{9,11},{10,... | collective-permute-start | bytes 393224 | tf_op jit(solution)/shard_map/ppermute | solution.py:13
  107.3 0.9 collective-permute-done.24
  108.2 10.0 %collective-permute-done.23 = bf16[2,512,64]{1,2,0:T(8,128)(2,1)S(1)} collective-permute-done((bf16[2,512,64]{1,2,0:T(8,128)(2,1)S(1)}, bf16[2,512,64]{1,2,0:T(8,128)(2,1)S(1)}, u32[]{:S(2)}, u32[]{:S(2)}) %collective-permute-start.23) | collective-permute-done | bytes 131104 | tf_op jit(solution)/shard_map/ppermute | solution.py:13
  118.2 3.1 %collective-permute-done.21 = bf16[2,512,64]{1,2,0:T(8,128)(2,1)S(1)} collective-permute-done((bf16[2,512,64]{1,2,0:T(8,128)(2,1)S(1)}, bf16[2,512,64]{1,2,0:T(8,128)(2,1)S(1)}, u32[]{:S(2)}, u32[]{:S(2)}) %collective-permute-start.21) | collective-permute-done | bytes 131104 | tf_op jit(solution)/shard_map/ppermute | solution.py:13
  121.4 5.5 %collective-permute-done.19 = bf16[2,512,64]{1,2,0:T(8,128)(2,1)S(1)} collective-permute-done((bf16[2,512,64]{1,2,0:T(8,128)(2,1)S(1)}, bf16[2,512,64]{1,2,0:T(8,128)(2,1)S(1)}, u32[]{:S(2)}, u32[]{:S(2)}) %collective-permute-start.19) | collective-permute-done | bytes 131104 | tf_op jit(solution)/shard_map/ppermute | solution.py:13
  126.9 0.8 fusion.26
  (72 shorter events, 3.0 us)
Async XLA Ops:
  0.0 86.0 %copy-start = (bf16[2,512,512]{2,1,0:T(8,128)(2,1)S(1)}, bf16[2,512,512]{2,1,0:T(8,128)(2,1)}, u32[]{:S(2)}) copy-start(bf16[2,512,512]{2,1,0:T(8,128)(2,1)} %param.19) | copy-start | bytes 3145732
  0.0 8.6 %collective-permute-start.1 = (bf16[2,64,512]{2,1,0:T(8,128)(2,1)}, bf16[2,64,512]{2,1,0:T(8,128)(2,1)S(1)}, u32[]{:S(2)}, u32[]{:S(2)}) collective-permute-start(bf16[2,64,512]{2,1,0:T(8,128)(2,1)} %param.11), channel_id=1, source_target_pairs={{0,64},{8,72},{16,80},{24,88},{32,96},{40,104},{48,112},{56,120},{... | collective-permute-start | bytes 393224 | tf_op jit(solution)/shard_map/ppermute | solution.py:71
  2.0 5.1 %collective-permute-start = (bf16[2,64,512]{2,1,0:T(8,128)(2,1)}, bf16[2,64,512]{2,1,0:T(8,128)(2,1)S(1)}, u32[]{:S(2)}, u32[]{:S(2)}) collective-permute-start(bf16[2,64,512]{2,1,0:T(8,128)(2,1)} %param.11), channel_id=1, source_target_pairs={{0,192},{8,200},{16,208},{24,216},{32,224},{40,232},{48,240},{56,2... | collective-permute-start | bytes 393224 | tf_op jit(solution)/shard_map/ppermute | solution.py:71
  7.1 3.2 %collective-permute-start.3 = (bf16[1,64,512]{2,1,0:T(8,128)(2,1)S(1)}, bf16[1,64,512]{2,1,0:T(8,128)(2,1)S(1)}, u32[]{:S(2)}, u32[]{:S(2)}) collective-permute-start(bf16[1,64,512]{2,1,0:T(8,128)(2,1)S(1)} %slice.65), channel_id=1, source_target_pairs={{0,192},{8,200},{16,208},{24,216},{32,224},{40,232},{48,240},{56,2... | collective-permute-start | bytes 196616 | tf_op jit(solution)/shard_map/ppermute | solution.py:71
  8.7 4.4 %collective-permute-start.2 = (bf16[1,64,512]{2,1,0:T(8,128)(2,1)S(1)}, bf16[1,64,512]{2,1,0:T(8,128)(2,1)S(1)}, u32[]{:S(2)}, u32[]{:S(2)}) collective-permute-start(bf16[1,64,512]{2,1,0:T(8,128)(2,1)S(1)} %slice.64), channel_id=1, source_target_pairs={{0,64},{8,72},{16,80},{24,88},{32,96},{40,104},{48,112},{56,120},{... | collective-permute-start | bytes 196616 | tf_op jit(solution)/shard_map/ppermute | solution.py:71
  13.3 16.0 %copy-start.5 = (f32[2,64]{1,0:T(2,128)S(1)}, f32[2,64]{1,0:T(2,128)}, u32[]{:S(2)}) copy-start(f32[2,64]{1,0:T(2,128)} %param.20) | copy-start | bytes 1540
  15.3 10.8 %collective-permute-start.4 = (bf16[4,2,64,512]{3,0,1,2:T(4,128)(2,1)}, bf16[4,2,64,512]{3,0,1,2:T(4,128)(2,1)}, u32[]{:S(2)}, u32[]{:S(2)}) collective-permute-start(bf16[4,2,64,512]{3,0,1,2:T(4,128)(2,1)} %pad_maximum_fusion), channel_id=1, source_target_pairs={{0,48},{8,56},{16,0},{24,8},{32,16},{40,24},{48,32},{56,40},{64,11... | collective-permute-start | bytes 1572872 | tf_op jit(solution)/shard_map/ppermute | solution.py:71
  18.2 11.1 %collective-permute-start.5 = (bf16[4,2,64,512]{3,0,1,2:T(4,128)(2,1)}, bf16[4,2,64,512]{3,0,1,2:T(4,128)(2,1)}, u32[]{:S(2)}, u32[]{:S(2)}) collective-permute-start(bf16[4,2,64,512]{3,0,1,2:T(4,128)(2,1)} %pad_maximum_fusion), channel_id=1, source_target_pairs={{0,16},{8,24},{16,32},{24,40},{32,48},{40,56},{48,0},{56,8},{64,80... | collective-permute-start | bytes 1572872 | tf_op jit(solution)/shard_map/ppermute | solution.py:71
  18.4 34.9 %collective-permute-start.8 = (bf16[4,2,64,512]{3,0,1,2:T(4,128)(2,1)}, bf16[4,2,64,512]{3,0,1,2:T(4,128)(2,1)S(1)}, u32[]{:S(2)}, u32[]{:S(2)}) collective-permute-start(bf16[4,2,64,512]{3,0,1,2:T(4,128)(2,1)} %pad_maximum_fusion), channel_id=1, source_target_pairs={{0,8},{8,0},{16,24},{24,16},{32,40},{40,32},{48,56},{56,48},{64,72... | collective-permute-start | bytes 1572872 | tf_op jit(solution)/shard_map/ppermute | solution.py:71
  29.3 24.2 %collective-permute-start.12 = (f32[1,2,64]{2,1,0:T(2,128)S(1)}, f32[1,2,64]{2,1,0:T(2,128)S(1)}, u32[]{:S(2)}, u32[]{:S(2)}) collective-permute-start(f32[1,2,64]{2,1,0:T(2,128)S(1)} %bitcast.229), channel_id=1, source_target_pairs={{0,1},{1,2},{2,3},{3,4},{4,5},{5,6},{6,7},{7,0},{8,9},{9,10},{10,1... | collective-permute-start | bytes 1544 | tf_op jit(solution)/shard_map/ppermute | solution.py:115
  30.9 22.6 %collective-permute-start.13 = (f32[1,2,64]{2,1,0:T(2,128)S(1)}, f32[1,2,64]{2,1,0:T(2,128)S(1)}, u32[]{:S(2)}, u32[]{:S(2)}) collective-permute-start(f32[1,2,64]{2,1,0:T(2,128)S(1)} %bitcast.230), channel_id=1, source_target_pairs={{0,2},{1,3},{2,4},{3,5},{4,6},{5,7},{6,0},{7,1},{8,10},{9,11},{10,... | collective-permute-start | bytes 1544 | tf_op jit(solution)/shard_map/ppermute | solution.py:115
  33.9 23.1 %collective-permute-start.14 = (f32[1,2,64]{2,1,0:T(2,128)S(1)}, f32[1,2,64]{2,1,0:T(2,128)S(1)}, u32[]{:S(2)}, u32[]{:S(2)}) collective-permute-start(f32[1,2,64]{2,1,0:T(2,128)S(1)} %bitcast.231), channel_id=1, source_target_pairs={{0,3},{1,4},{2,5},{3,6},{4,7},{5,0},{6,1},{7,2},{8,11},{9,12},{10,... | collective-permute-start | bytes 1544 | tf_op jit(solution)/shard_map/ppermute | solution.py:115
  37.7 35.6 %collective-permute-start.9 = (bf16[4,2,64,512]{3,0,1,2:T(4,128)(2,1)}, bf16[4,2,64,512]{3,0,1,2:T(4,128)(2,1)}, u32[]{:S(2)}, u32[]{:S(2)}) collective-permute-start(bf16[4,2,64,512]{3,0,1,2:T(4,128)(2,1)} %collective-permute-done.4), channel_id=1, source_target_pairs={{0,8},{8,0},{16,24},{24,16},{32,40},{40,32},{48,56},{56,48},{64,72... | collective-permute-start | bytes 1572872 | tf_op jit(solution)/shard_map/ppermute | solution.py:71
  53.2 8.5 %collective-permute-start.15 = (f32[1,2,64]{2,1,0:T(2,128)S(1)}, f32[1,2,64]{2,1,0:T(2,128)S(1)}, u32[]{:S(2)}, u32[]{:S(2)}) collective-permute-start(f32[1,2,64]{2,1,0:T(2,128)S(1)} %bitcast.232), channel_id=1, source_target_pairs={{0,4},{1,5},{2,6},{3,7},{4,0},{5,1},{6,2},{7,3},{8,12},{9,13},{10,... | collective-permute-start | bytes 1544 | tf_op jit(solution)/shard_map/ppermute | solution.py:115
  53.5 14.1 %collective-permute-start.7 = (bf16[2,2,64,512]{3,0,1,2:T(2,128)(2,1)}, bf16[2,2,64,512]{3,0,1,2:T(2,128)(2,1)S(1)}, u32[]{:S(2)}, u32[]{:S(2)}) collective-permute-start(bf16[2,2,64,512]{3,0,1,2:T(2,128)(2,1)} %slice.54), channel_id=1, source_target_pairs={{0,48},{8,56},{16,0},{24,8},{32,16},{40,24},{48,32},{56,40},{64,11... | collective-permute-start | bytes 786440 | tf_op jit(solution)/shard_map/ppermute | solution.py:71
  53.5 14.0 %collective-permute-start.6 = (bf16[2,2,64,512]{3,0,1,2:T(2,128)(2,1)}, bf16[2,2,64,512]{3,0,1,2:T(2,128)(2,1)}, u32[]{:S(2)}, u32[]{:S(2)}) collective-permute-start(bf16[2,2,64,512]{3,0,1,2:T(2,128)(2,1)} %slice.53), channel_id=1, source_target_pairs={{0,16},{8,24},{16,32},{24,40},{32,48},{40,56},{48,0},{56,8},{64,80... | collective-permute-start | bytes 786440 | tf_op jit(solution)/shard_map/ppermute | solution.py:71
  57.0 7.2 %collective-permute-start.16 = (f32[1,2,64]{2,1,0:T(2,128)S(1)}, f32[1,2,64]{2,1,0:T(2,128)S(1)}, u32[]{:S(2)}, u32[]{:S(2)}) collective-permute-start(f32[1,2,64]{2,1,0:T(2,128)S(1)} %bitcast.233), channel_id=1, source_target_pairs={{0,5},{1,6},{2,7},{3,0},{4,1},{5,2},{6,3},{7,4},{8,13},{9,14},{10,... | collective-permute-start | bytes 1544 | tf_op jit(solution)/shard_map/ppermute | solution.py:115
  61.7 3.4 %collective-permute-start.17 = (f32[1,2,64]{2,1,0:T(2,128)S(1)}, f32[1,2,64]{2,1,0:T(2,128)S(1)}, u32[]{:S(2)}, u32[]{:S(2)}) collective-permute-start(f32[1,2,64]{2,1,0:T(2,128)S(1)} %bitcast.235), channel_id=1, source_target_pairs={{0,6},{1,7},{2,0},{3,1},{4,2},{5,3},{6,4},{7,5},{8,14},{9,15},{10,... | collective-permute-start | bytes 1544 | tf_op jit(solution)/shard_map/ppermute | solution.py:115
  64.2 3.2 %collective-permute-start.18 = (f32[1,2,64]{2,1,0:T(2,128)S(1)}, f32[1,2,64]{2,1,0:T(2,128)S(1)}, u32[]{:S(2)}, u32[]{:S(2)}) collective-permute-start(f32[1,2,64]{2,1,0:T(2,128)S(1)} %bitcast.236), channel_id=1, source_target_pairs={{0,7},{1,0},{2,1},{3,2},{4,3},{5,4},{6,5},{7,6},{8,15},{9,8},{10,9... | collective-permute-start | bytes 1544 | tf_op jit(solution)/shard_map/ppermute | solution.py:115
  65.1 10.6 %collective-permute-start.11 = (bf16[4,2,64,512]{3,0,1,2:T(4,128)(2,1)}, bf16[4,2,64,512]{3,0,1,2:T(4,128)(2,1)}, u32[]{:S(2)}, u32[]{:S(2)}) collective-permute-start(bf16[4,2,64,512]{3,0,1,2:T(4,128)(2,1)} %collective-permute-done.5), channel_id=1, source_target_pairs={{0,8},{8,0},{16,24},{24,16},{32,40},{40,32},{48,56},{56,48},{64,72... | collective-permute-start | bytes 1572872 | tf_op jit(solution)/shard_map/ppermute | solution.py:71
  69.1 6.0 %collective-permute-start.10 = (bf16[4,2,64,512]{3,0,1,2:T(4,128)(2,1)S(1)}, bf16[4,2,64,512]{3,0,1,2:T(4,128)(2,1)S(1)}, u32[]{:S(2)}, u32[]{:S(2)}) collective-permute-start(bf16[4,2,64,512]{3,0,1,2:T(4,128)(2,1)S(1)} %pad_maximum_fusion.1), channel_id=1, source_target_pairs={{0,8},{8,0},{16,24},{24,16},{32,40},{40,32},{48,56},{56,48},{64,72... | collective-permute-start | bytes 1572872 | tf_op jit(solution)/shard_map/ppermute | solution.py:71
  71.2 4.6 %copy-start.3 = (f32[16,64,512,1]{2,0,3,1:T(8,128)S(1)}, f32[16,64,512,1]{2,0,3,1:T(8,128)}, u32[]{:S(2)}) copy-start(f32[16,64,512,1]{2,0,3,1:T(8,128)} %fusion.40) | copy-start | bytes 6291460
  73.3 2.5 %copy-start.1 = (f32[16,64,512,1]{2,0,3,1:T(8,128)S(1)}, f32[16,64,512,1]{2,0,3,1:T(8,128)}, u32[]{:S(2)}) copy-start(f32[16,64,512,1]{2,0,3,1:T(8,128)} %fusion.46) | copy-start | bytes 6291460
  73.3 2.5 %copy-start.2 = (f32[16,64,512,1]{2,0,3,1:T(8,128)S(1)}, f32[16,64,512,1]{2,0,3,1:T(8,128)}, u32[]{:S(2)}) copy-start(f32[16,64,512,1]{2,0,3,1:T(8,128)} %fusion.42) | copy-start | bytes 6291460
  79.0 6.9 %copy-start.6 = (bf16[2,512,512]{2,1,0:T(8,128)(2,1)S(1)}, bf16[2,512,512]{2,1,0:T(8,128)(2,1)}, u32[]{:S(2)}) copy-start(bf16[2,512,512]{2,1,0:T(8,128)(2,1)} %param.17) | copy-start | bytes 3145732
  86.0 4.0 %copy-start.7 = (bf16[2,512,512]{2,1,0:T(8,128)(2,1)S(1)}, bf16[2,512,512]{2,1,0:T(8,128)(2,1)}, u32[]{:S(2)}) copy-start(bf16[2,512,512]{2,1,0:T(8,128)(2,1)} %param.18) | copy-start | bytes 3145732
  86.0 4.0 %copy-start.8 = (f32[2,512]{1,0:T(2,128)S(1)}, f32[2,512]{1,0:T(2,128)}, u32[]{:S(2)}) copy-start(f32[2,512]{1,0:T(2,128)} %param.21) | copy-start | bytes 12292
  89.9 2.6 %copy-start.4 = (bf16[2,512,512]{2,1,0:T(8,128)(2,1)S(1)}, bf16[2,512,512]{2,1,0:T(8,128)(2,1)}, u32[]{:S(2)}) copy-start(bf16[2,512,512]{2,1,0:T(8,128)(2,1)} %param.16) | copy-start | bytes 3145732
  93.4 10.3 %collective-permute-start.25 = (bf16[2,512,64]{1,2,0:T(8,128)(2,1)S(1)}, bf16[2,512,64]{1,2,0:T(8,128)(2,1)S(1)}, u32[]{:S(2)}, u32[]{:S(2)}) collective-permute-start(bf16[2,512,64]{1,2,0:T(8,128)(2,1)S(1)} %get-tuple-element.16), channel_id=1, source_target_pairs={{0,7},{1,0},{2,1},{3,2},{4,3},{5,4},{6,5},{7,6},{8,15},{9,8},{10,9... | collective-permute-start | bytes 393224 | tf_op jit(solution)/shard_map/ppermute | solution.py:13
  95.7 12.4 %collective-permute-start.24 = (bf16[2,512,64]{1,2,0:T(8,128)(2,1)S(1)}, bf16[2,512,64]{1,2,0:T(8,128)(2,1)S(1)}, u32[]{:S(2)}, u32[]{:S(2)}) collective-permute-start(bf16[2,512,64]{1,2,0:T(8,128)(2,1)S(1)} %get-tuple-element.17), channel_id=1, source_target_pairs={{0,6},{1,7},{2,0},{3,1},{4,2},{5,3},{6,4},{7,5},{8,14},{9,15},{10,... | collective-permute-start | bytes 393224 | tf_op jit(solution)/shard_map/ppermute | solution.py:13
  97.1 21.1 %collective-permute-start.23 = (bf16[2,512,64]{1,2,0:T(8,128)(2,1)S(1)}, bf16[2,512,64]{1,2,0:T(8,128)(2,1)S(1)}, u32[]{:S(2)}, u32[]{:S(2)}) collective-permute-start(bf16[2,512,64]{1,2,0:T(8,128)(2,1)S(1)} %get-tuple-element.12), channel_id=1, source_target_pairs={{0,5},{1,6},{2,7},{3,0},{4,1},{5,2},{6,3},{7,4},{8,13},{9,14},{10,... | collective-permute-start | bytes 393224 | tf_op jit(solution)/shard_map/ppermute | solution.py:13
  100.5 17.7 %collective-permute-start.22 = (bf16[2,512,64]{1,2,0:T(8,128)(2,1)S(1)}, bf16[2,512,64]{1,2,0:T(8,128)(2,1)S(1)}, u32[]{:S(2)}, u32[]{:S(2)}) collective-permute-start(bf16[2,512,64]{1,2,0:T(8,128)(2,1)S(1)} %get-tuple-element.13), channel_id=1, source_target_pairs={{0,4},{1,5},{2,6},{3,7},{4,0},{5,1},{6,2},{7,3},{8,12},{9,13},{10,... | collective-permute-start | bytes 393224 | tf_op jit(solution)/shard_map/ppermute | solution.py:13
  101.2 20.2 %collective-permute-start.21 = (bf16[2,512,64]{1,2,0:T(8,128)(2,1)S(1)}, bf16[2,512,64]{1,2,0:T(8,128)(2,1)S(1)}, u32[]{:S(2)}, u32[]{:S(2)}) collective-permute-start(bf16[2,512,64]{1,2,0:T(8,128)(2,1)S(1)} %get-tuple-element.14), channel_id=1, source_target_pairs={{0,3},{1,4},{2,5},{3,6},{4,7},{5,0},{6,1},{7,2},{8,11},{9,12},{10,... | collective-permute-start | bytes 393224 | tf_op jit(solution)/shard_map/ppermute | solution.py:13
  103.7 17.6 %collective-permute-start.20 = (bf16[2,512,64]{1,2,0:T(8,128)(2,1)S(1)}, bf16[2,512,64]{1,2,0:T(8,128)(2,1)S(1)}, u32[]{:S(2)}, u32[]{:S(2)}) collective-permute-start(bf16[2,512,64]{1,2,0:T(8,128)(2,1)S(1)} %get-tuple-element.15), channel_id=1, source_target_pairs={{0,2},{1,3},{2,4},{3,5},{4,6},{5,7},{6,0},{7,1},{8,10},{9,11},{10,... | collective-permute-start | bytes 393224 | tf_op jit(solution)/shard_map/ppermute | solution.py:13
  108.2 18.7 %collective-permute-start.19 = (bf16[2,512,64]{1,2,0:T(8,128)(2,1)S(1)}, bf16[2,512,64]{1,2,0:T(8,128)(2,1)S(1)}, u32[]{:S(2)}, u32[]{:S(2)}) collective-permute-start(bf16[2,512,64]{1,2,0:T(8,128)(2,1)S(1)} %get-tuple-element.11), channel_id=1, source_target_pairs={{0,1},{1,2},{2,3},{3,4},{4,5},{5,6},{6,7},{7,0},{8,9},{9,10},{10,1... | collective-permute-start | bytes 393224 | tf_op jit(solution)/shard_map/ppermute | solution.py:13

commit v6 on v5

--- a/solution.py
+++ b/solution.py
@@ -80,9 +80,6 @@
     side_x = move(x_row, 0, 0, sibling=True)
     from_below = move(x_row, 0, 1)
     from_above = move(x_row, 0, -1)
-    rates_seed, from_above, from_below = lax.optimization_barrier(
-        (left_rates[None], from_above, from_below)
-    )
     side_above = move(from_above, 0, 0, sibling=True)
     side_below = move(from_below, 0, 0, sibling=True)
     half_ring = ring // 2
@@ -109,28 +106,23 @@
         "ktrn,tmn->ktrm", pooled, right_factor, preferred_element_type=jnp.float32
     ).astype(jnp.bfloat16)
     left_part = lax.dynamic_slice_in_dim(left_factor, part * row_count, row_count, axis=2)
-    rates_parts = jnp.zeros((pieces,) + left_rates.shape, left_rates.dtype)
-    rates_parts = lax.dynamic_update_index_in_dim(rates_parts, rates_seed, part, 0)
-    for k in range(1, pieces):
-        came = lax.ppermute(rates_seed, "sub", [(j, (j + k) % pieces) for j in range(pieces)])
-        rates_parts = lax.dynamic_update_index_in_dim(rates_parts, came, (part - k) % pieces, 0)
-    rates_full = jnp.moveaxis(rates_parts, 0, 1).reshape(local_blocks, width_two)
     partial = jnp.einsum(
         "tab,ktbc->kac", left_part, right_done, preferred_element_type=jnp.float32
     ).astype(jnp.bfloat16)
     dual_cols = jnp.einsum(
         "jab,jbc->jac", left_dual, partial, preferred_element_type=jnp.float32
     ).astype(jnp.bfloat16)
-    mixed = jnp.einsum("jrn,jmn->jrm", dual_cols, right_dual, preferred_element_type=jnp.float32)
-    scaled = (mixed / (rates_full[:, :, None] + right_rates[:, None, :])).astype(jnp.bfloat16)
+    dual_cols = dual_cols.reshape(local_blocks, pieces, row_count, width_two)
+    mixed_parts = jnp.einsum(
+        "jsrn,jmn->sjrm", dual_cols, right_dual, preferred_element_type=jnp.float32
+    ).astype(jnp.bfloat16)
+    mixed = scatter_sum(mixed_parts, "sub")
+    scaled = (mixed / (left_rates[:, :, None] + right_rates[:, None, :])).astype(jnp.bfloat16)
     basis_rows = jnp.einsum(
         "jrm,jkm->jrk", scaled, right_eigenvector_matrix, preferred_element_type=jnp.float32
     ).astype(jnp.bfloat16)
-    basis_rows = basis_rows.reshape(local_blocks, width_two, pieces, cols)
-    spread = jnp.einsum(
-        "jab,jbkc->kjac", left_basis, basis_rows, preferred_element_type=jnp.float32
-    ).astype(jnp.bfloat16)
-    return scatter_sum(spread, "sub")
+    basis_cols = lax.all_to_all(basis_rows, "sub", split_axis=2, concat_axis=1, tiled=True)
+    return jnp.einsum("jab,jbc->jac", left_basis, basis_cols, preferred_element_type=jnp.float32)
 
 
 def solution(mesh):

time: 128 us -> 101 us (0.79)
  the two profiles are of different devices: /device:TPU:1 before, /device:TPU:24 now
where the time goes in v6:
time: 101 us
  starting transfers between devices  32.3 us (32%)
  waiting for transfers between devices  28.3 us (28%)
  matrix products  16.1 us (16%)
  blocking collectives  14.4 us (14%)
  local copies, waits for them, and re-layouts  7.45 us (7%)
  other arithmetic  2.11 us (2%)
    ppermute x7, starting transfers between devices, scatter_sum(): got = lax.ppermute(send, axis, [(j, (j + k) % n) for j in range(n)])  20.8 us
    ppermute x12, waiting for transfers between devices, move(): return lax.ppermute(piece, 'blk', pairs_list)  15.2 us
    all_to_all x1, blocking collectives, local(): lax.all_to_all(basis_rows, 'sub', split_axis=2, concat_axis=1, tiled=True)  14.4 us
    ppermute x7, waiting for transfers between devices, scatter_sum(): got = lax.ppermute(send, axis, [(j, (j + k) % n) for j in range(n)])  13.1 us
    ppermute x12, starting transfers between devices, move(): return lax.ppermute(piece, 'blk', pairs_list)  11.5 us
    dot_general x8, matrix products, pool(): jnp.einsum('kab,abrn->krn', w, piece, preferred_element_type=jnp.float32)  5.69 us
    dot_general x1, matrix products, local(): jnp.einsum('tab,ktbc->kac', left_part, right_done, preferred_element_type...  5.57 us
    dot_general x1, matrix products, local(): jnp.einsum('jrm,jkm->jrk', scaled, right_eigenvector_matrix, preferred_el...  2.07 us
  transfers between devices with their start and end apart: 19, of which 11 were waited for; matrix products, arithmetic and copies ran while one was open for 10% of the time, Pallas kernels for 0%

profile of v6, /device:TPU:24, one launch (start us, length us, event | category | flops | bytes accessed | tf_op | source)
XLA Modules:
  0.0 101.0 jit_solution(14843841143560049608)
XLA Ops:
  0.0 1.5 %collective-permute-start.1 = (bf16[2,64,512]{2,1,0:T(8,128)(2,1)}, bf16[2,64,512]{2,1,0:T(8,128)(2,1)S(1)}, u32[]{:S(2)}, u32[]{:S(2)}) collective-permute-start(bf16[2,64,512]{2,1,0:T(8,128)(2,1)} %param.11), channel_id=1, source_target_pairs={{0,64},{8,72},{16,80},{24,88},{32,96},{40,104},{48,112},{56,120},{... | collective-permute-start | bytes 393224 | tf_op jit(solution)/shard_map/ppermute | solution.py:71
  1.5 1.7 %collective-permute-start = (bf16[2,64,512]{2,1,0:T(8,128)(2,1)}, bf16[2,64,512]{2,1,0:T(8,128)(2,1)S(1)}, u32[]{:S(2)}, u32[]{:S(2)}) collective-permute-start(bf16[2,64,512]{2,1,0:T(8,128)(2,1)} %param.11), channel_id=1, source_target_pairs={{0,192},{8,200},{16,208},{24,216},{32,224},{40,232},{48,240},{56,2... | collective-permute-start | bytes 393224 | tf_op jit(solution)/shard_map/ppermute | solution.py:71
  3.6 1.1 %constant_dynamic-slice_fusion = s32[32,1,2,3]{1,2,3,0:T(2,128)S(1)} fusion(s32[32,32,2,3]{1,2,3,0:T(2,128)} %param.14, s32[]{:T(128)S(6)} %select_n.102), kind=kLoop, calls=%fused_computation.61 | loop fusion | bytes 1540 | tf_op jit(solution)/shard_map/jit(dynamic_index_in_dim)/dynamic_slice | solution.py:42
  4.7 0.9 dynamic-slice_reduce_fusion
  5.7 1.0 collective-permute-done.1
  7.0 3.0 %collective-permute-start.3 = (bf16[1,64,512]{2,1,0:T(8,128)(2,1)S(1)}, bf16[1,64,512]{2,1,0:T(8,128)(2,1)S(1)}, u32[]{:S(2)}, u32[]{:S(2)}) collective-permute-start(bf16[1,64,512]{2,1,0:T(8,128)(2,1)S(1)} %slice.65), channel_id=1, source_target_pairs={{0,192},{8,200},{16,208},{24,216},{32,224},{40,232},{48,240},{56,2... | collective-permute-start | bytes 196616 | tf_op jit(solution)/shard_map/ppermute | solution.py:71
  10.1 1.1 %copy.83 = bf16[1,2,64,512]{3,0,1,2:T(2,128)(2,1)S(1)} copy(bf16[1,2,64,512]{3,2,1,0:T(8,128)(2,1)} %bitcast.195) | data formatting | bytes 262144 | tf_op jit(solution)/shard_map/stack | solution.py:79
  11.6 0.5 collective-permute-done.2
  12.4 1.2 %pad_maximum_fusion = bf16[4,2,64,512]{3,0,1,2:T(4,128)(2,1)S(1)} fusion(bf16[1,2,64,512]{3,0,1,2:T(2,128)(2,1)S(1)} %copy.86, bf16[1,2,64,512]{3,0,1,2:T(2,128)(2,1)S(1)} %copy.85, bf16[1,2,64,512]{3,0,1,2:T(2,128)(2,1)S(1)} %copy.84, bf16[1,2,64,512]{3,0,1,2:T(2,128)(2,1)S(1)} %copy.83), kind=kLoop, calls=%fused_computation.24 | loop fusion | flops 2097152 | bytes 1048576 | tf_op jit(solution)/shard_map/stack | solution.py:79
  13.6 1.8 %collective-permute-start.5 = (bf16[4,2,64,512]{3,0,1,2:T(4,128)(2,1)S(1)}, bf16[4,2,64,512]{3,0,1,2:T(4,128)(2,1)S(1)}, u32[]{:S(2)}, u32[]{:S(2)}) collective-permute-start(bf16[4,2,64,512]{3,0,1,2:T(4,128)(2,1)S(1)} %pad_maximum_fusion), channel_id=1, source_target_pairs={{0,16},{8,24},{16,32},{24,40},{32,48},{40,56},{48,0},{56,8},{64,80... | collective-permute-start | bytes 1572872 | tf_op jit(solution)/shard_map/ppermute | solution.py:71
  15.4 0.3 collective-permute-start.4
  16.2 0.6 fusion.54
  16.8 8.7 %collective-permute-done.5 = bf16[4,2,64,512]{3,0,1,2:T(4,128)(2,1)S(1)} collective-permute-done((bf16[4,2,64,512]{3,0,1,2:T(4,128)(2,1)S(1)}, bf16[4,2,64,512]{3,0,1,2:T(4,128)(2,1)S(1)}, u32[]{:S(2)}, u32[]{:S(2)}) %collective-permute-start.5) | collective-permute-done | bytes 524320 | tf_op jit(solution)/shard_map/ppermute | solution.py:71
  25.7 1.6 %collective-permute-start.6 = (bf16[2,2,64,512]{3,0,1,2:T(2,128)(2,1)S(1)}, bf16[2,2,64,512]{3,0,1,2:T(2,128)(2,1)S(1)}, u32[]{:S(2)}, u32[]{:S(2)}) collective-permute-start(bf16[2,2,64,512]{3,0,1,2:T(2,128)(2,1)S(1)} %slice.68), channel_id=1, source_target_pairs={{0,16},{8,24},{16,32},{24,40},{32,48},{40,56},{48,0},{56,8},{64,80... | collective-permute-start | bytes 786440 | tf_op jit(solution)/shard_map/ppermute | solution.py:71
  27.6 0.6 collective-permute-start.7
  28.2 0.5 collective-permute-start.11
  28.7 0.6 fusion.48
  29.3 0.6 fusion.52
  29.9 0.6 fusion.46
  30.5 1.6 %collective-permute-done.6 = bf16[2,2,64,512]{3,0,1,2:T(2,128)(2,1)S(1)} collective-permute-done((bf16[2,2,64,512]{3,0,1,2:T(2,128)(2,1)S(1)}, bf16[2,2,64,512]{3,0,1,2:T(2,128)(2,1)S(1)}, u32[]{:S(2)}, u32[]{:S(2)}) %collective-permute-start.6) | collective-permute-done | bytes 262176 | tf_op jit(solution)/shard_map/ppermute | solution.py:71
  32.1 3.1 %collective-permute-done.7 = bf16[2,2,64,512]{3,0,1,2:T(2,128)(2,1)S(1)} collective-permute-done((bf16[2,2,64,512]{3,0,1,2:T(2,128)(2,1)S(1)}, bf16[2,2,64,512]{3,0,1,2:T(2,128)(2,1)S(1)}, u32[]{:S(2)}, u32[]{:S(2)}) %collective-permute-start.7) | collective-permute-done | bytes 262176 | tf_op jit(solution)/shard_map/ppermute | solution.py:71
  35.2 0.5 pad_maximum_fusion.1
  35.9 1.0 fusion.50
  36.9 0.6 fusion.44
  37.5 0.3 collective-permute-done.10
  37.8 0.6 fusion.42
  38.4 1.1 %fusion.9 = bf16[2,8,64,512]{3,1,0,2:T(8,128)(2,1)S(1)} fusion(bf16[4,2,64,512]{3,0,1,2:T(4,128)(2,1)S(1)} %collective-permute-done.11, f32[16,64,512,1]{2,0,3,1:T(8,128)S(1)} %fusion.42, f32[16,64,512,1]{2,0,3,1:T(8,128)S(1)} %fusion.44, f32[16,64,512,1]{2,0,3,1:T(8,128)S(1)} %fusion.46, f32[16,64,512,1]{2,0,3,1:T(8,128)S(1)} %fusion.48, ...), kind=kOutput, calls=%fused_computation.15 | convolution fusion | flops 12582912 | bytes 16253184 | tf_op jit(solution)/shard_map/kab,abrn->krn/dot_general | solution.py:92
  39.5 5.6 %bitcast_convert_fusion = bf16[2,512,512]{2,1,0:T(8,128)(2,1)S(1)} fusion(bf16[8,512,512]{2,1,0:T(8,128)(2,1)} %param.12, s32[]{:T(128)S(6)} %select_n.109, bf16[8,512,512]{2,1,0:T(8,128)(2,1)} %param.13, bf16[2,8,64,512]{3,1,0,2:T(8,128)(2,1)S(1)} %fusion.9), kind=kOutput, calls=%fused_computation.2 | convolution fusion | flops 1074790400 | bytes 7340036 | tf_op jit(solution)/shard_map/tab,ktbc->kac/dot_general | solution.py:109
  45.1 0.7 convolution_convert_fusion.1
  45.8 0.5 copy-done.1
  46.3 0.7 convolution_convert_fusion
  47.0 0.8 dynamic-slice_bitcast_fusion.6
  47.8 1.8 %collective-permute-start.12 = (bf16[2,64,512]{2,1,0:T(8,128)(2,1)S(1)}, bf16[2,64,512]{2,1,0:T(8,128)(2,1)S(1)}, u32[]{:S(2)}, u32[]{:S(2)}) collective-permute-start(bf16[2,64,512]{2,1,0:T(8,128)(2,1)S(1)} %get-tuple-element.5), channel_id=1, source_target_pairs={{0,1},{1,2},{2,3},{3,4},{4,5},{5,6},{6,7},{7,0},{8,9},{9,10},{10,1... | collective-permute-start | bytes 393224 | tf_op jit(solution)/shard_map/ppermute | solution.py:13
  49.7 3.3 %collective-permute-start.13 = (bf16[2,64,512]{2,1,0:T(8,128)(2,1)S(1)}, bf16[2,64,512]{2,1,0:T(8,128)(2,1)S(1)}, u32[]{:S(2)}, u32[]{:S(2)}) collective-permute-start(bf16[2,64,512]{2,1,0:T(8,128)(2,1)S(1)} %get-tuple-element.11), channel_id=1, source_target_pairs={{0,2},{1,3},{2,4},{3,5},{4,6},{5,7},{6,0},{7,1},{8,10},{9,11},{10,... | collective-permute-start | bytes 393224 | tf_op jit(solution)/shard_map/ppermute | solution.py:13
  53.0 4.0 %collective-permute-start.14 = (bf16[2,64,512]{2,1,0:T(8,128)(2,1)}, bf16[2,64,512]{2,1,0:T(8,128)(2,1)}, u32[]{:S(2)}, u32[]{:S(2)}) collective-permute-start(bf16[2,64,512]{2,1,0:T(8,128)(2,1)} %get-tuple-element.10), channel_id=1, source_target_pairs={{0,3},{1,4},{2,5},{3,6},{4,7},{5,0},{6,1},{7,2},{8,11},{9,12},{10,... | collective-permute-start | bytes 393224 | tf_op jit(solution)/shard_map/ppermute | solution.py:13
  57.0 0.5 collective-permute-start.15
  57.5 4.9 %collective-permute-start.16 = (bf16[2,64,512]{2,1,0:T(8,128)(2,1)S(1)}, bf16[2,64,512]{2,1,0:T(8,128)(2,1)}, u32[]{:S(2)}, u32[]{:S(2)}) collective-permute-start(bf16[2,64,512]{2,1,0:T(8,128)(2,1)S(1)} %get-tuple-element.8), channel_id=1, source_target_pairs={{0,5},{1,6},{2,7},{3,0},{4,1},{5,2},{6,3},{7,4},{8,13},{9,14},{10,... | collective-permute-start | bytes 393224 | tf_op jit(solution)/shard_map/ppermute | solution.py:13
  62.5 2.7 %collective-permute-start.17 = (bf16[2,64,512]{2,1,0:T(8,128)(2,1)S(1)}, bf16[2,64,512]{2,1,0:T(8,128)(2,1)}, u32[]{:S(2)}, u32[]{:S(2)}) collective-permute-start(bf16[2,64,512]{2,1,0:T(8,128)(2,1)S(1)} %get-tuple-element.7), channel_id=1, source_target_pairs={{0,6},{1,7},{2,0},{3,1},{4,2},{5,3},{6,4},{7,5},{8,14},{9,15},{10,... | collective-permute-start | bytes 393224 | tf_op jit(solution)/shard_map/ppermute | solution.py:13
  65.2 0.7 collective-permute-done.13
  65.9 0.6 copy-done.4
  66.5 3.5 %collective-permute-start.18 = (bf16[2,64,512]{2,1,0:T(8,128)(2,1)S(1)}, bf16[2,64,512]{2,1,0:T(8,128)(2,1)}, u32[]{:S(2)}, u32[]{:S(2)}) collective-permute-start(bf16[2,64,512]{2,1,0:T(8,128)(2,1)S(1)} %get-tuple-element.6), channel_id=1, source_target_pairs={{0,7},{1,0},{2,1},{3,2},{4,3},{5,4},{6,5},{7,6},{8,15},{9,8},{10,9... | collective-permute-start | bytes 393224 | tf_op jit(solution)/shard_map/ppermute | solution.py:13
  70.0 4.9 %collective-permute-done.14 = bf16[2,64,512]{2,1,0:T(8,128)(2,1)} collective-permute-done((bf16[2,64,512]{2,1,0:T(8,128)(2,1)}, bf16[2,64,512]{2,1,0:T(8,128)(2,1)}, u32[]{:S(2)}, u32[]{:S(2)}) %collective-permute-start.14) | collective-permute-done | bytes 131104 | tf_op jit(solution)/shard_map/ppermute | solution.py:13
  74.9 3.5 %collective-permute-done.16 = bf16[2,64,512]{2,1,0:T(8,128)(2,1)} collective-permute-done((bf16[2,64,512]{2,1,0:T(8,128)(2,1)S(1)}, bf16[2,64,512]{2,1,0:T(8,128)(2,1)}, u32[]{:S(2)}, u32[]{:S(2)}) %collective-permute-start.16) | collective-permute-done | bytes 131104 | tf_op jit(solution)/shard_map/ppermute | solution.py:13
  78.4 3.4 %collective-permute-done.17 = bf16[2,64,512]{2,1,0:T(8,128)(2,1)} collective-permute-done((bf16[2,64,512]{2,1,0:T(8,128)(2,1)S(1)}, bf16[2,64,512]{2,1,0:T(8,128)(2,1)}, u32[]{:S(2)}, u32[]{:S(2)}) %collective-permute-start.17) | collective-permute-done | bytes 131104 | tf_op jit(solution)/shard_map/ppermute | solution.py:13
  81.9 0.5 collective-permute-done.18
  82.4 2.1 %convolution_convert_fusion.2 = bf16[2,64,512]{2,1,0:T(8,128)(2,1)S(1)} fusion(bf16[2,512,512]{2,1,0:T(8,128)(2,1)} %param.18, bf16[2,64,512]{2,1,0:T(8,128)(2,1)} %collective-permute-done.18, bf16[2,64,512]{2,1,0:T(8,128)(2,1)} %collective-permute-done.17, bf16[2,64,512]{2,1,0:T(8,128)(2,1)} %collective-permute-done.16, ...), kind=kOutput, calls=%fused_computation.17 | convolution fusion | flops 68354048 | bytes 2233348 | tf_op jit(solution)/shard_map/jrm,jkm->jrk/dot_general | solution.py:121
  84.9 14.4 %all_to_all.18 = bf16[8,2,4096]{2,1,0:T(2,128)(2,1)S(1)} all-to-all(bf16[8,2,4096]{2,1,0:T(2,128)(2,1)S(1)} %reshape.182), channel_id=1, replica_groups=mesh['blk'=32,'sub'=8] {'sub'}, dimensions={0} | all-to-all | bytes 262144 | tf_op jit(solution)/shard_map/all_to_all | solution.py:124
  99.9 1.1 %convolution_bitcast_fusion = f32[2,512,64]{1,2,0:T(8,128)} fusion(bf16[2,512,64]{1,2,0:T(8,128)(2,1)S(1)} %all_to_all.16, bf16[2,512,512]{2,1,0:T(8,128)(2,1)S(1)} %copy-done.2), kind=kOutput, calls=%fused_computation.16 | convolution fusion | flops 67108864 | bytes 1441792 | tf_op jit(solution)/shard_map/jab,jbc->jac/dot_general | solution.py:125
  (50 shorter events, 3.5 us)
Async XLA Ops:
  0.0 45.1 %copy-start = (bf16[2,512,512]{2,1,0:T(8,128)(2,1)S(1)}, bf16[2,512,512]{2,1,0:T(8,128)(2,1)}, u32[]{:S(2)}) copy-start(bf16[2,512,512]{2,1,0:T(8,128)(2,1)} %param.17) | copy-start | bytes 3145732
  0.0 6.7 %collective-permute-start.1 = (bf16[2,64,512]{2,1,0:T(8,128)(2,1)}, bf16[2,64,512]{2,1,0:T(8,128)(2,1)S(1)}, u32[]{:S(2)}, u32[]{:S(2)}) collective-permute-start(bf16[2,64,512]{2,1,0:T(8,128)(2,1)} %param.11), channel_id=1, source_target_pairs={{0,64},{8,72},{16,80},{24,88},{32,96},{40,104},{48,112},{56,120},{... | collective-permute-start | bytes 393224 | tf_op jit(solution)/shard_map/ppermute | solution.py:71
  1.5 5.5 %collective-permute-start = (bf16[2,64,512]{2,1,0:T(8,128)(2,1)}, bf16[2,64,512]{2,1,0:T(8,128)(2,1)S(1)}, u32[]{:S(2)}, u32[]{:S(2)}) collective-permute-start(bf16[2,64,512]{2,1,0:T(8,128)(2,1)} %param.11), channel_id=1, source_target_pairs={{0,192},{8,200},{16,208},{24,216},{32,224},{40,232},{48,240},{56,2... | collective-permute-start | bytes 393224 | tf_op jit(solution)/shard_map/ppermute | solution.py:71
  6.7 5.5 %collective-permute-start.2 = (bf16[1,64,512]{2,1,0:T(8,128)(2,1)S(1)}, bf16[1,64,512]{2,1,0:T(8,128)(2,1)S(1)}, u32[]{:S(2)}, u32[]{:S(2)}) collective-permute-start(bf16[1,64,512]{2,1,0:T(8,128)(2,1)S(1)} %slice.64), channel_id=1, source_target_pairs={{0,64},{8,72},{16,80},{24,88},{32,96},{40,104},{48,112},{56,120},{... | collective-permute-start | bytes 196616 | tf_op jit(solution)/shard_map/ppermute | solution.py:71
  7.0 5.2 %collective-permute-start.3 = (bf16[1,64,512]{2,1,0:T(8,128)(2,1)S(1)}, bf16[1,64,512]{2,1,0:T(8,128)(2,1)S(1)}, u32[]{:S(2)}, u32[]{:S(2)}) collective-permute-start(bf16[1,64,512]{2,1,0:T(8,128)(2,1)S(1)} %slice.65), channel_id=1, source_target_pairs={{0,192},{8,200},{16,208},{24,216},{32,224},{40,232},{48,240},{56,2... | collective-permute-start | bytes 196616 | tf_op jit(solution)/shard_map/ppermute | solution.py:71
  13.6 11.9 %collective-permute-start.5 = (bf16[4,2,64,512]{3,0,1,2:T(4,128)(2,1)S(1)}, bf16[4,2,64,512]{3,0,1,2:T(4,128)(2,1)S(1)}, u32[]{:S(2)}, u32[]{:S(2)}) collective-permute-start(bf16[4,2,64,512]{3,0,1,2:T(4,128)(2,1)S(1)} %pad_maximum_fusion), channel_id=1, source_target_pairs={{0,16},{8,24},{16,32},{24,40},{32,48},{40,56},{48,0},{56,8},{64,80... | collective-permute-start | bytes 1572872 | tf_op jit(solution)/shard_map/ppermute | solution.py:71
  15.4 11.9 %collective-permute-start.4 = (bf16[4,2,64,512]{3,0,1,2:T(4,128)(2,1)S(1)}, bf16[4,2,64,512]{3,0,1,2:T(4,128)(2,1)S(1)}, u32[]{:S(2)}, u32[]{:S(2)}) collective-permute-start(bf16[4,2,64,512]{3,0,1,2:T(4,128)(2,1)S(1)} %pad_maximum_fusion), channel_id=1, source_target_pairs={{0,48},{8,56},{16,0},{24,8},{32,16},{40,24},{48,32},{56,40},{64,11... | collective-permute-start | bytes 1572872 | tf_op jit(solution)/shard_map/ppermute | solution.py:71
  16.1 13.8 %collective-permute-start.8 = (bf16[4,2,64,512]{3,0,1,2:T(4,128)(2,1)S(1)}, bf16[4,2,64,512]{3,0,1,2:T(4,128)(2,1)S(1)}, u32[]{:S(2)}, u32[]{:S(2)}) collective-permute-start(bf16[4,2,64,512]{3,0,1,2:T(4,128)(2,1)S(1)} %pad_maximum_fusion), channel_id=1, source_target_pairs={{0,8},{8,0},{16,24},{24,16},{32,40},{40,32},{48,56},{56,48},{64,72... | collective-permute-start | bytes 1572872 | tf_op jit(solution)/shard_map/ppermute | solution.py:71
  25.7 6.4 %collective-permute-start.6 = (bf16[2,2,64,512]{3,0,1,2:T(2,128)(2,1)S(1)}, bf16[2,2,64,512]{3,0,1,2:T(2,128)(2,1)S(1)}, u32[]{:S(2)}, u32[]{:S(2)}) collective-permute-start(bf16[2,2,64,512]{3,0,1,2:T(2,128)(2,1)S(1)} %slice.68), channel_id=1, source_target_pairs={{0,16},{8,24},{16,32},{24,40},{32,48},{40,56},{48,0},{56,8},{64,80... | collective-permute-start | bytes 786440 | tf_op jit(solution)/shard_map/ppermute | solution.py:71
  27.6 7.7 %collective-permute-start.7 = (bf16[2,2,64,512]{3,0,1,2:T(2,128)(2,1)S(1)}, bf16[2,2,64,512]{3,0,1,2:T(2,128)(2,1)S(1)}, u32[]{:S(2)}, u32[]{:S(2)}) collective-permute-start(bf16[2,2,64,512]{3,0,1,2:T(2,128)(2,1)S(1)} %slice.69), channel_id=1, source_target_pairs={{0,48},{8,56},{16,0},{24,8},{32,16},{40,24},{48,32},{56,40},{64,11... | collective-permute-start | bytes 786440 | tf_op jit(solution)/shard_map/ppermute | solution.py:71
  28.2 8.7 %collective-permute-start.9 = (bf16[4,2,64,512]{3,0,1,2:T(4,128)(2,1)S(1)}, bf16[4,2,64,512]{3,0,1,2:T(4,128)(2,1)S(1)}, u32[]{:S(2)}, u32[]{:S(2)}) collective-permute-start(bf16[4,2,64,512]{3,0,1,2:T(4,128)(2,1)S(1)} %collective-permute-done.4), channel_id=1, source_target_pairs={{0,8},{8,0},{16,24},{24,16},{32,40},{40,32},{48,56},{56,48},{64,72... | collective-permute-start | bytes 1572872 | tf_op jit(solution)/shard_map/ppermute | solution.py:71
  28.2 10.2 %collective-permute-start.11 = (bf16[4,2,64,512]{3,0,1,2:T(4,128)(2,1)S(1)}, bf16[4,2,64,512]{3,0,1,2:T(4,128)(2,1)S(1)}, u32[]{:S(2)}, u32[]{:S(2)}) collective-permute-start(bf16[4,2,64,512]{3,0,1,2:T(4,128)(2,1)S(1)} %collective-permute-done.5), channel_id=1, source_target_pairs={{0,8},{8,0},{16,24},{24,16},{32,40},{40,32},{48,56},{56,48},{64,72... | collective-permute-start | bytes 1572872 | tf_op jit(solution)/shard_map/ppermute | solution.py:71
  35.8 2.0 %collective-permute-start.10 = (bf16[4,2,64,512]{3,0,1,2:T(4,128)(2,1)S(1)}, bf16[4,2,64,512]{3,0,1,2:T(4,128)(2,1)S(1)}, u32[]{:S(2)}, u32[]{:S(2)}) collective-permute-start(bf16[4,2,64,512]{3,0,1,2:T(4,128)(2,1)S(1)} %pad_maximum_fusion.1), channel_id=1, source_target_pairs={{0,8},{8,0},{16,24},{24,16},{32,40},{40,32},{48,56},{56,48},{64,72... | collective-permute-start | bytes 1572872 | tf_op jit(solution)/shard_map/ppermute | solution.py:71
  45.1 1.2 %copy-start.1 = (bf16[2,512,512]{2,1,0:T(8,128)(2,1)S(1)}, bf16[2,512,512]{2,1,0:T(8,128)(2,1)}, u32[]{:S(2)}) copy-start(bf16[2,512,512]{2,1,0:T(8,128)(2,1)} %param.19) | copy-start | bytes 3145732
  46.3 36.1 %copy-start.5 = (f32[2,512]{1,0:T(2,128)S(1)}, f32[2,512]{1,0:T(2,128)}, u32[]{:S(2)}) copy-start(f32[2,512]{1,0:T(2,128)} %param.21) | copy-start | bytes 12292
  46.3 36.1 %copy-start.6 = (f32[2,64]{1,0:T(2,128)S(1)}, f32[2,64]{1,0:T(2,128)}, u32[]{:S(2)}) copy-start(f32[2,64]{1,0:T(2,128)} %param.20) | copy-start | bytes 1540
  47.8 14.6 %collective-permute-start.12 = (bf16[2,64,512]{2,1,0:T(8,128)(2,1)S(1)}, bf16[2,64,512]{2,1,0:T(8,128)(2,1)S(1)}, u32[]{:S(2)}, u32[]{:S(2)}) collective-permute-start(bf16[2,64,512]{2,1,0:T(8,128)(2,1)S(1)} %get-tuple-element.5), channel_id=1, source_target_pairs={{0,1},{1,2},{2,3},{3,4},{4,5},{5,6},{6,7},{7,0},{8,9},{9,10},{10,1... | collective-permute-start | bytes 393224 | tf_op jit(solution)/shard_map/ppermute | solution.py:13
  49.7 16.2 %collective-permute-start.13 = (bf16[2,64,512]{2,1,0:T(8,128)(2,1)S(1)}, bf16[2,64,512]{2,1,0:T(8,128)(2,1)S(1)}, u32[]{:S(2)}, u32[]{:S(2)}) collective-permute-start(bf16[2,64,512]{2,1,0:T(8,128)(2,1)S(1)} %get-tuple-element.11), channel_id=1, source_target_pairs={{0,2},{1,3},{2,4},{3,5},{4,6},{5,7},{6,0},{7,1},{8,10},{9,11},{10,... | collective-permute-start | bytes 393224 | tf_op jit(solution)/shard_map/ppermute | solution.py:13
  53.0 22.0 %collective-permute-start.14 = (bf16[2,64,512]{2,1,0:T(8,128)(2,1)}, bf16[2,64,512]{2,1,0:T(8,128)(2,1)}, u32[]{:S(2)}, u32[]{:S(2)}) collective-permute-start(bf16[2,64,512]{2,1,0:T(8,128)(2,1)} %get-tuple-element.10), channel_id=1, source_target_pairs={{0,3},{1,4},{2,5},{3,6},{4,7},{5,0},{6,1},{7,2},{8,11},{9,12},{10,... | collective-permute-start | bytes 393224 | tf_op jit(solution)/shard_map/ppermute | solution.py:13
  57.0 17.9 %collective-permute-start.15 = (bf16[2,64,512]{2,1,0:T(8,128)(2,1)}, bf16[2,64,512]{2,1,0:T(8,128)(2,1)}, u32[]{:S(2)}, u32[]{:S(2)}) collective-permute-start(bf16[2,64,512]{2,1,0:T(8,128)(2,1)} %get-tuple-element.9), channel_id=1, source_target_pairs={{0,4},{1,5},{2,6},{3,7},{4,0},{5,1},{6,2},{7,3},{8,12},{9,13},{10,... | collective-permute-start | bytes 393224 | tf_op jit(solution)/shard_map/ppermute | solution.py:13
  57.5 20.9 %collective-permute-start.16 = (bf16[2,64,512]{2,1,0:T(8,128)(2,1)S(1)}, bf16[2,64,512]{2,1,0:T(8,128)(2,1)}, u32[]{:S(2)}, u32[]{:S(2)}) collective-permute-start(bf16[2,64,512]{2,1,0:T(8,128)(2,1)S(1)} %get-tuple-element.8), channel_id=1, source_target_pairs={{0,5},{1,6},{2,7},{3,0},{4,1},{5,2},{6,3},{7,4},{8,13},{9,14},{10,... | collective-permute-start | bytes 393224 | tf_op jit(solution)/shard_map/ppermute | solution.py:13
  62.5 3.4 %copy-start.3 = (bf16[2,64,512]{2,1,0:T(8,128)(2,1)}, bf16[2,64,512]{2,1,0:T(8,128)(2,1)S(1)}, u32[]{:S(2)}) copy-start(bf16[2,64,512]{2,1,0:T(8,128)(2,1)S(1)} %collective-permute-done.12) | copy-start | bytes 393220
  62.5 19.4 %collective-permute-start.17 = (bf16[2,64,512]{2,1,0:T(8,128)(2,1)S(1)}, bf16[2,64,512]{2,1,0:T(8,128)(2,1)}, u32[]{:S(2)}, u32[]{:S(2)}) collective-permute-start(bf16[2,64,512]{2,1,0:T(8,128)(2,1)S(1)} %get-tuple-element.7), channel_id=1, source_target_pairs={{0,6},{1,7},{2,0},{3,1},{4,2},{5,3},{6,4},{7,5},{8,14},{9,15},{10,... | collective-permute-start | bytes 393224 | tf_op jit(solution)/shard_map/ppermute | solution.py:13
  65.9 0.6 copy-start.4
  66.5 15.9 %collective-permute-start.18 = (bf16[2,64,512]{2,1,0:T(8,128)(2,1)S(1)}, bf16[2,64,512]{2,1,0:T(8,128)(2,1)}, u32[]{:S(2)}, u32[]{:S(2)}) collective-permute-start(bf16[2,64,512]{2,1,0:T(8,128)(2,1)S(1)} %get-tuple-element.6), channel_id=1, source_target_pairs={{0,7},{1,0},{2,1},{3,2},{4,3},{5,4},{6,5},{7,6},{8,15},{9,8},{10,9... | collective-permute-start | bytes 393224 | tf_op jit(solution)/shard_map/ppermute | solution.py:13
  70.0 29.8 %copy-start.2 = (bf16[2,512,512]{2,1,0:T(8,128)(2,1)S(1)}, bf16[2,512,512]{2,1,0:T(8,128)(2,1)}, u32[]{:S(2)}) copy-start(bf16[2,512,512]{2,1,0:T(8,128)(2,1)} %param.16) | copy-start | bytes 3145732

commit v7 on v4

--- a/solution.py
+++ b/solution.py
@@ -107,13 +107,14 @@
     ).astype(jnp.bfloat16)
     left_part = lax.dynamic_slice_in_dim(left_factor, part * row_count, row_count, axis=2)
     rates_run, pooled = lax.optimization_barrier((left_rates[None], pooled))
-    step = 1
-    while step < pieces:
-        came = lax.ppermute(rates_run, "sub", [(j, (j + step) % pieces) for j in range(pieces)])
-        rates_run = jnp.concatenate([came, rates_run], axis=0)
-        step *= 2
+
+    def shift_sub(piece, k):
+        return lax.ppermute(piece, "sub", [(j, (j + k) % pieces) for j in range(pieces)])
+
+    trio = jnp.concatenate([shift_sub(rates_run, 1), rates_run, shift_sub(rates_run, -1)], axis=0)
+    rates_run = jnp.concatenate([shift_sub(trio, 3), trio, shift_sub(trio, -3)[:2]], axis=0)
     rates_twice = jnp.concatenate([rates_run, rates_run], axis=0)
-    rates_parts = lax.dynamic_slice_in_dim(rates_twice, (pieces - 1 - part) % pieces, pieces, axis=0)
+    rates_parts = lax.dynamic_slice_in_dim(rates_twice, (4 - part) % pieces, pieces, axis=0)
     rates_full = jnp.moveaxis(rates_parts, 0, 1).reshape(local_blocks, width_two)
     partial = jnp.einsum(
         "tab,ktbc->kac", left_part, right_done, preferred_element_type=jnp.float32

time: 102 us -> 102 us (level)
  starting transfers between devices: 26.7 us -> 34.6 us
  waiting for transfers between devices: 46.6 us -> 38.8 us
    ppermute x3 -> x4, starting transfers between devices: 6.8 us -> 11.2 us  [shift_sub(): lax.ppermute(piece, 'sub', [(j, (j + k) % pieces) for j in range(pieces)])]
    ppermute x3 -> x4, waiting for transfers between devices: 11.1 us -> 6.76 us  [shift_sub(): lax.ppermute(piece, 'sub', [(j, (j + k) % pieces) for j in range(pieces)])]
    ppermute x7, starting transfers between devices: 8.38 us -> 11.9 us  [scatter_sum(): got = lax.ppermute(send, axis, [(j, (j + k) % n) for j in range(n)])]
    ppermute x7, waiting for transfers between devices: 20.2 us -> 16.8 us  [scatter_sum(): got = lax.ppermute(send, axis, [(j, (j + k) % n) for j in range(n)])]
  transfers between devices with their start and end apart: 22 -> 23, of which waited for: 14 -> 12; matrix products, arithmetic and copies ran while one was open for 16% -> 16% of each run, Pallas kernels for 0% -> 0%
where the time goes in v7:
time: 102 us; the launch traced here: 101 us
  waiting for transfers between devices  38.8 us (38%)
  starting transfers between devices  34.6 us (34%)
  matrix products  18.9 us (19%)
  local copies, waits for them, and re-layouts  4.81 us (5%)
  other arithmetic  3.85 us (4%)
    ppermute x7, waiting for transfers between devices, scatter_sum(): got = lax.ppermute(send, axis, [(j, (j + k) % n) for j in range(n)])  16.8 us
    ppermute x12, waiting for transfers between devices, move(): return lax.ppermute(piece, 'blk', pairs_list)  15.3 us
    ppermute x7, starting transfers between devices, scatter_sum(): got = lax.ppermute(send, axis, [(j, (j + k) % n) for j in range(n)])  11.9 us
    ppermute x12, starting transfers between devices, move(): return lax.ppermute(piece, 'blk', pairs_list)  11.5 us
    ppermute x4, starting transfers between devices, shift_sub(): lax.ppermute(piece, 'sub', [(j, (j + k) % pieces) for j in range(pieces)])  11.2 us
    ppermute x4, waiting for transfers between devices, shift_sub(): lax.ppermute(piece, 'sub', [(j, (j + k) % pieces) for j in range(pieces)])  6.76 us
    dot_general x1, matrix products, local(): jnp.einsum('tab,ktbc->kac', left_part, right_done, preferred_element_type...  6.58 us
    dot_general x8, matrix products, pool(): jnp.einsum('kab,abrn->krn', w, piece, preferred_element_type=jnp.float32)  5.7 us
  transfers between devices with their start and end apart: 23, of which 12 were waited for; matrix products, arithmetic and copies ran while one was open for 16% of the time, Pallas kernels for 0%

profile of v7, /device:TPU:24, one launch (start us, length us, event | category | flops | bytes accessed | tf_op | source)
XLA Modules:
  0.0 101.2 jit_solution(4724796438319368412)
XLA Ops:
  0.0 1.5 %collective-permute-start.1 = (bf16[2,64,512]{2,1,0:T(8,128)(2,1)}, bf16[2,64,512]{2,1,0:T(8,128)(2,1)S(1)}, u32[]{:S(2)}, u32[]{:S(2)}) collective-permute-start(bf16[2,64,512]{2,1,0:T(8,128)(2,1)} %param.11), channel_id=1, source_target_pairs={{0,64},{8,72},{16,80},{24,88},{32,96},{40,104},{48,112},{56,120},{... | collective-permute-start | bytes 393224 | tf_op jit(solution)/shard_map/ppermute | solution.py:71
  1.5 1.7 %collective-permute-start = (bf16[2,64,512]{2,1,0:T(8,128)(2,1)}, bf16[2,64,512]{2,1,0:T(8,128)(2,1)S(1)}, u32[]{:S(2)}, u32[]{:S(2)}) collective-permute-start(bf16[2,64,512]{2,1,0:T(8,128)(2,1)} %param.11), channel_id=1, source_target_pairs={{0,192},{8,200},{16,208},{24,216},{32,224},{40,232},{48,240},{56,2... | collective-permute-start | bytes 393224 | tf_op jit(solution)/shard_map/ppermute | solution.py:71
  3.6 1.1 %constant_dynamic-slice_fusion = s32[32,1,2,3]{1,2,3,0:T(2,128)S(1)} fusion(s32[32,32,2,3]{1,2,3,0:T(2,128)} %param.14, s32[]{:T(128)S(6)} %select_n.109), kind=kLoop, calls=%fused_computation.67 | loop fusion | bytes 1540 | tf_op jit(solution)/shard_map/jit(dynamic_index_in_dim)/dynamic_slice | solution.py:42
  4.7 0.9 dynamic-slice_reduce_fusion
  5.7 1.0 collective-permute-done.1
  6.7 0.3 collective-permute-start.2
  7.0 3.0 %collective-permute-start.3 = (bf16[1,64,512]{2,1,0:T(8,128)(2,1)S(1)}, bf16[1,64,512]{2,1,0:T(8,128)(2,1)S(1)}, u32[]{:S(2)}, u32[]{:S(2)}) collective-permute-start(bf16[1,64,512]{2,1,0:T(8,128)(2,1)S(1)} %slice.69), channel_id=1, source_target_pairs={{0,192},{8,200},{16,208},{24,216},{32,224},{40,232},{48,240},{56,2... | collective-permute-start | bytes 196616 | tf_op jit(solution)/shard_map/ppermute | solution.py:71
  10.1 1.1 %copy.87 = bf16[1,2,64,512]{3,0,1,2:T(2,128)(2,1)S(1)} copy(bf16[1,2,64,512]{3,2,1,0:T(8,128)(2,1)} %bitcast.219) | data formatting | bytes 262144 | tf_op jit(solution)/shard_map/stack | solution.py:79
  11.6 0.5 collective-permute-done.2
  12.4 1.2 %pad_maximum_fusion = bf16[4,2,64,512]{3,0,1,2:T(4,128)(2,1)S(1)} fusion(bf16[1,2,64,512]{3,0,1,2:T(2,128)(2,1)S(1)} %copy.90, bf16[1,2,64,512]{3,0,1,2:T(2,128)(2,1)S(1)} %copy.89, bf16[1,2,64,512]{3,0,1,2:T(2,128)(2,1)S(1)} %copy.88, bf16[1,2,64,512]{3,0,1,2:T(2,128)(2,1)S(1)} %copy.87), kind=kLoop, calls=%fused_computation.24 | loop fusion | flops 2097152 | bytes 1048576 | tf_op jit(solution)/shard_map/stack | solution.py:79
  13.6 1.8 %collective-permute-start.5 = (bf16[4,2,64,512]{3,0,1,2:T(4,128)(2,1)S(1)}, bf16[4,2,64,512]{3,0,1,2:T(4,128)(2,1)S(1)}, u32[]{:S(2)}, u32[]{:S(2)}) collective-permute-start(bf16[4,2,64,512]{3,0,1,2:T(4,128)(2,1)S(1)} %pad_maximum_fusion), channel_id=1, source_target_pairs={{0,16},{8,24},{16,32},{24,40},{32,48},{40,56},{48,0},{56,8},{64,80... | collective-permute-start | bytes 1572872 | tf_op jit(solution)/shard_map/ppermute | solution.py:71
  15.4 0.3 collective-permute-start.4
  16.1 0.6 fusion.46
  16.8 8.8 %collective-permute-done.5 = bf16[4,2,64,512]{3,0,1,2:T(4,128)(2,1)S(1)} collective-permute-done((bf16[4,2,64,512]{3,0,1,2:T(4,128)(2,1)S(1)}, bf16[4,2,64,512]{3,0,1,2:T(4,128)(2,1)S(1)}, u32[]{:S(2)}, u32[]{:S(2)}) %collective-permute-start.5) | collective-permute-done | bytes 524320 | tf_op jit(solution)/shard_map/ppermute | solution.py:71
  25.7 1.6 %collective-permute-start.6 = (bf16[2,2,64,512]{3,0,1,2:T(2,128)(2,1)S(1)}, bf16[2,2,64,512]{3,0,1,2:T(2,128)(2,1)S(1)}, u32[]{:S(2)}, u32[]{:S(2)}) collective-permute-start(bf16[2,2,64,512]{3,0,1,2:T(2,128)(2,1)S(1)} %slice.72), channel_id=1, source_target_pairs={{0,16},{8,24},{16,32},{24,40},{32,48},{40,56},{48,0},{56,8},{64,80... | collective-permute-start | bytes 786440 | tf_op jit(solution)/shard_map/ppermute | solution.py:71
  27.3 0.3 slice.73
  27.6 0.6 collective-permute-start.7
  28.2 0.5 collective-permute-start.11
  28.7 0.6 fusion.40
  29.3 0.6 fusion.44
  29.9 0.6 fusion.38
  30.5 1.6 %collective-permute-done.6 = bf16[2,2,64,512]{3,0,1,2:T(2,128)(2,1)S(1)} collective-permute-done((bf16[2,2,64,512]{3,0,1,2:T(2,128)(2,1)S(1)}, bf16[2,2,64,512]{3,0,1,2:T(2,128)(2,1)S(1)}, u32[]{:S(2)}, u32[]{:S(2)}) %collective-permute-start.6) | collective-permute-done | bytes 262176 | tf_op jit(solution)/shard_map/ppermute | solution.py:71
  32.1 3.1 %collective-permute-done.7 = bf16[2,2,64,512]{3,0,1,2:T(2,128)(2,1)S(1)} collective-permute-done((bf16[2,2,64,512]{3,0,1,2:T(2,128)(2,1)S(1)}, bf16[2,2,64,512]{3,0,1,2:T(2,128)(2,1)S(1)}, u32[]{:S(2)}, u32[]{:S(2)}) %collective-permute-start.7) | collective-permute-done | bytes 262176 | tf_op jit(solution)/shard_map/ppermute | solution.py:71
  35.2 0.5 pad_maximum_fusion.1
  35.9 1.0 fusion.42
  36.9 0.6 fusion.36
  37.5 0.3 collective-permute-done.10
  37.8 0.6 fusion.34
  38.4 1.1 %fusion.9 = bf16[2,8,64,512]{3,1,0,2:T(8,128)(2,1)S(1)} fusion(bf16[4,2,64,512]{3,0,1,2:T(4,128)(2,1)S(1)} %collective-permute-done.11, f32[16,64,512,1]{2,0,3,1:T(8,128)S(1)} %fusion.34, f32[16,64,512,1]{2,0,3,1:T(8,128)S(1)} %fusion.36, f32[16,64,512,1]{2,0,3,1:T(8,128)S(1)} %fusion.38, f32[16,64,512,1]{2,0,3,1:T(8,128)S(1)} %fusion.40, ...), kind=kOutput, calls=%fused_computation.17 | convolution fusion | flops 12582912 | bytes 16253184 | tf_op jit(solution)/shard_map/kab,abrn->krn/dot_general | solution.py:92
  39.5 1.9 %collective-permute-start.12 = (f32[1,2,64]{2,1,0:T(2,128)S(1)}, f32[1,2,64]{2,1,0:T(2,128)S(1)}, u32[]{:S(2)}, u32[]{:S(2)}) collective-permute-start(f32[1,2,64]{2,1,0:T(2,128)S(1)} %bitcast.222), channel_id=1, source_target_pairs={{0,1},{1,2},{2,3},{3,4},{4,5},{5,6},{6,7},{7,0},{8,9},{9,10},{10,1... | collective-permute-start | bytes 1544 | tf_op jit(solution)/shard_map/ppermute | solution.py:112
  41.4 4.1 %collective-permute-start.13 = (f32[1,2,64]{2,1,0:T(2,128)S(1)}, f32[1,2,64]{2,1,0:T(2,128)S(1)}, u32[]{:S(2)}, u32[]{:S(2)}) collective-permute-start(f32[1,2,64]{2,1,0:T(2,128)S(1)} %bitcast.223), channel_id=1, source_target_pairs={{0,7},{1,0},{2,1},{3,2},{4,3},{5,4},{6,5},{7,6},{8,15},{9,8},{10,9... | collective-permute-start | bytes 1544 | tf_op jit(solution)/shard_map/ppermute | solution.py:112
  45.5 1.4 %collective-permute-done.12 = f32[1,2,64]{2,1,0:T(2,128)S(1)} collective-permute-done((f32[1,2,64]{2,1,0:T(2,128)S(1)}, f32[1,2,64]{2,1,0:T(2,128)S(1)}, u32[]{:S(2)}, u32[]{:S(2)}) %collective-permute-start.12) | collective-permute-done | bytes 544 | tf_op jit(solution)/shard_map/ppermute | solution.py:112
  47.0 5.2 %collective-permute-start.14 = (f32[3,2,64]{2,1,0:T(2,128)S(1)}, f32[3,2,64]{2,1,0:T(2,128)S(1)}, u32[]{:S(2)}, u32[]{:S(2)}) collective-permute-start(f32[3,2,64]{2,1,0:T(2,128)S(1)} %constant_dynamic-update-slice_fusion), channel_id=1, source_target_pairs={{0,3},{1,4},{2,5},{3,6},{4,7},{5,0},{6,1},{7,2},{8,11},{9,12},{10,... | collective-permute-start | bytes 4616 | tf_op jit(solution)/shard_map/ppermute | solution.py:112
  52.1 6.6 %bitcast_convert_fusion = bf16[2,512,512]{2,1,0:T(8,128)(2,1)} fusion(bf16[8,512,512]{2,1,0:T(8,128)(2,1)} %param.12, s32[]{:T(128)S(6)} %select_n.116, bf16[8,512,512]{2,1,0:T(8,128)(2,1)} %param.13, bf16[2,8,64,512]{3,1,0,2:T(8,128)(2,1)S(1)} %fusion.9), kind=kOutput, calls=%fused_computation.2 | convolution fusion | flops 1074790400 | bytes 7340036 | tf_op jit(solution)/shard_map/tab,ktbc->kac/dot_general | solution.py:119
  58.8 5.3 %collective-permute-done.15 = f32[3,2,64]{2,1,0:T(2,128)S(1)} collective-permute-done((f32[3,2,64]{2,1,0:T(2,128)S(1)}, f32[3,2,64]{2,1,0:T(2,128)S(1)}, u32[]{:S(2)}, u32[]{:S(2)}) %collective-permute-start.15) | collective-permute-done | bytes 1568 | tf_op jit(solution)/shard_map/ppermute | solution.py:112
  64.3 3.6 %divide_convert_fusion = bf16[2,512,512]{2,1,0:T(8,128)(2,1)} fusion(bf16[2,512,512]{2,1,0:T(8,128)(2,1)S(1)} %copy-done, bf16[2,512,512]{2,1,0:T(8,128)(2,1)} %bitcast_convert_fusion, bf16[2,512,512]{2,1,0:T(8,128)(2,1)S(1)} %copy-done.3, f32[2,512]{1,0:T(2,128)S(1)} %copy-done.5, f32[2,512]{1,0:T(2,128)S(1)} %add.291), kind=kOutput, calls=%fused_computation.11 | convolution fusion | flops 1075838976 | bytes 4202496 | tf_op jit(solution)/shard_map/jrn,jmn->jrm/dot_general | solution.py:125
  67.9 2.1 %convolution_convert_fusion.1 = bf16[2,512,512]{1,2,0:T(8,128)(2,1)S(1)} fusion(bf16[2,512,512]{2,1,0:T(8,128)(2,1)} %divide_convert_fusion, bf16[2,512,512]{2,1,0:T(8,128)(2,1)S(1)} %copy-done.4), kind=kOutput, calls=%fused_computation.14 | convolution fusion | flops 537395200 | bytes 3145728 | tf_op jit(solution)/shard_map/jrm,jkm->jrk/dot_general | solution.py:127
  70.0 0.7 convolution_convert_fusion
  70.8 1.3 %collective-permute-start.16 = (bf16[2,512,64]{1,2,0:T(8,128)(2,1)S(1)}, bf16[2,512,64]{1,2,0:T(8,128)(2,1)S(1)}, u32[]{:S(2)}, u32[]{:S(2)}) collective-permute-start(bf16[2,512,64]{1,2,0:T(8,128)(2,1)S(1)} %get-tuple-element.7), channel_id=1, source_target_pairs={{0,1},{1,2},{2,3},{3,4},{4,5},{5,6},{6,7},{7,0},{8,9},{9,10},{10,1... | collective-permute-start | bytes 393224 | tf_op jit(solution)/shard_map/ppermute | solution.py:13
  72.1 1.2 %collective-permute-start.17 = (bf16[2,512,64]{1,2,0:T(8,128)(2,1)S(1)}, bf16[2,512,64]{1,2,0:T(8,128)(2,1)S(1)}, u32[]{:S(2)}, u32[]{:S(2)}) collective-permute-start(bf16[2,512,64]{1,2,0:T(8,128)(2,1)S(1)} %get-tuple-element.11), channel_id=1, source_target_pairs={{0,2},{1,3},{2,4},{3,5},{4,6},{5,7},{6,0},{7,1},{8,10},{9,11},{10,... | collective-permute-start | bytes 393224 | tf_op jit(solution)/shard_map/ppermute | solution.py:13
  73.6 5.2 %collective-permute-start.19 = (bf16[2,512,64]{1,2,0:T(8,128)(2,1)S(1)}, bf16[2,512,64]{1,2,0:T(8,128)(2,1)S(1)}, u32[]{:S(2)}, u32[]{:S(2)}) collective-permute-start(bf16[2,512,64]{1,2,0:T(8,128)(2,1)S(1)} %get-tuple-element.9), channel_id=1, source_target_pairs={{0,4},{1,5},{2,6},{3,7},{4,0},{5,1},{6,2},{7,3},{8,12},{9,13},{10,... | collective-permute-start | bytes 393224 | tf_op jit(solution)/shard_map/ppermute | solution.py:13
  78.8 2.1 %collective-permute-start.20 = (bf16[2,512,64]{1,2,0:T(8,128)(2,1)S(1)}, bf16[2,512,64]{1,2,0:T(8,128)(2,1)S(1)}, u32[]{:S(2)}, u32[]{:S(2)}) collective-permute-start(bf16[2,512,64]{1,2,0:T(8,128)(2,1)S(1)} %get-tuple-element.8), channel_id=1, source_target_pairs={{0,5},{1,6},{2,7},{3,0},{4,1},{5,2},{6,3},{7,4},{8,13},{9,14},{10,... | collective-permute-start | bytes 393224 | tf_op jit(solution)/shard_map/ppermute | solution.py:13
  80.9 1.8 %collective-permute-start.21 = (bf16[2,512,64]{1,2,0:T(8,128)(2,1)S(1)}, bf16[2,512,64]{1,2,0:T(8,128)(2,1)S(1)}, u32[]{:S(2)}, u32[]{:S(2)}) collective-permute-start(bf16[2,512,64]{1,2,0:T(8,128)(2,1)S(1)} %get-tuple-element.13), channel_id=1, source_target_pairs={{0,6},{1,7},{2,0},{3,1},{4,2},{5,3},{6,4},{7,5},{8,14},{9,15},{10,... | collective-permute-start | bytes 393224 | tf_op jit(solution)/shard_map/ppermute | solution.py:13
  82.7 4.4 %collective-permute-done.17 = bf16[2,512,64]{1,2,0:T(8,128)(2,1)S(1)} collective-permute-done((bf16[2,512,64]{1,2,0:T(8,128)(2,1)S(1)}, bf16[2,512,64]{1,2,0:T(8,128)(2,1)S(1)}, u32[]{:S(2)}, u32[]{:S(2)}) %collective-permute-start.17) | collective-permute-done | bytes 131104 | tf_op jit(solution)/shard_map/ppermute | solution.py:13
  87.1 6.2 %collective-permute-done.18 = bf16[2,512,64]{1,2,0:T(8,128)(2,1)S(1)} collective-permute-done((bf16[2,512,64]{1,2,0:T(8,128)(2,1)S(1)}, bf16[2,512,64]{1,2,0:T(8,128)(2,1)S(1)}, u32[]{:S(2)}, u32[]{:S(2)}) %collective-permute-start.18) | collective-permute-done | bytes 131104 | tf_op jit(solution)/shard_map/ppermute | solution.py:13
  93.3 5.5 %collective-permute-done.21 = bf16[2,512,64]{1,2,0:T(8,128)(2,1)S(1)} collective-permute-done((bf16[2,512,64]{1,2,0:T(8,128)(2,1)S(1)}, bf16[2,512,64]{1,2,0:T(8,128)(2,1)S(1)}, u32[]{:S(2)}, u32[]{:S(2)}) %collective-permute-start.21) | collective-permute-done | bytes 131104 | tf_op jit(solution)/shard_map/ppermute | solution.py:13
  98.9 0.6 collective-permute-done.22
  99.5 1.7 %fusion.24 = f32[2,512,64]{1,2,0:T(8,128)} fusion(bf16[2,512,64]{1,2,0:T(8,128)(2,1)} %collective-permute-done.22, bf16[2,512,64]{1,2,0:T(8,128)(2,1)S(1)} %collective-permute-done.21, bf16[2,512,64]{1,2,0:T(8,128)(2,1)S(1)} %collective-permute-done.20, bf16[2,512,64]{1,2,0:T(8,128)(2,1)S(1)} %collective-permute-done.19, ...), kind=kLoop, calls=%fused_computation.32 | loop fusion | flops 983040 | bytes 1310724 | tf_op jit(solution)/shard_map/add | solution.py:14
  (66 shorter events, 2.5 us)
Async XLA Ops:
  0.0 64.3 %copy-start = (bf16[2,512,512]{2,1,0:T(8,128)(2,1)S(1)}, bf16[2,512,512]{2,1,0:T(8,128)(2,1)}, u32[]{:S(2)}) copy-start(bf16[2,512,512]{2,1,0:T(8,128)(2,1)} %param.19) | copy-start | bytes 3145732
  0.0 6.7 %collective-permute-start.1 = (bf16[2,64,512]{2,1,0:T(8,128)(2,1)}, bf16[2,64,512]{2,1,0:T(8,128)(2,1)S(1)}, u32[]{:S(2)}, u32[]{:S(2)}) collective-permute-start(bf16[2,64,512]{2,1,0:T(8,128)(2,1)} %param.11), channel_id=1, source_target_pairs={{0,64},{8,72},{16,80},{24,88},{32,96},{40,104},{48,112},{56,120},{... | collective-permute-start | bytes 393224 | tf_op jit(solution)/shard_map/ppermute | solution.py:71
  1.5 5.5 %collective-permute-start = (bf16[2,64,512]{2,1,0:T(8,128)(2,1)}, bf16[2,64,512]{2,1,0:T(8,128)(2,1)S(1)}, u32[]{:S(2)}, u32[]{:S(2)}) collective-permute-start(bf16[2,64,512]{2,1,0:T(8,128)(2,1)} %param.11), channel_id=1, source_target_pairs={{0,192},{8,200},{16,208},{24,216},{32,224},{40,232},{48,240},{56,2... | collective-permute-start | bytes 393224 | tf_op jit(solution)/shard_map/ppermute | solution.py:71
  6.7 5.5 %collective-permute-start.2 = (bf16[1,64,512]{2,1,0:T(8,128)(2,1)S(1)}, bf16[1,64,512]{2,1,0:T(8,128)(2,1)S(1)}, u32[]{:S(2)}, u32[]{:S(2)}) collective-permute-start(bf16[1,64,512]{2,1,0:T(8,128)(2,1)S(1)} %slice.68), channel_id=1, source_target_pairs={{0,64},{8,72},{16,80},{24,88},{32,96},{40,104},{48,112},{56,120},{... | collective-permute-start | bytes 196616 | tf_op jit(solution)/shard_map/ppermute | solution.py:71
  7.0 5.2 %collective-permute-start.3 = (bf16[1,64,512]{2,1,0:T(8,128)(2,1)S(1)}, bf16[1,64,512]{2,1,0:T(8,128)(2,1)S(1)}, u32[]{:S(2)}, u32[]{:S(2)}) collective-permute-start(bf16[1,64,512]{2,1,0:T(8,128)(2,1)S(1)} %slice.69), channel_id=1, source_target_pairs={{0,192},{8,200},{16,208},{24,216},{32,224},{40,232},{48,240},{56,2... | collective-permute-start | bytes 196616 | tf_op jit(solution)/shard_map/ppermute | solution.py:71
  13.6 11.9 %collective-permute-start.5 = (bf16[4,2,64,512]{3,0,1,2:T(4,128)(2,1)S(1)}, bf16[4,2,64,512]{3,0,1,2:T(4,128)(2,1)S(1)}, u32[]{:S(2)}, u32[]{:S(2)}) collective-permute-start(bf16[4,2,64,512]{3,0,1,2:T(4,128)(2,1)S(1)} %pad_maximum_fusion), channel_id=1, source_target_pairs={{0,16},{8,24},{16,32},{24,40},{32,48},{40,56},{48,0},{56,8},{64,80... | collective-permute-start | bytes 1572872 | tf_op jit(solution)/shard_map/ppermute | solution.py:71
  15.4 11.9 %collective-permute-start.4 = (bf16[4,2,64,512]{3,0,1,2:T(4,128)(2,1)S(1)}, bf16[4,2,64,512]{3,0,1,2:T(4,128)(2,1)S(1)}, u32[]{:S(2)}, u32[]{:S(2)}) collective-permute-start(bf16[4,2,64,512]{3,0,1,2:T(4,128)(2,1)S(1)} %pad_maximum_fusion), channel_id=1, source_target_pairs={{0,48},{8,56},{16,0},{24,8},{32,16},{40,24},{48,32},{56,40},{64,11... | collective-permute-start | bytes 1572872 | tf_op jit(solution)/shard_map/ppermute | solution.py:71
  16.0 13.9 %collective-permute-start.8 = (bf16[4,2,64,512]{3,0,1,2:T(4,128)(2,1)S(1)}, bf16[4,2,64,512]{3,0,1,2:T(4,128)(2,1)S(1)}, u32[]{:S(2)}, u32[]{:S(2)}) collective-permute-start(bf16[4,2,64,512]{3,0,1,2:T(4,128)(2,1)S(1)} %pad_maximum_fusion), channel_id=1, source_target_pairs={{0,8},{8,0},{16,24},{24,16},{32,40},{40,32},{48,56},{56,48},{64,72... | collective-permute-start | bytes 1572872 | tf_op jit(solution)/shard_map/ppermute | solution.py:71
  25.7 6.4 %collective-permute-start.6 = (bf16[2,2,64,512]{3,0,1,2:T(2,128)(2,1)S(1)}, bf16[2,2,64,512]{3,0,1,2:T(2,128)(2,1)S(1)}, u32[]{:S(2)}, u32[]{:S(2)}) collective-permute-start(bf16[2,2,64,512]{3,0,1,2:T(2,128)(2,1)S(1)} %slice.72), channel_id=1, source_target_pairs={{0,16},{8,24},{16,32},{24,40},{32,48},{40,56},{48,0},{56,8},{64,80... | collective-permute-start | bytes 786440 | tf_op jit(solution)/shard_map/ppermute | solution.py:71
  27.6 7.7 %collective-permute-start.7 = (bf16[2,2,64,512]{3,0,1,2:T(2,128)(2,1)S(1)}, bf16[2,2,64,512]{3,0,1,2:T(2,128)(2,1)S(1)}, u32[]{:S(2)}, u32[]{:S(2)}) collective-permute-start(bf16[2,2,64,512]{3,0,1,2:T(2,128)(2,1)S(1)} %slice.73), channel_id=1, source_target_pairs={{0,48},{8,56},{16,0},{24,8},{32,16},{40,24},{48,32},{56,40},{64,11... | collective-permute-start | bytes 786440 | tf_op jit(solution)/shard_map/ppermute | solution.py:71
  28.2 8.7 %collective-permute-start.9 = (bf16[4,2,64,512]{3,0,1,2:T(4,128)(2,1)S(1)}, bf16[4,2,64,512]{3,0,1,2:T(4,128)(2,1)S(1)}, u32[]{:S(2)}, u32[]{:S(2)}) collective-permute-start(bf16[4,2,64,512]{3,0,1,2:T(4,128)(2,1)S(1)} %collective-permute-done.4), channel_id=1, source_target_pairs={{0,8},{8,0},{16,24},{24,16},{32,40},{40,32},{48,56},{56,48},{64,72... | collective-permute-start | bytes 1572872 | tf_op jit(solution)/shard_map/ppermute | solution.py:71
  28.2 10.2 %collective-permute-start.11 = (bf16[4,2,64,512]{3,0,1,2:T(4,128)(2,1)S(1)}, bf16[4,2,64,512]{3,0,1,2:T(4,128)(2,1)S(1)}, u32[]{:S(2)}, u32[]{:S(2)}) collective-permute-start(bf16[4,2,64,512]{3,0,1,2:T(4,128)(2,1)S(1)} %collective-permute-done.5), channel_id=1, source_target_pairs={{0,8},{8,0},{16,24},{24,16},{32,40},{40,32},{48,56},{56,48},{64,72... | collective-permute-start | bytes 1572872 | tf_op jit(solution)/shard_map/ppermute | solution.py:71
  35.8 2.0 %collective-permute-start.10 = (bf16[4,2,64,512]{3,0,1,2:T(4,128)(2,1)S(1)}, bf16[4,2,64,512]{3,0,1,2:T(4,128)(2,1)S(1)}, u32[]{:S(2)}, u32[]{:S(2)}) collective-permute-start(bf16[4,2,64,512]{3,0,1,2:T(4,128)(2,1)S(1)} %pad_maximum_fusion.1), channel_id=1, source_target_pairs={{0,8},{8,0},{16,24},{24,16},{32,40},{40,32},{48,56},{56,48},{64,72... | collective-permute-start | bytes 1572872 | tf_op jit(solution)/shard_map/ppermute | solution.py:71
  38.4 1.1 %copy-start.2 = (f32[2,64]{1,0:T(2,128)S(1)}, f32[2,64]{1,0:T(2,128)}, u32[]{:S(2)}) copy-start(f32[2,64]{1,0:T(2,128)} %param.20) | copy-start | bytes 1540
  39.5 7.4 %collective-permute-start.12 = (f32[1,2,64]{2,1,0:T(2,128)S(1)}, f32[1,2,64]{2,1,0:T(2,128)S(1)}, u32[]{:S(2)}, u32[]{:S(2)}) collective-permute-start(f32[1,2,64]{2,1,0:T(2,128)S(1)} %bitcast.222), channel_id=1, source_target_pairs={{0,1},{1,2},{2,3},{3,4},{4,5},{5,6},{6,7},{7,0},{8,9},{9,10},{10,1... | collective-permute-start | bytes 1544 | tf_op jit(solution)/shard_map/ppermute | solution.py:112
  41.4 5.5 %collective-permute-start.13 = (f32[1,2,64]{2,1,0:T(2,128)S(1)}, f32[1,2,64]{2,1,0:T(2,128)S(1)}, u32[]{:S(2)}, u32[]{:S(2)}) collective-permute-start(f32[1,2,64]{2,1,0:T(2,128)S(1)} %bitcast.223), channel_id=1, source_target_pairs={{0,7},{1,0},{2,1},{3,2},{4,3},{5,4},{6,5},{7,6},{8,15},{9,8},{10,9... | collective-permute-start | bytes 1544 | tf_op jit(solution)/shard_map/ppermute | solution.py:112
  46.9 17.3 %copy-start.3 = (bf16[2,512,512]{2,1,0:T(8,128)(2,1)S(1)}, bf16[2,512,512]{2,1,0:T(8,128)(2,1)}, u32[]{:S(2)}) copy-start(bf16[2,512,512]{2,1,0:T(8,128)(2,1)} %param.17) | copy-start | bytes 3145732
  47.0 17.3 %copy-start.5 = (f32[2,512]{1,0:T(2,128)S(1)}, f32[2,512]{1,0:T(2,128)}, u32[]{:S(2)}) copy-start(f32[2,512]{1,0:T(2,128)} %param.21) | copy-start | bytes 12292
  47.0 11.8 %collective-permute-start.14 = (f32[3,2,64]{2,1,0:T(2,128)S(1)}, f32[3,2,64]{2,1,0:T(2,128)S(1)}, u32[]{:S(2)}, u32[]{:S(2)}) collective-permute-start(f32[3,2,64]{2,1,0:T(2,128)S(1)} %constant_dynamic-update-slice_fusion), channel_id=1, source_target_pairs={{0,3},{1,4},{2,5},{3,6},{4,7},{5,0},{6,1},{7,2},{8,11},{9,12},{10,... | collective-permute-start | bytes 4616 | tf_op jit(solution)/shard_map/ppermute | solution.py:112
  58.7 5.4 %collective-permute-start.15 = (f32[3,2,64]{2,1,0:T(2,128)S(1)}, f32[3,2,64]{2,1,0:T(2,128)S(1)}, u32[]{:S(2)}, u32[]{:S(2)}) collective-permute-start(f32[3,2,64]{2,1,0:T(2,128)S(1)} %constant_dynamic-update-slice_fusion), channel_id=1, source_target_pairs={{0,5},{1,6},{2,7},{3,0},{4,1},{5,2},{6,3},{7,4},{8,13},{9,14},{10,... | collective-permute-start | bytes 4616 | tf_op jit(solution)/shard_map/ppermute | solution.py:112
  64.3 3.6 %copy-start.4 = (bf16[2,512,512]{2,1,0:T(8,128)(2,1)S(1)}, bf16[2,512,512]{2,1,0:T(8,128)(2,1)}, u32[]{:S(2)}) copy-start(bf16[2,512,512]{2,1,0:T(8,128)(2,1)} %param.18) | copy-start | bytes 3145732
  67.9 2.1 %copy-start.1 = (bf16[2,512,512]{2,1,0:T(8,128)(2,1)S(1)}, bf16[2,512,512]{2,1,0:T(8,128)(2,1)}, u32[]{:S(2)}) copy-start(bf16[2,512,512]{2,1,0:T(8,128)(2,1)} %param.16) | copy-start | bytes 3145732
  70.8 10.2 %collective-permute-start.16 = (bf16[2,512,64]{1,2,0:T(8,128)(2,1)S(1)}, bf16[2,512,64]{1,2,0:T(8,128)(2,1)S(1)}, u32[]{:S(2)}, u32[]{:S(2)}) collective-permute-start(bf16[2,512,64]{1,2,0:T(8,128)(2,1)S(1)} %get-tuple-element.7), channel_id=1, source_target_pairs={{0,1},{1,2},{2,3},{3,4},{4,5},{5,6},{6,7},{7,0},{8,9},{9,10},{10,1... | collective-permute-start | bytes 393224 | tf_op jit(solution)/shard_map/ppermute | solution.py:13
  72.1 15.0 %collective-permute-start.17 = (bf16[2,512,64]{1,2,0:T(8,128)(2,1)S(1)}, bf16[2,512,64]{1,2,0:T(8,128)(2,1)S(1)}, u32[]{:S(2)}, u32[]{:S(2)}) collective-permute-start(bf16[2,512,64]{1,2,0:T(8,128)(2,1)S(1)} %get-tuple-element.11), channel_id=1, source_target_pairs={{0,2},{1,3},{2,4},{3,5},{4,6},{5,7},{6,0},{7,1},{8,10},{9,11},{10,... | collective-permute-start | bytes 393224 | tf_op jit(solution)/shard_map/ppermute | solution.py:13
  73.4 20.0 %collective-permute-start.18 = (bf16[2,512,64]{1,2,0:T(8,128)(2,1)S(1)}, bf16[2,512,64]{1,2,0:T(8,128)(2,1)S(1)}, u32[]{:S(2)}, u32[]{:S(2)}) collective-permute-start(bf16[2,512,64]{1,2,0:T(8,128)(2,1)S(1)} %get-tuple-element.10), channel_id=1, source_target_pairs={{0,3},{1,4},{2,5},{3,6},{4,7},{5,0},{6,1},{7,2},{8,11},{9,12},{10,... | collective-permute-start | bytes 393224 | tf_op jit(solution)/shard_map/ppermute | solution.py:13
  73.6 19.7 %collective-permute-start.19 = (bf16[2,512,64]{1,2,0:T(8,128)(2,1)S(1)}, bf16[2,512,64]{1,2,0:T(8,128)(2,1)S(1)}, u32[]{:S(2)}, u32[]{:S(2)}) collective-permute-start(bf16[2,512,64]{1,2,0:T(8,128)(2,1)S(1)} %get-tuple-element.9), channel_id=1, source_target_pairs={{0,4},{1,5},{2,6},{3,7},{4,0},{5,1},{6,2},{7,3},{8,12},{9,13},{10,... | collective-permute-start | bytes 393224 | tf_op jit(solution)/shard_map/ppermute | solution.py:13
  78.8 14.5 %collective-permute-start.20 = (bf16[2,512,64]{1,2,0:T(8,128)(2,1)S(1)}, bf16[2,512,64]{1,2,0:T(8,128)(2,1)S(1)}, u32[]{:S(2)}, u32[]{:S(2)}) collective-permute-start(bf16[2,512,64]{1,2,0:T(8,128)(2,1)S(1)} %get-tuple-element.8), channel_id=1, source_target_pairs={{0,5},{1,6},{2,7},{3,0},{4,1},{5,2},{6,3},{7,4},{8,13},{9,14},{10,... | collective-permute-start | bytes 393224 | tf_op jit(solution)/shard_map/ppermute | solution.py:13
  80.9 17.9 %collective-permute-start.21 = (bf16[2,512,64]{1,2,0:T(8,128)(2,1)S(1)}, bf16[2,512,64]{1,2,0:T(8,128)(2,1)S(1)}, u32[]{:S(2)}, u32[]{:S(2)}) collective-permute-start(bf16[2,512,64]{1,2,0:T(8,128)(2,1)S(1)} %get-tuple-element.13), channel_id=1, source_target_pairs={{0,6},{1,7},{2,0},{3,1},{4,2},{5,3},{6,4},{7,5},{8,14},{9,15},{10,... | collective-permute-start | bytes 393224 | tf_op jit(solution)/shard_map/ppermute | solution.py:13
  87.1 12.4 %collective-permute-start.22 = (bf16[2,512,64]{1,2,0:T(8,128)(2,1)S(1)}, bf16[2,512,64]{1,2,0:T(8,128)(2,1)}, u32[]{:S(2)}, u32[]{:S(2)}) collective-permute-start(bf16[2,512,64]{1,2,0:T(8,128)(2,1)S(1)} %get-tuple-element.12), channel_id=1, source_target_pairs={{0,7},{1,0},{2,1},{3,2},{4,3},{5,4},{6,5},{7,6},{8,15},{9,8},{10,9... | collective-permute-start | bytes 393224 | tf_op jit(solution)/shard_map/ppermute | solution.py:13

commit v8 on v7

--- a/solution.py
+++ b/solution.py
@@ -77,6 +77,7 @@
         [move(from_left[:half_blocks], 1, 0), move(from_right[half_blocks:], -1, 0)], axis=0
     )
     x_row = jnp.stack([block_vec, from_right, far, from_left])
+    rates_seed, x_row = lax.optimization_barrier((left_rates[None], x_row))
     side_x = move(x_row, 0, 0, sibling=True)
     from_below = move(x_row, 0, 1)
     from_above = move(x_row, 0, -1)
@@ -106,7 +107,7 @@
         "ktrn,tmn->ktrm", pooled, right_factor, preferred_element_type=jnp.float32
     ).astype(jnp.bfloat16)
     left_part = lax.dynamic_slice_in_dim(left_factor, part * row_count, row_count, axis=2)
-    rates_run, pooled = lax.optimization_barrier((left_rates[None], pooled))
+    rates_run = rates_seed
 
     def shift_sub(piece, k):
         return lax.ppermute(piece, "sub", [(j, (j + k) % pieces) for j in range(pieces)])

time: 102 us -> 106 us (1.039)
  the two profiles are of different devices: /device:TPU:24 before, /device:TPU:1 now
where the time goes in v8:
time: 106 us
  starting transfers between devices  41.5 us (39%)
  waiting for transfers between devices  27.7 us (26%)
  matrix products  24.5 us (23%)
  local copies, waits for them, and re-layouts  6.9 us (7%)
  other arithmetic  4.65 us (4%)
    ppermute x7, waiting for transfers between devices, scatter_sum(): got = lax.ppermute(send, axis, [(j, (j + k) % n) for j in range(n)])  20.2 us
    ppermute x12, starting transfers between devices, move(): return lax.ppermute(piece, 'blk', pairs_list)  19.9 us
    dot_general x8, matrix products, pool(): jnp.einsum('kab,abrn->krn', w, piece, preferred_element_type=jnp.float32)  11 us
    ppermute x7, starting transfers between devices, scatter_sum(): got = lax.ppermute(send, axis, [(j, (j + k) % n) for j in range(n)])  11 us
    ppermute x4, starting transfers between devices, shift_sub(): lax.ppermute(piece, 'sub', [(j, (j + k) % pieces) for j in range(pieces)])  10.7 us
    dot_general x1, matrix products, local(): jnp.einsum('tab,ktbc->kac', left_part, right_done, preferred_element_type...  6.92 us
    ppermute x4, waiting for transfers between devices, shift_sub(): lax.ppermute(piece, 'sub', [(j, (j + k) % pieces) for j in range(pieces)])  4.89 us
    dot_general x1, matrix products, local(): jnp.einsum('jrn,jmn->jrm', dual_cols, right_dual, preferred_element_type=...  3.59 us
  transfers between devices with their start and end apart: 23, of which 8 were waited for; matrix products, arithmetic and copies ran while one was open for 16% of the time, Pallas kernels for 0%

profile of v8, /device:TPU:1, one launch (start us, length us, event | category | flops | bytes accessed | tf_op | source)
XLA Modules:
  0.0 105.8 jit_solution(12652635475202431792)
XLA Ops:
  0.0 2.0 %collective-permute-start.1 = (bf16[2,64,512]{2,1,0:T(8,128)(2,1)}, bf16[2,64,512]{2,1,0:T(8,128)(2,1)S(1)}, u32[]{:S(2)}, u32[]{:S(2)}) collective-permute-start(bf16[2,64,512]{2,1,0:T(8,128)(2,1)} %param.11), channel_id=1, source_target_pairs={{0,64},{8,72},{16,80},{24,88},{32,96},{40,104},{48,112},{56,120},{... | collective-permute-start | bytes 393224 | tf_op jit(solution)/shard_map/ppermute | solution.py:71
  2.0 1.4 %collective-permute-start = (bf16[2,64,512]{2,1,0:T(8,128)(2,1)}, bf16[2,64,512]{2,1,0:T(8,128)(2,1)S(1)}, u32[]{:S(2)}, u32[]{:S(2)}) collective-permute-start(bf16[2,64,512]{2,1,0:T(8,128)(2,1)} %param.11), channel_id=1, source_target_pairs={{0,192},{8,200},{16,208},{24,216},{32,224},{40,232},{48,240},{56,2... | collective-permute-start | bytes 393224 | tf_op jit(solution)/shard_map/ppermute | solution.py:71
  3.7 1.1 %constant_dynamic-slice_fusion = s32[32,1,2,3]{1,2,3,0:T(2,128)S(1)} fusion(s32[32,32,2,3]{1,2,3,0:T(2,128)} %param.14, s32[]{:T(128)S(6)} %select_n.109), kind=kLoop, calls=%fused_computation.67 | loop fusion | bytes 1540 | tf_op jit(solution)/shard_map/jit(dynamic_index_in_dim)/dynamic_slice | solution.py:42
  4.9 0.9 dynamic-slice_reduce_fusion
  6.3 2.4 %collective-permute-start.3 = (bf16[1,64,512]{2,1,0:T(8,128)(2,1)S(1)}, bf16[1,64,512]{2,1,0:T(8,128)(2,1)S(1)}, u32[]{:S(2)}, u32[]{:S(2)}) collective-permute-start(bf16[1,64,512]{2,1,0:T(8,128)(2,1)S(1)} %slice.69), channel_id=1, source_target_pairs={{0,192},{8,200},{16,208},{24,216},{32,224},{40,232},{48,240},{56,2... | collective-permute-start | bytes 196616 | tf_op jit(solution)/shard_map/ppermute | solution.py:71
  8.9 1.1 %copy.87 = bf16[1,2,64,512]{3,0,1,2:T(2,128)(2,1)S(1)} copy(bf16[1,2,64,512]{3,2,1,0:T(8,128)(2,1)} %bitcast.219) | data formatting | bytes 262144 | tf_op jit(solution)/shard_map/stack | solution.py:79
  10.0 0.2 copy.90
  10.2 0.2 copy.88
  10.4 2.6 %collective-permute-done.2 = bf16[1,64,512]{2,1,0:T(8,128)(2,1)S(1)} collective-permute-done((bf16[1,64,512]{2,1,0:T(8,128)(2,1)S(1)}, bf16[1,64,512]{2,1,0:T(8,128)(2,1)S(1)}, u32[]{:S(2)}, u32[]{:S(2)}) %collective-permute-start.2) | collective-permute-done | bytes 65568 | tf_op jit(solution)/shard_map/ppermute | solution.py:71
  13.3 2.0 %pad_maximum_fusion = bf16[4,2,64,512]{3,0,1,2:T(4,128)(2,1)} fusion(bf16[1,2,64,512]{3,0,1,2:T(2,128)(2,1)S(1)} %copy.90, bf16[1,2,64,512]{3,0,1,2:T(2,128)(2,1)S(1)} %copy.89, bf16[1,2,64,512]{3,0,1,2:T(2,128)(2,1)S(1)} %copy.88, bf16[1,2,64,512]{3,0,1,2:T(2,128)(2,1)S(1)} %copy.87), kind=kLoop, calls=%fused_computation.24 | loop fusion | flops 2097152 | bytes 1048576 | tf_op jit(solution)/shard_map/stack | solution.py:79
  15.3 1.8 %collective-permute-start.12 = (f32[1,2,64]{2,1,0:T(2,128)S(1)}, f32[1,2,64]{2,1,0:T(2,128)S(1)}, u32[]{:S(2)}, u32[]{:S(2)}) collective-permute-start(f32[1,2,64]{2,1,0:T(2,128)S(1)} %bitcast.222), channel_id=1, source_target_pairs={{0,1},{1,2},{2,3},{3,4},{4,5},{5,6},{6,7},{7,0},{8,9},{9,10},{10,1... | collective-permute-start | bytes 1544 | tf_op jit(solution)/shard_map/ppermute | solution.py:113
  17.1 1.3 %collective-permute-start.5 = (bf16[4,2,64,512]{3,0,1,2:T(4,128)(2,1)}, bf16[4,2,64,512]{3,0,1,2:T(4,128)(2,1)}, u32[]{:S(2)}, u32[]{:S(2)}) collective-permute-start(bf16[4,2,64,512]{3,0,1,2:T(4,128)(2,1)} %pad_maximum_fusion), channel_id=1, source_target_pairs={{0,16},{8,24},{16,32},{24,40},{32,48},{40,56},{48,0},{56,8},{64,80... | collective-permute-start | bytes 1572872 | tf_op jit(solution)/shard_map/ppermute | solution.py:71
  18.4 1.4 %collective-permute-start.4 = (bf16[4,2,64,512]{3,0,1,2:T(4,128)(2,1)}, bf16[4,2,64,512]{3,0,1,2:T(4,128)(2,1)}, u32[]{:S(2)}, u32[]{:S(2)}) collective-permute-start(bf16[4,2,64,512]{3,0,1,2:T(4,128)(2,1)} %pad_maximum_fusion), channel_id=1, source_target_pairs={{0,48},{8,56},{16,0},{24,8},{32,16},{40,24},{48,32},{56,40},{64,11... | collective-permute-start | bytes 1572872 | tf_op jit(solution)/shard_map/ppermute | solution.py:71
  19.8 4.3 %collective-permute-start.8 = (bf16[4,2,64,512]{3,0,1,2:T(4,128)(2,1)}, bf16[4,2,64,512]{3,0,1,2:T(4,128)(2,1)}, u32[]{:S(2)}, u32[]{:S(2)}) collective-permute-start(bf16[4,2,64,512]{3,0,1,2:T(4,128)(2,1)} %pad_maximum_fusion), channel_id=1, source_target_pairs={{0,8},{8,0},{16,24},{24,16},{32,40},{40,32},{48,56},{56,48},{64,72... | collective-permute-start | bytes 1572872 | tf_op jit(solution)/shard_map/ppermute | solution.py:71
  24.1 3.7 %collective-permute-start.13 = (f32[1,2,64]{2,1,0:T(2,128)S(1)}, f32[1,2,64]{2,1,0:T(2,128)S(1)}, u32[]{:S(2)}, u32[]{:S(2)}) collective-permute-start(f32[1,2,64]{2,1,0:T(2,128)S(1)} %bitcast.223), channel_id=1, source_target_pairs={{0,7},{1,0},{2,1},{3,2},{4,3},{5,4},{6,5},{7,6},{8,15},{9,8},{10,9... | collective-permute-start | bytes 1544 | tf_op jit(solution)/shard_map/ppermute | solution.py:113
  27.8 0.7 collective-permute-done.13
  28.5 5.2 %collective-permute-start.14 = (f32[3,2,64]{2,1,0:T(2,128)S(1)}, f32[3,2,64]{2,1,0:T(2,128)S(1)}, u32[]{:S(2)}, u32[]{:S(2)}) collective-permute-start(f32[3,2,64]{2,1,0:T(2,128)S(1)} %constant_dynamic-update-slice_fusion), channel_id=1, source_target_pairs={{0,3},{1,4},{2,5},{3,6},{4,7},{5,0},{6,1},{7,2},{8,11},{9,12},{10,... | collective-permute-start | bytes 4616 | tf_op jit(solution)/shard_map/ppermute | solution.py:113
  33.7 1.6 %fusion.46 = f32[16,64,512,1]{2,0,3,1:T(8,128)S(1)} fusion(bf16[4,2,64,512]{3,0,1,2:T(4,128)(2,1)} %pad_maximum_fusion, bf16[16,1,1,4,2]{0,4,3,2,1:T(2,128)(2,1)S(1)} %get-tuple-element.23), kind=kOutput, calls=%fused_computation.85 | convolution fusion | flops 8388608 | bytes 2621696 | tf_op jit(solution)/shard_map/kab,abrn->krn/dot_general | solution.py:93
  35.5 4.2 %collective-permute-done.15 = f32[3,2,64]{2,1,0:T(2,128)S(1)} collective-permute-done((f32[3,2,64]{2,1,0:T(2,128)S(1)}, f32[3,2,64]{2,1,0:T(2,128)S(1)}, u32[]{:S(2)}, u32[]{:S(2)}) %collective-permute-start.15) | collective-permute-done | bytes 1568 | tf_op jit(solution)/shard_map/ppermute | solution.py:113
  39.9 1.3 %slice.73 = bf16[2,2,64,512]{3,0,1,2:T(2,128)(2,1)S(1)} slice(bf16[4,2,64,512]{3,0,1,2:T(4,128)(2,1)} %collective-permute-done.4), slice={[2:4], [0:2], [0:64], [0:512]} | slice | bytes 524288 | tf_op jit(solution)/shard_map/slice | solution.py:88
  41.2 1.8 %collective-permute-start.7 = (bf16[2,2,64,512]{3,0,1,2:T(2,128)(2,1)S(1)}, bf16[2,2,64,512]{3,0,1,2:T(2,128)(2,1)S(1)}, u32[]{:S(2)}, u32[]{:S(2)}) collective-permute-start(bf16[2,2,64,512]{3,0,1,2:T(2,128)(2,1)S(1)} %slice.73), channel_id=1, source_target_pairs={{0,48},{8,56},{16,0},{24,8},{32,16},{40,24},{48,32},{56,40},{64,11... | collective-permute-start | bytes 786440 | tf_op jit(solution)/shard_map/ppermute | solution.py:71
  43.0 1.2 %slice.72 = bf16[2,2,64,512]{3,0,1,2:T(2,128)(2,1)S(1)} slice(bf16[4,2,64,512]{3,0,1,2:T(4,128)(2,1)} %collective-permute-done.5), slice={[0:2], [0:2], [0:64], [0:512]} | slice | bytes 524288 | tf_op jit(solution)/shard_map/slice | solution.py:88
  44.3 2.7 %collective-permute-start.11 = (bf16[4,2,64,512]{3,0,1,2:T(4,128)(2,1)}, bf16[4,2,64,512]{3,0,1,2:T(4,128)(2,1)S(1)}, u32[]{:S(2)}, u32[]{:S(2)}) collective-permute-start(bf16[4,2,64,512]{3,0,1,2:T(4,128)(2,1)} %collective-permute-done.5), channel_id=1, source_target_pairs={{0,8},{8,0},{16,24},{24,16},{32,40},{40,32},{48,56},{56,48},{64,72... | collective-permute-start | bytes 1572872 | tf_op jit(solution)/shard_map/ppermute | solution.py:71
  47.0 1.6 %fusion.40 = f32[16,64,512,1]{2,0,3,1:T(8,128)S(1)} fusion(bf16[4,2,64,512]{3,0,1,2:T(4,128)(2,1)} %collective-permute-done.5, bf16[16,1,1,4,2]{0,4,3,2,1:T(2,128)(2,1)S(1)} %get-tuple-element.20), kind=kOutput, calls=%fused_computation.79 | convolution fusion | flops 8388608 | bytes 2621696 | tf_op jit(solution)/shard_map/kab,abrn->krn/dot_general | solution.py:93
  48.6 1.7 %fusion.44 = f32[16,64,512,1]{2,0,3,1:T(8,128)S(1)} fusion(bf16[4,2,64,512]{3,0,1,2:T(4,128)(2,1)} %collective-permute-done.4, bf16[16,1,1,4,2]{0,4,3,2,1:T(2,128)(2,1)S(1)} %get-tuple-element.22), kind=kOutput, calls=%fused_computation.83 | convolution fusion | flops 8388608 | bytes 2621696 | tf_op jit(solution)/shard_map/kab,abrn->krn/dot_general | solution.py:93
  50.3 1.6 %fusion.38 = f32[16,64,512,1]{2,0,3,1:T(8,128)S(1)} fusion(bf16[4,2,64,512]{3,0,1,2:T(4,128)(2,1)} %collective-permute-done.8, bf16[16,1,1,4,2]{0,4,3,2,1:T(2,128)(2,1)S(1)} %get-tuple-element.19), kind=kOutput, calls=%fused_computation.77 | convolution fusion | flops 8388608 | bytes 2621696 | tf_op jit(solution)/shard_map/kab,abrn->krn/dot_general | solution.py:93
  52.0 0.5 pad_maximum_fusion.1
  52.5 2.4 %collective-permute-start.10 = (bf16[4,2,64,512]{3,0,1,2:T(4,128)(2,1)S(1)}, bf16[4,2,64,512]{3,0,1,2:T(4,128)(2,1)S(1)}, u32[]{:S(2)}, u32[]{:S(2)}) collective-permute-start(bf16[4,2,64,512]{3,0,1,2:T(4,128)(2,1)S(1)} %pad_maximum_fusion.1), channel_id=1, source_target_pairs={{0,8},{8,0},{16,24},{24,16},{32,40},{40,32},{48,56},{56,48},{64,72... | collective-permute-start | bytes 1572872 | tf_op jit(solution)/shard_map/ppermute | solution.py:71
  55.0 1.0 fusion.42
  55.9 0.6 fusion.36
  56.6 0.6 fusion.34
  57.2 2.3 %fusion.9 = bf16[2,8,64,512]{3,1,0,2:T(8,128)(2,1)} fusion(bf16[4,2,64,512]{3,0,1,2:T(4,128)(2,1)S(1)} %collective-permute-done.11, f32[16,64,512,1]{2,0,3,1:T(8,128)S(1)} %fusion.34, f32[16,64,512,1]{2,0,3,1:T(8,128)S(1)} %fusion.36, f32[16,64,512,1]{2,0,3,1:T(8,128)S(1)} %fusion.38, f32[16,64,512,1]{2,0,3,1:T(8,128)S(1)} %fusion.40, ...), kind=kOutput, calls=%fused_computation.17 | convolution fusion | flops 12582912 | bytes 16253184 | tf_op jit(solution)/shard_map/kab,abrn->krn/dot_general | solution.py:93
  59.4 6.9 %bitcast_convert_fusion = bf16[2,512,512]{2,1,0:T(8,128)(2,1)} fusion(bf16[8,512,512]{2,1,0:T(8,128)(2,1)} %param.12, s32[]{:T(128)S(6)} %select_n.116, bf16[8,512,512]{2,1,0:T(8,128)(2,1)} %param.13, bf16[2,8,64,512]{3,1,0,2:T(8,128)(2,1)} %fusion.9), kind=kOutput, calls=%fused_computation.2 | convolution fusion | flops 1074790400 | bytes 7340036 | tf_op jit(solution)/shard_map/tab,ktbc->kac/dot_general | solution.py:120
  66.4 3.6 %divide_convert_fusion = bf16[2,512,512]{2,1,0:T(8,128)(2,1)} fusion(bf16[2,512,512]{2,1,0:T(8,128)(2,1)S(1)} %copy-done, bf16[2,512,512]{2,1,0:T(8,128)(2,1)} %bitcast_convert_fusion, bf16[2,512,512]{2,1,0:T(8,128)(2,1)S(1)} %copy-done.3, f32[2,512]{1,0:T(2,128)S(1)} %copy-done.5, f32[2,512]{1,0:T(2,128)S(1)} %add.291), kind=kOutput, calls=%fused_computation.11 | convolution fusion | flops 1075838976 | bytes 4202496 | tf_op jit(solution)/shard_map/jrn,jmn->jrm/dot_general | solution.py:126
  70.0 2.1 %convolution_convert_fusion.1 = bf16[2,512,512]{1,2,0:T(8,128)(2,1)S(1)} fusion(bf16[2,512,512]{2,1,0:T(8,128)(2,1)} %divide_convert_fusion, bf16[2,512,512]{2,1,0:T(8,128)(2,1)S(1)} %copy-done.4), kind=kOutput, calls=%fused_computation.14 | convolution fusion | flops 537395200 | bytes 3145728 | tf_op jit(solution)/shard_map/jrm,jkm->jrk/dot_general | solution.py:128
  72.1 0.7 convolution_convert_fusion
  72.9 1.2 %collective-permute-start.22 = (bf16[2,512,64]{1,2,0:T(8,128)(2,1)S(1)}, bf16[2,512,64]{1,2,0:T(8,128)(2,1)S(1)}, u32[]{:S(2)}, u32[]{:S(2)}) collective-permute-start(bf16[2,512,64]{1,2,0:T(8,128)(2,1)S(1)} %get-tuple-element.14), channel_id=1, source_target_pairs={{0,7},{1,0},{2,1},{3,2},{4,3},{5,4},{6,5},{7,6},{8,15},{9,8},{10,9... | collective-permute-start | bytes 393224 | tf_op jit(solution)/shard_map/ppermute | solution.py:13
  74.1 0.3 collective-permute-start.21
  74.4 3.4 %collective-permute-start.20 = (bf16[2,512,64]{1,2,0:T(8,128)(2,1)S(1)}, bf16[2,512,64]{1,2,0:T(8,128)(2,1)S(1)}, u32[]{:S(2)}, u32[]{:S(2)}) collective-permute-start(bf16[2,512,64]{1,2,0:T(8,128)(2,1)S(1)} %get-tuple-element.10), channel_id=1, source_target_pairs={{0,5},{1,6},{2,7},{3,0},{4,1},{5,2},{6,3},{7,4},{8,13},{9,14},{10,... | collective-permute-start | bytes 393224 | tf_op jit(solution)/shard_map/ppermute | solution.py:13
  77.8 1.8 %collective-permute-start.19 = (bf16[2,512,64]{1,2,0:T(8,128)(2,1)S(1)}, bf16[2,512,64]{1,2,0:T(8,128)(2,1)S(1)}, u32[]{:S(2)}, u32[]{:S(2)}) collective-permute-start(bf16[2,512,64]{1,2,0:T(8,128)(2,1)S(1)} %get-tuple-element.11), channel_id=1, source_target_pairs={{0,4},{1,5},{2,6},{3,7},{4,0},{5,1},{6,2},{7,3},{8,12},{9,13},{10,... | collective-permute-start | bytes 393224 | tf_op jit(solution)/shard_map/ppermute | solution.py:13
  79.5 1.9 %collective-permute-start.18 = (bf16[2,512,64]{1,2,0:T(8,128)(2,1)S(1)}, bf16[2,512,64]{1,2,0:T(8,128)(2,1)S(1)}, u32[]{:S(2)}, u32[]{:S(2)}) collective-permute-start(bf16[2,512,64]{1,2,0:T(8,128)(2,1)S(1)} %get-tuple-element.12), channel_id=1, source_target_pairs={{0,3},{1,4},{2,5},{3,6},{4,7},{5,0},{6,1},{7,2},{8,11},{9,12},{10,... | collective-permute-start | bytes 393224 | tf_op jit(solution)/shard_map/ppermute | solution.py:13
  81.5 2.4 %collective-permute-start.17 = (bf16[2,512,64]{1,2,0:T(8,128)(2,1)S(1)}, bf16[2,512,64]{1,2,0:T(8,128)(2,1)S(1)}, u32[]{:S(2)}, u32[]{:S(2)}) collective-permute-start(bf16[2,512,64]{1,2,0:T(8,128)(2,1)S(1)} %get-tuple-element.13), channel_id=1, source_target_pairs={{0,2},{1,3},{2,4},{3,5},{4,6},{5,7},{6,0},{7,1},{8,10},{9,11},{10,... | collective-permute-start | bytes 393224 | tf_op jit(solution)/shard_map/ppermute | solution.py:13
  83.9 1.5 %collective-permute-done.21 = bf16[2,512,64]{1,2,0:T(8,128)(2,1)S(1)} collective-permute-done((bf16[2,512,64]{1,2,0:T(8,128)(2,1)S(1)}, bf16[2,512,64]{1,2,0:T(8,128)(2,1)S(1)}, u32[]{:S(2)}, u32[]{:S(2)}) %collective-permute-start.21) | collective-permute-done | bytes 131104 | tf_op jit(solution)/shard_map/ppermute | solution.py:13
  85.3 3.5 %collective-permute-done.20 = bf16[2,512,64]{1,2,0:T(8,128)(2,1)S(1)} collective-permute-done((bf16[2,512,64]{1,2,0:T(8,128)(2,1)S(1)}, bf16[2,512,64]{1,2,0:T(8,128)(2,1)S(1)}, u32[]{:S(2)}, u32[]{:S(2)}) %collective-permute-start.20) | collective-permute-done | bytes 131104 | tf_op jit(solution)/shard_map/ppermute | solution.py:13
  88.8 0.9 collective-permute-done.19
  89.7 10.0 %collective-permute-done.18 = bf16[2,512,64]{1,2,0:T(8,128)(2,1)S(1)} collective-permute-done((bf16[2,512,64]{1,2,0:T(8,128)(2,1)S(1)}, bf16[2,512,64]{1,2,0:T(8,128)(2,1)S(1)}, u32[]{:S(2)}, u32[]{:S(2)}) %collective-permute-start.18) | collective-permute-done | bytes 131104 | tf_op jit(solution)/shard_map/ppermute | solution.py:13
  99.7 4.4 %collective-permute-done.16 = bf16[2,512,64]{1,2,0:T(8,128)(2,1)} collective-permute-done((bf16[2,512,64]{1,2,0:T(8,128)(2,1)S(1)}, bf16[2,512,64]{1,2,0:T(8,128)(2,1)}, u32[]{:S(2)}, u32[]{:S(2)}) %collective-permute-start.16) | collective-permute-done | bytes 131104 | tf_op jit(solution)/shard_map/ppermute | solution.py:13
  104.0 1.7 %fusion.24 = f32[2,512,64]{1,2,0:T(8,128)} fusion(bf16[2,512,64]{1,2,0:T(8,128)(2,1)S(1)} %collective-permute-done.22, bf16[2,512,64]{1,2,0:T(8,128)(2,1)S(1)} %collective-permute-done.21, bf16[2,512,64]{1,2,0:T(8,128)(2,1)S(1)} %collective-permute-done.20, bf16[2,512,64]{1,2,0:T(8,128)(2,1)S(1)} %collective-permute-done.19, ...), kind=kLoop, calls=%fused_computation.32 | loop fusion | flops 983040 | bytes 1310724 | tf_op jit(solution)/shard_map/add | solution.py:14
  (66 shorter events, 1.7 us)
Async XLA Ops:
  0.0 66.4 %copy-start = (bf16[2,512,512]{2,1,0:T(8,128)(2,1)S(1)}, bf16[2,512,512]{2,1,0:T(8,128)(2,1)}, u32[]{:S(2)}) copy-start(bf16[2,512,512]{2,1,0:T(8,128)(2,1)} %param.19) | copy-start | bytes 3145732
  0.0 8.6 %collective-permute-start.1 = (bf16[2,64,512]{2,1,0:T(8,128)(2,1)}, bf16[2,64,512]{2,1,0:T(8,128)(2,1)S(1)}, u32[]{:S(2)}, u32[]{:S(2)}) collective-permute-start(bf16[2,64,512]{2,1,0:T(8,128)(2,1)} %param.11), channel_id=1, source_target_pairs={{0,64},{8,72},{16,80},{24,88},{32,96},{40,104},{48,112},{56,120},{... | collective-permute-start | bytes 393224 | tf_op jit(solution)/shard_map/ppermute | solution.py:71
  2.0 4.2 %collective-permute-start = (bf16[2,64,512]{2,1,0:T(8,128)(2,1)}, bf16[2,64,512]{2,1,0:T(8,128)(2,1)S(1)}, u32[]{:S(2)}, u32[]{:S(2)}) collective-permute-start(bf16[2,64,512]{2,1,0:T(8,128)(2,1)} %param.11), channel_id=1, source_target_pairs={{0,192},{8,200},{16,208},{24,216},{32,224},{40,232},{48,240},{56,2... | collective-permute-start | bytes 393224 | tf_op jit(solution)/shard_map/ppermute | solution.py:71
  4.8 10.5 %copy-start.2 = (f32[2,64]{1,0:T(2,128)S(1)}, f32[2,64]{1,0:T(2,128)}, u32[]{:S(2)}) copy-start(f32[2,64]{1,0:T(2,128)} %param.20) | copy-start | bytes 1540
  6.3 4.2 %collective-permute-start.3 = (bf16[1,64,512]{2,1,0:T(8,128)(2,1)S(1)}, bf16[1,64,512]{2,1,0:T(8,128)(2,1)S(1)}, u32[]{:S(2)}, u32[]{:S(2)}) collective-permute-start(bf16[1,64,512]{2,1,0:T(8,128)(2,1)S(1)} %slice.69), channel_id=1, source_target_pairs={{0,192},{8,200},{16,208},{24,216},{32,224},{40,232},{48,240},{56,2... | collective-permute-start | bytes 196616 | tf_op jit(solution)/shard_map/ppermute | solution.py:71
  8.7 4.4 %collective-permute-start.2 = (bf16[1,64,512]{2,1,0:T(8,128)(2,1)S(1)}, bf16[1,64,512]{2,1,0:T(8,128)(2,1)S(1)}, u32[]{:S(2)}, u32[]{:S(2)}) collective-permute-start(bf16[1,64,512]{2,1,0:T(8,128)(2,1)S(1)} %slice.68), channel_id=1, source_target_pairs={{0,64},{8,72},{16,80},{24,88},{32,96},{40,104},{48,112},{56,120},{... | collective-permute-start | bytes 196616 | tf_op jit(solution)/shard_map/ppermute | solution.py:71
  15.3 12.5 %collective-permute-start.12 = (f32[1,2,64]{2,1,0:T(2,128)S(1)}, f32[1,2,64]{2,1,0:T(2,128)S(1)}, u32[]{:S(2)}, u32[]{:S(2)}) collective-permute-start(f32[1,2,64]{2,1,0:T(2,128)S(1)} %bitcast.222), channel_id=1, source_target_pairs={{0,1},{1,2},{2,3},{3,4},{4,5},{5,6},{6,7},{7,0},{8,9},{9,10},{10,1... | collective-permute-start | bytes 1544 | tf_op jit(solution)/shard_map/ppermute | solution.py:113
  17.1 25.9 %collective-permute-start.5 = (bf16[4,2,64,512]{3,0,1,2:T(4,128)(2,1)}, bf16[4,2,64,512]{3,0,1,2:T(4,128)(2,1)}, u32[]{:S(2)}, u32[]{:S(2)}) collective-permute-start(bf16[4,2,64,512]{3,0,1,2:T(4,128)(2,1)} %pad_maximum_fusion), channel_id=1, source_target_pairs={{0,16},{8,24},{16,32},{24,40},{32,48},{40,56},{48,0},{56,8},{64,80... | collective-permute-start | bytes 1572872 | tf_op jit(solution)/shard_map/ppermute | solution.py:71
  18.4 21.5 %collective-permute-start.4 = (bf16[4,2,64,512]{3,0,1,2:T(4,128)(2,1)}, bf16[4,2,64,512]{3,0,1,2:T(4,128)(2,1)}, u32[]{:S(2)}, u32[]{:S(2)}) collective-permute-start(bf16[4,2,64,512]{3,0,1,2:T(4,128)(2,1)} %pad_maximum_fusion), channel_id=1, source_target_pairs={{0,48},{8,56},{16,0},{24,8},{32,16},{40,24},{48,32},{56,40},{64,11... | collective-permute-start | bytes 1572872 | tf_op jit(solution)/shard_map/ppermute | solution.py:71
  19.8 30.5 %collective-permute-start.8 = (bf16[4,2,64,512]{3,0,1,2:T(4,128)(2,1)}, bf16[4,2,64,512]{3,0,1,2:T(4,128)(2,1)}, u32[]{:S(2)}, u32[]{:S(2)}) collective-permute-start(bf16[4,2,64,512]{3,0,1,2:T(4,128)(2,1)} %pad_maximum_fusion), channel_id=1, source_target_pairs={{0,8},{8,0},{16,24},{24,16},{32,40},{40,32},{48,56},{56,48},{64,72... | collective-permute-start | bytes 1572872 | tf_op jit(solution)/shard_map/ppermute | solution.py:71
  24.1 4.4 %collective-permute-start.13 = (f32[1,2,64]{2,1,0:T(2,128)S(1)}, f32[1,2,64]{2,1,0:T(2,128)S(1)}, u32[]{:S(2)}, u32[]{:S(2)}) collective-permute-start(f32[1,2,64]{2,1,0:T(2,128)S(1)} %bitcast.223), channel_id=1, source_target_pairs={{0,7},{1,0},{2,1},{3,2},{4,3},{5,4},{6,5},{7,6},{8,15},{9,8},{10,9... | collective-permute-start | bytes 1544 | tf_op jit(solution)/shard_map/ppermute | solution.py:113
  28.5 6.9 %collective-permute-start.14 = (f32[3,2,64]{2,1,0:T(2,128)S(1)}, f32[3,2,64]{2,1,0:T(2,128)S(1)}, u32[]{:S(2)}, u32[]{:S(2)}) collective-permute-start(f32[3,2,64]{2,1,0:T(2,128)S(1)} %constant_dynamic-update-slice_fusion), channel_id=1, source_target_pairs={{0,3},{1,4},{2,5},{3,6},{4,7},{5,0},{6,1},{7,2},{8,11},{9,12},{10,... | collective-permute-start | bytes 4616 | tf_op jit(solution)/shard_map/ppermute | solution.py:113
  35.4 4.3 %collective-permute-start.15 = (f32[3,2,64]{2,1,0:T(2,128)S(1)}, f32[3,2,64]{2,1,0:T(2,128)S(1)}, u32[]{:S(2)}, u32[]{:S(2)}) collective-permute-start(f32[3,2,64]{2,1,0:T(2,128)S(1)} %constant_dynamic-update-slice_fusion), channel_id=1, source_target_pairs={{0,5},{1,6},{2,7},{3,0},{4,1},{5,2},{6,3},{7,4},{8,13},{9,14},{10,... | collective-permute-start | bytes 4616 | tf_op jit(solution)/shard_map/ppermute | solution.py:113
  41.2 10.8 %collective-permute-start.7 = (bf16[2,2,64,512]{3,0,1,2:T(2,128)(2,1)S(1)}, bf16[2,2,64,512]{3,0,1,2:T(2,128)(2,1)S(1)}, u32[]{:S(2)}, u32[]{:S(2)}) collective-permute-start(bf16[2,2,64,512]{3,0,1,2:T(2,128)(2,1)S(1)} %slice.73), channel_id=1, source_target_pairs={{0,48},{8,56},{16,0},{24,8},{32,16},{40,24},{48,32},{56,40},{64,11... | collective-permute-start | bytes 786440 | tf_op jit(solution)/shard_map/ppermute | solution.py:71
  44.2 7.8 %collective-permute-start.6 = (bf16[2,2,64,512]{3,0,1,2:T(2,128)(2,1)S(1)}, bf16[2,2,64,512]{3,0,1,2:T(2,128)(2,1)S(1)}, u32[]{:S(2)}, u32[]{:S(2)}) collective-permute-start(bf16[2,2,64,512]{3,0,1,2:T(2,128)(2,1)S(1)} %slice.72), channel_id=1, source_target_pairs={{0,16},{8,24},{16,32},{24,40},{32,48},{40,56},{48,0},{56,8},{64,80... | collective-permute-start | bytes 786440 | tf_op jit(solution)/shard_map/ppermute | solution.py:71
  44.3 12.9 %collective-permute-start.11 = (bf16[4,2,64,512]{3,0,1,2:T(4,128)(2,1)}, bf16[4,2,64,512]{3,0,1,2:T(4,128)(2,1)S(1)}, u32[]{:S(2)}, u32[]{:S(2)}) collective-permute-start(bf16[4,2,64,512]{3,0,1,2:T(4,128)(2,1)} %collective-permute-done.5), channel_id=1, source_target_pairs={{0,8},{8,0},{16,24},{24,16},{32,40},{40,32},{48,56},{56,48},{64,72... | collective-permute-start | bytes 1572872 | tf_op jit(solution)/shard_map/ppermute | solution.py:71
  47.0 9.0 %collective-permute-start.9 = (bf16[4,2,64,512]{3,0,1,2:T(4,128)(2,1)}, bf16[4,2,64,512]{3,0,1,2:T(4,128)(2,1)S(1)}, u32[]{:S(2)}, u32[]{:S(2)}) collective-permute-start(bf16[4,2,64,512]{3,0,1,2:T(4,128)(2,1)} %collective-permute-done.4), channel_id=1, source_target_pairs={{0,8},{8,0},{16,24},{24,16},{32,40},{40,32},{48,56},{56,48},{64,72... | collective-permute-start | bytes 1572872 | tf_op jit(solution)/shard_map/ppermute | solution.py:71
  52.5 4.0 %collective-permute-start.10 = (bf16[4,2,64,512]{3,0,1,2:T(4,128)(2,1)S(1)}, bf16[4,2,64,512]{3,0,1,2:T(4,128)(2,1)S(1)}, u32[]{:S(2)}, u32[]{:S(2)}) collective-permute-start(bf16[4,2,64,512]{3,0,1,2:T(4,128)(2,1)S(1)} %pad_maximum_fusion.1), channel_id=1, source_target_pairs={{0,8},{8,0},{16,24},{24,16},{32,40},{40,32},{48,56},{56,48},{64,72... | collective-permute-start | bytes 1572872 | tf_op jit(solution)/shard_map/ppermute | solution.py:71
  59.4 6.9 %copy-start.3 = (bf16[2,512,512]{2,1,0:T(8,128)(2,1)S(1)}, bf16[2,512,512]{2,1,0:T(8,128)(2,1)}, u32[]{:S(2)}) copy-start(bf16[2,512,512]{2,1,0:T(8,128)(2,1)} %param.17) | copy-start | bytes 3145732
  59.4 6.9 %copy-start.5 = (f32[2,512]{1,0:T(2,128)S(1)}, f32[2,512]{1,0:T(2,128)}, u32[]{:S(2)}) copy-start(f32[2,512]{1,0:T(2,128)} %param.21) | copy-start | bytes 12292
  66.4 3.6 %copy-start.4 = (bf16[2,512,512]{2,1,0:T(8,128)(2,1)S(1)}, bf16[2,512,512]{2,1,0:T(8,128)(2,1)}, u32[]{:S(2)}) copy-start(bf16[2,512,512]{2,1,0:T(8,128)(2,1)} %param.18) | copy-start | bytes 3145732
  70.0 2.1 %copy-start.1 = (bf16[2,512,512]{2,1,0:T(8,128)(2,1)S(1)}, bf16[2,512,512]{2,1,0:T(8,128)(2,1)}, u32[]{:S(2)}) copy-start(bf16[2,512,512]{2,1,0:T(8,128)(2,1)} %param.16) | copy-start | bytes 3145732
  72.9 8.6 %collective-permute-start.22 = (bf16[2,512,64]{1,2,0:T(8,128)(2,1)S(1)}, bf16[2,512,64]{1,2,0:T(8,128)(2,1)S(1)}, u32[]{:S(2)}, u32[]{:S(2)}) collective-permute-start(bf16[2,512,64]{1,2,0:T(8,128)(2,1)S(1)} %get-tuple-element.14), channel_id=1, source_target_pairs={{0,7},{1,0},{2,1},{3,2},{4,3},{5,4},{6,5},{7,6},{8,15},{9,8},{10,9... | collective-permute-start | bytes 393224 | tf_op jit(solution)/shard_map/ppermute | solution.py:13
  74.1 11.2 %collective-permute-start.21 = (bf16[2,512,64]{1,2,0:T(8,128)(2,1)S(1)}, bf16[2,512,64]{1,2,0:T(8,128)(2,1)S(1)}, u32[]{:S(2)}, u32[]{:S(2)}) collective-permute-start(bf16[2,512,64]{1,2,0:T(8,128)(2,1)S(1)} %get-tuple-element.15), channel_id=1, source_target_pairs={{0,6},{1,7},{2,0},{3,1},{4,2},{5,3},{6,4},{7,5},{8,14},{9,15},{10,... | collective-permute-start | bytes 393224 | tf_op jit(solution)/shard_map/ppermute | solution.py:13
  74.4 14.4 %collective-permute-start.20 = (bf16[2,512,64]{1,2,0:T(8,128)(2,1)S(1)}, bf16[2,512,64]{1,2,0:T(8,128)(2,1)S(1)}, u32[]{:S(2)}, u32[]{:S(2)}) collective-permute-start(bf16[2,512,64]{1,2,0:T(8,128)(2,1)S(1)} %get-tuple-element.10), channel_id=1, source_target_pairs={{0,5},{1,6},{2,7},{3,0},{4,1},{5,2},{6,3},{7,4},{8,13},{9,14},{10,... | collective-permute-start | bytes 393224 | tf_op jit(solution)/shard_map/ppermute | solution.py:13
  77.8 12.0 %collective-permute-start.19 = (bf16[2,512,64]{1,2,0:T(8,128)(2,1)S(1)}, bf16[2,512,64]{1,2,0:T(8,128)(2,1)S(1)}, u32[]{:S(2)}, u32[]{:S(2)}) collective-permute-start(bf16[2,512,64]{1,2,0:T(8,128)(2,1)S(1)} %get-tuple-element.11), channel_id=1, source_target_pairs={{0,4},{1,5},{2,6},{3,7},{4,0},{5,1},{6,2},{7,3},{8,12},{9,13},{10,... | collective-permute-start | bytes 393224 | tf_op jit(solution)/shard_map/ppermute | solution.py:13
  79.5 20.1 %collective-permute-start.18 = (bf16[2,512,64]{1,2,0:T(8,128)(2,1)S(1)}, bf16[2,512,64]{1,2,0:T(8,128)(2,1)S(1)}, u32[]{:S(2)}, u32[]{:S(2)}) collective-permute-start(bf16[2,512,64]{1,2,0:T(8,128)(2,1)S(1)} %get-tuple-element.12), channel_id=1, source_target_pairs={{0,3},{1,4},{2,5},{3,6},{4,7},{5,0},{6,1},{7,2},{8,11},{9,12},{10,... | collective-permute-start | bytes 393224 | tf_op jit(solution)/shard_map/ppermute | solution.py:13
  81.5 18.2 %collective-permute-start.17 = (bf16[2,512,64]{1,2,0:T(8,128)(2,1)S(1)}, bf16[2,512,64]{1,2,0:T(8,128)(2,1)S(1)}, u32[]{:S(2)}, u32[]{:S(2)}) collective-permute-start(bf16[2,512,64]{1,2,0:T(8,128)(2,1)S(1)} %get-tuple-element.13), channel_id=1, source_target_pairs={{0,2},{1,3},{2,4},{3,5},{4,6},{5,7},{6,0},{7,1},{8,10},{9,11},{10,... | collective-permute-start | bytes 393224 | tf_op jit(solution)/shard_map/ppermute | solution.py:13
  85.3 18.7 %collective-permute-start.16 = (bf16[2,512,64]{1,2,0:T(8,128)(2,1)S(1)}, bf16[2,512,64]{1,2,0:T(8,128)(2,1)}, u32[]{:S(2)}, u32[]{:S(2)}) collective-permute-start(bf16[2,512,64]{1,2,0:T(8,128)(2,1)S(1)} %get-tuple-element.9), channel_id=1, source_target_pairs={{0,1},{1,2},{2,3},{3,4},{4,5},{5,6},{6,7},{7,0},{8,9},{9,10},{10,1... | collective-permute-start | bytes 393224 | tf_op jit(solution)/shard_map/ppermute | solution.py:13

commit v9 on v7

--- a/solution.py
+++ b/solution.py
@@ -106,7 +106,7 @@
         "ktrn,tmn->ktrm", pooled, right_factor, preferred_element_type=jnp.float32
     ).astype(jnp.bfloat16)
     left_part = lax.dynamic_slice_in_dim(left_factor, part * row_count, row_count, axis=2)
-    rates_run, pooled = lax.optimization_barrier((left_rates[None], pooled))
+    rates_run = left_rates[None]
 
     def shift_sub(piece, k):
         return lax.ppermute(piece, "sub", [(j, (j + k) % pieces) for j in range(pieces)])

time: 102 us -> 104 us (1.020)
  waiting for transfers between devices: 38.8 us -> 35.8 us
  starting transfers between devices: 34.6 us -> 36.6 us
  local copies, waits for them, and re-layouts: 4.81 us -> 6.16 us
    ppermute x4, waiting for transfers between devices: 6.76 us -> 3.62 us  [shift_sub(): lax.ppermute(piece, 'sub', [(j, (j + k) % pieces) for j in range(pieces)])]
    ppermute x7, starting transfers between devices: 11.9 us -> 13.9 us  [scatter_sum(): got = lax.ppermute(send, axis, [(j, (j + k) % n) for j in range(n)])]
    unnamed x23 -> x19, local copies, waits for them, and re-layouts: 0.11 us -> 1.44 us
  transfers between devices with their start and end apart: 23 -> 23, of which waited for: 12 -> 12; matrix products, arithmetic and copies ran while one was open for 16% -> 12% of each run, Pallas kernels for 0% -> 0%
where the time goes in v9:
time: 104 us; the launch traced here: 103 us
  starting transfers between devices  36.6 us (35%)
  waiting for transfers between devices  35.8 us (34%)
  matrix products  19.2 us (18%)
  local copies, waits for them, and re-layouts  6.16 us (6%)
  other arithmetic  4.54 us (4%)
    ppermute x7, waiting for transfers between devices, scatter_sum(): got = lax.ppermute(send, axis, [(j, (j + k) % n) for j in range(n)])  17.6 us
    ppermute x12, waiting for transfers between devices, move(): return lax.ppermute(piece, 'blk', pairs_list)  14.5 us
    ppermute x7, starting transfers between devices, scatter_sum(): got = lax.ppermute(send, axis, [(j, (j + k) % n) for j in range(n)])  13.9 us
    ppermute x12, starting transfers between devices, move(): return lax.ppermute(piece, 'blk', pairs_list)  11.7 us
    ppermute x4, starting transfers between devices, shift_sub(): lax.ppermute(piece, 'sub', [(j, (j + k) % pieces) for j in range(pieces)])  11 us
    dot_general x1, matrix products, local(): jnp.einsum('tab,ktbc->kac', left_part, right_done, preferred_element_type...  6.77 us
    dot_general x8, matrix products, pool(): jnp.einsum('kab,abrn->krn', w, piece, preferred_element_type=jnp.float32)  5.86 us
    ppermute x4, waiting for transfers between devices, shift_sub(): lax.ppermute(piece, 'sub', [(j, (j + k) % pieces) for j in range(pieces)])  3.62 us
  transfers between devices with their start and end apart: 23, of which 12 were waited for; matrix products, arithmetic and copies ran while one was open for 12% of the time, Pallas kernels for 0%

profile of v9, /device:TPU:24, one launch (start us, length us, event | category | flops | bytes accessed | tf_op | source)
XLA Modules:
  0.0 102.6 jit_solution(11658215865870079148)
XLA Ops:
  0.0 1.5 %collective-permute-start.1 = (bf16[2,64,512]{2,1,0:T(8,128)(2,1)}, bf16[2,64,512]{2,1,0:T(8,128)(2,1)S(1)}, u32[]{:S(2)}, u32[]{:S(2)}) collective-permute-start(bf16[2,64,512]{2,1,0:T(8,128)(2,1)} %param.11), channel_id=1, source_target_pairs={{0,64},{8,72},{16,80},{24,88},{32,96},{40,104},{48,112},{56,120},{... | collective-permute-start | bytes 393224 | tf_op jit(solution)/shard_map/ppermute | solution.py:71
  1.5 1.7 %collective-permute-start = (bf16[2,64,512]{2,1,0:T(8,128)(2,1)}, bf16[2,64,512]{2,1,0:T(8,128)(2,1)S(1)}, u32[]{:S(2)}, u32[]{:S(2)}) collective-permute-start(bf16[2,64,512]{2,1,0:T(8,128)(2,1)} %param.11), channel_id=1, source_target_pairs={{0,192},{8,200},{16,208},{24,216},{32,224},{40,232},{48,240},{56,2... | collective-permute-start | bytes 393224 | tf_op jit(solution)/shard_map/ppermute | solution.py:71
  3.2 1.9 %collective-permute-start.12 = (f32[1,2,64]{2,1,0:T(2,128)}, f32[1,2,64]{2,1,0:T(2,128)S(1)}, u32[]{:S(2)}, u32[]{:S(2)}) collective-permute-start(f32[1,2,64]{2,1,0:T(2,128)} %bitcast.224), channel_id=1, source_target_pairs={{0,1},{1,2},{2,3},{3,4},{4,5},{5,6},{6,7},{7,0},{8,9},{9,10},{10,1... | collective-permute-start | bytes 1544 | tf_op jit(solution)/shard_map/ppermute | solution.py:112
  5.2 3.9 %collective-permute-start.13 = (f32[1,2,64]{2,1,0:T(2,128)}, f32[1,2,64]{2,1,0:T(2,128)S(1)}, u32[]{:S(2)}, u32[]{:S(2)}) collective-permute-start(f32[1,2,64]{2,1,0:T(2,128)} %bitcast.225), channel_id=1, source_target_pairs={{0,7},{1,0},{2,1},{3,2},{4,3},{5,4},{6,5},{7,6},{8,15},{9,8},{10,9... | collective-permute-start | bytes 1544 | tf_op jit(solution)/shard_map/ppermute | solution.py:112
  9.5 1.1 %constant_dynamic-slice_fusion = s32[32,1,2,3]{1,2,3,0:T(2,128)S(1)} fusion(s32[32,32,2,3]{1,2,3,0:T(2,128)} %param.14, s32[]{:T(128)S(6)} %select_n.109), kind=kLoop, calls=%fused_computation.65 | loop fusion | bytes 1540 | tf_op jit(solution)/shard_map/jit(dynamic_index_in_dim)/dynamic_slice | solution.py:42
  10.7 0.9 dynamic-slice_reduce_fusion
  12.0 0.7 pad_maximum_fusion.2
  12.7 4.0 %collective-permute-start.14 = (f32[3,2,64]{2,1,0:T(2,128)S(1)}, f32[3,2,64]{2,1,0:T(2,128)S(1)}, u32[]{:S(2)}, u32[]{:S(2)}) collective-permute-start(f32[3,2,64]{2,1,0:T(2,128)S(1)} %pad_maximum_fusion.2), channel_id=1, source_target_pairs={{0,3},{1,4},{2,5},{3,6},{4,7},{5,0},{6,1},{7,2},{8,11},{9,12},{10,... | collective-permute-start | bytes 4616 | tf_op jit(solution)/shard_map/ppermute | solution.py:112
  16.7 1.1 %copy.87 = bf16[1,2,64,512]{3,0,1,2:T(2,128)(2,1)S(1)} copy(bf16[1,2,64,512]{3,2,1,0:T(8,128)(2,1)} %bitcast.221) | data formatting | bytes 262144 | tf_op jit(solution)/shard_map/stack | solution.py:79
  17.8 1.1 %collective-permute-start.15 = (f32[3,2,64]{2,1,0:T(2,128)S(1)}, f32[3,2,64]{2,1,0:T(2,128)S(1)}, u32[]{:S(2)}, u32[]{:S(2)}) collective-permute-start(f32[3,2,64]{2,1,0:T(2,128)S(1)} %pad_maximum_fusion.2), channel_id=1, source_target_pairs={{0,5},{1,6},{2,7},{3,0},{4,1},{5,2},{6,3},{7,4},{8,13},{9,14},{10,... | collective-permute-start | bytes 4616 | tf_op jit(solution)/shard_map/ppermute | solution.py:112
  19.3 0.7 constant_dynamic-update-slice_fusion.7
  20.0 3.3 %collective-permute-done.15 = f32[3,2,64]{2,1,0:T(2,128)S(1)} collective-permute-done((f32[3,2,64]{2,1,0:T(2,128)S(1)}, f32[3,2,64]{2,1,0:T(2,128)S(1)}, u32[]{:S(2)}, u32[]{:S(2)}) %collective-permute-start.15) | collective-permute-done | bytes 1568 | tf_op jit(solution)/shard_map/ppermute | solution.py:112
  23.3 0.7 constant_dynamic-update-slice_fusion.2
  24.4 3.0 %collective-permute-start.3 = (bf16[1,64,512]{2,1,0:T(8,128)(2,1)S(1)}, bf16[1,64,512]{2,1,0:T(8,128)(2,1)S(1)}, u32[]{:S(2)}, u32[]{:S(2)}) collective-permute-start(bf16[1,64,512]{2,1,0:T(8,128)(2,1)S(1)} %slice.69), channel_id=1, source_target_pairs={{0,192},{8,200},{16,208},{24,216},{32,224},{40,232},{48,240},{56,2... | collective-permute-start | bytes 196616 | tf_op jit(solution)/shard_map/ppermute | solution.py:71
  27.9 1.7 %collective-permute-done.2 = bf16[1,64,512]{2,1,0:T(8,128)(2,1)S(1)} collective-permute-done((bf16[1,64,512]{2,1,0:T(8,128)(2,1)S(1)}, bf16[1,64,512]{2,1,0:T(8,128)(2,1)S(1)}, u32[]{:S(2)}, u32[]{:S(2)}) %collective-permute-start.2) | collective-permute-done | bytes 65568 | tf_op jit(solution)/shard_map/ppermute | solution.py:71
  29.8 1.2 %pad_maximum_fusion = bf16[4,2,64,512]{3,0,1,2:T(4,128)(2,1)S(1)} fusion(bf16[1,2,64,512]{3,0,1,2:T(2,128)(2,1)S(1)} %copy.90, bf16[1,2,64,512]{3,0,1,2:T(2,128)(2,1)S(1)} %copy.89, bf16[1,2,64,512]{3,0,1,2:T(2,128)(2,1)S(1)} %copy.88, bf16[1,2,64,512]{3,0,1,2:T(2,128)(2,1)S(1)} %copy.87), kind=kLoop, calls=%fused_computation.24 | loop fusion | flops 2097152 | bytes 1048576 | tf_op jit(solution)/shard_map/stack | solution.py:79
  31.3 1.8 %collective-permute-start.4 = (bf16[4,2,64,512]{3,0,1,2:T(4,128)(2,1)S(1)}, bf16[4,2,64,512]{3,0,1,2:T(4,128)(2,1)S(1)}, u32[]{:S(2)}, u32[]{:S(2)}) collective-permute-start(bf16[4,2,64,512]{3,0,1,2:T(4,128)(2,1)S(1)} %pad_maximum_fusion), channel_id=1, source_target_pairs={{0,48},{8,56},{16,0},{24,8},{32,16},{40,24},{48,32},{56,40},{64,11... | collective-permute-start | bytes 1572872 | tf_op jit(solution)/shard_map/ppermute | solution.py:71
  33.3 0.6 fusion.46
  33.9 9.2 %collective-permute-done.5 = bf16[4,2,64,512]{3,0,1,2:T(4,128)(2,1)S(1)} collective-permute-done((bf16[4,2,64,512]{3,0,1,2:T(4,128)(2,1)S(1)}, bf16[4,2,64,512]{3,0,1,2:T(4,128)(2,1)S(1)}, u32[]{:S(2)}, u32[]{:S(2)}) %collective-permute-start.5) | collective-permute-done | bytes 524320 | tf_op jit(solution)/shard_map/ppermute | solution.py:71
  43.3 0.4 collective-permute-start.6
  44.0 1.9 %collective-permute-start.7 = (bf16[2,2,64,512]{3,0,1,2:T(2,128)(2,1)S(1)}, bf16[2,2,64,512]{3,0,1,2:T(2,128)(2,1)S(1)}, u32[]{:S(2)}, u32[]{:S(2)}) collective-permute-start(bf16[2,2,64,512]{3,0,1,2:T(2,128)(2,1)S(1)} %slice.73), channel_id=1, source_target_pairs={{0,48},{8,56},{16,0},{24,8},{32,16},{40,24},{48,32},{56,40},{64,11... | collective-permute-start | bytes 786440 | tf_op jit(solution)/shard_map/ppermute | solution.py:71
  45.9 0.5 collective-permute-start.11
  46.4 0.6 fusion.40
  47.1 0.6 fusion.44
  47.7 0.6 fusion.38
  48.3 1.6 %collective-permute-done.6 = bf16[2,2,64,512]{3,0,1,2:T(2,128)(2,1)S(1)} collective-permute-done((bf16[2,2,64,512]{3,0,1,2:T(2,128)(2,1)S(1)}, bf16[2,2,64,512]{3,0,1,2:T(2,128)(2,1)S(1)}, u32[]{:S(2)}, u32[]{:S(2)}) %collective-permute-start.6) | collective-permute-done | bytes 262176 | tf_op jit(solution)/shard_map/ppermute | solution.py:71
  49.9 1.7 %collective-permute-done.7 = bf16[2,2,64,512]{3,0,1,2:T(2,128)(2,1)S(1)} collective-permute-done((bf16[2,2,64,512]{3,0,1,2:T(2,128)(2,1)S(1)}, bf16[2,2,64,512]{3,0,1,2:T(2,128)(2,1)S(1)}, u32[]{:S(2)}, u32[]{:S(2)}) %collective-permute-start.7) | collective-permute-done | bytes 262176 | tf_op jit(solution)/shard_map/ppermute | solution.py:71
  51.6 0.5 pad_maximum_fusion.1
  52.3 1.0 fusion.42
  53.3 0.6 fusion.36
  54.2 0.6 fusion.34
  54.8 1.2 %fusion.9 = bf16[2,8,64,512]{3,1,0,2:T(8,128)(2,1)S(1)} fusion(bf16[4,2,64,512]{3,0,1,2:T(4,128)(2,1)S(1)} %collective-permute-done.11, f32[16,64,512,1]{2,0,3,1:T(8,128)S(1)} %fusion.34, f32[16,64,512,1]{2,0,3,1:T(8,128)S(1)} %fusion.36, f32[16,64,512,1]{2,0,3,1:T(8,128)S(1)} %fusion.38, f32[16,64,512,1]{2,0,3,1:T(8,128)S(1)} %fusion.40, ...), kind=kOutput, calls=%fused_computation.17 | convolution fusion | flops 12582912 | bytes 16253184 | tf_op jit(solution)/shard_map/kab,abrn->krn/dot_general | solution.py:92
  56.0 6.8 %bitcast_convert_fusion = bf16[2,512,512]{2,1,0:T(8,128)(2,1)} fusion(bf16[8,512,512]{2,1,0:T(8,128)(2,1)} %param.12, s32[]{:T(128)S(6)} %select_n.116, bf16[8,512,512]{2,1,0:T(8,128)(2,1)} %param.13, bf16[2,8,64,512]{3,1,0,2:T(8,128)(2,1)S(1)} %fusion.9), kind=kOutput, calls=%fused_computation.2 | convolution fusion | flops 1074790400 | bytes 7340036 | tf_op jit(solution)/shard_map/tab,ktbc->kac/dot_general | solution.py:119
  62.8 3.6 %divide_convert_fusion = bf16[2,512,512]{2,1,0:T(8,128)(2,1)} fusion(bf16[2,512,512]{2,1,0:T(8,128)(2,1)S(1)} %copy-done, bf16[2,512,512]{2,1,0:T(8,128)(2,1)} %bitcast_convert_fusion, bf16[2,512,512]{2,1,0:T(8,128)(2,1)S(1)} %copy-done.2, f32[2,512]{1,0:T(2,128)S(1)} %copy-done.4, f32[2,512]{1,0:T(2,128)S(1)} %add.291), kind=kOutput, calls=%fused_computation.11 | convolution fusion | flops 1075838976 | bytes 4202496 | tf_op jit(solution)/shard_map/jrn,jmn->jrm/dot_general | solution.py:125
  66.4 2.0 %convolution_convert_fusion.1 = bf16[2,512,512]{1,2,0:T(8,128)(2,1)S(1)} fusion(bf16[2,512,512]{2,1,0:T(8,128)(2,1)} %divide_convert_fusion, bf16[2,512,512]{2,1,0:T(8,128)(2,1)S(1)} %copy-done.3), kind=kOutput, calls=%fused_computation.14 | convolution fusion | flops 537395200 | bytes 3145728 | tf_op jit(solution)/shard_map/jrm,jkm->jrk/dot_general | solution.py:127
  68.5 0.7 convolution_convert_fusion
  69.3 2.2 %collective-permute-start.16 = (bf16[2,512,64]{1,2,0:T(8,128)(2,1)S(1)}, bf16[2,512,64]{1,2,0:T(8,128)(2,1)S(1)}, u32[]{:S(2)}, u32[]{:S(2)}) collective-permute-start(bf16[2,512,64]{1,2,0:T(8,128)(2,1)S(1)} %get-tuple-element.5), channel_id=1, source_target_pairs={{0,1},{1,2},{2,3},{3,4},{4,5},{5,6},{6,7},{7,0},{8,9},{9,10},{10,1... | collective-permute-start | bytes 393224 | tf_op jit(solution)/shard_map/ppermute | solution.py:13
  71.8 1.2 %collective-permute-start.18 = (bf16[2,512,64]{1,2,0:T(8,128)(2,1)S(1)}, bf16[2,512,64]{1,2,0:T(8,128)(2,1)S(1)}, u32[]{:S(2)}, u32[]{:S(2)}) collective-permute-start(bf16[2,512,64]{1,2,0:T(8,128)(2,1)S(1)} %get-tuple-element.8), channel_id=1, source_target_pairs={{0,3},{1,4},{2,5},{3,6},{4,7},{5,0},{6,1},{7,2},{8,11},{9,12},{10,... | collective-permute-start | bytes 393224 | tf_op jit(solution)/shard_map/ppermute | solution.py:13
  73.0 4.6 %collective-permute-start.19 = (bf16[2,512,64]{1,2,0:T(8,128)(2,1)S(1)}, bf16[2,512,64]{1,2,0:T(8,128)(2,1)S(1)}, u32[]{:S(2)}, u32[]{:S(2)}) collective-permute-start(bf16[2,512,64]{1,2,0:T(8,128)(2,1)S(1)} %get-tuple-element.7), channel_id=1, source_target_pairs={{0,4},{1,5},{2,6},{3,7},{4,0},{5,1},{6,2},{7,3},{8,12},{9,13},{10,... | collective-permute-start | bytes 393224 | tf_op jit(solution)/shard_map/ppermute | solution.py:13
  77.5 1.7 %collective-permute-start.20 = (bf16[2,512,64]{1,2,0:T(8,128)(2,1)S(1)}, bf16[2,512,64]{1,2,0:T(8,128)(2,1)S(1)}, u32[]{:S(2)}, u32[]{:S(2)}) collective-permute-start(bf16[2,512,64]{1,2,0:T(8,128)(2,1)S(1)} %get-tuple-element.6), channel_id=1, source_target_pairs={{0,5},{1,6},{2,7},{3,0},{4,1},{5,2},{6,3},{7,4},{8,13},{9,14},{10,... | collective-permute-start | bytes 393224 | tf_op jit(solution)/shard_map/ppermute | solution.py:13
  79.2 2.8 %collective-permute-start.21 = (bf16[2,512,64]{1,2,0:T(8,128)(2,1)S(1)}, bf16[2,512,64]{1,2,0:T(8,128)(2,1)S(1)}, u32[]{:S(2)}, u32[]{:S(2)}) collective-permute-start(bf16[2,512,64]{1,2,0:T(8,128)(2,1)S(1)} %get-tuple-element.11), channel_id=1, source_target_pairs={{0,6},{1,7},{2,0},{3,1},{4,2},{5,3},{6,4},{7,5},{8,14},{9,15},{10,... | collective-permute-start | bytes 393224 | tf_op jit(solution)/shard_map/ppermute | solution.py:13
  82.1 1.2 %collective-permute-done.17 = bf16[2,512,64]{1,2,0:T(8,128)(2,1)S(1)} collective-permute-done((bf16[2,512,64]{1,2,0:T(8,128)(2,1)S(1)}, bf16[2,512,64]{1,2,0:T(8,128)(2,1)S(1)}, u32[]{:S(2)}, u32[]{:S(2)}) %collective-permute-start.17) | collective-permute-done | bytes 131104 | tf_op jit(solution)/shard_map/ppermute | solution.py:13
  83.3 1.2 %collective-permute-start.22 = (bf16[2,512,64]{1,2,0:T(8,128)(2,1)S(1)}, bf16[2,512,64]{1,2,0:T(8,128)(2,1)}, u32[]{:S(2)}, u32[]{:S(2)}) collective-permute-start(bf16[2,512,64]{1,2,0:T(8,128)(2,1)S(1)} %get-tuple-element.10), channel_id=1, source_target_pairs={{0,7},{1,0},{2,1},{3,2},{4,3},{5,4},{6,5},{7,6},{8,15},{9,8},{10,9... | collective-permute-start | bytes 393224 | tf_op jit(solution)/shard_map/ppermute | solution.py:13
  84.5 6.8 %collective-permute-done.18 = bf16[2,512,64]{1,2,0:T(8,128)(2,1)S(1)} collective-permute-done((bf16[2,512,64]{1,2,0:T(8,128)(2,1)S(1)}, bf16[2,512,64]{1,2,0:T(8,128)(2,1)S(1)}, u32[]{:S(2)}, u32[]{:S(2)}) %collective-permute-start.18) | collective-permute-done | bytes 131104 | tf_op jit(solution)/shard_map/ppermute | solution.py:13
  91.3 3.5 %collective-permute-done.19 = bf16[2,512,64]{1,2,0:T(8,128)(2,1)S(1)} collective-permute-done((bf16[2,512,64]{1,2,0:T(8,128)(2,1)S(1)}, bf16[2,512,64]{1,2,0:T(8,128)(2,1)S(1)}, u32[]{:S(2)}, u32[]{:S(2)}) %collective-permute-start.19) | collective-permute-done | bytes 131104 | tf_op jit(solution)/shard_map/ppermute | solution.py:13
  94.7 5.5 %collective-permute-done.21 = bf16[2,512,64]{1,2,0:T(8,128)(2,1)S(1)} collective-permute-done((bf16[2,512,64]{1,2,0:T(8,128)(2,1)S(1)}, bf16[2,512,64]{1,2,0:T(8,128)(2,1)S(1)}, u32[]{:S(2)}, u32[]{:S(2)}) %collective-permute-start.21) | collective-permute-done | bytes 131104 | tf_op jit(solution)/shard_map/ppermute | solution.py:13
  100.2 0.6 collective-permute-done.22
  100.9 1.7 %fusion.24 = f32[2,512,64]{1,2,0:T(8,128)} fusion(bf16[2,512,64]{1,2,0:T(8,128)(2,1)} %collective-permute-done.22, bf16[2,512,64]{1,2,0:T(8,128)(2,1)S(1)} %collective-permute-done.21, bf16[2,512,64]{1,2,0:T(8,128)(2,1)S(1)} %collective-permute-done.20, bf16[2,512,64]{1,2,0:T(8,128)(2,1)S(1)} %collective-permute-done.19, ...), kind=kLoop, calls=%fused_computation.32 | loop fusion | flops 983040 | bytes 1310724 | tf_op jit(solution)/shard_map/add | solution.py:14
  (62 shorter events, 3.9 us)
Async XLA Ops:
  0.0 62.8 %copy-start = (bf16[2,512,512]{2,1,0:T(8,128)(2,1)S(1)}, bf16[2,512,512]{2,1,0:T(8,128)(2,1)}, u32[]{:S(2)}) copy-start(bf16[2,512,512]{2,1,0:T(8,128)(2,1)} %param.19) | copy-start | bytes 3145732
  0.0 24.0 %collective-permute-start.1 = (bf16[2,64,512]{2,1,0:T(8,128)(2,1)}, bf16[2,64,512]{2,1,0:T(8,128)(2,1)S(1)}, u32[]{:S(2)}, u32[]{:S(2)}) collective-permute-start(bf16[2,64,512]{2,1,0:T(8,128)(2,1)} %param.11), channel_id=1, source_target_pairs={{0,64},{8,72},{16,80},{24,88},{32,96},{40,104},{48,112},{56,120},{... | collective-permute-start | bytes 393224 | tf_op jit(solution)/shard_map/ppermute | solution.py:71
  1.5 22.9 %collective-permute-start = (bf16[2,64,512]{2,1,0:T(8,128)(2,1)}, bf16[2,64,512]{2,1,0:T(8,128)(2,1)S(1)}, u32[]{:S(2)}, u32[]{:S(2)}) collective-permute-start(bf16[2,64,512]{2,1,0:T(8,128)(2,1)} %param.11), channel_id=1, source_target_pairs={{0,192},{8,200},{16,208},{24,216},{32,224},{40,232},{48,240},{56,2... | collective-permute-start | bytes 393224 | tf_op jit(solution)/shard_map/ppermute | solution.py:71
  3.2 8.8 %collective-permute-start.12 = (f32[1,2,64]{2,1,0:T(2,128)}, f32[1,2,64]{2,1,0:T(2,128)S(1)}, u32[]{:S(2)}, u32[]{:S(2)}) collective-permute-start(f32[1,2,64]{2,1,0:T(2,128)} %bitcast.224), channel_id=1, source_target_pairs={{0,1},{1,2},{2,3},{3,4},{4,5},{5,6},{6,7},{7,0},{8,9},{9,10},{10,1... | collective-permute-start | bytes 1544 | tf_op jit(solution)/shard_map/ppermute | solution.py:112
  5.2 6.9 %collective-permute-start.13 = (f32[1,2,64]{2,1,0:T(2,128)}, f32[1,2,64]{2,1,0:T(2,128)S(1)}, u32[]{:S(2)}, u32[]{:S(2)}) collective-permute-start(f32[1,2,64]{2,1,0:T(2,128)} %bitcast.225), channel_id=1, source_target_pairs={{0,7},{1,0},{2,1},{3,2},{4,3},{5,4},{6,5},{7,6},{8,15},{9,8},{10,9... | collective-permute-start | bytes 1544 | tf_op jit(solution)/shard_map/ppermute | solution.py:112
  12.7 6.6 %collective-permute-start.14 = (f32[3,2,64]{2,1,0:T(2,128)S(1)}, f32[3,2,64]{2,1,0:T(2,128)S(1)}, u32[]{:S(2)}, u32[]{:S(2)}) collective-permute-start(f32[3,2,64]{2,1,0:T(2,128)S(1)} %pad_maximum_fusion.2), channel_id=1, source_target_pairs={{0,3},{1,4},{2,5},{3,6},{4,7},{5,0},{6,1},{7,2},{8,11},{9,12},{10,... | collective-permute-start | bytes 4616 | tf_op jit(solution)/shard_map/ppermute | solution.py:112
  17.8 5.5 %collective-permute-start.15 = (f32[3,2,64]{2,1,0:T(2,128)S(1)}, f32[3,2,64]{2,1,0:T(2,128)S(1)}, u32[]{:S(2)}, u32[]{:S(2)}) collective-permute-start(f32[3,2,64]{2,1,0:T(2,128)S(1)} %pad_maximum_fusion.2), channel_id=1, source_target_pairs={{0,5},{1,6},{2,7},{3,0},{4,1},{5,2},{6,3},{7,4},{8,13},{9,14},{10,... | collective-permute-start | bytes 4616 | tf_op jit(solution)/shard_map/ppermute | solution.py:112
  24.0 5.6 %collective-permute-start.2 = (bf16[1,64,512]{2,1,0:T(8,128)(2,1)S(1)}, bf16[1,64,512]{2,1,0:T(8,128)(2,1)S(1)}, u32[]{:S(2)}, u32[]{:S(2)}) collective-permute-start(bf16[1,64,512]{2,1,0:T(8,128)(2,1)S(1)} %slice.68), channel_id=1, source_target_pairs={{0,64},{8,72},{16,80},{24,88},{32,96},{40,104},{48,112},{56,120},{... | collective-permute-start | bytes 196616 | tf_op jit(solution)/shard_map/ppermute | solution.py:71
  24.4 5.2 %collective-permute-start.3 = (bf16[1,64,512]{2,1,0:T(8,128)(2,1)S(1)}, bf16[1,64,512]{2,1,0:T(8,128)(2,1)S(1)}, u32[]{:S(2)}, u32[]{:S(2)}) collective-permute-start(bf16[1,64,512]{2,1,0:T(8,128)(2,1)S(1)} %slice.69), channel_id=1, source_target_pairs={{0,192},{8,200},{16,208},{24,216},{32,224},{40,232},{48,240},{56,2... | collective-permute-start | bytes 196616 | tf_op jit(solution)/shard_map/ppermute | solution.py:71
  31.0 12.0 %collective-permute-start.5 = (bf16[4,2,64,512]{3,0,1,2:T(4,128)(2,1)S(1)}, bf16[4,2,64,512]{3,0,1,2:T(4,128)(2,1)S(1)}, u32[]{:S(2)}, u32[]{:S(2)}) collective-permute-start(bf16[4,2,64,512]{3,0,1,2:T(4,128)(2,1)S(1)} %pad_maximum_fusion), channel_id=1, source_target_pairs={{0,16},{8,24},{16,32},{24,40},{32,48},{40,56},{48,0},{56,8},{64,80... | collective-permute-start | bytes 1572872 | tf_op jit(solution)/shard_map/ppermute | solution.py:71
  31.3 12.3 %collective-permute-start.4 = (bf16[4,2,64,512]{3,0,1,2:T(4,128)(2,1)S(1)}, bf16[4,2,64,512]{3,0,1,2:T(4,128)(2,1)S(1)}, u32[]{:S(2)}, u32[]{:S(2)}) collective-permute-start(bf16[4,2,64,512]{3,0,1,2:T(4,128)(2,1)S(1)} %pad_maximum_fusion), channel_id=1, source_target_pairs={{0,48},{8,56},{16,0},{24,8},{32,16},{40,24},{48,32},{56,40},{64,11... | collective-permute-start | bytes 1572872 | tf_op jit(solution)/shard_map/ppermute | solution.py:71
  33.2 14.4 %collective-permute-start.8 = (bf16[4,2,64,512]{3,0,1,2:T(4,128)(2,1)S(1)}, bf16[4,2,64,512]{3,0,1,2:T(4,128)(2,1)S(1)}, u32[]{:S(2)}, u32[]{:S(2)}) collective-permute-start(bf16[4,2,64,512]{3,0,1,2:T(4,128)(2,1)S(1)} %pad_maximum_fusion), channel_id=1, source_target_pairs={{0,8},{8,0},{16,24},{24,16},{32,40},{40,32},{48,56},{56,48},{64,72... | collective-permute-start | bytes 1572872 | tf_op jit(solution)/shard_map/ppermute | solution.py:71
  43.3 6.6 %collective-permute-start.6 = (bf16[2,2,64,512]{3,0,1,2:T(2,128)(2,1)S(1)}, bf16[2,2,64,512]{3,0,1,2:T(2,128)(2,1)S(1)}, u32[]{:S(2)}, u32[]{:S(2)}) collective-permute-start(bf16[2,2,64,512]{3,0,1,2:T(2,128)(2,1)S(1)} %slice.72), channel_id=1, source_target_pairs={{0,16},{8,24},{16,32},{24,40},{32,48},{40,56},{48,0},{56,8},{64,80... | collective-permute-start | bytes 786440 | tf_op jit(solution)/shard_map/ppermute | solution.py:71
  44.0 7.7 %collective-permute-start.7 = (bf16[2,2,64,512]{3,0,1,2:T(2,128)(2,1)S(1)}, bf16[2,2,64,512]{3,0,1,2:T(2,128)(2,1)S(1)}, u32[]{:S(2)}, u32[]{:S(2)}) collective-permute-start(bf16[2,2,64,512]{3,0,1,2:T(2,128)(2,1)S(1)} %slice.73), channel_id=1, source_target_pairs={{0,48},{8,56},{16,0},{24,8},{32,16},{40,24},{48,32},{56,40},{64,11... | collective-permute-start | bytes 786440 | tf_op jit(solution)/shard_map/ppermute | solution.py:71
  45.9 7.4 %collective-permute-start.9 = (bf16[4,2,64,512]{3,0,1,2:T(4,128)(2,1)S(1)}, bf16[4,2,64,512]{3,0,1,2:T(4,128)(2,1)S(1)}, u32[]{:S(2)}, u32[]{:S(2)}) collective-permute-start(bf16[4,2,64,512]{3,0,1,2:T(4,128)(2,1)S(1)} %collective-permute-done.4), channel_id=1, source_target_pairs={{0,8},{8,0},{16,24},{24,16},{32,40},{40,32},{48,56},{56,48},{64,72... | collective-permute-start | bytes 1572872 | tf_op jit(solution)/shard_map/ppermute | solution.py:71
  45.9 8.9 %collective-permute-start.11 = (bf16[4,2,64,512]{3,0,1,2:T(4,128)(2,1)S(1)}, bf16[4,2,64,512]{3,0,1,2:T(4,128)(2,1)S(1)}, u32[]{:S(2)}, u32[]{:S(2)}) collective-permute-start(bf16[4,2,64,512]{3,0,1,2:T(4,128)(2,1)S(1)} %collective-permute-done.5), channel_id=1, source_target_pairs={{0,8},{8,0},{16,24},{24,16},{32,40},{40,32},{48,56},{56,48},{64,72... | collective-permute-start | bytes 1572872 | tf_op jit(solution)/shard_map/ppermute | solution.py:71
  52.2 2.0 %collective-permute-start.10 = (bf16[4,2,64,512]{3,0,1,2:T(4,128)(2,1)S(1)}, bf16[4,2,64,512]{3,0,1,2:T(4,128)(2,1)S(1)}, u32[]{:S(2)}, u32[]{:S(2)}) collective-permute-start(bf16[4,2,64,512]{3,0,1,2:T(4,128)(2,1)S(1)} %pad_maximum_fusion.1), channel_id=1, source_target_pairs={{0,8},{8,0},{16,24},{24,16},{32,40},{40,32},{48,56},{56,48},{64,72... | collective-permute-start | bytes 1572872 | tf_op jit(solution)/shard_map/ppermute | solution.py:71
  56.0 6.8 %copy-start.2 = (bf16[2,512,512]{2,1,0:T(8,128)(2,1)S(1)}, bf16[2,512,512]{2,1,0:T(8,128)(2,1)}, u32[]{:S(2)}) copy-start(bf16[2,512,512]{2,1,0:T(8,128)(2,1)} %param.17) | copy-start | bytes 3145732
  56.0 6.8 %copy-start.4 = (f32[2,512]{1,0:T(2,128)S(1)}, f32[2,512]{1,0:T(2,128)}, u32[]{:S(2)}) copy-start(f32[2,512]{1,0:T(2,128)} %param.21) | copy-start | bytes 12292
  62.8 3.6 %copy-start.3 = (bf16[2,512,512]{2,1,0:T(8,128)(2,1)S(1)}, bf16[2,512,512]{2,1,0:T(8,128)(2,1)}, u32[]{:S(2)}) copy-start(bf16[2,512,512]{2,1,0:T(8,128)(2,1)} %param.18) | copy-start | bytes 3145732
  66.4 2.1 %copy-start.1 = (bf16[2,512,512]{2,1,0:T(8,128)(2,1)S(1)}, bf16[2,512,512]{2,1,0:T(8,128)(2,1)}, u32[]{:S(2)}) copy-start(bf16[2,512,512]{2,1,0:T(8,128)(2,1)} %param.16) | copy-start | bytes 3145732
  69.3 9.9 %collective-permute-start.16 = (bf16[2,512,64]{1,2,0:T(8,128)(2,1)S(1)}, bf16[2,512,64]{1,2,0:T(8,128)(2,1)S(1)}, u32[]{:S(2)}, u32[]{:S(2)}) collective-permute-start(bf16[2,512,64]{1,2,0:T(8,128)(2,1)S(1)} %get-tuple-element.5), channel_id=1, source_target_pairs={{0,1},{1,2},{2,3},{3,4},{4,5},{5,6},{6,7},{7,0},{8,9},{9,10},{10,1... | collective-permute-start | bytes 393224 | tf_op jit(solution)/shard_map/ppermute | solution.py:13
  71.5 11.8 %collective-permute-start.17 = (bf16[2,512,64]{1,2,0:T(8,128)(2,1)S(1)}, bf16[2,512,64]{1,2,0:T(8,128)(2,1)S(1)}, u32[]{:S(2)}, u32[]{:S(2)}) collective-permute-start(bf16[2,512,64]{1,2,0:T(8,128)(2,1)S(1)} %get-tuple-element.9), channel_id=1, source_target_pairs={{0,2},{1,3},{2,4},{3,5},{4,6},{5,7},{6,0},{7,1},{8,10},{9,11},{10,... | collective-permute-start | bytes 393224 | tf_op jit(solution)/shard_map/ppermute | solution.py:13
  71.8 19.5 %collective-permute-start.18 = (bf16[2,512,64]{1,2,0:T(8,128)(2,1)S(1)}, bf16[2,512,64]{1,2,0:T(8,128)(2,1)S(1)}, u32[]{:S(2)}, u32[]{:S(2)}) collective-permute-start(bf16[2,512,64]{1,2,0:T(8,128)(2,1)S(1)} %get-tuple-element.8), channel_id=1, source_target_pairs={{0,3},{1,4},{2,5},{3,6},{4,7},{5,0},{6,1},{7,2},{8,11},{9,12},{10,... | collective-permute-start | bytes 393224 | tf_op jit(solution)/shard_map/ppermute | solution.py:13
  73.0 21.7 %collective-permute-start.19 = (bf16[2,512,64]{1,2,0:T(8,128)(2,1)S(1)}, bf16[2,512,64]{1,2,0:T(8,128)(2,1)S(1)}, u32[]{:S(2)}, u32[]{:S(2)}) collective-permute-start(bf16[2,512,64]{1,2,0:T(8,128)(2,1)S(1)} %get-tuple-element.7), channel_id=1, source_target_pairs={{0,4},{1,5},{2,6},{3,7},{4,0},{5,1},{6,2},{7,3},{8,12},{9,13},{10,... | collective-permute-start | bytes 393224 | tf_op jit(solution)/shard_map/ppermute | solution.py:13
  77.5 17.2 %collective-permute-start.20 = (bf16[2,512,64]{1,2,0:T(8,128)(2,1)S(1)}, bf16[2,512,64]{1,2,0:T(8,128)(2,1)S(1)}, u32[]{:S(2)}, u32[]{:S(2)}) collective-permute-start(bf16[2,512,64]{1,2,0:T(8,128)(2,1)S(1)} %get-tuple-element.6), channel_id=1, source_target_pairs={{0,5},{1,6},{2,7},{3,0},{4,1},{5,2},{6,3},{7,4},{8,13},{9,14},{10,... | collective-permute-start | bytes 393224 | tf_op jit(solution)/shard_map/ppermute | solution.py:13
  79.2 21.0 %collective-permute-start.21 = (bf16[2,512,64]{1,2,0:T(8,128)(2,1)S(1)}, bf16[2,512,64]{1,2,0:T(8,128)(2,1)S(1)}, u32[]{:S(2)}, u32[]{:S(2)}) collective-permute-start(bf16[2,512,64]{1,2,0:T(8,128)(2,1)S(1)} %get-tuple-element.11), channel_id=1, source_target_pairs={{0,6},{1,7},{2,0},{3,1},{4,2},{5,3},{6,4},{7,5},{8,14},{9,15},{10,... | collective-permute-start | bytes 393224 | tf_op jit(solution)/shard_map/ppermute | solution.py:13
  83.3 17.6 %collective-permute-start.22 = (bf16[2,512,64]{1,2,0:T(8,128)(2,1)S(1)}, bf16[2,512,64]{1,2,0:T(8,128)(2,1)}, u32[]{:S(2)}, u32[]{:S(2)}) collective-permute-start(bf16[2,512,64]{1,2,0:T(8,128)(2,1)S(1)} %get-tuple-element.10), channel_id=1, source_target_pairs={{0,7},{1,0},{2,1},{3,2},{4,3},{5,4},{6,5},{7,6},{8,15},{9,8},{10,9... | collective-permute-start | bytes 393224 | tf_op jit(solution)/shard_map/ppermute | solution.py:13

commit v10 on v6

--- a/solution.py
+++ b/solution.py
@@ -106,8 +106,11 @@
         "ktrn,tmn->ktrm", pooled, right_factor, preferred_element_type=jnp.float32
     ).astype(jnp.bfloat16)
     left_part = lax.dynamic_slice_in_dim(left_factor, part * row_count, row_count, axis=2)
+    left_flat = jnp.transpose(left_part, (1, 0, 2)).reshape(width_two, term_total * row_count)
+    done_flat = right_done.reshape(local_blocks, term_total * row_count, width_two)
+    left_flat, done_flat = lax.optimization_barrier((left_flat, done_flat))
     partial = jnp.einsum(
-        "tab,ktbc->kac", left_part, right_done, preferred_element_type=jnp.float32
+        "ak,jkc->jac", left_flat, done_flat, preferred_element_type=jnp.float32
     ).astype(jnp.bfloat16)
     dual_cols = jnp.einsum(
         "jab,jbc->jac", left_dual, partial, preferred_element_type=jnp.float32

time: 101 us -> 104 us (1.030)
  local copies, waits for them, and re-layouts: 7.45 us -> 11 us
  waiting for transfers between devices: 28.3 us -> 26.1 us
  matrix products: 16.1 us -> 17.3 us
    dot_general x1, matrix products: 5.57 us -> 1.62 us  [local(): jnp.einsum('ktrn,tmn->ktrm', pooled, right_factor, preferred_element_type...]
    dot_general x1, matrix products: 0.74 us -> 3.5 us  [local(): jnp.einsum('jab,jbc->jac', left_dual, partial, preferred_element_type=jnp...]
    ppermute x12, waiting for transfers between devices: 15.2 us -> 13 us  [move(): return lax.ppermute(piece, 'blk', pairs_list)]
    unnamed x16 -> x21, local copies, waits for them, and re-layouts: 1.58 us -> 3.37 us
    dynamic_slice x0 -> x1, local copies, waits for them, and re-layouts: none -> 1.58 us  [local(): lax.dynamic_slice_in_dim(left_factor, part * row_count, row_count, axis=2)]
    dot_general x1, matrix products: 0.74 us -> 1.99 us  [local(): jnp.einsum('jsrn,jmn->sjrm', dual_cols, right_dual, preferred_element_typ...]
    dot_general x8, matrix products: 5.69 us -> 6.74 us  [pool(): jnp.einsum('kab,abrn->krn', w, piece, preferred_element_type=jnp.float32)]
    slice x1, local copies, waits for them, and re-layouts: 0.29 us -> 1.34 us  [local(): from_above[half_ring:]]
  transfers between devices with their start and end apart: 19 -> 19, of which waited for: 11 -> 9; matrix products, arithmetic and copies ran while one was open for 10% -> 13% of each run, Pallas kernels for 0% -> 0%
where the time goes in v10:
time: 104 us
  starting transfers between devices  32.4 us (31%)
  waiting for transfers between devices  26.1 us (25%)
  matrix products  17.3 us (17%)
  blocking collectives  14.4 us (14%)
  local copies, waits for them, and re-layouts  11 us (11%)
  other arithmetic  2.11 us (2%)
    ppermute x7, starting transfers between devices, scatter_sum(): got = lax.ppermute(send, axis, [(j, (j + k) % n) for j in range(n)])  20.9 us
    all_to_all x1, blocking collectives, local(): lax.all_to_all(basis_rows, 'sub', split_axis=2, concat_axis=1, tiled=True)  14.4 us
    ppermute x7, waiting for transfers between devices, scatter_sum(): got = lax.ppermute(send, axis, [(j, (j + k) % n) for j in range(n)])  13.1 us
    ppermute x12, waiting for transfers between devices, move(): return lax.ppermute(piece, 'blk', pairs_list)  13 us
    ppermute x12, starting transfers between devices, move(): return lax.ppermute(piece, 'blk', pairs_list)  11.5 us
    dot_general x8, matrix products, pool(): jnp.einsum('kab,abrn->krn', w, piece, preferred_element_type=jnp.float32)  6.74 us
    dot_general x1, matrix products, local(): jnp.einsum('jab,jbc->jac', left_dual, partial, preferred_element_type=jnp...  3.5 us
    unnamed x21, local copies, waits for them, and re-layouts  3.37 us
  transfers between devices with their start and end apart: 19, of which 9 were waited for; matrix products, arithmetic and copies ran while one was open for 13% of the time, Pallas kernels for 0%

profile of v10, /device:TPU:24, one launch (start us, length us, event | category | flops | bytes accessed | tf_op | source)
XLA Modules:
  0.0 103.5 jit_solution(6468314780094004759)
XLA Ops:
  0.0 1.5 %collective-permute-start.1 = (bf16[2,64,512]{2,1,0:T(8,128)(2,1)}, bf16[2,64,512]{2,1,0:T(8,128)(2,1)S(1)}, u32[]{:S(2)}, u32[]{:S(2)}) collective-permute-start(bf16[2,64,512]{2,1,0:T(8,128)(2,1)} %param.11), channel_id=1, source_target_pairs={{0,64},{8,72},{16,80},{24,88},{32,96},{40,104},{48,112},{56,120},{... | collective-permute-start | bytes 393224 | tf_op jit(solution)/shard_map/ppermute | solution.py:71
  1.5 1.7 %collective-permute-start = (bf16[2,64,512]{2,1,0:T(8,128)(2,1)}, bf16[2,64,512]{2,1,0:T(8,128)(2,1)S(1)}, u32[]{:S(2)}, u32[]{:S(2)}) collective-permute-start(bf16[2,64,512]{2,1,0:T(8,128)(2,1)} %param.11), channel_id=1, source_target_pairs={{0,192},{8,200},{16,208},{24,216},{32,224},{40,232},{48,240},{56,2... | collective-permute-start | bytes 393224 | tf_op jit(solution)/shard_map/ppermute | solution.py:71
  3.6 1.1 %constant_dynamic-slice_fusion = s32[32,1,2,3]{1,2,3,0:T(2,128)S(1)} fusion(s32[32,32,2,3]{1,2,3,0:T(2,128)} %param.14, s32[]{:T(128)S(6)} %select_n.103), kind=kLoop, calls=%fused_computation.59 | loop fusion | bytes 1540 | tf_op jit(solution)/shard_map/jit(dynamic_index_in_dim)/dynamic_slice | solution.py:42
  4.7 0.9 dynamic-slice_reduce_fusion
  5.7 1.0 collective-permute-done.1
  7.0 3.0 %collective-permute-start.3 = (bf16[1,64,512]{2,1,0:T(8,128)(2,1)S(1)}, bf16[1,64,512]{2,1,0:T(8,128)(2,1)S(1)}, u32[]{:S(2)}, u32[]{:S(2)}) collective-permute-start(bf16[1,64,512]{2,1,0:T(8,128)(2,1)S(1)} %slice.65), channel_id=1, source_target_pairs={{0,192},{8,200},{16,208},{24,216},{32,224},{40,232},{48,240},{56,2... | collective-permute-start | bytes 196616 | tf_op jit(solution)/shard_map/ppermute | solution.py:71
  10.0 1.6 %constant_dynamic-slice_fusion.1 = bf16[8,512,64]{2,1,0:T(8,128)(2,1)S(1)} fusion(bf16[8,512,512]{2,1,0:T(8,128)(2,1)} %param.12, s32[]{:T(128)S(6)} %select_n.102), kind=kLoop, calls=%fused_computation.60 | loop fusion | bytes 1048580 | tf_op jit(solution)/shard_map/dynamic_slice | solution.py:108
  12.6 1.2 %pad_maximum_fusion = bf16[4,2,64,512]{3,0,1,2:T(4,128)(2,1)S(1)} fusion(bf16[1,2,64,512]{3,0,1,2:T(2,128)(2,1)S(1)} %copy.97, bf16[1,2,64,512]{3,0,1,2:T(2,128)(2,1)S(1)} %copy.96, bf16[1,2,64,512]{3,0,1,2:T(2,128)(2,1)S(1)} %copy.95, bf16[1,2,64,512]{3,0,1,2:T(2,128)(2,1)S(1)} %copy.94), kind=kLoop, calls=%fused_computation.22 | loop fusion | flops 2097152 | bytes 1048576 | tf_op jit(solution)/shard_map/stack | solution.py:79
  13.8 1.8 %collective-permute-start.5 = (bf16[4,2,64,512]{3,0,1,2:T(4,128)(2,1)S(1)}, bf16[4,2,64,512]{3,0,1,2:T(4,128)(2,1)S(1)}, u32[]{:S(2)}, u32[]{:S(2)}) collective-permute-start(bf16[4,2,64,512]{3,0,1,2:T(4,128)(2,1)S(1)} %pad_maximum_fusion), channel_id=1, source_target_pairs={{0,16},{8,24},{16,32},{24,40},{32,48},{40,56},{48,0},{56,8},{64,80... | collective-permute-start | bytes 1572872 | tf_op jit(solution)/shard_map/ppermute | solution.py:71
  15.6 0.3 collective-permute-start.4
  16.2 1.1 %copy.124 = bf16[8,512,64]{1,2,0:T(8,128)(2,1)} copy(bf16[8,512,64]{2,1,0:T(8,128)(2,1)S(1)} %constant_dynamic-slice_fusion.1) | data formatting | bytes 1048576
  17.5 0.6 fusion.49
  18.1 8.0 %collective-permute-done.5 = bf16[4,2,64,512]{3,0,1,2:T(4,128)(2,1)S(1)} collective-permute-done((bf16[4,2,64,512]{3,0,1,2:T(4,128)(2,1)S(1)}, bf16[4,2,64,512]{3,0,1,2:T(4,128)(2,1)S(1)}, u32[]{:S(2)}, u32[]{:S(2)}) %collective-permute-start.5) | collective-permute-done | bytes 524320 | tf_op jit(solution)/shard_map/ppermute | solution.py:71
  26.3 1.6 %collective-permute-start.6 = (bf16[2,2,64,512]{3,0,1,2:T(2,128)(2,1)S(1)}, bf16[2,2,64,512]{3,0,1,2:T(2,128)(2,1)S(1)}, u32[]{:S(2)}, u32[]{:S(2)}) collective-permute-start(bf16[2,2,64,512]{3,0,1,2:T(2,128)(2,1)S(1)} %slice.68), channel_id=1, source_target_pairs={{0,16},{8,24},{16,32},{24,40},{32,48},{40,56},{48,0},{56,8},{64,80... | collective-permute-start | bytes 786440 | tf_op jit(solution)/shard_map/ppermute | solution.py:71
  27.9 1.3 %slice.69 = bf16[2,2,64,512]{3,0,1,2:T(2,128)(2,1)S(1)} slice(bf16[4,2,64,512]{3,0,1,2:T(4,128)(2,1)} %collective-permute-done.4), slice={[2:4], [0:2], [0:64], [0:512]} | slice | bytes 524288 | tf_op jit(solution)/shard_map/slice | solution.py:87
  29.2 0.6 collective-permute-start.7
  29.8 0.5 collective-permute-start.11
  30.3 0.6 fusion.43
  31.0 1.7 %fusion.47 = f32[16,64,512,1]{2,0,3,1:T(8,128)S(1)} fusion(bf16[4,2,64,512]{3,0,1,2:T(4,128)(2,1)} %collective-permute-done.4, bf16[16,1,1,4,2]{0,4,3,2,1:T(2,128)(2,1)S(1)} %get-tuple-element.22), kind=kOutput, calls=%fused_computation.76 | convolution fusion | flops 8388608 | bytes 2621696 | tf_op jit(solution)/shard_map/kab,abrn->krn/dot_general | solution.py:92
  32.6 0.6 fusion.41
  33.2 3.6 %collective-permute-done.7 = bf16[2,2,64,512]{3,0,1,2:T(2,128)(2,1)S(1)} collective-permute-done((bf16[2,2,64,512]{3,0,1,2:T(2,128)(2,1)S(1)}, bf16[2,2,64,512]{3,0,1,2:T(2,128)(2,1)S(1)}, u32[]{:S(2)}, u32[]{:S(2)}) %collective-permute-start.7) | collective-permute-done | bytes 262176 | tf_op jit(solution)/shard_map/ppermute | solution.py:71
  36.9 0.5 pad_maximum_fusion.1
  37.5 1.0 fusion.45
  38.5 0.6 fusion.39
  39.1 0.3 collective-permute-done.10
  39.4 0.6 fusion.37
  40.1 1.1 %fusion.9 = bf16[2,8,64,512]{3,1,0,2:T(8,128)(2,1)S(1)} fusion(bf16[4,2,64,512]{3,0,1,2:T(4,128)(2,1)S(1)} %collective-permute-done.11, f32[16,64,512,1]{2,0,3,1:T(8,128)S(1)} %fusion.37, f32[16,64,512,1]{2,0,3,1:T(8,128)S(1)} %fusion.39, f32[16,64,512,1]{2,0,3,1:T(8,128)S(1)} %fusion.41, f32[16,64,512,1]{2,0,3,1:T(8,128)S(1)} %fusion.43, ...), kind=kOutput, calls=%fused_computation.15 | convolution fusion | flops 12582912 | bytes 16253184 | tf_op jit(solution)/shard_map/kab,abrn->krn/dot_general | solution.py:92
  41.2 1.1 %copy-done.1 = bf16[8,512,512]{2,1,0:T(8,128)(2,1)S(1)} copy-done((bf16[8,512,512]{2,1,0:T(8,128)(2,1)S(1)}, bf16[8,512,512]{2,1,0:T(8,128)(2,1)}, u32[]{:S(2)}) %copy-start.1) | copy-done | bytes 4194328
  42.2 1.6 %fusion.6 = bf16[2,8,64,512]{3,2,0,1:T(8,128)(2,1)S(1)} fusion(bf16[8,512,512]{2,1,0:T(8,128)(2,1)S(1)} %copy-done.1, bf16[2,8,64,512]{3,1,0,2:T(8,128)(2,1)S(1)} %fusion.9), kind=kOutput, calls=%fused_computation.14 | convolution fusion | flops 537395200 | bytes 6291456 | tf_op jit(solution)/shard_map/ktrn,tmn->ktrm/dot_general | solution.py:105
  44.0 3.5 %convolution_convert_fusion.1 = bf16[2,512,512]{1,2,0:T(8,128)(2,1)} fusion(bf16[2,512,512]{2,1,0:T(8,128)(2,1)S(1)} %copy-done, bf16[2,512,512]{2,1,0:T(8,128)(2,1)S(1)} %bitcast.187, bf16[512,512]{0,1:T(8,128)(2,1)} %bitcast.190), kind=kOutput, calls=%fused_computation.12 | convolution fusion | flops 1074790400 | bytes 3670016 | tf_op jit(solution)/shard_map/jab,jbc->jac/dot_general | solution.py:115
  47.5 2.0 %convolution_convert_fusion = bf16[2,8,64,512]{3,2,1,0:T(8,128)(2,1)S(1)} fusion(bf16[2,8,64,512]{3,2,1,0:T(8,128)(2,1)} %bitcast.185, bf16[2,512,512]{2,1,0:T(8,128)(2,1)S(1)} %copy-done.2), kind=kOutput, calls=%fused_computation.11 | convolution fusion | flops 537395200 | bytes 3145728 | tf_op jit(solution)/shard_map/jsrn,jmn->sjrm/dot_general | solution.py:119
  49.5 0.8 dynamic-slice_bitcast_fusion.6
  50.3 1.9 %collective-permute-start.12 = (bf16[2,64,512]{2,1,0:T(8,128)(2,1)S(1)}, bf16[2,64,512]{2,1,0:T(8,128)(2,1)S(1)}, u32[]{:S(2)}, u32[]{:S(2)}) collective-permute-start(bf16[2,64,512]{2,1,0:T(8,128)(2,1)S(1)} %get-tuple-element.9), channel_id=1, source_target_pairs={{0,1},{1,2},{2,3},{3,4},{4,5},{5,6},{6,7},{7,0},{8,9},{9,10},{10,1... | collective-permute-start | bytes 393224 | tf_op jit(solution)/shard_map/ppermute | solution.py:13
  52.2 3.3 %collective-permute-start.13 = (bf16[2,64,512]{2,1,0:T(8,128)(2,1)S(1)}, bf16[2,64,512]{2,1,0:T(8,128)(2,1)S(1)}, u32[]{:S(2)}, u32[]{:S(2)}) collective-permute-start(bf16[2,64,512]{2,1,0:T(8,128)(2,1)S(1)} %get-tuple-element.15), channel_id=1, source_target_pairs={{0,2},{1,3},{2,4},{3,5},{4,6},{5,7},{6,0},{7,1},{8,10},{9,11},{10,... | collective-permute-start | bytes 393224 | tf_op jit(solution)/shard_map/ppermute | solution.py:13
  55.5 4.0 %collective-permute-start.14 = (bf16[2,64,512]{2,1,0:T(8,128)(2,1)}, bf16[2,64,512]{2,1,0:T(8,128)(2,1)}, u32[]{:S(2)}, u32[]{:S(2)}) collective-permute-start(bf16[2,64,512]{2,1,0:T(8,128)(2,1)} %get-tuple-element.14), channel_id=1, source_target_pairs={{0,3},{1,4},{2,5},{3,6},{4,7},{5,0},{6,1},{7,2},{8,11},{9,12},{10,... | collective-permute-start | bytes 393224 | tf_op jit(solution)/shard_map/ppermute | solution.py:13
  59.5 0.5 collective-permute-start.15
  60.1 4.9 %collective-permute-start.16 = (bf16[2,64,512]{2,1,0:T(8,128)(2,1)S(1)}, bf16[2,64,512]{2,1,0:T(8,128)(2,1)}, u32[]{:S(2)}, u32[]{:S(2)}) collective-permute-start(bf16[2,64,512]{2,1,0:T(8,128)(2,1)S(1)} %get-tuple-element.12), channel_id=1, source_target_pairs={{0,5},{1,6},{2,7},{3,0},{4,1},{5,2},{6,3},{7,4},{8,13},{9,14},{10,... | collective-permute-start | bytes 393224 | tf_op jit(solution)/shard_map/ppermute | solution.py:13
  65.0 2.7 %collective-permute-start.17 = (bf16[2,64,512]{2,1,0:T(8,128)(2,1)S(1)}, bf16[2,64,512]{2,1,0:T(8,128)(2,1)}, u32[]{:S(2)}, u32[]{:S(2)}) collective-permute-start(bf16[2,64,512]{2,1,0:T(8,128)(2,1)S(1)} %get-tuple-element.11), channel_id=1, source_target_pairs={{0,6},{1,7},{2,0},{3,1},{4,2},{5,3},{6,4},{7,5},{8,14},{9,15},{10,... | collective-permute-start | bytes 393224 | tf_op jit(solution)/shard_map/ppermute | solution.py:13
  67.7 0.7 collective-permute-done.13
  68.4 0.6 copy-done.6
  69.0 3.5 %collective-permute-start.18 = (bf16[2,64,512]{2,1,0:T(8,128)(2,1)S(1)}, bf16[2,64,512]{2,1,0:T(8,128)(2,1)}, u32[]{:S(2)}, u32[]{:S(2)}) collective-permute-start(bf16[2,64,512]{2,1,0:T(8,128)(2,1)S(1)} %get-tuple-element.10), channel_id=1, source_target_pairs={{0,7},{1,0},{2,1},{3,2},{4,3},{5,4},{6,5},{7,6},{8,15},{9,8},{10,9... | collective-permute-start | bytes 393224 | tf_op jit(solution)/shard_map/ppermute | solution.py:13
  72.5 4.9 %collective-permute-done.14 = bf16[2,64,512]{2,1,0:T(8,128)(2,1)} collective-permute-done((bf16[2,64,512]{2,1,0:T(8,128)(2,1)}, bf16[2,64,512]{2,1,0:T(8,128)(2,1)}, u32[]{:S(2)}, u32[]{:S(2)}) %collective-permute-start.14) | collective-permute-done | bytes 131104 | tf_op jit(solution)/shard_map/ppermute | solution.py:13
  77.5 3.5 %collective-permute-done.16 = bf16[2,64,512]{2,1,0:T(8,128)(2,1)} collective-permute-done((bf16[2,64,512]{2,1,0:T(8,128)(2,1)S(1)}, bf16[2,64,512]{2,1,0:T(8,128)(2,1)}, u32[]{:S(2)}, u32[]{:S(2)}) %collective-permute-start.16) | collective-permute-done | bytes 131104 | tf_op jit(solution)/shard_map/ppermute | solution.py:13
  81.0 3.4 %collective-permute-done.17 = bf16[2,64,512]{2,1,0:T(8,128)(2,1)} collective-permute-done((bf16[2,64,512]{2,1,0:T(8,128)(2,1)S(1)}, bf16[2,64,512]{2,1,0:T(8,128)(2,1)}, u32[]{:S(2)}, u32[]{:S(2)}) %collective-permute-start.17) | collective-permute-done | bytes 131104 | tf_op jit(solution)/shard_map/ppermute | solution.py:13
  84.4 0.5 collective-permute-done.18
  84.9 2.1 %convolution_convert_fusion.3 = bf16[2,64,512]{2,1,0:T(8,128)(2,1)S(1)} fusion(bf16[2,512,512]{2,1,0:T(8,128)(2,1)} %param.18, bf16[2,64,512]{2,1,0:T(8,128)(2,1)} %collective-permute-done.18, bf16[2,64,512]{2,1,0:T(8,128)(2,1)} %collective-permute-done.17, bf16[2,64,512]{2,1,0:T(8,128)(2,1)} %collective-permute-done.16, ...), kind=kOutput, calls=%fused_computation.17 | convolution fusion | flops 68354048 | bytes 2233348 | tf_op jit(solution)/shard_map/jrm,jkm->jrk/dot_general | solution.py:124
  87.4 14.4 %all_to_all.18 = bf16[8,2,4096]{2,1,0:T(2,128)(2,1)S(1)} all-to-all(bf16[8,2,4096]{2,1,0:T(2,128)(2,1)S(1)} %reshape.189), channel_id=1, replica_groups=mesh['blk'=32,'sub'=8] {'sub'}, dimensions={0} | all-to-all | bytes 262144 | tf_op jit(solution)/shard_map/all_to_all | solution.py:127
  102.4 1.1 %convolution_bitcast_fusion = f32[2,512,64]{1,2,0:T(8,128)} fusion(bf16[2,512,64]{1,2,0:T(8,128)(2,1)S(1)} %all_to_all.16, bf16[2,512,512]{2,1,0:T(8,128)(2,1)S(1)} %copy-done.3), kind=kOutput, calls=%fused_computation.16 | convolution fusion | flops 67108864 | bytes 1441792 | tf_op jit(solution)/shard_map/jab,jbc->jac/dot_general | solution.py:128
  (57 shorter events, 3.5 us)
Async XLA Ops:
  0.0 44.0 %copy-start = (bf16[2,512,512]{2,1,0:T(8,128)(2,1)S(1)}, bf16[2,512,512]{2,1,0:T(8,128)(2,1)}, u32[]{:S(2)}) copy-start(bf16[2,512,512]{2,1,0:T(8,128)(2,1)} %param.17) | copy-start | bytes 3145732
  0.0 11.7 %copy-start.4 = (bf16[2,64,512]{2,1,0:T(8,128)(2,1)S(1)}, bf16[2,64,512]{2,1,0:T(8,128)(2,1)}, u32[]{:S(2)}) copy-start(bf16[2,64,512]{2,1,0:T(8,128)(2,1)} %param.11) | copy-start | bytes 393220
  0.0 6.7 %collective-permute-start.1 = (bf16[2,64,512]{2,1,0:T(8,128)(2,1)}, bf16[2,64,512]{2,1,0:T(8,128)(2,1)S(1)}, u32[]{:S(2)}, u32[]{:S(2)}) collective-permute-start(bf16[2,64,512]{2,1,0:T(8,128)(2,1)} %param.11), channel_id=1, source_target_pairs={{0,64},{8,72},{16,80},{24,88},{32,96},{40,104},{48,112},{56,120},{... | collective-permute-start | bytes 393224 | tf_op jit(solution)/shard_map/ppermute | solution.py:71
  1.5 5.5 %collective-permute-start = (bf16[2,64,512]{2,1,0:T(8,128)(2,1)}, bf16[2,64,512]{2,1,0:T(8,128)(2,1)S(1)}, u32[]{:S(2)}, u32[]{:S(2)}) collective-permute-start(bf16[2,64,512]{2,1,0:T(8,128)(2,1)} %param.11), channel_id=1, source_target_pairs={{0,192},{8,200},{16,208},{24,216},{32,224},{40,232},{48,240},{56,2... | collective-permute-start | bytes 393224 | tf_op jit(solution)/shard_map/ppermute | solution.py:71
  6.7 5.7 %collective-permute-start.2 = (bf16[1,64,512]{2,1,0:T(8,128)(2,1)S(1)}, bf16[1,64,512]{2,1,0:T(8,128)(2,1)S(1)}, u32[]{:S(2)}, u32[]{:S(2)}) collective-permute-start(bf16[1,64,512]{2,1,0:T(8,128)(2,1)S(1)} %slice.64), channel_id=1, source_target_pairs={{0,64},{8,72},{16,80},{24,88},{32,96},{40,104},{48,112},{56,120},{... | collective-permute-start | bytes 196616 | tf_op jit(solution)/shard_map/ppermute | solution.py:71
  7.0 5.4 %collective-permute-start.3 = (bf16[1,64,512]{2,1,0:T(8,128)(2,1)S(1)}, bf16[1,64,512]{2,1,0:T(8,128)(2,1)S(1)}, u32[]{:S(2)}, u32[]{:S(2)}) collective-permute-start(bf16[1,64,512]{2,1,0:T(8,128)(2,1)S(1)} %slice.65), channel_id=1, source_target_pairs={{0,192},{8,200},{16,208},{24,216},{32,224},{40,232},{48,240},{56,2... | collective-permute-start | bytes 196616 | tf_op jit(solution)/shard_map/ppermute | solution.py:71
  13.8 12.3 %collective-permute-start.5 = (bf16[4,2,64,512]{3,0,1,2:T(4,128)(2,1)S(1)}, bf16[4,2,64,512]{3,0,1,2:T(4,128)(2,1)S(1)}, u32[]{:S(2)}, u32[]{:S(2)}) collective-permute-start(bf16[4,2,64,512]{3,0,1,2:T(4,128)(2,1)S(1)} %pad_maximum_fusion), channel_id=1, source_target_pairs={{0,16},{8,24},{16,32},{24,40},{32,48},{40,56},{48,0},{56,8},{64,80... | collective-permute-start | bytes 1572872 | tf_op jit(solution)/shard_map/ppermute | solution.py:71
  15.6 12.3 %collective-permute-start.4 = (bf16[4,2,64,512]{3,0,1,2:T(4,128)(2,1)S(1)}, bf16[4,2,64,512]{3,0,1,2:T(4,128)(2,1)}, u32[]{:S(2)}, u32[]{:S(2)}) collective-permute-start(bf16[4,2,64,512]{3,0,1,2:T(4,128)(2,1)S(1)} %pad_maximum_fusion), channel_id=1, source_target_pairs={{0,48},{8,56},{16,0},{24,8},{32,16},{40,24},{48,32},{56,40},{64,11... | collective-permute-start | bytes 1572872 | tf_op jit(solution)/shard_map/ppermute | solution.py:71
  17.4 15.2 %collective-permute-start.8 = (bf16[4,2,64,512]{3,0,1,2:T(4,128)(2,1)S(1)}, bf16[4,2,64,512]{3,0,1,2:T(4,128)(2,1)S(1)}, u32[]{:S(2)}, u32[]{:S(2)}) collective-permute-start(bf16[4,2,64,512]{3,0,1,2:T(4,128)(2,1)S(1)} %pad_maximum_fusion), channel_id=1, source_target_pairs={{0,8},{8,0},{16,24},{24,16},{32,40},{40,32},{48,56},{56,48},{64,72... | collective-permute-start | bytes 1572872 | tf_op jit(solution)/shard_map/ppermute | solution.py:71
  26.3 6.9 %collective-permute-start.6 = (bf16[2,2,64,512]{3,0,1,2:T(2,128)(2,1)S(1)}, bf16[2,2,64,512]{3,0,1,2:T(2,128)(2,1)S(1)}, u32[]{:S(2)}, u32[]{:S(2)}) collective-permute-start(bf16[2,2,64,512]{3,0,1,2:T(2,128)(2,1)S(1)} %slice.68), channel_id=1, source_target_pairs={{0,16},{8,24},{16,32},{24,40},{32,48},{40,56},{48,0},{56,8},{64,80... | collective-permute-start | bytes 786440 | tf_op jit(solution)/shard_map/ppermute | solution.py:71
  29.2 7.7 %collective-permute-start.7 = (bf16[2,2,64,512]{3,0,1,2:T(2,128)(2,1)S(1)}, bf16[2,2,64,512]{3,0,1,2:T(2,128)(2,1)S(1)}, u32[]{:S(2)}, u32[]{:S(2)}) collective-permute-start(bf16[2,2,64,512]{3,0,1,2:T(2,128)(2,1)S(1)} %slice.69), channel_id=1, source_target_pairs={{0,48},{8,56},{16,0},{24,8},{32,16},{40,24},{48,32},{56,40},{64,11... | collective-permute-start | bytes 786440 | tf_op jit(solution)/shard_map/ppermute | solution.py:71
  29.8 8.7 %collective-permute-start.9 = (bf16[4,2,64,512]{3,0,1,2:T(4,128)(2,1)}, bf16[4,2,64,512]{3,0,1,2:T(4,128)(2,1)S(1)}, u32[]{:S(2)}, u32[]{:S(2)}) collective-permute-start(bf16[4,2,64,512]{3,0,1,2:T(4,128)(2,1)} %collective-permute-done.4), channel_id=1, source_target_pairs={{0,8},{8,0},{16,24},{24,16},{32,40},{40,32},{48,56},{56,48},{64,72... | collective-permute-start | bytes 1572872 | tf_op jit(solution)/shard_map/ppermute | solution.py:71
  29.8 10.2 %collective-permute-start.11 = (bf16[4,2,64,512]{3,0,1,2:T(4,128)(2,1)S(1)}, bf16[4,2,64,512]{3,0,1,2:T(4,128)(2,1)S(1)}, u32[]{:S(2)}, u32[]{:S(2)}) collective-permute-start(bf16[4,2,64,512]{3,0,1,2:T(4,128)(2,1)S(1)} %collective-permute-done.5), channel_id=1, source_target_pairs={{0,8},{8,0},{16,24},{24,16},{32,40},{40,32},{48,56},{56,48},{64,72... | collective-permute-start | bytes 1572872 | tf_op jit(solution)/shard_map/ppermute | solution.py:71
  37.4 2.0 %collective-permute-start.10 = (bf16[4,2,64,512]{3,0,1,2:T(4,128)(2,1)S(1)}, bf16[4,2,64,512]{3,0,1,2:T(4,128)(2,1)S(1)}, u32[]{:S(2)}, u32[]{:S(2)}) collective-permute-start(bf16[4,2,64,512]{3,0,1,2:T(4,128)(2,1)S(1)} %pad_maximum_fusion.1), channel_id=1, source_target_pairs={{0,8},{8,0},{16,24},{24,16},{32,40},{40,32},{48,56},{56,48},{64,72... | collective-permute-start | bytes 1572872 | tf_op jit(solution)/shard_map/ppermute | solution.py:71
  40.1 2.2 %copy-start.1 = (bf16[8,512,512]{2,1,0:T(8,128)(2,1)S(1)}, bf16[8,512,512]{2,1,0:T(8,128)(2,1)}, u32[]{:S(2)}) copy-start(bf16[8,512,512]{2,1,0:T(8,128)(2,1)} %param.13) | copy-start | bytes 12582916
  44.0 3.5 %copy-start.2 = (bf16[2,512,512]{2,1,0:T(8,128)(2,1)S(1)}, bf16[2,512,512]{2,1,0:T(8,128)(2,1)}, u32[]{:S(2)}) copy-start(bf16[2,512,512]{2,1,0:T(8,128)(2,1)} %param.19) | copy-start | bytes 3145732
  47.5 37.4 %copy-start.7 = (f32[2,512]{1,0:T(2,128)S(1)}, f32[2,512]{1,0:T(2,128)}, u32[]{:S(2)}) copy-start(f32[2,512]{1,0:T(2,128)} %param.21) | copy-start | bytes 12292
  47.5 37.4 %copy-start.8 = (f32[2,64]{1,0:T(2,128)S(1)}, f32[2,64]{1,0:T(2,128)}, u32[]{:S(2)}) copy-start(f32[2,64]{1,0:T(2,128)} %param.20) | copy-start | bytes 1540
  50.3 14.7 %collective-permute-start.12 = (bf16[2,64,512]{2,1,0:T(8,128)(2,1)S(1)}, bf16[2,64,512]{2,1,0:T(8,128)(2,1)S(1)}, u32[]{:S(2)}, u32[]{:S(2)}) collective-permute-start(bf16[2,64,512]{2,1,0:T(8,128)(2,1)S(1)} %get-tuple-element.9), channel_id=1, source_target_pairs={{0,1},{1,2},{2,3},{3,4},{4,5},{5,6},{6,7},{7,0},{8,9},{9,10},{10,1... | collective-permute-start | bytes 393224 | tf_op jit(solution)/shard_map/ppermute | solution.py:13
  52.2 16.2 %collective-permute-start.13 = (bf16[2,64,512]{2,1,0:T(8,128)(2,1)S(1)}, bf16[2,64,512]{2,1,0:T(8,128)(2,1)S(1)}, u32[]{:S(2)}, u32[]{:S(2)}) collective-permute-start(bf16[2,64,512]{2,1,0:T(8,128)(2,1)S(1)} %get-tuple-element.15), channel_id=1, source_target_pairs={{0,2},{1,3},{2,4},{3,5},{4,6},{5,7},{6,0},{7,1},{8,10},{9,11},{10,... | collective-permute-start | bytes 393224 | tf_op jit(solution)/shard_map/ppermute | solution.py:13
  55.5 22.0 %collective-permute-start.14 = (bf16[2,64,512]{2,1,0:T(8,128)(2,1)}, bf16[2,64,512]{2,1,0:T(8,128)(2,1)}, u32[]{:S(2)}, u32[]{:S(2)}) collective-permute-start(bf16[2,64,512]{2,1,0:T(8,128)(2,1)} %get-tuple-element.14), channel_id=1, source_target_pairs={{0,3},{1,4},{2,5},{3,6},{4,7},{5,0},{6,1},{7,2},{8,11},{9,12},{10,... | collective-permute-start | bytes 393224 | tf_op jit(solution)/shard_map/ppermute | solution.py:13
  59.5 17.9 %collective-permute-start.15 = (bf16[2,64,512]{2,1,0:T(8,128)(2,1)}, bf16[2,64,512]{2,1,0:T(8,128)(2,1)}, u32[]{:S(2)}, u32[]{:S(2)}) collective-permute-start(bf16[2,64,512]{2,1,0:T(8,128)(2,1)} %get-tuple-element.13), channel_id=1, source_target_pairs={{0,4},{1,5},{2,6},{3,7},{4,0},{5,1},{6,2},{7,3},{8,12},{9,13},{10,... | collective-permute-start | bytes 393224 | tf_op jit(solution)/shard_map/ppermute | solution.py:13
  60.1 20.9 %collective-permute-start.16 = (bf16[2,64,512]{2,1,0:T(8,128)(2,1)S(1)}, bf16[2,64,512]{2,1,0:T(8,128)(2,1)}, u32[]{:S(2)}, u32[]{:S(2)}) collective-permute-start(bf16[2,64,512]{2,1,0:T(8,128)(2,1)S(1)} %get-tuple-element.12), channel_id=1, source_target_pairs={{0,5},{1,6},{2,7},{3,0},{4,1},{5,2},{6,3},{7,4},{8,13},{9,14},{10,... | collective-permute-start | bytes 393224 | tf_op jit(solution)/shard_map/ppermute | solution.py:13
  65.0 3.4 %copy-start.5 = (bf16[2,64,512]{2,1,0:T(8,128)(2,1)}, bf16[2,64,512]{2,1,0:T(8,128)(2,1)S(1)}, u32[]{:S(2)}) copy-start(bf16[2,64,512]{2,1,0:T(8,128)(2,1)S(1)} %collective-permute-done.12) | copy-start | bytes 393220
  65.0 19.4 %collective-permute-start.17 = (bf16[2,64,512]{2,1,0:T(8,128)(2,1)S(1)}, bf16[2,64,512]{2,1,0:T(8,128)(2,1)}, u32[]{:S(2)}, u32[]{:S(2)}) collective-permute-start(bf16[2,64,512]{2,1,0:T(8,128)(2,1)S(1)} %get-tuple-element.11), channel_id=1, source_target_pairs={{0,6},{1,7},{2,0},{3,1},{4,2},{5,3},{6,4},{7,5},{8,14},{9,15},{10,... | collective-permute-start | bytes 393224 | tf_op jit(solution)/shard_map/ppermute | solution.py:13
  68.4 0.6 copy-start.6
  69.0 15.9 %collective-permute-start.18 = (bf16[2,64,512]{2,1,0:T(8,128)(2,1)S(1)}, bf16[2,64,512]{2,1,0:T(8,128)(2,1)}, u32[]{:S(2)}, u32[]{:S(2)}) collective-permute-start(bf16[2,64,512]{2,1,0:T(8,128)(2,1)S(1)} %get-tuple-element.10), channel_id=1, source_target_pairs={{0,7},{1,0},{2,1},{3,2},{4,3},{5,4},{6,5},{7,6},{8,15},{9,8},{10,9... | collective-permute-start | bytes 393224 | tf_op jit(solution)/shard_map/ppermute | solution.py:13
  72.5 29.8 %copy-start.3 = (bf16[2,512,512]{2,1,0:T(8,128)(2,1)S(1)}, bf16[2,512,512]{2,1,0:T(8,128)(2,1)}, u32[]{:S(2)}) copy-start(bf16[2,512,512]{2,1,0:T(8,128)(2,1)} %param.16) | copy-start | bytes 3145732

commit v11 on v7

--- a/solution.py
+++ b/solution.py
@@ -107,14 +107,9 @@
     ).astype(jnp.bfloat16)
     left_part = lax.dynamic_slice_in_dim(left_factor, part * row_count, row_count, axis=2)
     rates_run, pooled = lax.optimization_barrier((left_rates[None], pooled))
-
-    def shift_sub(piece, k):
-        return lax.ppermute(piece, "sub", [(j, (j + k) % pieces) for j in range(pieces)])
-
-    trio = jnp.concatenate([shift_sub(rates_run, 1), rates_run, shift_sub(rates_run, -1)], axis=0)
-    rates_run = jnp.concatenate([shift_sub(trio, 3), trio, shift_sub(trio, -3)[:2]], axis=0)
-    rates_twice = jnp.concatenate([rates_run, rates_run], axis=0)
-    rates_parts = lax.dynamic_slice_in_dim(rates_twice, (4 - part) % pieces, pieces, axis=0)
+    rates_parts = lax.all_to_all(
+        jnp.broadcast_to(rates_run, (pieces,) + left_rates.shape), "sub", 0, 0, tiled=True
+    )
     rates_full = jnp.moveaxis(rates_parts, 0, 1).reshape(local_blocks, width_two)
     partial = jnp.einsum(
         "tab,ktbc->kac", left_part, right_done, preferred_element_type=jnp.float32

time: 102 us -> 99.2 us (0.973)
  waiting for transfers between devices: 38.8 us -> 30.5 us
  starting transfers between devices: 34.6 us -> 37.6 us
  local copies, waits for them, and re-layouts: 4.81 us -> 5.99 us
    ppermute x4 -> x0, starting transfers between devices: 11.2 us -> none  [shift_sub(): lax.ppermute(piece, 'sub', [(j, (j + k) % pieces) for j in range(pieces)])]
    all_to_all x0 -> x1, starting transfers between devices: none -> 8.4 us  [local(): lax.all_to_all(jnp.broadcast_to(rates_run, (pieces,) + left_rates.shape),...]
    ppermute x4 -> x0, waiting for transfers between devices: 6.76 us -> none  [shift_sub(): lax.ppermute(piece, 'sub', [(j, (j + k) % pieces) for j in range(pieces)])]
    ppermute x7, starting transfers between devices: 11.9 us -> 17.6 us  [scatter_sum(): got = lax.ppermute(send, axis, [(j, (j + k) % n) for j in range(n)])]
    ppermute x7, waiting for transfers between devices: 16.8 us -> 14.4 us  [scatter_sum(): got = lax.ppermute(send, axis, [(j, (j + k) % n) for j in range(n)])]
  transfers between devices with their start and end apart: 23 -> 20, of which waited for: 12 -> 13; matrix products, arithmetic and copies ran while one was open for 16% -> 17% of each run, Pallas kernels for 0% -> 0%
where the time goes in v11:
time: 99.2 us; the launch traced here: 97.8 us
  starting transfers between devices  37.6 us (38%)
  waiting for transfers between devices  30.5 us (31%)
  matrix products  18.9 us (19%)
  local copies, waits for them, and re-layouts  5.99 us (6%)
  other arithmetic  4.51 us (5%)
    ppermute x7, starting transfers between devices, scatter_sum(): got = lax.ppermute(send, axis, [(j, (j + k) % n) for j in range(n)])  17.6 us
    ppermute x12, waiting for transfers between devices, move(): return lax.ppermute(piece, 'blk', pairs_list)  15.2 us
    ppermute x7, waiting for transfers between devices, scatter_sum(): got = lax.ppermute(send, axis, [(j, (j + k) % n) for j in range(n)])  14.4 us
    ppermute x12, starting transfers between devices, move(): return lax.ppermute(piece, 'blk', pairs_list)  11.5 us
    all_to_all x1, starting transfers between devices, local(): lax.all_to_all(jnp.broadcast_to(rates_run, (pieces,) + left_rates.shape),...  8.4 us
    dot_general x1, matrix products, local(): jnp.einsum('tab,ktbc->kac', left_part, right_done, preferred_element_type...  6.65 us
    dot_general x8, matrix products, pool(): jnp.einsum('kab,abrn->krn', w, piece, preferred_element_type=jnp.float32)  5.69 us
    dot_general x1, matrix products, local(): jnp.einsum('jrn,jmn->jrm', dual_cols, right_dual, preferred_element_type=...  3.59 us
  transfers between devices with their start and end apart: 20, of which 13 were waited for; matrix products, arithmetic and copies ran while one was open for 17% of the time, Pallas kernels for 0%

profile of v11, /device:TPU:24, one launch (start us, length us, event | category | flops | bytes accessed | tf_op | source)
XLA Modules:
  0.0 97.8 jit_solution(411874050572463288)
XLA Ops:
  0.0 1.5 %collective-permute-start.1 = (bf16[2,64,512]{2,1,0:T(8,128)(2,1)}, bf16[2,64,512]{2,1,0:T(8,128)(2,1)S(1)}, u32[]{:S(2)}, u32[]{:S(2)}) collective-permute-start(bf16[2,64,512]{2,1,0:T(8,128)(2,1)} %param.11), channel_id=1, source_target_pairs={{0,64},{8,72},{16,80},{24,88},{32,96},{40,104},{48,112},{56,120},{... | collective-permute-start | bytes 393224 | tf_op jit(solution)/shard_map/ppermute | solution.py:71
  1.5 1.7 %collective-permute-start = (bf16[2,64,512]{2,1,0:T(8,128)(2,1)}, bf16[2,64,512]{2,1,0:T(8,128)(2,1)S(1)}, u32[]{:S(2)}, u32[]{:S(2)}) collective-permute-start(bf16[2,64,512]{2,1,0:T(8,128)(2,1)} %param.11), channel_id=1, source_target_pairs={{0,192},{8,200},{16,208},{24,216},{32,224},{40,232},{48,240},{56,2... | collective-permute-start | bytes 393224 | tf_op jit(solution)/shard_map/ppermute | solution.py:71
  3.6 1.1 %constant_dynamic-slice_fusion = s32[32,1,2,3]{1,2,3,0:T(2,128)S(1)} fusion(s32[32,32,2,3]{1,2,3,0:T(2,128)} %param.14, s32[]{:T(128)S(6)} %select_n.102), kind=kLoop, calls=%fused_computation.53 | loop fusion | bytes 1540 | tf_op jit(solution)/shard_map/jit(dynamic_index_in_dim)/dynamic_slice | solution.py:42
  4.7 0.9 dynamic-slice_reduce_fusion
  5.7 1.0 %collective-permute-done.1 = bf16[2,64,512]{2,1,0:T(8,128)(2,1)S(1)} collective-permute-done((bf16[2,64,512]{2,1,0:T(8,128)(2,1)}, bf16[2,64,512]{2,1,0:T(8,128)(2,1)S(1)}, u32[]{:S(2)}, u32[]{:S(2)}) %collective-permute-start.1) | collective-permute-done | bytes 131104 | tf_op jit(solution)/shard_map/ppermute | solution.py:71
  7.0 3.0 %collective-permute-start.3 = (bf16[1,64,512]{2,1,0:T(8,128)(2,1)S(1)}, bf16[1,64,512]{2,1,0:T(8,128)(2,1)S(1)}, u32[]{:S(2)}, u32[]{:S(2)}) collective-permute-start(bf16[1,64,512]{2,1,0:T(8,128)(2,1)S(1)} %slice.65), channel_id=1, source_target_pairs={{0,192},{8,200},{16,208},{24,216},{32,224},{40,232},{48,240},{56,2... | collective-permute-start | bytes 196616 | tf_op jit(solution)/shard_map/ppermute | solution.py:71
  10.1 1.1 %copy.133 = bf16[1,2,64,512]{3,0,1,2:T(2,128)(2,1)S(1)} copy(bf16[1,2,64,512]{3,2,1,0:T(8,128)(2,1)} %bitcast.219) | data formatting | bytes 262144 | tf_op jit(solution)/shard_map/stack | solution.py:79
  11.6 0.5 collective-permute-done.2
  12.4 1.2 %pad_maximum_fusion = bf16[4,2,64,512]{3,0,1,2:T(4,128)(2,1)S(1)} fusion(bf16[1,2,64,512]{3,0,1,2:T(2,128)(2,1)S(1)} %copy.136, bf16[1,2,64,512]{3,0,1,2:T(2,128)(2,1)S(1)} %copy.135, bf16[1,2,64,512]{3,0,1,2:T(2,128)(2,1)S(1)} %copy.134, bf16[1,2,64,512]{3,0,1,2:T(2,128)(2,1)S(1)} %copy.133), kind=kLoop, calls=%fused_computation.24 | loop fusion | flops 2097152 | bytes 1048576 | tf_op jit(solution)/shard_map/stack | solution.py:79
  13.6 1.8 %collective-permute-start.5 = (bf16[4,2,64,512]{3,0,1,2:T(4,128)(2,1)S(1)}, bf16[4,2,64,512]{3,0,1,2:T(4,128)(2,1)S(1)}, u32[]{:S(2)}, u32[]{:S(2)}) collective-permute-start(bf16[4,2,64,512]{3,0,1,2:T(4,128)(2,1)S(1)} %pad_maximum_fusion), channel_id=1, source_target_pairs={{0,16},{8,24},{16,32},{24,40},{32,48},{40,56},{48,0},{56,8},{64,80... | collective-permute-start | bytes 1572872 | tf_op jit(solution)/shard_map/ppermute | solution.py:71
  16.2 0.6 fusion.46
  16.8 8.7 %collective-permute-done.5 = bf16[4,2,64,512]{3,0,1,2:T(4,128)(2,1)S(1)} collective-permute-done((bf16[4,2,64,512]{3,0,1,2:T(4,128)(2,1)S(1)}, bf16[4,2,64,512]{3,0,1,2:T(4,128)(2,1)S(1)}, u32[]{:S(2)}, u32[]{:S(2)}) %collective-permute-start.5) | collective-permute-done | bytes 524320 | tf_op jit(solution)/shard_map/ppermute | solution.py:71
  25.7 1.6 %collective-permute-start.6 = (bf16[2,2,64,512]{3,0,1,2:T(2,128)(2,1)S(1)}, bf16[2,2,64,512]{3,0,1,2:T(2,128)(2,1)S(1)}, u32[]{:S(2)}, u32[]{:S(2)}) collective-permute-start(bf16[2,2,64,512]{3,0,1,2:T(2,128)(2,1)S(1)} %slice.68), channel_id=1, source_target_pairs={{0,16},{8,24},{16,32},{24,40},{32,48},{40,56},{48,0},{56,8},{64,80... | collective-permute-start | bytes 786440 | tf_op jit(solution)/shard_map/ppermute | solution.py:71
  27.6 0.6 collective-permute-start.7
  28.2 0.5 collective-permute-start.11
  28.7 0.6 fusion.40
  29.3 0.6 fusion.44
  29.9 0.6 fusion.38
  30.5 1.6 %collective-permute-done.6 = bf16[2,2,64,512]{3,0,1,2:T(2,128)(2,1)S(1)} collective-permute-done((bf16[2,2,64,512]{3,0,1,2:T(2,128)(2,1)S(1)}, bf16[2,2,64,512]{3,0,1,2:T(2,128)(2,1)S(1)}, u32[]{:S(2)}, u32[]{:S(2)}) %collective-permute-start.6) | collective-permute-done | bytes 262176 | tf_op jit(solution)/shard_map/ppermute | solution.py:71
  32.1 3.1 %collective-permute-done.7 = bf16[2,2,64,512]{3,0,1,2:T(2,128)(2,1)S(1)} collective-permute-done((bf16[2,2,64,512]{3,0,1,2:T(2,128)(2,1)S(1)}, bf16[2,2,64,512]{3,0,1,2:T(2,128)(2,1)S(1)}, u32[]{:S(2)}, u32[]{:S(2)}) %collective-permute-start.7) | collective-permute-done | bytes 262176 | tf_op jit(solution)/shard_map/ppermute | solution.py:71
  35.2 0.5 pad_maximum_fusion.1
  35.9 1.0 fusion.42
  36.9 0.6 fusion.36
  37.8 0.6 fusion.34
  38.4 1.1 %fusion.9 = bf16[2,8,64,512]{3,1,0,2:T(8,128)(2,1)S(1)} fusion(bf16[4,2,64,512]{3,0,1,2:T(4,128)(2,1)S(1)} %collective-permute-done.11, f32[16,64,512,1]{2,0,3,1:T(8,128)S(1)} %fusion.34, f32[16,64,512,1]{2,0,3,1:T(8,128)S(1)} %fusion.36, f32[16,64,512,1]{2,0,3,1:T(8,128)S(1)} %fusion.38, f32[16,64,512,1]{2,0,3,1:T(8,128)S(1)} %fusion.40, ...), kind=kOutput, calls=%fused_computation.17 | convolution fusion | flops 12582912 | bytes 16253184 | tf_op jit(solution)/shard_map/kab,abrn->krn/dot_general | solution.py:92
  39.5 0.7 reshape.165
  40.2 8.4 %all-to-all-start = ((f32[8,1,128]{2,1,0:T(1,128)}), f32[8,1,128]{2,1,0:T(1,128)S(1)}, u32[]{:S(2)}, u32[]{:S(2)}) async-start(f32[8,1,128]{2,1,0:T(1,128)} %reshape.165), calls=%async_computation | async-start | bytes 8192 | tf_op jit(solution)/shard_map/all_to_all | solution.py:110
  48.6 6.7 %bitcast_convert_fusion = bf16[2,512,512]{2,1,0:T(8,128)(2,1)} fusion(bf16[8,512,512]{2,1,0:T(8,128)(2,1)} %param.12, s32[]{:T(128)S(6)} %select_n.109, bf16[8,512,512]{2,1,0:T(8,128)(2,1)} %param.13, bf16[2,8,64,512]{3,1,0,2:T(8,128)(2,1)S(1)} %fusion.9), kind=kOutput, calls=%fused_computation.2 | convolution fusion | flops 1074790400 | bytes 7340036 | tf_op jit(solution)/shard_map/tab,ktbc->kac/dot_general | solution.py:114
  55.3 0.9 all-to-all-done
  56.2 0.5 broadcast.165
  56.7 0.7 reduce.2
  57.6 3.6 %divide_convert_fusion = bf16[2,512,512]{2,1,0:T(8,128)(2,1)} fusion(bf16[2,512,512]{2,1,0:T(8,128)(2,1)S(1)} %copy-done, bf16[2,512,512]{2,1,0:T(8,128)(2,1)} %bitcast_convert_fusion, bf16[2,512,512]{2,1,0:T(8,128)(2,1)S(1)} %copy-done.3, f32[2,512]{1,0:T(2,128)S(1)} %copy-done.5, f32[2,512]{1,0:T(2,128)S(1)} %add.283), kind=kOutput, calls=%fused_computation.11 | convolution fusion | flops 1075838976 | bytes 4202496 | tf_op jit(solution)/shard_map/jrn,jmn->jrm/dot_general | solution.py:120
  61.2 2.0 %convolution_convert_fusion.1 = bf16[2,512,512]{1,2,0:T(8,128)(2,1)S(1)} fusion(bf16[2,512,512]{2,1,0:T(8,128)(2,1)} %divide_convert_fusion, bf16[2,512,512]{2,1,0:T(8,128)(2,1)S(1)} %copy-done.4), kind=kOutput, calls=%fused_computation.14 | convolution fusion | flops 537395200 | bytes 3145728 | tf_op jit(solution)/shard_map/jrm,jkm->jrk/dot_general | solution.py:122
  63.2 0.7 convolution_convert_fusion
  64.1 1.2 %collective-permute-start.12 = (bf16[2,512,64]{1,2,0:T(8,128)(2,1)S(1)}, bf16[2,512,64]{1,2,0:T(8,128)(2,1)S(1)}, u32[]{:S(2)}, u32[]{:S(2)}) collective-permute-start(bf16[2,512,64]{1,2,0:T(8,128)(2,1)S(1)} %get-tuple-element.7), channel_id=1, source_target_pairs={{0,1},{1,2},{2,3},{3,4},{4,5},{5,6},{6,7},{7,0},{8,9},{9,10},{10,1... | collective-permute-start | bytes 393224 | tf_op jit(solution)/shard_map/ppermute | solution.py:13
  65.2 2.4 %collective-permute-start.13 = (bf16[2,512,64]{1,2,0:T(8,128)(2,1)S(1)}, bf16[2,512,64]{1,2,0:T(8,128)(2,1)S(1)}, u32[]{:S(2)}, u32[]{:S(2)}) collective-permute-start(bf16[2,512,64]{1,2,0:T(8,128)(2,1)S(1)} %get-tuple-element.11), channel_id=1, source_target_pairs={{0,2},{1,3},{2,4},{3,5},{4,6},{5,7},{6,0},{7,1},{8,10},{9,11},{10,... | collective-permute-start | bytes 393224 | tf_op jit(solution)/shard_map/ppermute | solution.py:13
  67.6 2.7 %collective-permute-start.14 = (bf16[2,512,64]{1,2,0:T(8,128)(2,1)S(1)}, bf16[2,512,64]{1,2,0:T(8,128)(2,1)S(1)}, u32[]{:S(2)}, u32[]{:S(2)}) collective-permute-start(bf16[2,512,64]{1,2,0:T(8,128)(2,1)S(1)} %get-tuple-element.10), channel_id=1, source_target_pairs={{0,3},{1,4},{2,5},{3,6},{4,7},{5,0},{6,1},{7,2},{8,11},{9,12},{10,... | collective-permute-start | bytes 393224 | tf_op jit(solution)/shard_map/ppermute | solution.py:13
  70.3 2.4 %collective-permute-start.15 = (bf16[2,512,64]{1,2,0:T(8,128)(2,1)S(1)}, bf16[2,512,64]{1,2,0:T(8,128)(2,1)S(1)}, u32[]{:S(2)}, u32[]{:S(2)}) collective-permute-start(bf16[2,512,64]{1,2,0:T(8,128)(2,1)S(1)} %get-tuple-element.9), channel_id=1, source_target_pairs={{0,4},{1,5},{2,6},{3,7},{4,0},{5,1},{6,2},{7,3},{8,12},{9,13},{10,... | collective-permute-start | bytes 393224 | tf_op jit(solution)/shard_map/ppermute | solution.py:13
  72.6 2.7 %collective-permute-start.16 = (bf16[2,512,64]{1,2,0:T(8,128)(2,1)S(1)}, bf16[2,512,64]{1,2,0:T(8,128)(2,1)S(1)}, u32[]{:S(2)}, u32[]{:S(2)}) collective-permute-start(bf16[2,512,64]{1,2,0:T(8,128)(2,1)S(1)} %get-tuple-element.8), channel_id=1, source_target_pairs={{0,5},{1,6},{2,7},{3,0},{4,1},{5,2},{6,3},{7,4},{8,13},{9,14},{10,... | collective-permute-start | bytes 393224 | tf_op jit(solution)/shard_map/ppermute | solution.py:13
  75.3 3.6 %collective-permute-start.17 = (bf16[2,512,64]{1,2,0:T(8,128)(2,1)S(1)}, bf16[2,512,64]{1,2,0:T(8,128)(2,1)S(1)}, u32[]{:S(2)}, u32[]{:S(2)}) collective-permute-start(bf16[2,512,64]{1,2,0:T(8,128)(2,1)S(1)} %get-tuple-element.13), channel_id=1, source_target_pairs={{0,6},{1,7},{2,0},{3,1},{4,2},{5,3},{6,4},{7,5},{8,14},{9,15},{10,... | collective-permute-start | bytes 393224 | tf_op jit(solution)/shard_map/ppermute | solution.py:13
  78.9 1.3 %collective-permute-done.13 = bf16[2,512,64]{1,2,0:T(8,128)(2,1)S(1)} collective-permute-done((bf16[2,512,64]{1,2,0:T(8,128)(2,1)S(1)}, bf16[2,512,64]{1,2,0:T(8,128)(2,1)S(1)}, u32[]{:S(2)}, u32[]{:S(2)}) %collective-permute-start.13) | collective-permute-done | bytes 131104 | tf_op jit(solution)/shard_map/ppermute | solution.py:13
  80.1 2.8 %collective-permute-start.18 = (bf16[2,512,64]{1,2,0:T(8,128)(2,1)S(1)}, bf16[2,512,64]{1,2,0:T(8,128)(2,1)}, u32[]{:S(2)}, u32[]{:S(2)}) collective-permute-start(bf16[2,512,64]{1,2,0:T(8,128)(2,1)S(1)} %get-tuple-element.12), channel_id=1, source_target_pairs={{0,7},{1,0},{2,1},{3,2},{4,3},{5,4},{6,5},{7,6},{8,15},{9,8},{10,9... | collective-permute-start | bytes 393224 | tf_op jit(solution)/shard_map/ppermute | solution.py:13
  83.0 2.4 %collective-permute-done.14 = bf16[2,512,64]{1,2,0:T(8,128)(2,1)S(1)} collective-permute-done((bf16[2,512,64]{1,2,0:T(8,128)(2,1)S(1)}, bf16[2,512,64]{1,2,0:T(8,128)(2,1)S(1)}, u32[]{:S(2)}, u32[]{:S(2)}) %collective-permute-start.14) | collective-permute-done | bytes 131104 | tf_op jit(solution)/shard_map/ppermute | solution.py:13
  85.4 3.1 %collective-permute-done.15 = bf16[2,512,64]{1,2,0:T(8,128)(2,1)S(1)} collective-permute-done((bf16[2,512,64]{1,2,0:T(8,128)(2,1)S(1)}, bf16[2,512,64]{1,2,0:T(8,128)(2,1)S(1)}, u32[]{:S(2)}, u32[]{:S(2)}) %collective-permute-start.15) | collective-permute-done | bytes 131104 | tf_op jit(solution)/shard_map/ppermute | solution.py:13
  88.5 2.9 %collective-permute-done.16 = bf16[2,512,64]{1,2,0:T(8,128)(2,1)S(1)} collective-permute-done((bf16[2,512,64]{1,2,0:T(8,128)(2,1)S(1)}, bf16[2,512,64]{1,2,0:T(8,128)(2,1)S(1)}, u32[]{:S(2)}, u32[]{:S(2)}) %collective-permute-start.16) | collective-permute-done | bytes 131104 | tf_op jit(solution)/shard_map/ppermute | solution.py:13
  91.4 3.3 %collective-permute-done.17 = bf16[2,512,64]{1,2,0:T(8,128)(2,1)S(1)} collective-permute-done((bf16[2,512,64]{1,2,0:T(8,128)(2,1)S(1)}, bf16[2,512,64]{1,2,0:T(8,128)(2,1)S(1)}, u32[]{:S(2)}, u32[]{:S(2)}) %collective-permute-start.17) | collective-permute-done | bytes 131104 | tf_op jit(solution)/shard_map/ppermute | solution.py:13
  94.7 1.4 %collective-permute-done.18 = bf16[2,512,64]{1,2,0:T(8,128)(2,1)} collective-permute-done((bf16[2,512,64]{1,2,0:T(8,128)(2,1)S(1)}, bf16[2,512,64]{1,2,0:T(8,128)(2,1)}, u32[]{:S(2)}, u32[]{:S(2)}) %collective-permute-start.18) | collective-permute-done | bytes 131104 | tf_op jit(solution)/shard_map/ppermute | solution.py:13
  96.1 1.7 %fusion.24 = f32[2,512,64]{1,2,0:T(8,128)} fusion(bf16[2,512,64]{1,2,0:T(8,128)(2,1)} %collective-permute-done.18, bf16[2,512,64]{1,2,0:T(8,128)(2,1)S(1)} %collective-permute-done.17, bf16[2,512,64]{1,2,0:T(8,128)(2,1)S(1)} %collective-permute-done.16, bf16[2,512,64]{1,2,0:T(8,128)(2,1)S(1)} %collective-permute-done.15, ...), kind=kLoop, calls=%fused_computation.32 | loop fusion | flops 983040 | bytes 1310724 | tf_op jit(solution)/shard_map/add | solution.py:14
  (51 shorter events, 3.4 us)
Async XLA Ops:
  0.0 57.5 %copy-start = (bf16[2,512,512]{2,1,0:T(8,128)(2,1)S(1)}, bf16[2,512,512]{2,1,0:T(8,128)(2,1)}, u32[]{:S(2)}) copy-start(bf16[2,512,512]{2,1,0:T(8,128)(2,1)} %param.19) | copy-start | bytes 3145732
  0.0 6.7 %collective-permute-start.1 = (bf16[2,64,512]{2,1,0:T(8,128)(2,1)}, bf16[2,64,512]{2,1,0:T(8,128)(2,1)S(1)}, u32[]{:S(2)}, u32[]{:S(2)}) collective-permute-start(bf16[2,64,512]{2,1,0:T(8,128)(2,1)} %param.11), channel_id=1, source_target_pairs={{0,64},{8,72},{16,80},{24,88},{32,96},{40,104},{48,112},{56,120},{... | collective-permute-start | bytes 393224 | tf_op jit(solution)/shard_map/ppermute | solution.py:71
  1.5 5.5 %collective-permute-start = (bf16[2,64,512]{2,1,0:T(8,128)(2,1)}, bf16[2,64,512]{2,1,0:T(8,128)(2,1)S(1)}, u32[]{:S(2)}, u32[]{:S(2)}) collective-permute-start(bf16[2,64,512]{2,1,0:T(8,128)(2,1)} %param.11), channel_id=1, source_target_pairs={{0,192},{8,200},{16,208},{24,216},{32,224},{40,232},{48,240},{56,2... | collective-permute-start | bytes 393224 | tf_op jit(solution)/shard_map/ppermute | solution.py:71
  6.7 5.5 %collective-permute-start.2 = (bf16[1,64,512]{2,1,0:T(8,128)(2,1)S(1)}, bf16[1,64,512]{2,1,0:T(8,128)(2,1)S(1)}, u32[]{:S(2)}, u32[]{:S(2)}) collective-permute-start(bf16[1,64,512]{2,1,0:T(8,128)(2,1)S(1)} %slice.64), channel_id=1, source_target_pairs={{0,64},{8,72},{16,80},{24,88},{32,96},{40,104},{48,112},{56,120},{... | collective-permute-start | bytes 196616 | tf_op jit(solution)/shard_map/ppermute | solution.py:71
  7.0 5.2 %collective-permute-start.3 = (bf16[1,64,512]{2,1,0:T(8,128)(2,1)S(1)}, bf16[1,64,512]{2,1,0:T(8,128)(2,1)S(1)}, u32[]{:S(2)}, u32[]{:S(2)}) collective-permute-start(bf16[1,64,512]{2,1,0:T(8,128)(2,1)S(1)} %slice.65), channel_id=1, source_target_pairs={{0,192},{8,200},{16,208},{24,216},{32,224},{40,232},{48,240},{56,2... | collective-permute-start | bytes 196616 | tf_op jit(solution)/shard_map/ppermute | solution.py:71
  13.6 11.9 %collective-permute-start.5 = (bf16[4,2,64,512]{3,0,1,2:T(4,128)(2,1)S(1)}, bf16[4,2,64,512]{3,0,1,2:T(4,128)(2,1)S(1)}, u32[]{:S(2)}, u32[]{:S(2)}) collective-permute-start(bf16[4,2,64,512]{3,0,1,2:T(4,128)(2,1)S(1)} %pad_maximum_fusion), channel_id=1, source_target_pairs={{0,16},{8,24},{16,32},{24,40},{32,48},{40,56},{48,0},{56,8},{64,80... | collective-permute-start | bytes 1572872 | tf_op jit(solution)/shard_map/ppermute | solution.py:71
  15.4 11.9 %collective-permute-start.4 = (bf16[4,2,64,512]{3,0,1,2:T(4,128)(2,1)S(1)}, bf16[4,2,64,512]{3,0,1,2:T(4,128)(2,1)S(1)}, u32[]{:S(2)}, u32[]{:S(2)}) collective-permute-start(bf16[4,2,64,512]{3,0,1,2:T(4,128)(2,1)S(1)} %pad_maximum_fusion), channel_id=1, source_target_pairs={{0,48},{8,56},{16,0},{24,8},{32,16},{40,24},{48,32},{56,40},{64,11... | collective-permute-start | bytes 1572872 | tf_op jit(solution)/shard_map/ppermute | solution.py:71
  16.1 13.8 %collective-permute-start.8 = (bf16[4,2,64,512]{3,0,1,2:T(4,128)(2,1)S(1)}, bf16[4,2,64,512]{3,0,1,2:T(4,128)(2,1)S(1)}, u32[]{:S(2)}, u32[]{:S(2)}) collective-permute-start(bf16[4,2,64,512]{3,0,1,2:T(4,128)(2,1)S(1)} %pad_maximum_fusion), channel_id=1, source_target_pairs={{0,8},{8,0},{16,24},{24,16},{32,40},{40,32},{48,56},{56,48},{64,72... | collective-permute-start | bytes 1572872 | tf_op jit(solution)/shard_map/ppermute | solution.py:71
  25.7 6.4 %collective-permute-start.6 = (bf16[2,2,64,512]{3,0,1,2:T(2,128)(2,1)S(1)}, bf16[2,2,64,512]{3,0,1,2:T(2,128)(2,1)S(1)}, u32[]{:S(2)}, u32[]{:S(2)}) collective-permute-start(bf16[2,2,64,512]{3,0,1,2:T(2,128)(2,1)S(1)} %slice.68), channel_id=1, source_target_pairs={{0,16},{8,24},{16,32},{24,40},{32,48},{40,56},{48,0},{56,8},{64,80... | collective-permute-start | bytes 786440 | tf_op jit(solution)/shard_map/ppermute | solution.py:71
  27.6 7.7 %collective-permute-start.7 = (bf16[2,2,64,512]{3,0,1,2:T(2,128)(2,1)S(1)}, bf16[2,2,64,512]{3,0,1,2:T(2,128)(2,1)S(1)}, u32[]{:S(2)}, u32[]{:S(2)}) collective-permute-start(bf16[2,2,64,512]{3,0,1,2:T(2,128)(2,1)S(1)} %slice.69), channel_id=1, source_target_pairs={{0,48},{8,56},{16,0},{24,8},{32,16},{40,24},{48,32},{56,40},{64,11... | collective-permute-start | bytes 786440 | tf_op jit(solution)/shard_map/ppermute | solution.py:71
  28.2 8.7 %collective-permute-start.9 = (bf16[4,2,64,512]{3,0,1,2:T(4,128)(2,1)S(1)}, bf16[4,2,64,512]{3,0,1,2:T(4,128)(2,1)S(1)}, u32[]{:S(2)}, u32[]{:S(2)}) collective-permute-start(bf16[4,2,64,512]{3,0,1,2:T(4,128)(2,1)S(1)} %collective-permute-done.4), channel_id=1, source_target_pairs={{0,8},{8,0},{16,24},{24,16},{32,40},{40,32},{48,56},{56,48},{64,72... | collective-permute-start | bytes 1572872 | tf_op jit(solution)/shard_map/ppermute | solution.py:71
  28.2 10.2 %collective-permute-start.11 = (bf16[4,2,64,512]{3,0,1,2:T(4,128)(2,1)S(1)}, bf16[4,2,64,512]{3,0,1,2:T(4,128)(2,1)S(1)}, u32[]{:S(2)}, u32[]{:S(2)}) collective-permute-start(bf16[4,2,64,512]{3,0,1,2:T(4,128)(2,1)S(1)} %collective-permute-done.5), channel_id=1, source_target_pairs={{0,8},{8,0},{16,24},{24,16},{32,40},{40,32},{48,56},{56,48},{64,72... | collective-permute-start | bytes 1572872 | tf_op jit(solution)/shard_map/ppermute | solution.py:71
  35.8 2.0 %collective-permute-start.10 = (bf16[4,2,64,512]{3,0,1,2:T(4,128)(2,1)S(1)}, bf16[4,2,64,512]{3,0,1,2:T(4,128)(2,1)S(1)}, u32[]{:S(2)}, u32[]{:S(2)}) collective-permute-start(bf16[4,2,64,512]{3,0,1,2:T(4,128)(2,1)S(1)} %pad_maximum_fusion.1), channel_id=1, source_target_pairs={{0,8},{8,0},{16,24},{24,16},{32,40},{40,32},{48,56},{56,48},{64,72... | collective-permute-start | bytes 1572872 | tf_op jit(solution)/shard_map/ppermute | solution.py:71
  38.4 1.1 %copy-start.2 = (f32[2,64]{1,0:T(2,128)S(1)}, f32[2,64]{1,0:T(2,128)}, u32[]{:S(2)}) copy-start(f32[2,64]{1,0:T(2,128)} %param.20) | copy-start | bytes 1540
  40.2 16.0 %all-to-all-start = ((f32[8,1,128]{2,1,0:T(1,128)}), f32[8,1,128]{2,1,0:T(1,128)S(1)}, u32[]{:S(2)}, u32[]{:S(2)}) async-start(f32[8,1,128]{2,1,0:T(1,128)} %reshape.165), calls=%async_computation | async-start | bytes 8192 | tf_op jit(solution)/shard_map/all_to_all | solution.py:110
  48.6 8.9 %copy-start.3 = (bf16[2,512,512]{2,1,0:T(8,128)(2,1)S(1)}, bf16[2,512,512]{2,1,0:T(8,128)(2,1)}, u32[]{:S(2)}) copy-start(bf16[2,512,512]{2,1,0:T(8,128)(2,1)} %param.17) | copy-start | bytes 3145732
  48.6 8.9 %copy-start.5 = (f32[2,512]{1,0:T(2,128)S(1)}, f32[2,512]{1,0:T(2,128)}, u32[]{:S(2)}) copy-start(f32[2,512]{1,0:T(2,128)} %param.21) | copy-start | bytes 12292
  57.5 3.6 %copy-start.4 = (bf16[2,512,512]{2,1,0:T(8,128)(2,1)S(1)}, bf16[2,512,512]{2,1,0:T(8,128)(2,1)}, u32[]{:S(2)}) copy-start(bf16[2,512,512]{2,1,0:T(8,128)(2,1)} %param.18) | copy-start | bytes 3145732
  61.2 2.1 %copy-start.1 = (bf16[2,512,512]{2,1,0:T(8,128)(2,1)S(1)}, bf16[2,512,512]{2,1,0:T(8,128)(2,1)}, u32[]{:S(2)}) copy-start(bf16[2,512,512]{2,1,0:T(8,128)(2,1)} %param.16) | copy-start | bytes 3145732
  64.1 11.2 %collective-permute-start.12 = (bf16[2,512,64]{1,2,0:T(8,128)(2,1)S(1)}, bf16[2,512,64]{1,2,0:T(8,128)(2,1)S(1)}, u32[]{:S(2)}, u32[]{:S(2)}) collective-permute-start(bf16[2,512,64]{1,2,0:T(8,128)(2,1)S(1)} %get-tuple-element.7), channel_id=1, source_target_pairs={{0,1},{1,2},{2,3},{3,4},{4,5},{5,6},{6,7},{7,0},{8,9},{9,10},{10,1... | collective-permute-start | bytes 393224 | tf_op jit(solution)/shard_map/ppermute | solution.py:13
  65.2 14.9 %collective-permute-start.13 = (bf16[2,512,64]{1,2,0:T(8,128)(2,1)S(1)}, bf16[2,512,64]{1,2,0:T(8,128)(2,1)S(1)}, u32[]{:S(2)}, u32[]{:S(2)}) collective-permute-start(bf16[2,512,64]{1,2,0:T(8,128)(2,1)S(1)} %get-tuple-element.11), channel_id=1, source_target_pairs={{0,2},{1,3},{2,4},{3,5},{4,6},{5,7},{6,0},{7,1},{8,10},{9,11},{10,... | collective-permute-start | bytes 393224 | tf_op jit(solution)/shard_map/ppermute | solution.py:13
  67.6 17.8 %collective-permute-start.14 = (bf16[2,512,64]{1,2,0:T(8,128)(2,1)S(1)}, bf16[2,512,64]{1,2,0:T(8,128)(2,1)S(1)}, u32[]{:S(2)}, u32[]{:S(2)}) collective-permute-start(bf16[2,512,64]{1,2,0:T(8,128)(2,1)S(1)} %get-tuple-element.10), channel_id=1, source_target_pairs={{0,3},{1,4},{2,5},{3,6},{4,7},{5,0},{6,1},{7,2},{8,11},{9,12},{10,... | collective-permute-start | bytes 393224 | tf_op jit(solution)/shard_map/ppermute | solution.py:13
  70.3 18.3 %collective-permute-start.15 = (bf16[2,512,64]{1,2,0:T(8,128)(2,1)S(1)}, bf16[2,512,64]{1,2,0:T(8,128)(2,1)S(1)}, u32[]{:S(2)}, u32[]{:S(2)}) collective-permute-start(bf16[2,512,64]{1,2,0:T(8,128)(2,1)S(1)} %get-tuple-element.9), channel_id=1, source_target_pairs={{0,4},{1,5},{2,6},{3,7},{4,0},{5,1},{6,2},{7,3},{8,12},{9,13},{10,... | collective-permute-start | bytes 393224 | tf_op jit(solution)/shard_map/ppermute | solution.py:13
  72.6 18.8 %collective-permute-start.16 = (bf16[2,512,64]{1,2,0:T(8,128)(2,1)S(1)}, bf16[2,512,64]{1,2,0:T(8,128)(2,1)S(1)}, u32[]{:S(2)}, u32[]{:S(2)}) collective-permute-start(bf16[2,512,64]{1,2,0:T(8,128)(2,1)S(1)} %get-tuple-element.8), channel_id=1, source_target_pairs={{0,5},{1,6},{2,7},{3,0},{4,1},{5,2},{6,3},{7,4},{8,13},{9,14},{10,... | collective-permute-start | bytes 393224 | tf_op jit(solution)/shard_map/ppermute | solution.py:13
  75.3 19.4 %collective-permute-start.17 = (bf16[2,512,64]{1,2,0:T(8,128)(2,1)S(1)}, bf16[2,512,64]{1,2,0:T(8,128)(2,1)S(1)}, u32[]{:S(2)}, u32[]{:S(2)}) collective-permute-start(bf16[2,512,64]{1,2,0:T(8,128)(2,1)S(1)} %get-tuple-element.13), channel_id=1, source_target_pairs={{0,6},{1,7},{2,0},{3,1},{4,2},{5,3},{6,4},{7,5},{8,14},{9,15},{10,... | collective-permute-start | bytes 393224 | tf_op jit(solution)/shard_map/ppermute | solution.py:13
  80.1 15.9 %collective-permute-start.18 = (bf16[2,512,64]{1,2,0:T(8,128)(2,1)S(1)}, bf16[2,512,64]{1,2,0:T(8,128)(2,1)}, u32[]{:S(2)}, u32[]{:S(2)}) collective-permute-start(bf16[2,512,64]{1,2,0:T(8,128)(2,1)S(1)} %get-tuple-element.12), channel_id=1, source_target_pairs={{0,7},{1,0},{2,1},{3,2},{4,3},{5,4},{6,5},{7,6},{8,15},{9,8},{10,9... | collective-permute-start | bytes 393224 | tf_op jit(solution)/shard_map/ppermute | solution.py:13

commit v12 on v11

--- a/solution.py
+++ b/solution.py
@@ -106,7 +106,7 @@
         "ktrn,tmn->ktrm", pooled, right_factor, preferred_element_type=jnp.float32
     ).astype(jnp.bfloat16)
     left_part = lax.dynamic_slice_in_dim(left_factor, part * row_count, row_count, axis=2)
-    rates_run, pooled = lax.optimization_barrier((left_rates[None], pooled))
+    rates_run = left_rates[None]
     rates_parts = lax.all_to_all(
         jnp.broadcast_to(rates_run, (pieces,) + left_rates.shape), "sub", 0, 0, tiled=True
     )

time: 99.2 us -> 98.2 us (0.990)
  waiting for transfers between devices: 30.5 us -> 27.9 us
    ppermute x12, waiting for transfers between devices: 15.2 us -> 13 us  [move(): return lax.ppermute(piece, 'blk', pairs_list)]
  transfers between devices with their start and end apart: 20 -> 20, of which waited for: 13 -> 10; matrix products, arithmetic and copies ran while one was open for 17% -> 15% of each run, Pallas kernels for 0% -> 0%
where the time goes in v12:
time: 98.2 us; the launch traced here: 96.9 us
  starting transfers between devices  38.1 us (39%)
  waiting for transfers between devices  27.9 us (28%)
  matrix products  19.2 us (20%)
  local copies, waits for them, and re-layouts  6.66 us (7%)
  other arithmetic  4.52 us (5%)
    ppermute x7, starting transfers between devices, scatter_sum(): got = lax.ppermute(send, axis, [(j, (j + k) % n) for j in range(n)])  18.1 us
    ppermute x7, waiting for transfers between devices, scatter_sum(): got = lax.ppermute(send, axis, [(j, (j + k) % n) for j in range(n)])  15 us
    ppermute x12, waiting for transfers between devices, move(): return lax.ppermute(piece, 'blk', pairs_list)  13 us
    ppermute x12, starting transfers between devices, move(): return lax.ppermute(piece, 'blk', pairs_list)  11.5 us
    all_to_all x1, starting transfers between devices, local(): lax.all_to_all(jnp.broadcast_to(rates_run, (pieces,) + left_rates.shape),...  8.47 us
    dot_general x1, matrix products, local(): jnp.einsum('tab,ktbc->kac', left_part, right_done, preferred_element_type...  6.6 us
    dot_general x8, matrix products, pool(): jnp.einsum('kab,abrn->krn', w, piece, preferred_element_type=jnp.float32)  5.74 us
    dot_general x1, matrix products, local(): jnp.einsum('jrn,jmn->jrm', dual_cols, right_dual, preferred_element_type=...  3.91 us
  transfers between devices with their start and end apart: 20, of which 10 were waited for; matrix products, arithmetic and copies ran while one was open for 15% of the time, Pallas kernels for 0%

profile of v12, /device:TPU:24, one launch (start us, length us, event | category | flops | bytes accessed | tf_op | source)
XLA Modules:
  0.0 96.9 jit_solution(5705718942813187155)
XLA Ops:
  0.0 1.5 %collective-permute-start.1 = (bf16[2,64,512]{2,1,0:T(8,128)(2,1)}, bf16[2,64,512]{2,1,0:T(8,128)(2,1)S(1)}, u32[]{:S(2)}, u32[]{:S(2)}) collective-permute-start(bf16[2,64,512]{2,1,0:T(8,128)(2,1)} %param.11), channel_id=1, source_target_pairs={{0,64},{8,72},{16,80},{24,88},{32,96},{40,104},{48,112},{56,120},{... | collective-permute-start | bytes 393224 | tf_op jit(solution)/shard_map/ppermute | solution.py:71
  1.5 1.7 %collective-permute-start = (bf16[2,64,512]{2,1,0:T(8,128)(2,1)}, bf16[2,64,512]{2,1,0:T(8,128)(2,1)S(1)}, u32[]{:S(2)}, u32[]{:S(2)}) collective-permute-start(bf16[2,64,512]{2,1,0:T(8,128)(2,1)} %param.11), channel_id=1, source_target_pairs={{0,192},{8,200},{16,208},{24,216},{32,224},{40,232},{48,240},{56,2... | collective-permute-start | bytes 393224 | tf_op jit(solution)/shard_map/ppermute | solution.py:71
  3.2 0.7 broadcast_in_dim.2
  3.9 0.7 reshape.166
  4.6 8.5 %all-to-all-start = ((f32[8,1,128]{2,1,0:T(1,128)}), f32[8,1,128]{2,1,0:T(1,128)S(1)}, u32[]{:S(2)}, u32[]{:S(2)}) async-start(f32[8,1,128]{2,1,0:T(1,128)} %reshape.166), calls=%async_computation | async-start | bytes 8192 | tf_op jit(solution)/shard_map/all_to_all | solution.py:110
  13.4 1.1 %constant_dynamic-slice_fusion = s32[32,1,2,3]{1,2,3,0:T(2,128)S(1)} fusion(s32[32,32,2,3]{1,2,3,0:T(2,128)} %param.14, s32[]{:T(128)S(6)} %select_n.102), kind=kLoop, calls=%fused_computation.53 | loop fusion | bytes 1540 | tf_op jit(solution)/shard_map/jit(dynamic_index_in_dim)/dynamic_slice | solution.py:42
  14.6 0.9 dynamic-slice_reduce_fusion
  15.5 0.4 collective-permute-start.2
  15.9 3.0 %collective-permute-start.3 = (bf16[1,64,512]{2,1,0:T(8,128)(2,1)S(1)}, bf16[1,64,512]{2,1,0:T(8,128)(2,1)S(1)}, u32[]{:S(2)}, u32[]{:S(2)}) collective-permute-start(bf16[1,64,512]{2,1,0:T(8,128)(2,1)S(1)} %slice.65), channel_id=1, source_target_pairs={{0,192},{8,200},{16,208},{24,216},{32,224},{40,232},{48,240},{56,2... | collective-permute-start | bytes 196616 | tf_op jit(solution)/shard_map/ppermute | solution.py:71
  19.1 1.1 %copy.133 = bf16[1,2,64,512]{3,0,1,2:T(2,128)(2,1)S(1)} copy(bf16[1,2,64,512]{3,2,1,0:T(8,128)(2,1)} %bitcast.217) | data formatting | bytes 262144 | tf_op jit(solution)/shard_map/stack | solution.py:79
  20.6 0.5 collective-permute-done.2
  21.3 1.2 %pad_maximum_fusion = bf16[4,2,64,512]{3,0,1,2:T(4,128)(2,1)S(1)} fusion(bf16[1,2,64,512]{3,0,1,2:T(2,128)(2,1)S(1)} %copy.136, bf16[1,2,64,512]{3,0,1,2:T(2,128)(2,1)S(1)} %copy.135, bf16[1,2,64,512]{3,0,1,2:T(2,128)(2,1)S(1)} %copy.134, bf16[1,2,64,512]{3,0,1,2:T(2,128)(2,1)S(1)} %copy.133), kind=kLoop, calls=%fused_computation.24 | loop fusion | flops 2097152 | bytes 1048576 | tf_op jit(solution)/shard_map/stack | solution.py:79
  22.6 0.3 collective-permute-start.5
  22.9 1.8 %collective-permute-start.4 = (bf16[4,2,64,512]{3,0,1,2:T(4,128)(2,1)S(1)}, bf16[4,2,64,512]{3,0,1,2:T(4,128)(2,1)S(1)}, u32[]{:S(2)}, u32[]{:S(2)}) collective-permute-start(bf16[4,2,64,512]{3,0,1,2:T(4,128)(2,1)S(1)} %pad_maximum_fusion), channel_id=1, source_target_pairs={{0,48},{8,56},{16,0},{24,8},{32,16},{40,24},{48,32},{56,40},{64,11... | collective-permute-start | bytes 1572872 | tf_op jit(solution)/shard_map/ppermute | solution.py:71
  25.1 0.5 broadcast.166
  25.6 0.7 reduce.2
  26.5 0.6 fusion.46
  27.1 7.5 %collective-permute-done.5 = bf16[4,2,64,512]{3,0,1,2:T(4,128)(2,1)S(1)} collective-permute-done((bf16[4,2,64,512]{3,0,1,2:T(4,128)(2,1)S(1)}, bf16[4,2,64,512]{3,0,1,2:T(4,128)(2,1)S(1)}, u32[]{:S(2)}, u32[]{:S(2)}) %collective-permute-start.5) | collective-permute-done | bytes 524320 | tf_op jit(solution)/shard_map/ppermute | solution.py:71
  34.8 1.6 %collective-permute-start.6 = (bf16[2,2,64,512]{3,0,1,2:T(2,128)(2,1)S(1)}, bf16[2,2,64,512]{3,0,1,2:T(2,128)(2,1)S(1)}, u32[]{:S(2)}, u32[]{:S(2)}) collective-permute-start(bf16[2,2,64,512]{3,0,1,2:T(2,128)(2,1)S(1)} %slice.68), channel_id=1, source_target_pairs={{0,16},{8,24},{16,32},{24,40},{32,48},{40,56},{48,0},{56,8},{64,80... | collective-permute-start | bytes 786440 | tf_op jit(solution)/shard_map/ppermute | solution.py:71
  36.7 0.6 collective-permute-start.7
  37.3 0.5 collective-permute-start.11
  37.8 0.6 fusion.40
  38.4 0.6 fusion.44
  39.1 0.6 fusion.38
  39.7 1.6 %collective-permute-done.6 = bf16[2,2,64,512]{3,0,1,2:T(2,128)(2,1)S(1)} collective-permute-done((bf16[2,2,64,512]{3,0,1,2:T(2,128)(2,1)S(1)}, bf16[2,2,64,512]{3,0,1,2:T(2,128)(2,1)S(1)}, u32[]{:S(2)}, u32[]{:S(2)}) %collective-permute-start.6) | collective-permute-done | bytes 262176 | tf_op jit(solution)/shard_map/ppermute | solution.py:71
  41.2 3.1 %collective-permute-done.7 = bf16[2,2,64,512]{3,0,1,2:T(2,128)(2,1)S(1)} collective-permute-done((bf16[2,2,64,512]{3,0,1,2:T(2,128)(2,1)S(1)}, bf16[2,2,64,512]{3,0,1,2:T(2,128)(2,1)S(1)}, u32[]{:S(2)}, u32[]{:S(2)}) %collective-permute-start.7) | collective-permute-done | bytes 262176 | tf_op jit(solution)/shard_map/ppermute | solution.py:71
  44.3 0.5 pad_maximum_fusion.1
  45.0 1.0 %fusion.42 = f32[16,64,512,1]{2,0,3,1:T(8,128)S(1)} fusion(bf16[16,1,1,4,2]{0,4,3,2,1:T(2,128)(2,1)S(1)} %get-tuple-element.17, bf16[2,2,64,512]{3,0,1,2:T(2,128)(2,1)S(1)} %collective-permute-done.7, bf16[2,2,64,512]{3,0,1,2:T(2,128)(2,1)S(1)} %collective-permute-done.6), kind=kOutput, calls=%fused_computation.67 | convolution fusion | flops 9437184 | bytes 2621696 | tf_op jit(solution)/shard_map/kab,abrn->krn/dot_general | solution.py:92
  46.0 0.6 fusion.36
  46.9 0.6 fusion.34
  47.5 1.1 %fusion.9 = bf16[2,8,64,512]{3,1,0,2:T(8,128)(2,1)S(1)} fusion(bf16[4,2,64,512]{3,0,1,2:T(4,128)(2,1)S(1)} %collective-permute-done.11, f32[16,64,512,1]{2,0,3,1:T(8,128)S(1)} %fusion.34, f32[16,64,512,1]{2,0,3,1:T(8,128)S(1)} %fusion.36, f32[16,64,512,1]{2,0,3,1:T(8,128)S(1)} %fusion.38, f32[16,64,512,1]{2,0,3,1:T(8,128)S(1)} %fusion.40, ...), kind=kOutput, calls=%fused_computation.17 | convolution fusion | flops 12582912 | bytes 16253184 | tf_op jit(solution)/shard_map/kab,abrn->krn/dot_general | solution.py:92
  48.6 6.6 %bitcast_convert_fusion = bf16[2,512,512]{2,1,0:T(8,128)(2,1)} fusion(bf16[8,512,512]{2,1,0:T(8,128)(2,1)} %param.12, s32[]{:T(128)S(6)} %select_n.109, bf16[8,512,512]{2,1,0:T(8,128)(2,1)} %param.13, bf16[2,8,64,512]{3,1,0,2:T(8,128)(2,1)S(1)} %fusion.9), kind=kOutput, calls=%fused_computation.2 | convolution fusion | flops 1074790400 | bytes 7340036 | tf_op jit(solution)/shard_map/tab,ktbc->kac/dot_general | solution.py:114
  55.2 3.9 %divide_convert_fusion = bf16[2,512,512]{2,1,0:T(8,128)(2,1)} fusion(bf16[2,512,512]{2,1,0:T(8,128)(2,1)S(1)} %copy-done, bf16[2,512,512]{2,1,0:T(8,128)(2,1)} %bitcast_convert_fusion, bf16[2,512,512]{2,1,0:T(8,128)(2,1)} %param.17, f32[2,512]{1,0:T(2,128)S(1)} %copy-done.3, f32[2,512]{1,0:T(2,128)S(1)} %add.283), kind=kOutput, calls=%fused_computation.11 | convolution fusion | flops 1075838976 | bytes 4202496 | tf_op jit(solution)/shard_map/jrn,jmn->jrm/dot_general | solution.py:120
  59.1 2.1 %convolution_convert_fusion.1 = bf16[2,512,512]{1,2,0:T(8,128)(2,1)S(1)} fusion(bf16[2,512,512]{2,1,0:T(8,128)(2,1)} %divide_convert_fusion, bf16[2,512,512]{2,1,0:T(8,128)(2,1)S(1)} %copy-done.2), kind=kOutput, calls=%fused_computation.14 | convolution fusion | flops 537395200 | bytes 3145728 | tf_op jit(solution)/shard_map/jrm,jkm->jrk/dot_general | solution.py:122
  61.2 0.7 convolution_convert_fusion
  62.0 1.8 %collective-permute-start.12 = (bf16[2,512,64]{1,2,0:T(8,128)(2,1)S(1)}, bf16[2,512,64]{1,2,0:T(8,128)(2,1)S(1)}, u32[]{:S(2)}, u32[]{:S(2)}) collective-permute-start(bf16[2,512,64]{1,2,0:T(8,128)(2,1)S(1)} %get-tuple-element.5), channel_id=1, source_target_pairs={{0,1},{1,2},{2,3},{3,4},{4,5},{5,6},{6,7},{7,0},{8,9},{9,10},{10,1... | collective-permute-start | bytes 393224 | tf_op jit(solution)/shard_map/ppermute | solution.py:13
  63.8 2.2 %collective-permute-start.13 = (bf16[2,512,64]{1,2,0:T(8,128)(2,1)S(1)}, bf16[2,512,64]{1,2,0:T(8,128)(2,1)S(1)}, u32[]{:S(2)}, u32[]{:S(2)}) collective-permute-start(bf16[2,512,64]{1,2,0:T(8,128)(2,1)S(1)} %get-tuple-element.9), channel_id=1, source_target_pairs={{0,2},{1,3},{2,4},{3,5},{4,6},{5,7},{6,0},{7,1},{8,10},{9,11},{10,... | collective-permute-start | bytes 393224 | tf_op jit(solution)/shard_map/ppermute | solution.py:13
  66.0 2.7 %collective-permute-start.14 = (bf16[2,512,64]{1,2,0:T(8,128)(2,1)S(1)}, bf16[2,512,64]{1,2,0:T(8,128)(2,1)S(1)}, u32[]{:S(2)}, u32[]{:S(2)}) collective-permute-start(bf16[2,512,64]{1,2,0:T(8,128)(2,1)S(1)} %get-tuple-element.8), channel_id=1, source_target_pairs={{0,3},{1,4},{2,5},{3,6},{4,7},{5,0},{6,1},{7,2},{8,11},{9,12},{10,... | collective-permute-start | bytes 393224 | tf_op jit(solution)/shard_map/ppermute | solution.py:13
  68.7 2.4 %collective-permute-start.15 = (bf16[2,512,64]{1,2,0:T(8,128)(2,1)S(1)}, bf16[2,512,64]{1,2,0:T(8,128)(2,1)S(1)}, u32[]{:S(2)}, u32[]{:S(2)}) collective-permute-start(bf16[2,512,64]{1,2,0:T(8,128)(2,1)S(1)} %get-tuple-element.7), channel_id=1, source_target_pairs={{0,4},{1,5},{2,6},{3,7},{4,0},{5,1},{6,2},{7,3},{8,12},{9,13},{10,... | collective-permute-start | bytes 393224 | tf_op jit(solution)/shard_map/ppermute | solution.py:13
  71.0 2.7 %collective-permute-start.16 = (bf16[2,512,64]{1,2,0:T(8,128)(2,1)S(1)}, bf16[2,512,64]{1,2,0:T(8,128)(2,1)S(1)}, u32[]{:S(2)}, u32[]{:S(2)}) collective-permute-start(bf16[2,512,64]{1,2,0:T(8,128)(2,1)S(1)} %get-tuple-element.6), channel_id=1, source_target_pairs={{0,5},{1,6},{2,7},{3,0},{4,1},{5,2},{6,3},{7,4},{8,13},{9,14},{10,... | collective-permute-start | bytes 393224 | tf_op jit(solution)/shard_map/ppermute | solution.py:13
  73.7 3.6 %collective-permute-start.17 = (bf16[2,512,64]{1,2,0:T(8,128)(2,1)S(1)}, bf16[2,512,64]{1,2,0:T(8,128)(2,1)S(1)}, u32[]{:S(2)}, u32[]{:S(2)}) collective-permute-start(bf16[2,512,64]{1,2,0:T(8,128)(2,1)S(1)} %get-tuple-element.11), channel_id=1, source_target_pairs={{0,6},{1,7},{2,0},{3,1},{4,2},{5,3},{6,4},{7,5},{8,14},{9,15},{10,... | collective-permute-start | bytes 393224 | tf_op jit(solution)/shard_map/ppermute | solution.py:13
  77.3 2.9 %collective-permute-start.18 = (bf16[2,512,64]{1,2,0:T(8,128)(2,1)S(1)}, bf16[2,512,64]{1,2,0:T(8,128)(2,1)}, u32[]{:S(2)}, u32[]{:S(2)}) collective-permute-start(bf16[2,512,64]{1,2,0:T(8,128)(2,1)S(1)} %get-tuple-element.10), channel_id=1, source_target_pairs={{0,7},{1,0},{2,1},{3,2},{4,3},{5,4},{6,5},{7,6},{8,15},{9,8},{10,9... | collective-permute-start | bytes 393224 | tf_op jit(solution)/shard_map/ppermute | solution.py:13
  80.1 2.6 %collective-permute-done.14 = bf16[2,512,64]{1,2,0:T(8,128)(2,1)S(1)} collective-permute-done((bf16[2,512,64]{1,2,0:T(8,128)(2,1)S(1)}, bf16[2,512,64]{1,2,0:T(8,128)(2,1)S(1)}, u32[]{:S(2)}, u32[]{:S(2)}) %collective-permute-start.14) | collective-permute-done | bytes 131104 | tf_op jit(solution)/shard_map/ppermute | solution.py:13
  82.8 4.7 %collective-permute-done.15 = bf16[2,512,64]{1,2,0:T(8,128)(2,1)S(1)} collective-permute-done((bf16[2,512,64]{1,2,0:T(8,128)(2,1)S(1)}, bf16[2,512,64]{1,2,0:T(8,128)(2,1)S(1)}, u32[]{:S(2)}, u32[]{:S(2)}) %collective-permute-start.15) | collective-permute-done | bytes 131104 | tf_op jit(solution)/shard_map/ppermute | solution.py:13
  87.5 1.8 %collective-permute-done.16 = bf16[2,512,64]{1,2,0:T(8,128)(2,1)S(1)} collective-permute-done((bf16[2,512,64]{1,2,0:T(8,128)(2,1)S(1)}, bf16[2,512,64]{1,2,0:T(8,128)(2,1)S(1)}, u32[]{:S(2)}, u32[]{:S(2)}) %collective-permute-start.16) | collective-permute-done | bytes 131104 | tf_op jit(solution)/shard_map/ppermute | solution.py:13
  89.3 4.8 %collective-permute-done.17 = bf16[2,512,64]{1,2,0:T(8,128)(2,1)S(1)} collective-permute-done((bf16[2,512,64]{1,2,0:T(8,128)(2,1)S(1)}, bf16[2,512,64]{1,2,0:T(8,128)(2,1)S(1)}, u32[]{:S(2)}, u32[]{:S(2)}) %collective-permute-start.17) | collective-permute-done | bytes 131104 | tf_op jit(solution)/shard_map/ppermute | solution.py:13
  94.1 1.1 %collective-permute-done.18 = bf16[2,512,64]{1,2,0:T(8,128)(2,1)} collective-permute-done((bf16[2,512,64]{1,2,0:T(8,128)(2,1)S(1)}, bf16[2,512,64]{1,2,0:T(8,128)(2,1)}, u32[]{:S(2)}, u32[]{:S(2)}) %collective-permute-start.18) | collective-permute-done | bytes 131104 | tf_op jit(solution)/shard_map/ppermute | solution.py:13
  95.1 1.8 %fusion.24 = f32[2,512,64]{1,2,0:T(8,128)} fusion(bf16[2,512,64]{1,2,0:T(8,128)(2,1)} %collective-permute-done.18, bf16[2,512,64]{1,2,0:T(8,128)(2,1)S(1)} %collective-permute-done.17, bf16[2,512,64]{1,2,0:T(8,128)(2,1)S(1)} %collective-permute-done.16, bf16[2,512,64]{1,2,0:T(8,128)(2,1)S(1)} %collective-permute-done.15, ...), kind=kLoop, calls=%fused_computation.32 | loop fusion | flops 983040 | bytes 1310724 | tf_op jit(solution)/shard_map/add | solution.py:14
  (47 shorter events, 2.7 us)
Async XLA Ops:
  0.0 55.2 %copy-start = (bf16[2,512,512]{2,1,0:T(8,128)(2,1)S(1)}, bf16[2,512,512]{2,1,0:T(8,128)(2,1)}, u32[]{:S(2)}) copy-start(bf16[2,512,512]{2,1,0:T(8,128)(2,1)} %param.19) | copy-start | bytes 3145732
  0.0 15.5 %collective-permute-start.1 = (bf16[2,64,512]{2,1,0:T(8,128)(2,1)}, bf16[2,64,512]{2,1,0:T(8,128)(2,1)S(1)}, u32[]{:S(2)}, u32[]{:S(2)}) collective-permute-start(bf16[2,64,512]{2,1,0:T(8,128)(2,1)} %param.11), channel_id=1, source_target_pairs={{0,64},{8,72},{16,80},{24,88},{32,96},{40,104},{48,112},{56,120},{... | collective-permute-start | bytes 393224 | tf_op jit(solution)/shard_map/ppermute | solution.py:71
  1.5 14.4 %collective-permute-start = (bf16[2,64,512]{2,1,0:T(8,128)(2,1)}, bf16[2,64,512]{2,1,0:T(8,128)(2,1)S(1)}, u32[]{:S(2)}, u32[]{:S(2)}) collective-permute-start(bf16[2,64,512]{2,1,0:T(8,128)(2,1)} %param.11), channel_id=1, source_target_pairs={{0,192},{8,200},{16,208},{24,216},{32,224},{40,232},{48,240},{56,2... | collective-permute-start | bytes 393224 | tf_op jit(solution)/shard_map/ppermute | solution.py:71
  4.6 20.5 %all-to-all-start = ((f32[8,1,128]{2,1,0:T(1,128)}), f32[8,1,128]{2,1,0:T(1,128)S(1)}, u32[]{:S(2)}, u32[]{:S(2)}) async-start(f32[8,1,128]{2,1,0:T(1,128)} %reshape.166), calls=%async_computation | async-start | bytes 8192 | tf_op jit(solution)/shard_map/all_to_all | solution.py:110
  15.5 5.6 %collective-permute-start.2 = (bf16[1,64,512]{2,1,0:T(8,128)(2,1)S(1)}, bf16[1,64,512]{2,1,0:T(8,128)(2,1)S(1)}, u32[]{:S(2)}, u32[]{:S(2)}) collective-permute-start(bf16[1,64,512]{2,1,0:T(8,128)(2,1)S(1)} %slice.64), channel_id=1, source_target_pairs={{0,64},{8,72},{16,80},{24,88},{32,96},{40,104},{48,112},{56,120},{... | collective-permute-start | bytes 196616 | tf_op jit(solution)/shard_map/ppermute | solution.py:71
  15.9 5.2 %collective-permute-start.3 = (bf16[1,64,512]{2,1,0:T(8,128)(2,1)S(1)}, bf16[1,64,512]{2,1,0:T(8,128)(2,1)S(1)}, u32[]{:S(2)}, u32[]{:S(2)}) collective-permute-start(bf16[1,64,512]{2,1,0:T(8,128)(2,1)S(1)} %slice.65), channel_id=1, source_target_pairs={{0,192},{8,200},{16,208},{24,216},{32,224},{40,232},{48,240},{56,2... | collective-permute-start | bytes 196616 | tf_op jit(solution)/shard_map/ppermute | solution.py:71
  22.6 12.0 %collective-permute-start.5 = (bf16[4,2,64,512]{3,0,1,2:T(4,128)(2,1)S(1)}, bf16[4,2,64,512]{3,0,1,2:T(4,128)(2,1)S(1)}, u32[]{:S(2)}, u32[]{:S(2)}) collective-permute-start(bf16[4,2,64,512]{3,0,1,2:T(4,128)(2,1)S(1)} %pad_maximum_fusion), channel_id=1, source_target_pairs={{0,16},{8,24},{16,32},{24,40},{32,48},{40,56},{48,0},{56,8},{64,80... | collective-permute-start | bytes 1572872 | tf_op jit(solution)/shard_map/ppermute | solution.py:71
  22.9 13.5 %collective-permute-start.4 = (bf16[4,2,64,512]{3,0,1,2:T(4,128)(2,1)S(1)}, bf16[4,2,64,512]{3,0,1,2:T(4,128)(2,1)S(1)}, u32[]{:S(2)}, u32[]{:S(2)}) collective-permute-start(bf16[4,2,64,512]{3,0,1,2:T(4,128)(2,1)S(1)} %pad_maximum_fusion), channel_id=1, source_target_pairs={{0,48},{8,56},{16,0},{24,8},{32,16},{40,24},{48,32},{56,40},{64,11... | collective-permute-start | bytes 1572872 | tf_op jit(solution)/shard_map/ppermute | solution.py:71
  26.4 12.6 %collective-permute-start.8 = (bf16[4,2,64,512]{3,0,1,2:T(4,128)(2,1)S(1)}, bf16[4,2,64,512]{3,0,1,2:T(4,128)(2,1)S(1)}, u32[]{:S(2)}, u32[]{:S(2)}) collective-permute-start(bf16[4,2,64,512]{3,0,1,2:T(4,128)(2,1)S(1)} %pad_maximum_fusion), channel_id=1, source_target_pairs={{0,8},{8,0},{16,24},{24,16},{32,40},{40,32},{48,56},{56,48},{64,72... | collective-permute-start | bytes 1572872 | tf_op jit(solution)/shard_map/ppermute | solution.py:71
  34.8 6.4 %collective-permute-start.6 = (bf16[2,2,64,512]{3,0,1,2:T(2,128)(2,1)S(1)}, bf16[2,2,64,512]{3,0,1,2:T(2,128)(2,1)S(1)}, u32[]{:S(2)}, u32[]{:S(2)}) collective-permute-start(bf16[2,2,64,512]{3,0,1,2:T(2,128)(2,1)S(1)} %slice.68), channel_id=1, source_target_pairs={{0,16},{8,24},{16,32},{24,40},{32,48},{40,56},{48,0},{56,8},{64,80... | collective-permute-start | bytes 786440 | tf_op jit(solution)/shard_map/ppermute | solution.py:71
  36.7 7.7 %collective-permute-start.7 = (bf16[2,2,64,512]{3,0,1,2:T(2,128)(2,1)S(1)}, bf16[2,2,64,512]{3,0,1,2:T(2,128)(2,1)S(1)}, u32[]{:S(2)}, u32[]{:S(2)}) collective-permute-start(bf16[2,2,64,512]{3,0,1,2:T(2,128)(2,1)S(1)} %slice.69), channel_id=1, source_target_pairs={{0,48},{8,56},{16,0},{24,8},{32,16},{40,24},{48,32},{56,40},{64,11... | collective-permute-start | bytes 786440 | tf_op jit(solution)/shard_map/ppermute | solution.py:71
  37.3 8.7 %collective-permute-start.9 = (bf16[4,2,64,512]{3,0,1,2:T(4,128)(2,1)S(1)}, bf16[4,2,64,512]{3,0,1,2:T(4,128)(2,1)S(1)}, u32[]{:S(2)}, u32[]{:S(2)}) collective-permute-start(bf16[4,2,64,512]{3,0,1,2:T(4,128)(2,1)S(1)} %collective-permute-done.4), channel_id=1, source_target_pairs={{0,8},{8,0},{16,24},{24,16},{32,40},{40,32},{48,56},{56,48},{64,72... | collective-permute-start | bytes 1572872 | tf_op jit(solution)/shard_map/ppermute | solution.py:71
  37.3 10.2 %collective-permute-start.11 = (bf16[4,2,64,512]{3,0,1,2:T(4,128)(2,1)S(1)}, bf16[4,2,64,512]{3,0,1,2:T(4,128)(2,1)S(1)}, u32[]{:S(2)}, u32[]{:S(2)}) collective-permute-start(bf16[4,2,64,512]{3,0,1,2:T(4,128)(2,1)S(1)} %collective-permute-done.5), channel_id=1, source_target_pairs={{0,8},{8,0},{16,24},{24,16},{32,40},{40,32},{48,56},{56,48},{64,72... | collective-permute-start | bytes 1572872 | tf_op jit(solution)/shard_map/ppermute | solution.py:71
  44.9 2.0 %collective-permute-start.10 = (bf16[4,2,64,512]{3,0,1,2:T(4,128)(2,1)S(1)}, bf16[4,2,64,512]{3,0,1,2:T(4,128)(2,1)S(1)}, u32[]{:S(2)}, u32[]{:S(2)}) collective-permute-start(bf16[4,2,64,512]{3,0,1,2:T(4,128)(2,1)S(1)} %pad_maximum_fusion.1), channel_id=1, source_target_pairs={{0,8},{8,0},{16,24},{24,16},{32,40},{40,32},{48,56},{56,48},{64,72... | collective-permute-start | bytes 1572872 | tf_op jit(solution)/shard_map/ppermute | solution.py:71
  48.6 6.6 %copy-start.3 = (f32[2,512]{1,0:T(2,128)S(1)}, f32[2,512]{1,0:T(2,128)}, u32[]{:S(2)}) copy-start(f32[2,512]{1,0:T(2,128)} %param.21) | copy-start | bytes 12292
  55.2 3.9 %copy-start.2 = (bf16[2,512,512]{2,1,0:T(8,128)(2,1)S(1)}, bf16[2,512,512]{2,1,0:T(8,128)(2,1)}, u32[]{:S(2)}) copy-start(bf16[2,512,512]{2,1,0:T(8,128)(2,1)} %param.18) | copy-start | bytes 3145732
  59.1 2.1 %copy-start.1 = (bf16[2,512,512]{2,1,0:T(8,128)(2,1)S(1)}, bf16[2,512,512]{2,1,0:T(8,128)(2,1)}, u32[]{:S(2)}) copy-start(bf16[2,512,512]{2,1,0:T(8,128)(2,1)} %param.16) | copy-start | bytes 3145732
  62.0 11.7 %collective-permute-start.12 = (bf16[2,512,64]{1,2,0:T(8,128)(2,1)S(1)}, bf16[2,512,64]{1,2,0:T(8,128)(2,1)S(1)}, u32[]{:S(2)}, u32[]{:S(2)}) collective-permute-start(bf16[2,512,64]{1,2,0:T(8,128)(2,1)S(1)} %get-tuple-element.5), channel_id=1, source_target_pairs={{0,1},{1,2},{2,3},{3,4},{4,5},{5,6},{6,7},{7,0},{8,9},{9,10},{10,1... | collective-permute-start | bytes 393224 | tf_op jit(solution)/shard_map/ppermute | solution.py:13
  63.8 13.5 %collective-permute-start.13 = (bf16[2,512,64]{1,2,0:T(8,128)(2,1)S(1)}, bf16[2,512,64]{1,2,0:T(8,128)(2,1)S(1)}, u32[]{:S(2)}, u32[]{:S(2)}) collective-permute-start(bf16[2,512,64]{1,2,0:T(8,128)(2,1)S(1)} %get-tuple-element.9), channel_id=1, source_target_pairs={{0,2},{1,3},{2,4},{3,5},{4,6},{5,7},{6,0},{7,1},{8,10},{9,11},{10,... | collective-permute-start | bytes 393224 | tf_op jit(solution)/shard_map/ppermute | solution.py:13
  66.0 16.8 %collective-permute-start.14 = (bf16[2,512,64]{1,2,0:T(8,128)(2,1)S(1)}, bf16[2,512,64]{1,2,0:T(8,128)(2,1)S(1)}, u32[]{:S(2)}, u32[]{:S(2)}) collective-permute-start(bf16[2,512,64]{1,2,0:T(8,128)(2,1)S(1)} %get-tuple-element.8), channel_id=1, source_target_pairs={{0,3},{1,4},{2,5},{3,6},{4,7},{5,0},{6,1},{7,2},{8,11},{9,12},{10,... | collective-permute-start | bytes 393224 | tf_op jit(solution)/shard_map/ppermute | solution.py:13
  68.7 18.8 %collective-permute-start.15 = (bf16[2,512,64]{1,2,0:T(8,128)(2,1)S(1)}, bf16[2,512,64]{1,2,0:T(8,128)(2,1)S(1)}, u32[]{:S(2)}, u32[]{:S(2)}) collective-permute-start(bf16[2,512,64]{1,2,0:T(8,128)(2,1)S(1)} %get-tuple-element.7), channel_id=1, source_target_pairs={{0,4},{1,5},{2,6},{3,7},{4,0},{5,1},{6,2},{7,3},{8,12},{9,13},{10,... | collective-permute-start | bytes 393224 | tf_op jit(solution)/shard_map/ppermute | solution.py:13
  71.0 18.2 %collective-permute-start.16 = (bf16[2,512,64]{1,2,0:T(8,128)(2,1)S(1)}, bf16[2,512,64]{1,2,0:T(8,128)(2,1)S(1)}, u32[]{:S(2)}, u32[]{:S(2)}) collective-permute-start(bf16[2,512,64]{1,2,0:T(8,128)(2,1)S(1)} %get-tuple-element.6), channel_id=1, source_target_pairs={{0,5},{1,6},{2,7},{3,0},{4,1},{5,2},{6,3},{7,4},{8,13},{9,14},{10,... | collective-permute-start | bytes 393224 | tf_op jit(solution)/shard_map/ppermute | solution.py:13
  73.7 20.4 %collective-permute-start.17 = (bf16[2,512,64]{1,2,0:T(8,128)(2,1)S(1)}, bf16[2,512,64]{1,2,0:T(8,128)(2,1)S(1)}, u32[]{:S(2)}, u32[]{:S(2)}) collective-permute-start(bf16[2,512,64]{1,2,0:T(8,128)(2,1)S(1)} %get-tuple-element.11), channel_id=1, source_target_pairs={{0,6},{1,7},{2,0},{3,1},{4,2},{5,3},{6,4},{7,5},{8,14},{9,15},{10,... | collective-permute-start | bytes 393224 | tf_op jit(solution)/shard_map/ppermute | solution.py:13
  77.3 17.8 %collective-permute-start.18 = (bf16[2,512,64]{1,2,0:T(8,128)(2,1)S(1)}, bf16[2,512,64]{1,2,0:T(8,128)(2,1)}, u32[]{:S(2)}, u32[]{:S(2)}) collective-permute-start(bf16[2,512,64]{1,2,0:T(8,128)(2,1)S(1)} %get-tuple-element.10), channel_id=1, source_target_pairs={{0,7},{1,0},{2,1},{3,2},{4,3},{5,4},{6,5},{7,6},{8,15},{9,8},{10,9... | collective-permute-start | bytes 393224 | tf_op jit(solution)/shard_map/ppermute | solution.py:13

commit v13 on v12

--- a/solution.py
+++ b/solution.py
@@ -77,6 +77,7 @@
         [move(from_left[:half_blocks], 1, 0), move(from_right[half_blocks:], -1, 0)], axis=0
     )
     x_row = jnp.stack([block_vec, from_right, far, from_left])
+    rates_seed, x_row = lax.optimization_barrier((left_rates[None], x_row))
     side_x = move(x_row, 0, 0, sibling=True)
     from_below = move(x_row, 0, 1)
     from_above = move(x_row, 0, -1)
@@ -106,7 +107,7 @@
         "ktrn,tmn->ktrm", pooled, right_factor, preferred_element_type=jnp.float32
     ).astype(jnp.bfloat16)
     left_part = lax.dynamic_slice_in_dim(left_factor, part * row_count, row_count, axis=2)
-    rates_run = left_rates[None]
+    rates_run = rates_seed
     rates_parts = lax.all_to_all(
         jnp.broadcast_to(rates_run, (pieces,) + left_rates.shape), "sub", 0, 0, tiled=True
     )

time: 98.2 us -> 99.7 us (1.015)
  starting transfers between devices: 38.1 us -> 31.6 us
  matrix products: 19.2 us -> 24.5 us
  local copies, waits for them, and re-layouts: 6.66 us -> 8.06 us
    ppermute x12, waiting for transfers between devices: 13 us -> 3.93 us  [move(): return lax.ppermute(piece, 'blk', pairs_list)]
    ppermute x7, starting transfers between devices: 18.1 us -> 11.7 us  [scatter_sum(): got = lax.ppermute(send, axis, [(j, (j + k) % n) for j in range(n)])]
    all_to_all x1, waiting for transfers between devices: 0.01 us -> 5.95 us  [local(): lax.all_to_all(jnp.broadcast_to(rates_run, (pieces,) + left_rates.shape),...]
    dot_general x8, matrix products: 5.74 us -> 11 us  [pool(): jnp.einsum('kab,abrn->krn', w, piece, preferred_element_type=jnp.float32)]
    ppermute x7, waiting for transfers between devices: 15 us -> 18.5 us  [scatter_sum(): got = lax.ppermute(send, axis, [(j, (j + k) % n) for j in range(n)])]
    slice x1, local copies, waits for them, and re-layouts: 0.18 us -> 1.22 us  [local(): from_below[:half_ring]]
    slice x1, local copies, waits for them, and re-layouts: 0.29 us -> 1.34 us  [local(): from_above[half_ring:]]
  transfers between devices with their start and end apart: 20 -> 20, of which waited for: 10 -> 11; matrix products, arithmetic and copies ran while one was open for 15% -> 19% of each run, Pallas kernels for 0% -> 0%
where the time goes in v13:
time: 99.7 us; the launch traced here: 98.2 us
  starting transfers between devices  31.6 us (32%)
  waiting for transfers between devices  28.4 us (28%)
  matrix products  24.5 us (25%)
  local copies, waits for them, and re-layouts  8.06 us (8%)
  other arithmetic  5.31 us (5%)
    ppermute x7, waiting for transfers between devices, scatter_sum(): got = lax.ppermute(send, axis, [(j, (j + k) % n) for j in range(n)])  18.5 us
    ppermute x7, starting transfers between devices, scatter_sum(): got = lax.ppermute(send, axis, [(j, (j + k) % n) for j in range(n)])  11.7 us
    ppermute x12, starting transfers between devices, move(): return lax.ppermute(piece, 'blk', pairs_list)  11.5 us
    dot_general x8, matrix products, pool(): jnp.einsum('kab,abrn->krn', w, piece, preferred_element_type=jnp.float32)  11 us
    all_to_all x1, starting transfers between devices, local(): lax.all_to_all(jnp.broadcast_to(rates_run, (pieces,) + left_rates.shape),...  8.47 us
    dot_general x1, matrix products, local(): jnp.einsum('tab,ktbc->kac', left_part, right_done, preferred_element_type...  6.94 us
    all_to_all x1, waiting for transfers between devices, local(): lax.all_to_all(jnp.broadcast_to(rates_run, (pieces,) + left_rates.shape),...  5.95 us
    ppermute x12, waiting for transfers between devices, move(): return lax.ppermute(piece, 'blk', pairs_list)  3.93 us
  transfers between devices with their start and end apart: 20, of which 11 were waited for; matrix products, arithmetic and copies ran while one was open for 19% of the time, Pallas kernels for 0%

profile of v13, /device:TPU:24, one launch (start us, length us, event | category | flops | bytes accessed | tf_op | source)
XLA Modules:
  0.0 98.2 jit_solution(4275118131468654316)
XLA Ops:
  0.0 1.5 %collective-permute-start.1 = (bf16[2,64,512]{2,1,0:T(8,128)(2,1)}, bf16[2,64,512]{2,1,0:T(8,128)(2,1)S(1)}, u32[]{:S(2)}, u32[]{:S(2)}) collective-permute-start(bf16[2,64,512]{2,1,0:T(8,128)(2,1)} %param.11), channel_id=1, source_target_pairs={{0,64},{8,72},{16,80},{24,88},{32,96},{40,104},{48,112},{56,120},{... | collective-permute-start | bytes 393224 | tf_op jit(solution)/shard_map/ppermute | solution.py:71
  1.5 1.7 %collective-permute-start = (bf16[2,64,512]{2,1,0:T(8,128)(2,1)}, bf16[2,64,512]{2,1,0:T(8,128)(2,1)S(1)}, u32[]{:S(2)}, u32[]{:S(2)}) collective-permute-start(bf16[2,64,512]{2,1,0:T(8,128)(2,1)} %param.11), channel_id=1, source_target_pairs={{0,192},{8,200},{16,208},{24,216},{32,224},{40,232},{48,240},{56,2... | collective-permute-start | bytes 393224 | tf_op jit(solution)/shard_map/ppermute | solution.py:71
  3.6 1.1 %constant_dynamic-slice_fusion = s32[32,1,2,3]{1,2,3,0:T(2,128)S(1)} fusion(s32[32,32,2,3]{1,2,3,0:T(2,128)} %param.14, s32[]{:T(128)S(6)} %select_n.102), kind=kLoop, calls=%fused_computation.53 | loop fusion | bytes 1540 | tf_op jit(solution)/shard_map/jit(dynamic_index_in_dim)/dynamic_slice | solution.py:42
  4.8 0.9 dynamic-slice_reduce_fusion
  5.7 1.0 %collective-permute-done.1 = bf16[2,64,512]{2,1,0:T(8,128)(2,1)S(1)} collective-permute-done((bf16[2,64,512]{2,1,0:T(8,128)(2,1)}, bf16[2,64,512]{2,1,0:T(8,128)(2,1)S(1)}, u32[]{:S(2)}, u32[]{:S(2)}) %collective-permute-start.1) | collective-permute-done | bytes 131104 | tf_op jit(solution)/shard_map/ppermute | solution.py:71
  7.0 3.0 %collective-permute-start.3 = (bf16[1,64,512]{2,1,0:T(8,128)(2,1)S(1)}, bf16[1,64,512]{2,1,0:T(8,128)(2,1)S(1)}, u32[]{:S(2)}, u32[]{:S(2)}) collective-permute-start(bf16[1,64,512]{2,1,0:T(8,128)(2,1)S(1)} %slice.65), channel_id=1, source_target_pairs={{0,192},{8,200},{16,208},{24,216},{32,224},{40,232},{48,240},{56,2... | collective-permute-start | bytes 196616 | tf_op jit(solution)/shard_map/ppermute | solution.py:71
  10.1 1.1 %copy.133 = bf16[1,2,64,512]{3,0,1,2:T(2,128)(2,1)S(1)} copy(bf16[1,2,64,512]{3,2,1,0:T(8,128)(2,1)} %bitcast.219) | data formatting | bytes 262144 | tf_op jit(solution)/shard_map/stack | solution.py:79
  11.6 0.5 collective-permute-done.2
  12.4 2.0 %pad_maximum_fusion = bf16[4,2,64,512]{3,0,1,2:T(4,128)(2,1)} fusion(bf16[1,2,64,512]{3,0,1,2:T(2,128)(2,1)S(1)} %copy.136, bf16[1,2,64,512]{3,0,1,2:T(2,128)(2,1)S(1)} %copy.135, bf16[1,2,64,512]{3,0,1,2:T(2,128)(2,1)S(1)} %copy.134, bf16[1,2,64,512]{3,0,1,2:T(2,128)(2,1)S(1)} %copy.133), kind=kLoop, calls=%fused_computation.24 | loop fusion | flops 2097152 | bytes 1048576 | tf_op jit(solution)/shard_map/stack | solution.py:79
  14.4 1.7 %collective-permute-start.5 = (bf16[4,2,64,512]{3,0,1,2:T(4,128)(2,1)}, bf16[4,2,64,512]{3,0,1,2:T(4,128)(2,1)}, u32[]{:S(2)}, u32[]{:S(2)}) collective-permute-start(bf16[4,2,64,512]{3,0,1,2:T(4,128)(2,1)} %pad_maximum_fusion), channel_id=1, source_target_pairs={{0,16},{8,24},{16,32},{24,40},{32,48},{40,56},{48,0},{56,8},{64,80... | collective-permute-start | bytes 1572872 | tf_op jit(solution)/shard_map/ppermute | solution.py:71
  16.1 0.3 collective-permute-start.4
  16.9 0.7 reshape.165
  17.6 8.5 %all-to-all-start = ((f32[8,1,128]{2,1,0:T(1,128)}), f32[8,1,128]{2,1,0:T(1,128)S(1)}, u32[]{:S(2)}, u32[]{:S(2)}) async-start(f32[8,1,128]{2,1,0:T(1,128)} %reshape.165), calls=%async_computation | async-start | bytes 8192 | tf_op jit(solution)/shard_map/all_to_all | solution.py:111
  26.1 1.6 %fusion.46 = f32[16,64,512,1]{2,0,3,1:T(8,128)S(1)} fusion(bf16[4,2,64,512]{3,0,1,2:T(4,128)(2,1)} %pad_maximum_fusion, bf16[16,1,1,4,2]{0,4,3,2,1:T(2,128)(2,1)S(1)} %get-tuple-element.23), kind=kOutput, calls=%fused_computation.71 | convolution fusion | flops 8388608 | bytes 2621696 | tf_op jit(solution)/shard_map/kab,abrn->krn/dot_general | solution.py:93
  27.7 6.0 %all-to-all-done = f32[8,1,128]{2,1,0:T(1,128)S(1)} async-done(((f32[8,1,128]{2,1,0:T(1,128)}), f32[8,1,128]{2,1,0:T(1,128)S(1)}, u32[]{:S(2)}, u32[]{:S(2)}) %all-to-all-start) | async-done | bytes 4128 | tf_op jit(solution)/shard_map/all_to_all | solution.py:111
  33.7 0.5 broadcast.165
  34.2 0.7 reduce.2
  35.0 1.2 %slice.68 = bf16[2,2,64,512]{3,0,1,2:T(2,128)(2,1)S(1)} slice(bf16[4,2,64,512]{3,0,1,2:T(4,128)(2,1)} %collective-permute-done.5), slice={[0:2], [0:2], [0:64], [0:512]} | slice | bytes 524288 | tf_op jit(solution)/shard_map/slice | solution.py:88
  36.2 1.5 %collective-permute-start.6 = (bf16[2,2,64,512]{3,0,1,2:T(2,128)(2,1)S(1)}, bf16[2,2,64,512]{3,0,1,2:T(2,128)(2,1)S(1)}, u32[]{:S(2)}, u32[]{:S(2)}) collective-permute-start(bf16[2,2,64,512]{3,0,1,2:T(2,128)(2,1)S(1)} %slice.68), channel_id=1, source_target_pairs={{0,16},{8,24},{16,32},{24,40},{32,48},{40,56},{48,0},{56,8},{64,80... | collective-permute-start | bytes 786440 | tf_op jit(solution)/shard_map/ppermute | solution.py:71
  37.7 1.3 %slice.69 = bf16[2,2,64,512]{3,0,1,2:T(2,128)(2,1)S(1)} slice(bf16[4,2,64,512]{3,0,1,2:T(4,128)(2,1)} %collective-permute-done.4), slice={[2:4], [0:2], [0:64], [0:512]} | slice | bytes 524288 | tf_op jit(solution)/shard_map/slice | solution.py:88
  39.1 0.7 collective-permute-start.7
  39.8 0.5 collective-permute-start.11
  40.3 1.6 %fusion.40 = f32[16,64,512,1]{2,0,3,1:T(8,128)S(1)} fusion(bf16[4,2,64,512]{3,0,1,2:T(4,128)(2,1)} %collective-permute-done.5, bf16[16,1,1,4,2]{0,4,3,2,1:T(2,128)(2,1)S(1)} %get-tuple-element.20), kind=kOutput, calls=%fused_computation.65 | convolution fusion | flops 8388608 | bytes 2621696 | tf_op jit(solution)/shard_map/kab,abrn->krn/dot_general | solution.py:93
  41.9 1.6 %fusion.44 = f32[16,64,512,1]{2,0,3,1:T(8,128)S(1)} fusion(bf16[4,2,64,512]{3,0,1,2:T(4,128)(2,1)} %collective-permute-done.4, bf16[16,1,1,4,2]{0,4,3,2,1:T(2,128)(2,1)S(1)} %get-tuple-element.22), kind=kOutput, calls=%fused_computation.69 | convolution fusion | flops 8388608 | bytes 2621696 | tf_op jit(solution)/shard_map/kab,abrn->krn/dot_general | solution.py:93
  43.6 1.7 %fusion.38 = f32[16,64,512,1]{2,0,3,1:T(8,128)S(1)} fusion(bf16[4,2,64,512]{3,0,1,2:T(4,128)(2,1)} %collective-permute-done.8, bf16[16,1,1,4,2]{0,4,3,2,1:T(2,128)(2,1)S(1)} %get-tuple-element.19), kind=kOutput, calls=%fused_computation.63 | convolution fusion | flops 8388608 | bytes 2621696 | tf_op jit(solution)/shard_map/kab,abrn->krn/dot_general | solution.py:93
  45.2 2.1 %collective-permute-done.7 = bf16[2,2,64,512]{3,0,1,2:T(2,128)(2,1)S(1)} collective-permute-done((bf16[2,2,64,512]{3,0,1,2:T(2,128)(2,1)S(1)}, bf16[2,2,64,512]{3,0,1,2:T(2,128)(2,1)S(1)}, u32[]{:S(2)}, u32[]{:S(2)}) %collective-permute-start.7) | collective-permute-done | bytes 262176 | tf_op jit(solution)/shard_map/ppermute | solution.py:71
  47.4 0.5 pad_maximum_fusion.1
  48.0 1.0 fusion.42
  49.0 0.6 fusion.36
  49.9 0.6 fusion.34
  50.5 2.3 %fusion.9 = bf16[2,8,64,512]{3,1,0,2:T(8,128)(2,1)} fusion(bf16[4,2,64,512]{3,0,1,2:T(4,128)(2,1)S(1)} %collective-permute-done.11, f32[16,64,512,1]{2,0,3,1:T(8,128)S(1)} %fusion.34, f32[16,64,512,1]{2,0,3,1:T(8,128)S(1)} %fusion.36, f32[16,64,512,1]{2,0,3,1:T(8,128)S(1)} %fusion.38, f32[16,64,512,1]{2,0,3,1:T(8,128)S(1)} %fusion.40, ...), kind=kOutput, calls=%fused_computation.17 | convolution fusion | flops 12582912 | bytes 16253184 | tf_op jit(solution)/shard_map/kab,abrn->krn/dot_general | solution.py:93
  52.8 6.9 %bitcast_convert_fusion = bf16[2,512,512]{2,1,0:T(8,128)(2,1)} fusion(bf16[8,512,512]{2,1,0:T(8,128)(2,1)} %param.12, s32[]{:T(128)S(6)} %select_n.109, bf16[8,512,512]{2,1,0:T(8,128)(2,1)} %param.13, bf16[2,8,64,512]{3,1,0,2:T(8,128)(2,1)} %fusion.9), kind=kOutput, calls=%fused_computation.2 | convolution fusion | flops 1074790400 | bytes 7340036 | tf_op jit(solution)/shard_map/tab,ktbc->kac/dot_general | solution.py:115
  59.7 3.6 %divide_convert_fusion = bf16[2,512,512]{2,1,0:T(8,128)(2,1)} fusion(bf16[2,512,512]{2,1,0:T(8,128)(2,1)S(1)} %copy-done, bf16[2,512,512]{2,1,0:T(8,128)(2,1)} %bitcast_convert_fusion, bf16[2,512,512]{2,1,0:T(8,128)(2,1)S(1)} %copy-done.3, f32[2,512]{1,0:T(2,128)S(1)} %copy-done.5, f32[2,512]{1,0:T(2,128)S(1)} %add.283), kind=kOutput, calls=%fused_computation.11 | convolution fusion | flops 1075838976 | bytes 4202496 | tf_op jit(solution)/shard_map/jrn,jmn->jrm/dot_general | solution.py:121
  63.3 2.1 %convolution_convert_fusion.1 = bf16[2,512,512]{1,2,0:T(8,128)(2,1)S(1)} fusion(bf16[2,512,512]{2,1,0:T(8,128)(2,1)} %divide_convert_fusion, bf16[2,512,512]{2,1,0:T(8,128)(2,1)S(1)} %copy-done.4), kind=kOutput, calls=%fused_computation.14 | convolution fusion | flops 537395200 | bytes 3145728 | tf_op jit(solution)/shard_map/jrm,jkm->jrk/dot_general | solution.py:123
  65.4 0.7 convolution_convert_fusion
  66.2 0.6 collective-permute-start.12
  66.9 0.6 collective-permute-start.13
  67.5 2.4 %collective-permute-start.14 = (bf16[2,512,64]{1,2,0:T(8,128)(2,1)S(1)}, bf16[2,512,64]{1,2,0:T(8,128)(2,1)S(1)}, u32[]{:S(2)}, u32[]{:S(2)}) collective-permute-start(bf16[2,512,64]{1,2,0:T(8,128)(2,1)S(1)} %get-tuple-element.12), channel_id=1, source_target_pairs={{0,3},{1,4},{2,5},{3,6},{4,7},{5,0},{6,1},{7,2},{8,11},{9,12},{10,... | collective-permute-start | bytes 393224 | tf_op jit(solution)/shard_map/ppermute | solution.py:13
  69.8 3.6 %collective-permute-start.15 = (bf16[2,512,64]{1,2,0:T(8,128)(2,1)S(1)}, bf16[2,512,64]{1,2,0:T(8,128)(2,1)S(1)}, u32[]{:S(2)}, u32[]{:S(2)}) collective-permute-start(bf16[2,512,64]{1,2,0:T(8,128)(2,1)S(1)} %get-tuple-element.11), channel_id=1, source_target_pairs={{0,4},{1,5},{2,6},{3,7},{4,0},{5,1},{6,2},{7,3},{8,12},{9,13},{10,... | collective-permute-start | bytes 393224 | tf_op jit(solution)/shard_map/ppermute | solution.py:13
  73.4 2.4 %collective-permute-start.16 = (bf16[2,512,64]{1,2,0:T(8,128)(2,1)S(1)}, bf16[2,512,64]{1,2,0:T(8,128)(2,1)S(1)}, u32[]{:S(2)}, u32[]{:S(2)}) collective-permute-start(bf16[2,512,64]{1,2,0:T(8,128)(2,1)S(1)} %get-tuple-element.10), channel_id=1, source_target_pairs={{0,5},{1,6},{2,7},{3,0},{4,1},{5,2},{6,3},{7,4},{8,13},{9,14},{10,... | collective-permute-start | bytes 393224 | tf_op jit(solution)/shard_map/ppermute | solution.py:13
  75.7 0.7 collective-permute-done.12
  76.5 1.2 %collective-permute-start.17 = (bf16[2,512,64]{1,2,0:T(8,128)(2,1)S(1)}, bf16[2,512,64]{1,2,0:T(8,128)(2,1)S(1)}, u32[]{:S(2)}, u32[]{:S(2)}) collective-permute-start(bf16[2,512,64]{1,2,0:T(8,128)(2,1)S(1)} %get-tuple-element.15), channel_id=1, source_target_pairs={{0,6},{1,7},{2,0},{3,1},{4,2},{5,3},{6,4},{7,5},{8,14},{9,15},{10,... | collective-permute-start | bytes 393224 | tf_op jit(solution)/shard_map/ppermute | solution.py:13
  77.7 2.9 %collective-permute-done.13 = bf16[2,512,64]{1,2,0:T(8,128)(2,1)S(1)} collective-permute-done((bf16[2,512,64]{1,2,0:T(8,128)(2,1)S(1)}, bf16[2,512,64]{1,2,0:T(8,128)(2,1)S(1)}, u32[]{:S(2)}, u32[]{:S(2)}) %collective-permute-start.13) | collective-permute-done | bytes 131104 | tf_op jit(solution)/shard_map/ppermute | solution.py:13
  80.5 1.0 %collective-permute-start.18 = (bf16[2,512,64]{1,2,0:T(8,128)(2,1)S(1)}, bf16[2,512,64]{1,2,0:T(8,128)(2,1)}, u32[]{:S(2)}, u32[]{:S(2)}) collective-permute-start(bf16[2,512,64]{1,2,0:T(8,128)(2,1)S(1)} %get-tuple-element.14), channel_id=1, source_target_pairs={{0,7},{1,0},{2,1},{3,2},{4,3},{5,4},{6,5},{7,6},{8,15},{9,8},{10,9... | collective-permute-start | bytes 393224 | tf_op jit(solution)/shard_map/ppermute | solution.py:13
  81.6 7.6 %collective-permute-done.14 = bf16[2,512,64]{1,2,0:T(8,128)(2,1)S(1)} collective-permute-done((bf16[2,512,64]{1,2,0:T(8,128)(2,1)S(1)}, bf16[2,512,64]{1,2,0:T(8,128)(2,1)S(1)}, u32[]{:S(2)}, u32[]{:S(2)}) %collective-permute-start.14) | collective-permute-done | bytes 131104 | tf_op jit(solution)/shard_map/ppermute | solution.py:13
  89.5 5.9 %collective-permute-done.17 = bf16[2,512,64]{1,2,0:T(8,128)(2,1)S(1)} collective-permute-done((bf16[2,512,64]{1,2,0:T(8,128)(2,1)S(1)}, bf16[2,512,64]{1,2,0:T(8,128)(2,1)S(1)}, u32[]{:S(2)}, u32[]{:S(2)}) %collective-permute-start.17) | collective-permute-done | bytes 131104 | tf_op jit(solution)/shard_map/ppermute | solution.py:13
  95.5 1.0 %collective-permute-done.18 = bf16[2,512,64]{1,2,0:T(8,128)(2,1)} collective-permute-done((bf16[2,512,64]{1,2,0:T(8,128)(2,1)S(1)}, bf16[2,512,64]{1,2,0:T(8,128)(2,1)}, u32[]{:S(2)}, u32[]{:S(2)}) %collective-permute-start.18) | collective-permute-done | bytes 131104 | tf_op jit(solution)/shard_map/ppermute | solution.py:13
  96.5 1.7 %fusion.24 = f32[2,512,64]{1,2,0:T(8,128)} fusion(bf16[2,512,64]{1,2,0:T(8,128)(2,1)} %collective-permute-done.18, bf16[2,512,64]{1,2,0:T(8,128)(2,1)S(1)} %collective-permute-done.17, bf16[2,512,64]{1,2,0:T(8,128)(2,1)S(1)} %collective-permute-done.16, bf16[2,512,64]{1,2,0:T(8,128)(2,1)S(1)} %collective-permute-done.15, ...), kind=kLoop, calls=%fused_computation.32 | loop fusion | flops 983040 | bytes 1310724 | tf_op jit(solution)/shard_map/add | solution.py:14
  (51 shorter events, 2.9 us)
Async XLA Ops:
  0.0 59.7 %copy-start = (bf16[2,512,512]{2,1,0:T(8,128)(2,1)S(1)}, bf16[2,512,512]{2,1,0:T(8,128)(2,1)}, u32[]{:S(2)}) copy-start(bf16[2,512,512]{2,1,0:T(8,128)(2,1)} %param.19) | copy-start | bytes 3145732
  0.0 6.7 %collective-permute-start.1 = (bf16[2,64,512]{2,1,0:T(8,128)(2,1)}, bf16[2,64,512]{2,1,0:T(8,128)(2,1)S(1)}, u32[]{:S(2)}, u32[]{:S(2)}) collective-permute-start(bf16[2,64,512]{2,1,0:T(8,128)(2,1)} %param.11), channel_id=1, source_target_pairs={{0,64},{8,72},{16,80},{24,88},{32,96},{40,104},{48,112},{56,120},{... | collective-permute-start | bytes 393224 | tf_op jit(solution)/shard_map/ppermute | solution.py:71
  1.5 5.5 %collective-permute-start = (bf16[2,64,512]{2,1,0:T(8,128)(2,1)}, bf16[2,64,512]{2,1,0:T(8,128)(2,1)S(1)}, u32[]{:S(2)}, u32[]{:S(2)}) collective-permute-start(bf16[2,64,512]{2,1,0:T(8,128)(2,1)} %param.11), channel_id=1, source_target_pairs={{0,192},{8,200},{16,208},{24,216},{32,224},{40,232},{48,240},{56,2... | collective-permute-start | bytes 393224 | tf_op jit(solution)/shard_map/ppermute | solution.py:71
  4.6 12.3 %copy-start.2 = (f32[2,64]{1,0:T(2,128)S(1)}, f32[2,64]{1,0:T(2,128)}, u32[]{:S(2)}) copy-start(f32[2,64]{1,0:T(2,128)} %param.20) | copy-start | bytes 1540
  6.7 5.5 %collective-permute-start.2 = (bf16[1,64,512]{2,1,0:T(8,128)(2,1)S(1)}, bf16[1,64,512]{2,1,0:T(8,128)(2,1)S(1)}, u32[]{:S(2)}, u32[]{:S(2)}) collective-permute-start(bf16[1,64,512]{2,1,0:T(8,128)(2,1)S(1)} %slice.64), channel_id=1, source_target_pairs={{0,64},{8,72},{16,80},{24,88},{32,96},{40,104},{48,112},{56,120},{... | collective-permute-start | bytes 196616 | tf_op jit(solution)/shard_map/ppermute | solution.py:71
  7.0 5.2 %collective-permute-start.3 = (bf16[1,64,512]{2,1,0:T(8,128)(2,1)S(1)}, bf16[1,64,512]{2,1,0:T(8,128)(2,1)S(1)}, u32[]{:S(2)}, u32[]{:S(2)}) collective-permute-start(bf16[1,64,512]{2,1,0:T(8,128)(2,1)S(1)} %slice.65), channel_id=1, source_target_pairs={{0,192},{8,200},{16,208},{24,216},{32,224},{40,232},{48,240},{56,2... | collective-permute-start | bytes 196616 | tf_op jit(solution)/shard_map/ppermute | solution.py:71
  14.4 20.6 %collective-permute-start.5 = (bf16[4,2,64,512]{3,0,1,2:T(4,128)(2,1)}, bf16[4,2,64,512]{3,0,1,2:T(4,128)(2,1)}, u32[]{:S(2)}, u32[]{:S(2)}) collective-permute-start(bf16[4,2,64,512]{3,0,1,2:T(4,128)(2,1)} %pad_maximum_fusion), channel_id=1, source_target_pairs={{0,16},{8,24},{16,32},{24,40},{32,48},{40,56},{48,0},{56,8},{64,80... | collective-permute-start | bytes 1572872 | tf_op jit(solution)/shard_map/ppermute | solution.py:71
  16.1 21.7 %collective-permute-start.4 = (bf16[4,2,64,512]{3,0,1,2:T(4,128)(2,1)}, bf16[4,2,64,512]{3,0,1,2:T(4,128)(2,1)}, u32[]{:S(2)}, u32[]{:S(2)}) collective-permute-start(bf16[4,2,64,512]{3,0,1,2:T(4,128)(2,1)} %pad_maximum_fusion), channel_id=1, source_target_pairs={{0,48},{8,56},{16,0},{24,8},{32,16},{40,24},{48,32},{56,40},{64,11... | collective-permute-start | bytes 1572872 | tf_op jit(solution)/shard_map/ppermute | solution.py:71
  16.8 26.8 %collective-permute-start.8 = (bf16[4,2,64,512]{3,0,1,2:T(4,128)(2,1)}, bf16[4,2,64,512]{3,0,1,2:T(4,128)(2,1)}, u32[]{:S(2)}, u32[]{:S(2)}) collective-permute-start(bf16[4,2,64,512]{3,0,1,2:T(4,128)(2,1)} %pad_maximum_fusion), channel_id=1, source_target_pairs={{0,8},{8,0},{16,24},{24,16},{32,40},{40,32},{48,56},{56,48},{64,72... | collective-permute-start | bytes 1572872 | tf_op jit(solution)/shard_map/ppermute | solution.py:71
  17.6 16.1 %all-to-all-start = ((f32[8,1,128]{2,1,0:T(1,128)}), f32[8,1,128]{2,1,0:T(1,128)S(1)}, u32[]{:S(2)}, u32[]{:S(2)}) async-start(f32[8,1,128]{2,1,0:T(1,128)} %reshape.165), calls=%async_computation | async-start | bytes 8192 | tf_op jit(solution)/shard_map/all_to_all | solution.py:111
  36.2 9.0 %collective-permute-start.6 = (bf16[2,2,64,512]{3,0,1,2:T(2,128)(2,1)S(1)}, bf16[2,2,64,512]{3,0,1,2:T(2,128)(2,1)S(1)}, u32[]{:S(2)}, u32[]{:S(2)}) collective-permute-start(bf16[2,2,64,512]{3,0,1,2:T(2,128)(2,1)S(1)} %slice.68), channel_id=1, source_target_pairs={{0,16},{8,24},{16,32},{24,40},{32,48},{40,56},{48,0},{56,8},{64,80... | collective-permute-start | bytes 786440 | tf_op jit(solution)/shard_map/ppermute | solution.py:71
  39.1 8.3 %collective-permute-start.7 = (bf16[2,2,64,512]{3,0,1,2:T(2,128)(2,1)S(1)}, bf16[2,2,64,512]{3,0,1,2:T(2,128)(2,1)S(1)}, u32[]{:S(2)}, u32[]{:S(2)}) collective-permute-start(bf16[2,2,64,512]{3,0,1,2:T(2,128)(2,1)S(1)} %slice.69), channel_id=1, source_target_pairs={{0,48},{8,56},{16,0},{24,8},{32,16},{40,24},{48,32},{56,40},{64,11... | collective-permute-start | bytes 786440 | tf_op jit(solution)/shard_map/ppermute | solution.py:71
  39.8 9.2 %collective-permute-start.9 = (bf16[4,2,64,512]{3,0,1,2:T(4,128)(2,1)}, bf16[4,2,64,512]{3,0,1,2:T(4,128)(2,1)S(1)}, u32[]{:S(2)}, u32[]{:S(2)}) collective-permute-start(bf16[4,2,64,512]{3,0,1,2:T(4,128)(2,1)} %collective-permute-done.4), channel_id=1, source_target_pairs={{0,8},{8,0},{16,24},{24,16},{32,40},{40,32},{48,56},{56,48},{64,72... | collective-permute-start | bytes 1572872 | tf_op jit(solution)/shard_map/ppermute | solution.py:71
  39.8 10.8 %collective-permute-start.11 = (bf16[4,2,64,512]{3,0,1,2:T(4,128)(2,1)}, bf16[4,2,64,512]{3,0,1,2:T(4,128)(2,1)S(1)}, u32[]{:S(2)}, u32[]{:S(2)}) collective-permute-start(bf16[4,2,64,512]{3,0,1,2:T(4,128)(2,1)} %collective-permute-done.5), channel_id=1, source_target_pairs={{0,8},{8,0},{16,24},{24,16},{32,40},{40,32},{48,56},{56,48},{64,72... | collective-permute-start | bytes 1572872 | tf_op jit(solution)/shard_map/ppermute | solution.py:71
  47.9 2.0 %collective-permute-start.10 = (bf16[4,2,64,512]{3,0,1,2:T(4,128)(2,1)S(1)}, bf16[4,2,64,512]{3,0,1,2:T(4,128)(2,1)S(1)}, u32[]{:S(2)}, u32[]{:S(2)}) collective-permute-start(bf16[4,2,64,512]{3,0,1,2:T(4,128)(2,1)S(1)} %pad_maximum_fusion.1), channel_id=1, source_target_pairs={{0,8},{8,0},{16,24},{24,16},{32,40},{40,32},{48,56},{56,48},{64,72... | collective-permute-start | bytes 1572872 | tf_op jit(solution)/shard_map/ppermute | solution.py:71
  52.8 6.9 %copy-start.3 = (bf16[2,512,512]{2,1,0:T(8,128)(2,1)S(1)}, bf16[2,512,512]{2,1,0:T(8,128)(2,1)}, u32[]{:S(2)}) copy-start(bf16[2,512,512]{2,1,0:T(8,128)(2,1)} %param.17) | copy-start | bytes 3145732
  52.8 6.9 %copy-start.5 = (f32[2,512]{1,0:T(2,128)S(1)}, f32[2,512]{1,0:T(2,128)}, u32[]{:S(2)}) copy-start(f32[2,512]{1,0:T(2,128)} %param.21) | copy-start | bytes 12292
  59.7 3.6 %copy-start.4 = (bf16[2,512,512]{2,1,0:T(8,128)(2,1)S(1)}, bf16[2,512,512]{2,1,0:T(8,128)(2,1)}, u32[]{:S(2)}) copy-start(bf16[2,512,512]{2,1,0:T(8,128)(2,1)} %param.18) | copy-start | bytes 3145732
  63.3 2.1 %copy-start.1 = (bf16[2,512,512]{2,1,0:T(8,128)(2,1)S(1)}, bf16[2,512,512]{2,1,0:T(8,128)(2,1)}, u32[]{:S(2)}) copy-start(bf16[2,512,512]{2,1,0:T(8,128)(2,1)} %param.16) | copy-start | bytes 3145732
  66.2 10.2 %collective-permute-start.12 = (bf16[2,512,64]{1,2,0:T(8,128)(2,1)S(1)}, bf16[2,512,64]{1,2,0:T(8,128)(2,1)S(1)}, u32[]{:S(2)}, u32[]{:S(2)}) collective-permute-start(bf16[2,512,64]{1,2,0:T(8,128)(2,1)S(1)} %get-tuple-element.9), channel_id=1, source_target_pairs={{0,1},{1,2},{2,3},{3,4},{4,5},{5,6},{6,7},{7,0},{8,9},{9,10},{10,1... | collective-permute-start | bytes 393224 | tf_op jit(solution)/shard_map/ppermute | solution.py:13
  66.9 13.7 %collective-permute-start.13 = (bf16[2,512,64]{1,2,0:T(8,128)(2,1)S(1)}, bf16[2,512,64]{1,2,0:T(8,128)(2,1)S(1)}, u32[]{:S(2)}, u32[]{:S(2)}) collective-permute-start(bf16[2,512,64]{1,2,0:T(8,128)(2,1)S(1)} %get-tuple-element.13), channel_id=1, source_target_pairs={{0,2},{1,3},{2,4},{3,5},{4,6},{5,7},{6,0},{7,1},{8,10},{9,11},{10,... | collective-permute-start | bytes 393224 | tf_op jit(solution)/shard_map/ppermute | solution.py:13
  67.5 21.7 %collective-permute-start.14 = (bf16[2,512,64]{1,2,0:T(8,128)(2,1)S(1)}, bf16[2,512,64]{1,2,0:T(8,128)(2,1)S(1)}, u32[]{:S(2)}, u32[]{:S(2)}) collective-permute-start(bf16[2,512,64]{1,2,0:T(8,128)(2,1)S(1)} %get-tuple-element.12), channel_id=1, source_target_pairs={{0,3},{1,4},{2,5},{3,6},{4,7},{5,0},{6,1},{7,2},{8,11},{9,12},{10,... | collective-permute-start | bytes 393224 | tf_op jit(solution)/shard_map/ppermute | solution.py:13
  69.8 19.4 %collective-permute-start.15 = (bf16[2,512,64]{1,2,0:T(8,128)(2,1)S(1)}, bf16[2,512,64]{1,2,0:T(8,128)(2,1)S(1)}, u32[]{:S(2)}, u32[]{:S(2)}) collective-permute-start(bf16[2,512,64]{1,2,0:T(8,128)(2,1)S(1)} %get-tuple-element.11), channel_id=1, source_target_pairs={{0,4},{1,5},{2,6},{3,7},{4,0},{5,1},{6,2},{7,3},{8,12},{9,13},{10,... | collective-permute-start | bytes 393224 | tf_op jit(solution)/shard_map/ppermute | solution.py:13
  73.4 16.2 %collective-permute-start.16 = (bf16[2,512,64]{1,2,0:T(8,128)(2,1)S(1)}, bf16[2,512,64]{1,2,0:T(8,128)(2,1)S(1)}, u32[]{:S(2)}, u32[]{:S(2)}) collective-permute-start(bf16[2,512,64]{1,2,0:T(8,128)(2,1)S(1)} %get-tuple-element.10), channel_id=1, source_target_pairs={{0,5},{1,6},{2,7},{3,0},{4,1},{5,2},{6,3},{7,4},{8,13},{9,14},{10,... | collective-permute-start | bytes 393224 | tf_op jit(solution)/shard_map/ppermute | solution.py:13
  76.5 19.0 %collective-permute-start.17 = (bf16[2,512,64]{1,2,0:T(8,128)(2,1)S(1)}, bf16[2,512,64]{1,2,0:T(8,128)(2,1)S(1)}, u32[]{:S(2)}, u32[]{:S(2)}) collective-permute-start(bf16[2,512,64]{1,2,0:T(8,128)(2,1)S(1)} %get-tuple-element.15), channel_id=1, source_target_pairs={{0,6},{1,7},{2,0},{3,1},{4,2},{5,3},{6,4},{7,5},{8,14},{9,15},{10,... | collective-permute-start | bytes 393224 | tf_op jit(solution)/shard_map/ppermute | solution.py:13
  80.5 16.0 %collective-permute-start.18 = (bf16[2,512,64]{1,2,0:T(8,128)(2,1)S(1)}, bf16[2,512,64]{1,2,0:T(8,128)(2,1)}, u32[]{:S(2)}, u32[]{:S(2)}) collective-permute-start(bf16[2,512,64]{1,2,0:T(8,128)(2,1)S(1)} %get-tuple-element.14), channel_id=1, source_target_pairs={{0,7},{1,0},{2,1},{3,2},{4,3},{5,4},{6,5},{7,6},{8,15},{9,8},{10,9... | collective-permute-start | bytes 393224 | tf_op jit(solution)/shard_map/ppermute | solution.py:13

commit v14 on v12

--- a/solution.py
+++ b/solution.py
@@ -111,8 +111,11 @@
         jnp.broadcast_to(rates_run, (pieces,) + left_rates.shape), "sub", 0, 0, tiled=True
     )
     rates_full = jnp.moveaxis(rates_parts, 0, 1).reshape(local_blocks, width_two)
+    left_flat = jnp.transpose(left_part, (1, 0, 2)).reshape(width_two, term_total * row_count)
+    done_flat = right_done.reshape(local_blocks, term_total * row_count, width_two)
+    left_flat, done_flat = lax.optimization_barrier((left_flat, done_flat))
     partial = jnp.einsum(
-        "tab,ktbc->kac", left_part, right_done, preferred_element_type=jnp.float32
+        "ak,jkc->jac", left_flat, done_flat, preferred_element_type=jnp.float32
     ).astype(jnp.bfloat16)
     dual_cols = jnp.einsum(
         "jab,jbc->jac", left_dual, partial, preferred_element_type=jnp.float32

time: 98.2 us -> 98.7 us (level)
  local copies, waits for them, and re-layouts: 6.66 us -> 12.6 us
  waiting for transfers between devices: 27.9 us -> 24.5 us
  matrix products: 19.2 us -> 17.2 us
    dot_general x2, matrix products: 10.5 us -> 3.89 us  [the longest x1 2.27 us: local(): jnp.einsum('jab,jbc->jac', left_dual, partial, preferred_element_type=jnp...]
    ppermute x12, waiting for transfers between devices: 13 us -> 9.32 us  [move(): return lax.ppermute(piece, 'blk', pairs_list)]
    unnamed x10 -> x13, local copies, waits for them, and re-layouts: 0.78 us -> 4.01 us
    dot_general x1, matrix products: 2.05 us -> 4.38 us  [local(): jnp.einsum('jrm,jkm->jrk', scaled, right_eigenvector_matrix, preferred_el...]
    dynamic_slice x0 -> x1, local copies, waits for them, and re-layouts: none -> 1.58 us  [local(): lax.dynamic_slice_in_dim(left_factor, part * row_count, row_count, axis=2)]
    dot_general x1, matrix products: 0.74 us -> 1.96 us  [local(): jnp.einsum('jab,jbkc->kjac', left_basis, basis_rows, preferred_element_ty...]
    slice x1, local copies, waits for them, and re-layouts: 0.29 us -> 1.34 us  [local(): from_above[half_ring:]]
    dot_general x8, matrix products: 5.74 us -> 6.78 us  [pool(): jnp.einsum('kab,abrn->krn', w, piece, preferred_element_type=jnp.float32)]
  transfers between devices with their start and end apart: 20 -> 20, of which waited for: 10 -> 9; matrix products, arithmetic and copies ran while one was open for 15% -> 20% of each run, Pallas kernels for 0% -> 0%
where the time goes in v14:
time: 98.7 us; the launch traced here: 97.3 us
  starting transfers between devices  38.1 us (39%)
  waiting for transfers between devices  24.5 us (25%)
  matrix products  17.2 us (17%)
  local copies, waits for them, and re-layouts  12.6 us (13%)
  other arithmetic  4.52 us (5%)
    ppermute x7, starting transfers between devices, scatter_sum(): got = lax.ppermute(send, axis, [(j, (j + k) % n) for j in range(n)])  18.1 us
    ppermute x7, waiting for transfers between devices, scatter_sum(): got = lax.ppermute(send, axis, [(j, (j + k) % n) for j in range(n)])  15.2 us
    ppermute x12, starting transfers between devices, move(): return lax.ppermute(piece, 'blk', pairs_list)  11.5 us
    ppermute x12, waiting for transfers between devices, move(): return lax.ppermute(piece, 'blk', pairs_list)  9.32 us
    all_to_all x1, starting transfers between devices, local(): lax.all_to_all(jnp.broadcast_to(rates_run, (pieces,) + left_rates.shape),...  8.47 us
    dot_general x8, matrix products, pool(): jnp.einsum('kab,abrn->krn', w, piece, preferred_element_type=jnp.float32)  6.78 us
    dot_general x1, matrix products, local(): jnp.einsum('jrm,jkm->jrk', scaled, right_eigenvector_matrix, preferred_el...  4.38 us
    unnamed x13, local copies, waits for them, and re-layouts  4.01 us
  transfers between devices with their start and end apart: 20, of which 9 were waited for; matrix products, arithmetic and copies ran while one was open for 20% of the time, Pallas kernels for 0%

profile of v14, /device:TPU:24, one launch (start us, length us, event | category | flops | bytes accessed | tf_op | source)
XLA Modules:
  0.0 97.3 jit_solution(4138382686900108400)
XLA Ops:
  0.0 1.5 %collective-permute-start.1 = (bf16[2,64,512]{2,1,0:T(8,128)(2,1)}, bf16[2,64,512]{2,1,0:T(8,128)(2,1)S(1)}, u32[]{:S(2)}, u32[]{:S(2)}) collective-permute-start(bf16[2,64,512]{2,1,0:T(8,128)(2,1)} %param.11), channel_id=1, source_target_pairs={{0,64},{8,72},{16,80},{24,88},{32,96},{40,104},{48,112},{56,120},{... | collective-permute-start | bytes 393224 | tf_op jit(solution)/shard_map/ppermute | solution.py:71
  1.5 1.7 %collective-permute-start = (bf16[2,64,512]{2,1,0:T(8,128)(2,1)}, bf16[2,64,512]{2,1,0:T(8,128)(2,1)S(1)}, u32[]{:S(2)}, u32[]{:S(2)}) collective-permute-start(bf16[2,64,512]{2,1,0:T(8,128)(2,1)} %param.11), channel_id=1, source_target_pairs={{0,192},{8,200},{16,208},{24,216},{32,224},{40,232},{48,240},{56,2... | collective-permute-start | bytes 393224 | tf_op jit(solution)/shard_map/ppermute | solution.py:71
  3.2 0.7 broadcast_in_dim.2
  3.9 0.7 reshape.173
  4.6 8.5 %all-to-all-start = ((f32[8,1,128]{2,1,0:T(1,128)}), f32[8,1,128]{2,1,0:T(1,128)S(1)}, u32[]{:S(2)}, u32[]{:S(2)}) async-start(f32[8,1,128]{2,1,0:T(1,128)} %reshape.173), calls=%async_computation | async-start | bytes 8192 | tf_op jit(solution)/shard_map/all_to_all | solution.py:110
  13.5 1.1 %constant_dynamic-slice_fusion = s32[32,1,2,3]{1,2,3,0:T(2,128)S(1)} fusion(s32[32,32,2,3]{1,2,3,0:T(2,128)} %param.14, s32[]{:T(128)S(6)} %select_n.103), kind=kLoop, calls=%fused_computation.53 | loop fusion | bytes 1540 | tf_op jit(solution)/shard_map/jit(dynamic_index_in_dim)/dynamic_slice | solution.py:42
  14.7 0.9 dynamic-slice_reduce_fusion
  16.0 3.0 %collective-permute-start.3 = (bf16[1,64,512]{2,1,0:T(8,128)(2,1)S(1)}, bf16[1,64,512]{2,1,0:T(8,128)(2,1)S(1)}, u32[]{:S(2)}, u32[]{:S(2)}) collective-permute-start(bf16[1,64,512]{2,1,0:T(8,128)(2,1)S(1)} %slice.65), channel_id=1, source_target_pairs={{0,192},{8,200},{16,208},{24,216},{32,224},{40,232},{48,240},{56,2... | collective-permute-start | bytes 196616 | tf_op jit(solution)/shard_map/ppermute | solution.py:71
  19.4 1.1 %copy.147 = bf16[1,2,64,512]{3,0,1,2:T(2,128)(2,1)S(1)} copy(bf16[1,2,64,512]{3,2,1,0:T(8,128)(2,1)} %bitcast.215) | data formatting | bytes 262144 | tf_op jit(solution)/shard_map/stack | solution.py:79
  21.5 1.2 %pad_maximum_fusion = bf16[4,2,64,512]{3,0,1,2:T(4,128)(2,1)S(1)} fusion(bf16[1,2,64,512]{3,0,1,2:T(2,128)(2,1)S(1)} %copy.150, bf16[1,2,64,512]{3,0,1,2:T(2,128)(2,1)S(1)} %copy.149, bf16[1,2,64,512]{3,0,1,2:T(2,128)(2,1)S(1)} %copy.148, bf16[1,2,64,512]{3,0,1,2:T(2,128)(2,1)S(1)} %copy.147), kind=kLoop, calls=%fused_computation.24 | loop fusion | flops 2097152 | bytes 1048576 | tf_op jit(solution)/shard_map/stack | solution.py:79
  23.0 1.8 %collective-permute-start.4 = (bf16[4,2,64,512]{3,0,1,2:T(4,128)(2,1)S(1)}, bf16[4,2,64,512]{3,0,1,2:T(4,128)(2,1)}, u32[]{:S(2)}, u32[]{:S(2)}) collective-permute-start(bf16[4,2,64,512]{3,0,1,2:T(4,128)(2,1)S(1)} %pad_maximum_fusion), channel_id=1, source_target_pairs={{0,48},{8,56},{16,0},{24,8},{32,16},{40,24},{48,32},{56,40},{64,11... | collective-permute-start | bytes 1572872 | tf_op jit(solution)/shard_map/ppermute | solution.py:71
  24.8 1.6 %constant_dynamic-slice_fusion.1 = bf16[8,512,64]{2,1,0:T(8,128)(2,1)S(1)} fusion(bf16[8,512,512]{2,1,0:T(8,128)(2,1)} %param.12, s32[]{:T(128)S(6)} %select_n.102), kind=kLoop, calls=%fused_computation.54 | loop fusion | bytes 1048580 | tf_op jit(solution)/shard_map/dynamic_slice | solution.py:108
  26.5 1.2 %copy.185 = bf16[8,512,64]{1,2,0:T(8,128)(2,1)} copy(bf16[8,512,64]{2,1,0:T(8,128)(2,1)S(1)} %constant_dynamic-slice_fusion.1) | data formatting | bytes 1048576
  27.7 0.5 broadcast.166
  28.2 0.7 reduce.2
  29.0 0.6 fusion.43
  29.7 5.1 %collective-permute-done.5 = bf16[4,2,64,512]{3,0,1,2:T(4,128)(2,1)S(1)} collective-permute-done((bf16[4,2,64,512]{3,0,1,2:T(4,128)(2,1)S(1)}, bf16[4,2,64,512]{3,0,1,2:T(4,128)(2,1)S(1)}, u32[]{:S(2)}, u32[]{:S(2)}) %collective-permute-start.5) | collective-permute-done | bytes 524320 | tf_op jit(solution)/shard_map/ppermute | solution.py:71
  34.9 1.6 %collective-permute-start.6 = (bf16[2,2,64,512]{3,0,1,2:T(2,128)(2,1)S(1)}, bf16[2,2,64,512]{3,0,1,2:T(2,128)(2,1)S(1)}, u32[]{:S(2)}, u32[]{:S(2)}) collective-permute-start(bf16[2,2,64,512]{3,0,1,2:T(2,128)(2,1)S(1)} %slice.68), channel_id=1, source_target_pairs={{0,16},{8,24},{16,32},{24,40},{32,48},{40,56},{48,0},{56,8},{64,80... | collective-permute-start | bytes 786440 | tf_op jit(solution)/shard_map/ppermute | solution.py:71
  36.5 1.3 %slice.69 = bf16[2,2,64,512]{3,0,1,2:T(2,128)(2,1)S(1)} slice(bf16[4,2,64,512]{3,0,1,2:T(4,128)(2,1)} %collective-permute-done.4), slice={[2:4], [0:2], [0:64], [0:512]} | slice | bytes 524288 | tf_op jit(solution)/shard_map/slice | solution.py:87
  37.8 0.6 collective-permute-start.7
  39.0 0.6 fusion.37
  39.6 1.7 %fusion.41 = f32[16,64,512,1]{2,0,3,1:T(8,128)S(1)} fusion(bf16[4,2,64,512]{3,0,1,2:T(4,128)(2,1)} %collective-permute-done.4, bf16[16,1,1,4,2]{0,4,3,2,1:T(2,128)(2,1)S(1)} %get-tuple-element.22), kind=kOutput, calls=%fused_computation.70 | convolution fusion | flops 8388608 | bytes 2621696 | tf_op jit(solution)/shard_map/kab,abrn->krn/dot_general | solution.py:92
  41.3 0.6 fusion.35
  41.9 3.6 %collective-permute-done.7 = bf16[2,2,64,512]{3,0,1,2:T(2,128)(2,1)S(1)} collective-permute-done((bf16[2,2,64,512]{3,0,1,2:T(2,128)(2,1)S(1)}, bf16[2,2,64,512]{3,0,1,2:T(2,128)(2,1)S(1)}, u32[]{:S(2)}, u32[]{:S(2)}) %collective-permute-start.7) | collective-permute-done | bytes 262176 | tf_op jit(solution)/shard_map/ppermute | solution.py:71
  45.5 0.5 pad_maximum_fusion.1
  46.2 1.0 %fusion.39 = f32[16,64,512,1]{2,0,3,1:T(8,128)S(1)} fusion(bf16[16,1,1,4,2]{0,4,3,2,1:T(2,128)(2,1)S(1)} %get-tuple-element.21, bf16[2,2,64,512]{3,0,1,2:T(2,128)(2,1)S(1)} %collective-permute-done.7, bf16[2,2,64,512]{3,0,1,2:T(2,128)(2,1)S(1)} %collective-permute-done.6), kind=kOutput, calls=%fused_computation.68 | convolution fusion | flops 9437184 | bytes 2621696 | tf_op jit(solution)/shard_map/kab,abrn->krn/dot_general | solution.py:92
  47.2 0.6 fusion.33
  48.1 0.6 fusion.31
  48.7 1.1 %fusion.9 = bf16[2,8,64,512]{3,1,0,2:T(8,128)(2,1)S(1)} fusion(bf16[4,2,64,512]{3,0,1,2:T(4,128)(2,1)S(1)} %collective-permute-done.11, f32[16,64,512,1]{2,0,3,1:T(8,128)S(1)} %fusion.31, f32[16,64,512,1]{2,0,3,1:T(8,128)S(1)} %fusion.33, f32[16,64,512,1]{2,0,3,1:T(8,128)S(1)} %fusion.35, f32[16,64,512,1]{2,0,3,1:T(8,128)S(1)} %fusion.37, ...), kind=kOutput, calls=%fused_computation.17 | convolution fusion | flops 12582912 | bytes 16253184 | tf_op jit(solution)/shard_map/kab,abrn->krn/dot_general | solution.py:92
  49.8 1.1 %copy-done.1 = bf16[8,512,512]{2,1,0:T(8,128)(2,1)S(1)} copy-done((bf16[8,512,512]{2,1,0:T(8,128)(2,1)S(1)}, bf16[8,512,512]{2,1,0:T(8,128)(2,1)}, u32[]{:S(2)}) %copy-start.1) | copy-done | bytes 4194328
  50.9 1.6 %fusion.6 = bf16[2,8,64,512]{3,2,0,1:T(8,128)(2,1)S(1)} fusion(bf16[8,512,512]{2,1,0:T(8,128)(2,1)S(1)} %copy-done.1, bf16[2,8,64,512]{3,1,0,2:T(8,128)(2,1)S(1)} %fusion.9), kind=kOutput, calls=%fused_computation.16 | convolution fusion | flops 537395200 | bytes 6291456 | tf_op jit(solution)/shard_map/ktrn,tmn->ktrm/dot_general | solution.py:105
  52.6 1.0 copy-done.3
  53.6 2.3 %convolution_convert_fusion.2 = bf16[2,512,512]{2,1,0:T(8,128)(2,1)} fusion(bf16[2,512,512]{2,1,0:T(8,128)(2,1)S(1)} %copy-done, bf16[2,512,512]{2,1,0:T(8,128)(2,1)S(1)} %bitcast.211, bf16[512,512]{0,1:T(8,128)(2,1)S(1)} %bitcast.212), kind=kOutput, calls=%fused_computation.14 | convolution fusion | flops 1074790400 | bytes 3670016 | tf_op jit(solution)/shard_map/jab,jbc->jac/dot_general | solution.py:120
  55.8 4.4 %convolution_convert_fusion.1 = bf16[2,512,512]{1,2,0:T(8,128)(2,1)} fusion(bf16[2,512,512]{2,1,0:T(8,128)(2,1)} %param.18, bf16[2,512,512]{2,1,0:T(8,128)(2,1)} %convolution_convert_fusion.2, bf16[2,512,512]{2,1,0:T(8,128)(2,1)} %param.19, f32[2,512]{1,0:T(2,128)S(1)} %copy-done.4, f32[2,512]{1,0:T(2,128)S(1)} %add.283), kind=kOutput, calls=%fused_computation.13 | convolution fusion | flops 1075838976 | bytes 4202496 | tf_op jit(solution)/shard_map/jrm,jkm->jrk/dot_general | solution.py:125
  60.2 2.0 %convolution_convert_fusion = bf16[2,8,64,512]{3,2,1,0:T(8,128)(2,1)S(1)} fusion(bf16[2,512,8,64]{1,3,2,0:T(8,128)(2,1)} %bitcast.210, bf16[2,512,512]{2,1,0:T(8,128)(2,1)S(1)} %copy-done.2), kind=kOutput, calls=%fused_computation.12 | convolution fusion | flops 537395200 | bytes 3145728 | tf_op jit(solution)/shard_map/jab,jbkc->kjac/dot_general | solution.py:129
  62.3 1.8 %collective-permute-start.12 = (bf16[2,512,64]{1,2,0:T(8,128)(2,1)S(1)}, bf16[2,512,64]{1,2,0:T(8,128)(2,1)S(1)}, u32[]{:S(2)}, u32[]{:S(2)}) collective-permute-start(bf16[2,512,64]{1,2,0:T(8,128)(2,1)S(1)} %get-tuple-element.9), channel_id=1, source_target_pairs={{0,1},{1,2},{2,3},{3,4},{4,5},{5,6},{6,7},{7,0},{8,9},{9,10},{10,1... | collective-permute-start | bytes 393224 | tf_op jit(solution)/shard_map/ppermute | solution.py:13
  64.1 2.4 %collective-permute-start.13 = (bf16[2,512,64]{1,2,0:T(8,128)(2,1)S(1)}, bf16[2,512,64]{1,2,0:T(8,128)(2,1)S(1)}, u32[]{:S(2)}, u32[]{:S(2)}) collective-permute-start(bf16[2,512,64]{1,2,0:T(8,128)(2,1)S(1)} %get-tuple-element.13), channel_id=1, source_target_pairs={{0,2},{1,3},{2,4},{3,5},{4,6},{5,7},{6,0},{7,1},{8,10},{9,11},{10,... | collective-permute-start | bytes 393224 | tf_op jit(solution)/shard_map/ppermute | solution.py:13
  66.4 2.7 %collective-permute-start.14 = (bf16[2,512,64]{1,2,0:T(8,128)(2,1)S(1)}, bf16[2,512,64]{1,2,0:T(8,128)(2,1)S(1)}, u32[]{:S(2)}, u32[]{:S(2)}) collective-permute-start(bf16[2,512,64]{1,2,0:T(8,128)(2,1)S(1)} %get-tuple-element.12), channel_id=1, source_target_pairs={{0,3},{1,4},{2,5},{3,6},{4,7},{5,0},{6,1},{7,2},{8,11},{9,12},{10,... | collective-permute-start | bytes 393224 | tf_op jit(solution)/shard_map/ppermute | solution.py:13
  69.1 2.4 %collective-permute-start.15 = (bf16[2,512,64]{1,2,0:T(8,128)(2,1)S(1)}, bf16[2,512,64]{1,2,0:T(8,128)(2,1)S(1)}, u32[]{:S(2)}, u32[]{:S(2)}) collective-permute-start(bf16[2,512,64]{1,2,0:T(8,128)(2,1)S(1)} %get-tuple-element.11), channel_id=1, source_target_pairs={{0,4},{1,5},{2,6},{3,7},{4,0},{5,1},{6,2},{7,3},{8,12},{9,13},{10,... | collective-permute-start | bytes 393224 | tf_op jit(solution)/shard_map/ppermute | solution.py:13
  71.5 2.7 %collective-permute-start.16 = (bf16[2,512,64]{1,2,0:T(8,128)(2,1)S(1)}, bf16[2,512,64]{1,2,0:T(8,128)(2,1)S(1)}, u32[]{:S(2)}, u32[]{:S(2)}) collective-permute-start(bf16[2,512,64]{1,2,0:T(8,128)(2,1)S(1)} %get-tuple-element.10), channel_id=1, source_target_pairs={{0,5},{1,6},{2,7},{3,0},{4,1},{5,2},{6,3},{7,4},{8,13},{9,14},{10,... | collective-permute-start | bytes 393224 | tf_op jit(solution)/shard_map/ppermute | solution.py:13
  74.1 3.6 %collective-permute-start.17 = (bf16[2,512,64]{1,2,0:T(8,128)(2,1)S(1)}, bf16[2,512,64]{1,2,0:T(8,128)(2,1)S(1)}, u32[]{:S(2)}, u32[]{:S(2)}) collective-permute-start(bf16[2,512,64]{1,2,0:T(8,128)(2,1)S(1)} %get-tuple-element.15), channel_id=1, source_target_pairs={{0,6},{1,7},{2,0},{3,1},{4,2},{5,3},{6,4},{7,5},{8,14},{9,15},{10,... | collective-permute-start | bytes 393224 | tf_op jit(solution)/shard_map/ppermute | solution.py:13
  77.7 2.7 %collective-permute-start.18 = (bf16[2,512,64]{1,2,0:T(8,128)(2,1)S(1)}, bf16[2,512,64]{1,2,0:T(8,128)(2,1)}, u32[]{:S(2)}, u32[]{:S(2)}) collective-permute-start(bf16[2,512,64]{1,2,0:T(8,128)(2,1)S(1)} %get-tuple-element.14), channel_id=1, source_target_pairs={{0,7},{1,0},{2,1},{3,2},{4,3},{5,4},{6,5},{7,6},{8,15},{9,8},{10,9... | collective-permute-start | bytes 393224 | tf_op jit(solution)/shard_map/ppermute | solution.py:13
  80.4 2.6 %collective-permute-done.14 = bf16[2,512,64]{1,2,0:T(8,128)(2,1)S(1)} collective-permute-done((bf16[2,512,64]{1,2,0:T(8,128)(2,1)S(1)}, bf16[2,512,64]{1,2,0:T(8,128)(2,1)S(1)}, u32[]{:S(2)}, u32[]{:S(2)}) %collective-permute-start.14) | collective-permute-done | bytes 131104 | tf_op jit(solution)/shard_map/ppermute | solution.py:13
  83.0 5.0 %collective-permute-done.15 = bf16[2,512,64]{1,2,0:T(8,128)(2,1)S(1)} collective-permute-done((bf16[2,512,64]{1,2,0:T(8,128)(2,1)S(1)}, bf16[2,512,64]{1,2,0:T(8,128)(2,1)S(1)}, u32[]{:S(2)}, u32[]{:S(2)}) %collective-permute-start.15) | collective-permute-done | bytes 131104 | tf_op jit(solution)/shard_map/ppermute | solution.py:13
  87.9 2.2 %collective-permute-done.16 = bf16[2,512,64]{1,2,0:T(8,128)(2,1)S(1)} collective-permute-done((bf16[2,512,64]{1,2,0:T(8,128)(2,1)S(1)}, bf16[2,512,64]{1,2,0:T(8,128)(2,1)S(1)}, u32[]{:S(2)}, u32[]{:S(2)}) %collective-permute-start.16) | collective-permute-done | bytes 131104 | tf_op jit(solution)/shard_map/ppermute | solution.py:13
  90.1 4.3 %collective-permute-done.17 = bf16[2,512,64]{1,2,0:T(8,128)(2,1)S(1)} collective-permute-done((bf16[2,512,64]{1,2,0:T(8,128)(2,1)S(1)}, bf16[2,512,64]{1,2,0:T(8,128)(2,1)S(1)}, u32[]{:S(2)}, u32[]{:S(2)}) %collective-permute-start.17) | collective-permute-done | bytes 131104 | tf_op jit(solution)/shard_map/ppermute | solution.py:13
  94.4 1.1 %collective-permute-done.18 = bf16[2,512,64]{1,2,0:T(8,128)(2,1)} collective-permute-done((bf16[2,512,64]{1,2,0:T(8,128)(2,1)S(1)}, bf16[2,512,64]{1,2,0:T(8,128)(2,1)}, u32[]{:S(2)}, u32[]{:S(2)}) %collective-permute-start.18) | collective-permute-done | bytes 131104 | tf_op jit(solution)/shard_map/ppermute | solution.py:13
  95.5 1.8 %fusion.22 = f32[2,512,64]{1,2,0:T(8,128)} fusion(bf16[2,512,64]{1,2,0:T(8,128)(2,1)} %collective-permute-done.18, bf16[2,512,64]{1,2,0:T(8,128)(2,1)S(1)} %collective-permute-done.17, bf16[2,512,64]{1,2,0:T(8,128)(2,1)S(1)} %collective-permute-done.16, bf16[2,512,64]{1,2,0:T(8,128)(2,1)S(1)} %collective-permute-done.15, ...), kind=kLoop, calls=%fused_computation.33 | loop fusion | flops 983040 | bytes 1310724 | tf_op jit(solution)/shard_map/add | solution.py:14
  (52 shorter events, 3.9 us)
Async XLA Ops:
  0.0 52.6 %copy-start = (bf16[2,512,512]{2,1,0:T(8,128)(2,1)S(1)}, bf16[2,512,512]{2,1,0:T(8,128)(2,1)}, u32[]{:S(2)}) copy-start(bf16[2,512,512]{2,1,0:T(8,128)(2,1)} %param.17) | copy-start | bytes 3145732
  0.0 15.7 %collective-permute-start.1 = (bf16[2,64,512]{2,1,0:T(8,128)(2,1)}, bf16[2,64,512]{2,1,0:T(8,128)(2,1)S(1)}, u32[]{:S(2)}, u32[]{:S(2)}) collective-permute-start(bf16[2,64,512]{2,1,0:T(8,128)(2,1)} %param.11), channel_id=1, source_target_pairs={{0,64},{8,72},{16,80},{24,88},{32,96},{40,104},{48,112},{56,120},{... | collective-permute-start | bytes 393224 | tf_op jit(solution)/shard_map/ppermute | solution.py:71
  1.5 14.5 %collective-permute-start = (bf16[2,64,512]{2,1,0:T(8,128)(2,1)}, bf16[2,64,512]{2,1,0:T(8,128)(2,1)S(1)}, u32[]{:S(2)}, u32[]{:S(2)}) collective-permute-start(bf16[2,64,512]{2,1,0:T(8,128)(2,1)} %param.11), channel_id=1, source_target_pairs={{0,192},{8,200},{16,208},{24,216},{32,224},{40,232},{48,240},{56,2... | collective-permute-start | bytes 393224 | tf_op jit(solution)/shard_map/ppermute | solution.py:71
  4.6 23.1 %all-to-all-start = ((f32[8,1,128]{2,1,0:T(1,128)}), f32[8,1,128]{2,1,0:T(1,128)S(1)}, u32[]{:S(2)}, u32[]{:S(2)}) async-start(f32[8,1,128]{2,1,0:T(1,128)} %reshape.173), calls=%async_computation | async-start | bytes 8192 | tf_op jit(solution)/shard_map/all_to_all | solution.py:110
  15.7 5.6 %collective-permute-start.2 = (bf16[1,64,512]{2,1,0:T(8,128)(2,1)S(1)}, bf16[1,64,512]{2,1,0:T(8,128)(2,1)S(1)}, u32[]{:S(2)}, u32[]{:S(2)}) collective-permute-start(bf16[1,64,512]{2,1,0:T(8,128)(2,1)S(1)} %slice.64), channel_id=1, source_target_pairs={{0,64},{8,72},{16,80},{24,88},{32,96},{40,104},{48,112},{56,120},{... | collective-permute-start | bytes 196616 | tf_op jit(solution)/shard_map/ppermute | solution.py:71
  16.0 5.2 %collective-permute-start.3 = (bf16[1,64,512]{2,1,0:T(8,128)(2,1)S(1)}, bf16[1,64,512]{2,1,0:T(8,128)(2,1)S(1)}, u32[]{:S(2)}, u32[]{:S(2)}) collective-permute-start(bf16[1,64,512]{2,1,0:T(8,128)(2,1)S(1)} %slice.65), channel_id=1, source_target_pairs={{0,192},{8,200},{16,208},{24,216},{32,224},{40,232},{48,240},{56,2... | collective-permute-start | bytes 196616 | tf_op jit(solution)/shard_map/ppermute | solution.py:71
  22.7 12.1 %collective-permute-start.5 = (bf16[4,2,64,512]{3,0,1,2:T(4,128)(2,1)S(1)}, bf16[4,2,64,512]{3,0,1,2:T(4,128)(2,1)S(1)}, u32[]{:S(2)}, u32[]{:S(2)}) collective-permute-start(bf16[4,2,64,512]{3,0,1,2:T(4,128)(2,1)S(1)} %pad_maximum_fusion), channel_id=1, source_target_pairs={{0,16},{8,24},{16,32},{24,40},{32,48},{40,56},{48,0},{56,8},{64,80... | collective-permute-start | bytes 1572872 | tf_op jit(solution)/shard_map/ppermute | solution.py:71
  23.0 13.5 %collective-permute-start.4 = (bf16[4,2,64,512]{3,0,1,2:T(4,128)(2,1)S(1)}, bf16[4,2,64,512]{3,0,1,2:T(4,128)(2,1)}, u32[]{:S(2)}, u32[]{:S(2)}) collective-permute-start(bf16[4,2,64,512]{3,0,1,2:T(4,128)(2,1)S(1)} %pad_maximum_fusion), channel_id=1, source_target_pairs={{0,48},{8,56},{16,0},{24,8},{32,16},{40,24},{48,32},{56,40},{64,11... | collective-permute-start | bytes 1572872 | tf_op jit(solution)/shard_map/ppermute | solution.py:71
  29.0 12.2 %collective-permute-start.8 = (bf16[4,2,64,512]{3,0,1,2:T(4,128)(2,1)S(1)}, bf16[4,2,64,512]{3,0,1,2:T(4,128)(2,1)S(1)}, u32[]{:S(2)}, u32[]{:S(2)}) collective-permute-start(bf16[4,2,64,512]{3,0,1,2:T(4,128)(2,1)S(1)} %pad_maximum_fusion), channel_id=1, source_target_pairs={{0,8},{8,0},{16,24},{24,16},{32,40},{40,32},{48,56},{56,48},{64,72... | collective-permute-start | bytes 1572872 | tf_op jit(solution)/shard_map/ppermute | solution.py:71
  34.9 6.9 %collective-permute-start.6 = (bf16[2,2,64,512]{3,0,1,2:T(2,128)(2,1)S(1)}, bf16[2,2,64,512]{3,0,1,2:T(2,128)(2,1)S(1)}, u32[]{:S(2)}, u32[]{:S(2)}) collective-permute-start(bf16[2,2,64,512]{3,0,1,2:T(2,128)(2,1)S(1)} %slice.68), channel_id=1, source_target_pairs={{0,16},{8,24},{16,32},{24,40},{32,48},{40,56},{48,0},{56,8},{64,80... | collective-permute-start | bytes 786440 | tf_op jit(solution)/shard_map/ppermute | solution.py:71
  37.8 7.7 %collective-permute-start.7 = (bf16[2,2,64,512]{3,0,1,2:T(2,128)(2,1)S(1)}, bf16[2,2,64,512]{3,0,1,2:T(2,128)(2,1)S(1)}, u32[]{:S(2)}, u32[]{:S(2)}) collective-permute-start(bf16[2,2,64,512]{3,0,1,2:T(2,128)(2,1)S(1)} %slice.69), channel_id=1, source_target_pairs={{0,48},{8,56},{16,0},{24,8},{32,16},{40,24},{48,32},{56,40},{64,11... | collective-permute-start | bytes 786440 | tf_op jit(solution)/shard_map/ppermute | solution.py:71
  38.5 8.7 %collective-permute-start.9 = (bf16[4,2,64,512]{3,0,1,2:T(4,128)(2,1)}, bf16[4,2,64,512]{3,0,1,2:T(4,128)(2,1)S(1)}, u32[]{:S(2)}, u32[]{:S(2)}) collective-permute-start(bf16[4,2,64,512]{3,0,1,2:T(4,128)(2,1)} %collective-permute-done.4), channel_id=1, source_target_pairs={{0,8},{8,0},{16,24},{24,16},{32,40},{40,32},{48,56},{56,48},{64,72... | collective-permute-start | bytes 1572872 | tf_op jit(solution)/shard_map/ppermute | solution.py:71
  38.5 10.2 %collective-permute-start.11 = (bf16[4,2,64,512]{3,0,1,2:T(4,128)(2,1)S(1)}, bf16[4,2,64,512]{3,0,1,2:T(4,128)(2,1)S(1)}, u32[]{:S(2)}, u32[]{:S(2)}) collective-permute-start(bf16[4,2,64,512]{3,0,1,2:T(4,128)(2,1)S(1)} %collective-permute-done.5), channel_id=1, source_target_pairs={{0,8},{8,0},{16,24},{24,16},{32,40},{40,32},{48,56},{56,48},{64,72... | collective-permute-start | bytes 1572872 | tf_op jit(solution)/shard_map/ppermute | solution.py:71
  46.1 2.0 %collective-permute-start.10 = (bf16[4,2,64,512]{3,0,1,2:T(4,128)(2,1)S(1)}, bf16[4,2,64,512]{3,0,1,2:T(4,128)(2,1)S(1)}, u32[]{:S(2)}, u32[]{:S(2)}) collective-permute-start(bf16[4,2,64,512]{3,0,1,2:T(4,128)(2,1)S(1)} %pad_maximum_fusion.1), channel_id=1, source_target_pairs={{0,8},{8,0},{16,24},{24,16},{32,40},{40,32},{48,56},{56,48},{64,72... | collective-permute-start | bytes 1572872 | tf_op jit(solution)/shard_map/ppermute | solution.py:71
  48.7 2.2 %copy-start.1 = (bf16[8,512,512]{2,1,0:T(8,128)(2,1)S(1)}, bf16[8,512,512]{2,1,0:T(8,128)(2,1)}, u32[]{:S(2)}) copy-start(bf16[8,512,512]{2,1,0:T(8,128)(2,1)} %param.13) | copy-start | bytes 12582916
  52.5 1.1 %copy-start.3 = (bf16[8,512,64]{1,2,0:T(8,128)(2,1)S(1)}, bf16[8,512,64]{1,2,0:T(8,128)(2,1)}, u32[]{:S(2)}) copy-start(bf16[8,512,64]{1,2,0:T(8,128)(2,1)} %copy.185) | copy-start | bytes 1572868
  53.6 2.3 %copy-start.4 = (f32[2,512]{1,0:T(2,128)S(1)}, f32[2,512]{1,0:T(2,128)}, u32[]{:S(2)}) copy-start(f32[2,512]{1,0:T(2,128)} %param.21) | copy-start | bytes 12292
  55.8 4.4 %copy-start.2 = (bf16[2,512,512]{2,1,0:T(8,128)(2,1)S(1)}, bf16[2,512,512]{2,1,0:T(8,128)(2,1)}, u32[]{:S(2)}) copy-start(bf16[2,512,512]{2,1,0:T(8,128)(2,1)} %param.16) | copy-start | bytes 3145732
  62.3 11.9 %collective-permute-start.12 = (bf16[2,512,64]{1,2,0:T(8,128)(2,1)S(1)}, bf16[2,512,64]{1,2,0:T(8,128)(2,1)S(1)}, u32[]{:S(2)}, u32[]{:S(2)}) collective-permute-start(bf16[2,512,64]{1,2,0:T(8,128)(2,1)S(1)} %get-tuple-element.9), channel_id=1, source_target_pairs={{0,1},{1,2},{2,3},{3,4},{4,5},{5,6},{6,7},{7,0},{8,9},{9,10},{10,1... | collective-permute-start | bytes 393224 | tf_op jit(solution)/shard_map/ppermute | solution.py:13
  64.1 13.6 %collective-permute-start.13 = (bf16[2,512,64]{1,2,0:T(8,128)(2,1)S(1)}, bf16[2,512,64]{1,2,0:T(8,128)(2,1)S(1)}, u32[]{:S(2)}, u32[]{:S(2)}) collective-permute-start(bf16[2,512,64]{1,2,0:T(8,128)(2,1)S(1)} %get-tuple-element.13), channel_id=1, source_target_pairs={{0,2},{1,3},{2,4},{3,5},{4,6},{5,7},{6,0},{7,1},{8,10},{9,11},{10,... | collective-permute-start | bytes 393224 | tf_op jit(solution)/shard_map/ppermute | solution.py:13
  66.4 16.5 %collective-permute-start.14 = (bf16[2,512,64]{1,2,0:T(8,128)(2,1)S(1)}, bf16[2,512,64]{1,2,0:T(8,128)(2,1)S(1)}, u32[]{:S(2)}, u32[]{:S(2)}) collective-permute-start(bf16[2,512,64]{1,2,0:T(8,128)(2,1)S(1)} %get-tuple-element.12), channel_id=1, source_target_pairs={{0,3},{1,4},{2,5},{3,6},{4,7},{5,0},{6,1},{7,2},{8,11},{9,12},{10,... | collective-permute-start | bytes 393224 | tf_op jit(solution)/shard_map/ppermute | solution.py:13
  69.1 18.8 %collective-permute-start.15 = (bf16[2,512,64]{1,2,0:T(8,128)(2,1)S(1)}, bf16[2,512,64]{1,2,0:T(8,128)(2,1)S(1)}, u32[]{:S(2)}, u32[]{:S(2)}) collective-permute-start(bf16[2,512,64]{1,2,0:T(8,128)(2,1)S(1)} %get-tuple-element.11), channel_id=1, source_target_pairs={{0,4},{1,5},{2,6},{3,7},{4,0},{5,1},{6,2},{7,3},{8,12},{9,13},{10,... | collective-permute-start | bytes 393224 | tf_op jit(solution)/shard_map/ppermute | solution.py:13
  71.5 18.7 %collective-permute-start.16 = (bf16[2,512,64]{1,2,0:T(8,128)(2,1)S(1)}, bf16[2,512,64]{1,2,0:T(8,128)(2,1)S(1)}, u32[]{:S(2)}, u32[]{:S(2)}) collective-permute-start(bf16[2,512,64]{1,2,0:T(8,128)(2,1)S(1)} %get-tuple-element.10), channel_id=1, source_target_pairs={{0,5},{1,6},{2,7},{3,0},{4,1},{5,2},{6,3},{7,4},{8,13},{9,14},{10,... | collective-permute-start | bytes 393224 | tf_op jit(solution)/shard_map/ppermute | solution.py:13
  74.1 20.3 %collective-permute-start.17 = (bf16[2,512,64]{1,2,0:T(8,128)(2,1)S(1)}, bf16[2,512,64]{1,2,0:T(8,128)(2,1)S(1)}, u32[]{:S(2)}, u32[]{:S(2)}) collective-permute-start(bf16[2,512,64]{1,2,0:T(8,128)(2,1)S(1)} %get-tuple-element.15), channel_id=1, source_target_pairs={{0,6},{1,7},{2,0},{3,1},{4,2},{5,3},{6,4},{7,5},{8,14},{9,15},{10,... | collective-permute-start | bytes 393224 | tf_op jit(solution)/shard_map/ppermute | solution.py:13
  77.7 17.8 %collective-permute-start.18 = (bf16[2,512,64]{1,2,0:T(8,128)(2,1)S(1)}, bf16[2,512,64]{1,2,0:T(8,128)(2,1)}, u32[]{:S(2)}, u32[]{:S(2)}) collective-permute-start(bf16[2,512,64]{1,2,0:T(8,128)(2,1)S(1)} %get-tuple-element.14), channel_id=1, source_target_pairs={{0,7},{1,0},{2,1},{3,2},{4,3},{5,4},{6,5},{7,6},{8,15},{9,8},{10,9... | collective-permute-start | bytes 393224 | tf_op jit(solution)/shard_map/ppermute | solution.py:13

commit v15 on v12

--- a/solution.py
+++ b/solution.py
@@ -8,7 +8,7 @@
     n = chunks.shape[0]
     me = lax.axis_index(axis)
     total = lax.dynamic_index_in_dim(chunks, me, 0, keepdims=False).astype(jnp.float32)
-    for k in range(1, n):
+    for k in sorted(range(1, n), key=lambda k: (-min(k, n - k), k)):
         send = lax.dynamic_index_in_dim(chunks, (me + k) % n, 0, keepdims=False)
         got = lax.ppermute(send, axis, [(j, (j + k) % n) for j in range(n)])
         total = total + got.astype(jnp.float32)

time: 98.2 us -> 93.9 us (0.956)
  starting transfers between devices: 38.1 us -> 34.7 us
    ppermute x7, starting transfers between devices: 18.1 us -> 14.7 us  [scatter_sum(): got = lax.ppermute(send, axis, [(j, (j + k) % n) for j in range(n)])]
  transfers between devices with their start and end apart: 20 -> 20, of which waited for: 10 -> 12; matrix products, arithmetic and copies ran while one was open for 15% -> 15% of each run, Pallas kernels for 0% -> 0%
where the time goes in v15:
time: 93.9 us; the launch traced here: 93.2 us
  starting transfers between devices  34.7 us (37%)
  waiting for transfers between devices  27.7 us (29%)
  matrix products  19.2 us (20%)
  local copies, waits for them, and re-layouts  6.66 us (7%)
  other arithmetic  4.52 us (5%)
    ppermute x7, waiting for transfers between devices, scatter_sum(): got = lax.ppermute(send, axis, [(j, (j + k) % n) for j in range(n)])  14.7 us
    ppermute x7, starting transfers between devices, scatter_sum(): got = lax.ppermute(send, axis, [(j, (j + k) % n) for j in range(n)])  14.7 us
    ppermute x12, waiting for transfers between devices, move(): return lax.ppermute(piece, 'blk', pairs_list)  13 us
    ppermute x12, starting transfers between devices, move(): return lax.ppermute(piece, 'blk', pairs_list)  11.5 us
    all_to_all x1, starting transfers between devices, local(): lax.all_to_all(jnp.broadcast_to(rates_run, (pieces,) + left_rates.shape),...  8.47 us
    dot_general x1, matrix products, local(): jnp.einsum('tab,ktbc->kac', left_part, right_done, preferred_element_type...  6.6 us
    dot_general x8, matrix products, pool(): jnp.einsum('kab,abrn->krn', w, piece, preferred_element_type=jnp.float32)  5.74 us
    dot_general x1, matrix products, local(): jnp.einsum('jrn,jmn->jrm', dual_cols, right_dual, preferred_element_type=...  3.91 us
  transfers between devices with their start and end apart: 20, of which 12 were waited for; matrix products, arithmetic and copies ran while one was open for 15% of the time, Pallas kernels for 0%

profile of v15, /device:TPU:24, one launch (start us, length us, event | category | flops | bytes accessed | tf_op | source)
XLA Modules:
  0.0 93.2 jit_solution(1129760406574961644)
XLA Ops:
  0.0 1.5 %collective-permute-start.1 = (bf16[2,64,512]{2,1,0:T(8,128)(2,1)}, bf16[2,64,512]{2,1,0:T(8,128)(2,1)S(1)}, u32[]{:S(2)}, u32[]{:S(2)}) collective-permute-start(bf16[2,64,512]{2,1,0:T(8,128)(2,1)} %param.11), channel_id=1, source_target_pairs={{0,64},{8,72},{16,80},{24,88},{32,96},{40,104},{48,112},{56,120},{... | collective-permute-start | bytes 393224 | tf_op jit(solution)/shard_map/ppermute | solution.py:71
  1.5 1.7 %collective-permute-start = (bf16[2,64,512]{2,1,0:T(8,128)(2,1)}, bf16[2,64,512]{2,1,0:T(8,128)(2,1)S(1)}, u32[]{:S(2)}, u32[]{:S(2)}) collective-permute-start(bf16[2,64,512]{2,1,0:T(8,128)(2,1)} %param.11), channel_id=1, source_target_pairs={{0,192},{8,200},{16,208},{24,216},{32,224},{40,232},{48,240},{56,2... | collective-permute-start | bytes 393224 | tf_op jit(solution)/shard_map/ppermute | solution.py:71
  3.2 0.7 broadcast_in_dim.2
  3.9 0.7 reshape.166
  4.6 8.5 %all-to-all-start = ((f32[8,1,128]{2,1,0:T(1,128)}), f32[8,1,128]{2,1,0:T(1,128)S(1)}, u32[]{:S(2)}, u32[]{:S(2)}) async-start(f32[8,1,128]{2,1,0:T(1,128)} %reshape.166), calls=%async_computation | async-start | bytes 8192 | tf_op jit(solution)/shard_map/all_to_all | solution.py:110
  13.4 1.1 %constant_dynamic-slice_fusion = s32[32,1,2,3]{1,2,3,0:T(2,128)S(1)} fusion(s32[32,32,2,3]{1,2,3,0:T(2,128)} %param.14, s32[]{:T(128)S(6)} %select_n.102), kind=kLoop, calls=%fused_computation.53 | loop fusion | bytes 1540 | tf_op jit(solution)/shard_map/jit(dynamic_index_in_dim)/dynamic_slice | solution.py:42
  14.6 0.9 dynamic-slice_reduce_fusion
  15.5 0.4 collective-permute-start.2
  15.9 3.0 %collective-permute-start.3 = (bf16[1,64,512]{2,1,0:T(8,128)(2,1)S(1)}, bf16[1,64,512]{2,1,0:T(8,128)(2,1)S(1)}, u32[]{:S(2)}, u32[]{:S(2)}) collective-permute-start(bf16[1,64,512]{2,1,0:T(8,128)(2,1)S(1)} %slice.65), channel_id=1, source_target_pairs={{0,192},{8,200},{16,208},{24,216},{32,224},{40,232},{48,240},{56,2... | collective-permute-start | bytes 196616 | tf_op jit(solution)/shard_map/ppermute | solution.py:71
  19.1 1.1 %copy.133 = bf16[1,2,64,512]{3,0,1,2:T(2,128)(2,1)S(1)} copy(bf16[1,2,64,512]{3,2,1,0:T(8,128)(2,1)} %bitcast.217) | data formatting | bytes 262144 | tf_op jit(solution)/shard_map/stack | solution.py:79
  20.6 0.5 collective-permute-done.2
  21.3 1.2 %pad_maximum_fusion = bf16[4,2,64,512]{3,0,1,2:T(4,128)(2,1)S(1)} fusion(bf16[1,2,64,512]{3,0,1,2:T(2,128)(2,1)S(1)} %copy.136, bf16[1,2,64,512]{3,0,1,2:T(2,128)(2,1)S(1)} %copy.135, bf16[1,2,64,512]{3,0,1,2:T(2,128)(2,1)S(1)} %copy.134, bf16[1,2,64,512]{3,0,1,2:T(2,128)(2,1)S(1)} %copy.133), kind=kLoop, calls=%fused_computation.24 | loop fusion | flops 2097152 | bytes 1048576 | tf_op jit(solution)/shard_map/stack | solution.py:79
  22.6 0.3 collective-permute-start.5
  22.9 1.8 %collective-permute-start.4 = (bf16[4,2,64,512]{3,0,1,2:T(4,128)(2,1)S(1)}, bf16[4,2,64,512]{3,0,1,2:T(4,128)(2,1)S(1)}, u32[]{:S(2)}, u32[]{:S(2)}) collective-permute-start(bf16[4,2,64,512]{3,0,1,2:T(4,128)(2,1)S(1)} %pad_maximum_fusion), channel_id=1, source_target_pairs={{0,48},{8,56},{16,0},{24,8},{32,16},{40,24},{48,32},{56,40},{64,11... | collective-permute-start | bytes 1572872 | tf_op jit(solution)/shard_map/ppermute | solution.py:71
  25.1 0.5 broadcast.166
  25.6 0.7 reduce.2
  26.5 0.6 fusion.46
  27.1 7.5 %collective-permute-done.5 = bf16[4,2,64,512]{3,0,1,2:T(4,128)(2,1)S(1)} collective-permute-done((bf16[4,2,64,512]{3,0,1,2:T(4,128)(2,1)S(1)}, bf16[4,2,64,512]{3,0,1,2:T(4,128)(2,1)S(1)}, u32[]{:S(2)}, u32[]{:S(2)}) %collective-permute-start.5) | collective-permute-done | bytes 524320 | tf_op jit(solution)/shard_map/ppermute | solution.py:71
  34.8 1.6 %collective-permute-start.6 = (bf16[2,2,64,512]{3,0,1,2:T(2,128)(2,1)S(1)}, bf16[2,2,64,512]{3,0,1,2:T(2,128)(2,1)S(1)}, u32[]{:S(2)}, u32[]{:S(2)}) collective-permute-start(bf16[2,2,64,512]{3,0,1,2:T(2,128)(2,1)S(1)} %slice.68), channel_id=1, source_target_pairs={{0,16},{8,24},{16,32},{24,40},{32,48},{40,56},{48,0},{56,8},{64,80... | collective-permute-start | bytes 786440 | tf_op jit(solution)/shard_map/ppermute | solution.py:71
  36.4 0.3 slice.69
  36.7 0.6 collective-permute-start.7
  37.3 0.5 collective-permute-start.11
  37.8 0.6 fusion.40
  38.4 0.6 fusion.44
  39.1 0.6 fusion.38
  39.7 1.6 %collective-permute-done.6 = bf16[2,2,64,512]{3,0,1,2:T(2,128)(2,1)S(1)} collective-permute-done((bf16[2,2,64,512]{3,0,1,2:T(2,128)(2,1)S(1)}, bf16[2,2,64,512]{3,0,1,2:T(2,128)(2,1)S(1)}, u32[]{:S(2)}, u32[]{:S(2)}) %collective-permute-start.6) | collective-permute-done | bytes 262176 | tf_op jit(solution)/shard_map/ppermute | solution.py:71
  41.2 3.1 %collective-permute-done.7 = bf16[2,2,64,512]{3,0,1,2:T(2,128)(2,1)S(1)} collective-permute-done((bf16[2,2,64,512]{3,0,1,2:T(2,128)(2,1)S(1)}, bf16[2,2,64,512]{3,0,1,2:T(2,128)(2,1)S(1)}, u32[]{:S(2)}, u32[]{:S(2)}) %collective-permute-start.7) | collective-permute-done | bytes 262176 | tf_op jit(solution)/shard_map/ppermute | solution.py:71
  44.3 0.5 pad_maximum_fusion.1
  45.0 1.0 %fusion.42 = f32[16,64,512,1]{2,0,3,1:T(8,128)S(1)} fusion(bf16[16,1,1,4,2]{0,4,3,2,1:T(2,128)(2,1)S(1)} %get-tuple-element.17, bf16[2,2,64,512]{3,0,1,2:T(2,128)(2,1)S(1)} %collective-permute-done.7, bf16[2,2,64,512]{3,0,1,2:T(2,128)(2,1)S(1)} %collective-permute-done.6), kind=kOutput, calls=%fused_computation.67 | convolution fusion | flops 9437184 | bytes 2621696 | tf_op jit(solution)/shard_map/kab,abrn->krn/dot_general | solution.py:92
  46.0 0.6 fusion.36
  46.9 0.6 fusion.34
  47.5 1.1 %fusion.9 = bf16[2,8,64,512]{3,1,0,2:T(8,128)(2,1)S(1)} fusion(bf16[4,2,64,512]{3,0,1,2:T(4,128)(2,1)S(1)} %collective-permute-done.11, f32[16,64,512,1]{2,0,3,1:T(8,128)S(1)} %fusion.34, f32[16,64,512,1]{2,0,3,1:T(8,128)S(1)} %fusion.36, f32[16,64,512,1]{2,0,3,1:T(8,128)S(1)} %fusion.38, f32[16,64,512,1]{2,0,3,1:T(8,128)S(1)} %fusion.40, ...), kind=kOutput, calls=%fused_computation.17 | convolution fusion | flops 12582912 | bytes 16253184 | tf_op jit(solution)/shard_map/kab,abrn->krn/dot_general | solution.py:92
  48.6 6.6 %bitcast_convert_fusion = bf16[2,512,512]{2,1,0:T(8,128)(2,1)} fusion(bf16[8,512,512]{2,1,0:T(8,128)(2,1)} %param.12, s32[]{:T(128)S(6)} %select_n.109, bf16[8,512,512]{2,1,0:T(8,128)(2,1)} %param.13, bf16[2,8,64,512]{3,1,0,2:T(8,128)(2,1)S(1)} %fusion.9), kind=kOutput, calls=%fused_computation.2 | convolution fusion | flops 1074790400 | bytes 7340036 | tf_op jit(solution)/shard_map/tab,ktbc->kac/dot_general | solution.py:114
  55.2 3.9 %divide_convert_fusion = bf16[2,512,512]{2,1,0:T(8,128)(2,1)} fusion(bf16[2,512,512]{2,1,0:T(8,128)(2,1)S(1)} %copy-done, bf16[2,512,512]{2,1,0:T(8,128)(2,1)} %bitcast_convert_fusion, bf16[2,512,512]{2,1,0:T(8,128)(2,1)} %param.17, f32[2,512]{1,0:T(2,128)S(1)} %copy-done.3, f32[2,512]{1,0:T(2,128)S(1)} %add.283), kind=kOutput, calls=%fused_computation.11 | convolution fusion | flops 1075838976 | bytes 4202496 | tf_op jit(solution)/shard_map/jrn,jmn->jrm/dot_general | solution.py:120
  59.1 2.1 %convolution_convert_fusion.1 = bf16[2,512,512]{1,2,0:T(8,128)(2,1)S(1)} fusion(bf16[2,512,512]{2,1,0:T(8,128)(2,1)} %divide_convert_fusion, bf16[2,512,512]{2,1,0:T(8,128)(2,1)S(1)} %copy-done.2), kind=kOutput, calls=%fused_computation.14 | convolution fusion | flops 537395200 | bytes 3145728 | tf_op jit(solution)/shard_map/jrm,jkm->jrk/dot_general | solution.py:122
  61.2 0.7 convolution_convert_fusion
  62.0 5.5 %collective-permute-start.12 = (bf16[2,512,64]{1,2,0:T(8,128)(2,1)S(1)}, bf16[2,512,64]{1,2,0:T(8,128)(2,1)S(1)}, u32[]{:S(2)}, u32[]{:S(2)}) collective-permute-start(bf16[2,512,64]{1,2,0:T(8,128)(2,1)S(1)} %get-tuple-element.5), channel_id=1, source_target_pairs={{0,4},{1,5},{2,6},{3,7},{4,0},{5,1},{6,2},{7,3},{8,12},{9,13},{10,... | collective-permute-start | bytes 393224 | tf_op jit(solution)/shard_map/ppermute | solution.py:13
  67.6 0.6 collective-permute-start.13
  68.1 4.5 %collective-permute-start.14 = (bf16[2,512,64]{1,2,0:T(8,128)(2,1)S(1)}, bf16[2,512,64]{1,2,0:T(8,128)(2,1)S(1)}, u32[]{:S(2)}, u32[]{:S(2)}) collective-permute-start(bf16[2,512,64]{1,2,0:T(8,128)(2,1)S(1)} %get-tuple-element.8), channel_id=1, source_target_pairs={{0,5},{1,6},{2,7},{3,0},{4,1},{5,2},{6,3},{7,4},{8,13},{9,14},{10,... | collective-permute-start | bytes 393224 | tf_op jit(solution)/shard_map/ppermute | solution.py:13
  72.6 0.6 collective-permute-start.15
  73.1 3.6 %collective-permute-start.16 = (bf16[2,512,64]{1,2,0:T(8,128)(2,1)S(1)}, bf16[2,512,64]{1,2,0:T(8,128)(2,1)S(1)}, u32[]{:S(2)}, u32[]{:S(2)}) collective-permute-start(bf16[2,512,64]{1,2,0:T(8,128)(2,1)S(1)} %get-tuple-element.6), channel_id=1, source_target_pairs={{0,6},{1,7},{2,0},{3,1},{4,2},{5,3},{6,4},{7,5},{8,14},{9,15},{10,... | collective-permute-start | bytes 393224 | tf_op jit(solution)/shard_map/ppermute | solution.py:13
  76.7 0.9 collective-permute-done.12
  77.6 5.7 %collective-permute-done.13 = bf16[2,512,64]{1,2,0:T(8,128)(2,1)S(1)} collective-permute-done((bf16[2,512,64]{1,2,0:T(8,128)(2,1)S(1)}, bf16[2,512,64]{1,2,0:T(8,128)(2,1)S(1)}, u32[]{:S(2)}, u32[]{:S(2)}) %collective-permute-start.13) | collective-permute-done | bytes 131104 | tf_op jit(solution)/shard_map/ppermute | solution.py:13
  83.4 2.3 %collective-permute-done.14 = bf16[2,512,64]{1,2,0:T(8,128)(2,1)S(1)} collective-permute-done((bf16[2,512,64]{1,2,0:T(8,128)(2,1)S(1)}, bf16[2,512,64]{1,2,0:T(8,128)(2,1)S(1)}, u32[]{:S(2)}, u32[]{:S(2)}) %collective-permute-start.14) | collective-permute-done | bytes 131104 | tf_op jit(solution)/shard_map/ppermute | solution.py:13
  85.6 2.5 %collective-permute-done.15 = bf16[2,512,64]{1,2,0:T(8,128)(2,1)S(1)} collective-permute-done((bf16[2,512,64]{1,2,0:T(8,128)(2,1)S(1)}, bf16[2,512,64]{1,2,0:T(8,128)(2,1)S(1)}, u32[]{:S(2)}, u32[]{:S(2)}) %collective-permute-start.15) | collective-permute-done | bytes 131104 | tf_op jit(solution)/shard_map/ppermute | solution.py:13
  88.1 0.6 collective-permute-done.16
  88.7 2.6 %collective-permute-done.17 = bf16[2,512,64]{1,2,0:T(8,128)(2,1)S(1)} collective-permute-done((bf16[2,512,64]{1,2,0:T(8,128)(2,1)S(1)}, bf16[2,512,64]{1,2,0:T(8,128)(2,1)S(1)}, u32[]{:S(2)}, u32[]{:S(2)}) %collective-permute-start.17) | collective-permute-done | bytes 131104 | tf_op jit(solution)/shard_map/ppermute | solution.py:13
  91.5 1.8 %fusion.24 = f32[2,512,64]{1,2,0:T(8,128)} fusion(bf16[2,512,64]{1,2,0:T(8,128)(2,1)} %collective-permute-done.18, bf16[2,512,64]{1,2,0:T(8,128)(2,1)S(1)} %collective-permute-done.17, bf16[2,512,64]{1,2,0:T(8,128)(2,1)S(1)} %collective-permute-done.16, bf16[2,512,64]{1,2,0:T(8,128)(2,1)S(1)} %collective-permute-done.15, ...), kind=kLoop, calls=%fused_computation.32 | loop fusion | flops 983040 | bytes 1310724 | tf_op jit(solution)/shard_map/add | solution.py:14
  (47 shorter events, 2.5 us)
Async XLA Ops:
  0.0 55.2 %copy-start = (bf16[2,512,512]{2,1,0:T(8,128)(2,1)S(1)}, bf16[2,512,512]{2,1,0:T(8,128)(2,1)}, u32[]{:S(2)}) copy-start(bf16[2,512,512]{2,1,0:T(8,128)(2,1)} %param.19) | copy-start | bytes 3145732
  0.0 15.5 %collective-permute-start.1 = (bf16[2,64,512]{2,1,0:T(8,128)(2,1)}, bf16[2,64,512]{2,1,0:T(8,128)(2,1)S(1)}, u32[]{:S(2)}, u32[]{:S(2)}) collective-permute-start(bf16[2,64,512]{2,1,0:T(8,128)(2,1)} %param.11), channel_id=1, source_target_pairs={{0,64},{8,72},{16,80},{24,88},{32,96},{40,104},{48,112},{56,120},{... | collective-permute-start | bytes 393224 | tf_op jit(solution)/shard_map/ppermute | solution.py:71
  1.5 14.4 %collective-permute-start = (bf16[2,64,512]{2,1,0:T(8,128)(2,1)}, bf16[2,64,512]{2,1,0:T(8,128)(2,1)S(1)}, u32[]{:S(2)}, u32[]{:S(2)}) collective-permute-start(bf16[2,64,512]{2,1,0:T(8,128)(2,1)} %param.11), channel_id=1, source_target_pairs={{0,192},{8,200},{16,208},{24,216},{32,224},{40,232},{48,240},{56,2... | collective-permute-start | bytes 393224 | tf_op jit(solution)/shard_map/ppermute | solution.py:71
  4.6 20.5 %all-to-all-start = ((f32[8,1,128]{2,1,0:T(1,128)}), f32[8,1,128]{2,1,0:T(1,128)S(1)}, u32[]{:S(2)}, u32[]{:S(2)}) async-start(f32[8,1,128]{2,1,0:T(1,128)} %reshape.166), calls=%async_computation | async-start | bytes 8192 | tf_op jit(solution)/shard_map/all_to_all | solution.py:110
  15.5 5.6 %collective-permute-start.2 = (bf16[1,64,512]{2,1,0:T(8,128)(2,1)S(1)}, bf16[1,64,512]{2,1,0:T(8,128)(2,1)S(1)}, u32[]{:S(2)}, u32[]{:S(2)}) collective-permute-start(bf16[1,64,512]{2,1,0:T(8,128)(2,1)S(1)} %slice.64), channel_id=1, source_target_pairs={{0,64},{8,72},{16,80},{24,88},{32,96},{40,104},{48,112},{56,120},{... | collective-permute-start | bytes 196616 | tf_op jit(solution)/shard_map/ppermute | solution.py:71
  15.9 5.2 %collective-permute-start.3 = (bf16[1,64,512]{2,1,0:T(8,128)(2,1)S(1)}, bf16[1,64,512]{2,1,0:T(8,128)(2,1)S(1)}, u32[]{:S(2)}, u32[]{:S(2)}) collective-permute-start(bf16[1,64,512]{2,1,0:T(8,128)(2,1)S(1)} %slice.65), channel_id=1, source_target_pairs={{0,192},{8,200},{16,208},{24,216},{32,224},{40,232},{48,240},{56,2... | collective-permute-start | bytes 196616 | tf_op jit(solution)/shard_map/ppermute | solution.py:71
  22.6 12.0 %collective-permute-start.5 = (bf16[4,2,64,512]{3,0,1,2:T(4,128)(2,1)S(1)}, bf16[4,2,64,512]{3,0,1,2:T(4,128)(2,1)S(1)}, u32[]{:S(2)}, u32[]{:S(2)}) collective-permute-start(bf16[4,2,64,512]{3,0,1,2:T(4,128)(2,1)S(1)} %pad_maximum_fusion), channel_id=1, source_target_pairs={{0,16},{8,24},{16,32},{24,40},{32,48},{40,56},{48,0},{56,8},{64,80... | collective-permute-start | bytes 1572872 | tf_op jit(solution)/shard_map/ppermute | solution.py:71
  22.9 13.5 %collective-permute-start.4 = (bf16[4,2,64,512]{3,0,1,2:T(4,128)(2,1)S(1)}, bf16[4,2,64,512]{3,0,1,2:T(4,128)(2,1)S(1)}, u32[]{:S(2)}, u32[]{:S(2)}) collective-permute-start(bf16[4,2,64,512]{3,0,1,2:T(4,128)(2,1)S(1)} %pad_maximum_fusion), channel_id=1, source_target_pairs={{0,48},{8,56},{16,0},{24,8},{32,16},{40,24},{48,32},{56,40},{64,11... | collective-permute-start | bytes 1572872 | tf_op jit(solution)/shard_map/ppermute | solution.py:71
  26.4 12.6 %collective-permute-start.8 = (bf16[4,2,64,512]{3,0,1,2:T(4,128)(2,1)S(1)}, bf16[4,2,64,512]{3,0,1,2:T(4,128)(2,1)S(1)}, u32[]{:S(2)}, u32[]{:S(2)}) collective-permute-start(bf16[4,2,64,512]{3,0,1,2:T(4,128)(2,1)S(1)} %pad_maximum_fusion), channel_id=1, source_target_pairs={{0,8},{8,0},{16,24},{24,16},{32,40},{40,32},{48,56},{56,48},{64,72... | collective-permute-start | bytes 1572872 | tf_op jit(solution)/shard_map/ppermute | solution.py:71
  34.8 6.4 %collective-permute-start.6 = (bf16[2,2,64,512]{3,0,1,2:T(2,128)(2,1)S(1)}, bf16[2,2,64,512]{3,0,1,2:T(2,128)(2,1)S(1)}, u32[]{:S(2)}, u32[]{:S(2)}) collective-permute-start(bf16[2,2,64,512]{3,0,1,2:T(2,128)(2,1)S(1)} %slice.68), channel_id=1, source_target_pairs={{0,16},{8,24},{16,32},{24,40},{32,48},{40,56},{48,0},{56,8},{64,80... | collective-permute-start | bytes 786440 | tf_op jit(solution)/shard_map/ppermute | solution.py:71
  36.7 7.7 %collective-permute-start.7 = (bf16[2,2,64,512]{3,0,1,2:T(2,128)(2,1)S(1)}, bf16[2,2,64,512]{3,0,1,2:T(2,128)(2,1)S(1)}, u32[]{:S(2)}, u32[]{:S(2)}) collective-permute-start(bf16[2,2,64,512]{3,0,1,2:T(2,128)(2,1)S(1)} %slice.69), channel_id=1, source_target_pairs={{0,48},{8,56},{16,0},{24,8},{32,16},{40,24},{48,32},{56,40},{64,11... | collective-permute-start | bytes 786440 | tf_op jit(solution)/shard_map/ppermute | solution.py:71
  37.3 8.7 %collective-permute-start.9 = (bf16[4,2,64,512]{3,0,1,2:T(4,128)(2,1)S(1)}, bf16[4,2,64,512]{3,0,1,2:T(4,128)(2,1)S(1)}, u32[]{:S(2)}, u32[]{:S(2)}) collective-permute-start(bf16[4,2,64,512]{3,0,1,2:T(4,128)(2,1)S(1)} %collective-permute-done.4), channel_id=1, source_target_pairs={{0,8},{8,0},{16,24},{24,16},{32,40},{40,32},{48,56},{56,48},{64,72... | collective-permute-start | bytes 1572872 | tf_op jit(solution)/shard_map/ppermute | solution.py:71
  37.3 10.2 %collective-permute-start.11 = (bf16[4,2,64,512]{3,0,1,2:T(4,128)(2,1)S(1)}, bf16[4,2,64,512]{3,0,1,2:T(4,128)(2,1)S(1)}, u32[]{:S(2)}, u32[]{:S(2)}) collective-permute-start(bf16[4,2,64,512]{3,0,1,2:T(4,128)(2,1)S(1)} %collective-permute-done.5), channel_id=1, source_target_pairs={{0,8},{8,0},{16,24},{24,16},{32,40},{40,32},{48,56},{56,48},{64,72... | collective-permute-start | bytes 1572872 | tf_op jit(solution)/shard_map/ppermute | solution.py:71
  44.9 2.0 %collective-permute-start.10 = (bf16[4,2,64,512]{3,0,1,2:T(4,128)(2,1)S(1)}, bf16[4,2,64,512]{3,0,1,2:T(4,128)(2,1)S(1)}, u32[]{:S(2)}, u32[]{:S(2)}) collective-permute-start(bf16[4,2,64,512]{3,0,1,2:T(4,128)(2,1)S(1)} %pad_maximum_fusion.1), channel_id=1, source_target_pairs={{0,8},{8,0},{16,24},{24,16},{32,40},{40,32},{48,56},{56,48},{64,72... | collective-permute-start | bytes 1572872 | tf_op jit(solution)/shard_map/ppermute | solution.py:71
  48.6 6.6 %copy-start.3 = (f32[2,512]{1,0:T(2,128)S(1)}, f32[2,512]{1,0:T(2,128)}, u32[]{:S(2)}) copy-start(f32[2,512]{1,0:T(2,128)} %param.21) | copy-start | bytes 12292
  55.2 3.9 %copy-start.2 = (bf16[2,512,512]{2,1,0:T(8,128)(2,1)S(1)}, bf16[2,512,512]{2,1,0:T(8,128)(2,1)}, u32[]{:S(2)}) copy-start(bf16[2,512,512]{2,1,0:T(8,128)(2,1)} %param.18) | copy-start | bytes 3145732
  59.1 2.1 %copy-start.1 = (bf16[2,512,512]{2,1,0:T(8,128)(2,1)S(1)}, bf16[2,512,512]{2,1,0:T(8,128)(2,1)}, u32[]{:S(2)}) copy-start(bf16[2,512,512]{2,1,0:T(8,128)(2,1)} %param.16) | copy-start | bytes 3145732
  62.0 15.6 %collective-permute-start.12 = (bf16[2,512,64]{1,2,0:T(8,128)(2,1)S(1)}, bf16[2,512,64]{1,2,0:T(8,128)(2,1)S(1)}, u32[]{:S(2)}, u32[]{:S(2)}) collective-permute-start(bf16[2,512,64]{1,2,0:T(8,128)(2,1)S(1)} %get-tuple-element.5), channel_id=1, source_target_pairs={{0,4},{1,5},{2,6},{3,7},{4,0},{5,1},{6,2},{7,3},{8,12},{9,13},{10,... | collective-permute-start | bytes 393224 | tf_op jit(solution)/shard_map/ppermute | solution.py:13
  67.6 15.8 %collective-permute-start.13 = (bf16[2,512,64]{1,2,0:T(8,128)(2,1)S(1)}, bf16[2,512,64]{1,2,0:T(8,128)(2,1)S(1)}, u32[]{:S(2)}, u32[]{:S(2)}) collective-permute-start(bf16[2,512,64]{1,2,0:T(8,128)(2,1)S(1)} %get-tuple-element.9), channel_id=1, source_target_pairs={{0,3},{1,4},{2,5},{3,6},{4,7},{5,0},{6,1},{7,2},{8,11},{9,12},{10,... | collective-permute-start | bytes 393224 | tf_op jit(solution)/shard_map/ppermute | solution.py:13
  68.1 17.5 %collective-permute-start.14 = (bf16[2,512,64]{1,2,0:T(8,128)(2,1)S(1)}, bf16[2,512,64]{1,2,0:T(8,128)(2,1)S(1)}, u32[]{:S(2)}, u32[]{:S(2)}) collective-permute-start(bf16[2,512,64]{1,2,0:T(8,128)(2,1)S(1)} %get-tuple-element.8), channel_id=1, source_target_pairs={{0,5},{1,6},{2,7},{3,0},{4,1},{5,2},{6,3},{7,4},{8,13},{9,14},{10,... | collective-permute-start | bytes 393224 | tf_op jit(solution)/shard_map/ppermute | solution.py:13
  72.6 15.5 %collective-permute-start.15 = (bf16[2,512,64]{1,2,0:T(8,128)(2,1)S(1)}, bf16[2,512,64]{1,2,0:T(8,128)(2,1)S(1)}, u32[]{:S(2)}, u32[]{:S(2)}) collective-permute-start(bf16[2,512,64]{1,2,0:T(8,128)(2,1)S(1)} %get-tuple-element.7), channel_id=1, source_target_pairs={{0,2},{1,3},{2,4},{3,5},{4,6},{5,7},{6,0},{7,1},{8,10},{9,11},{10,... | collective-permute-start | bytes 393224 | tf_op jit(solution)/shard_map/ppermute | solution.py:13
  73.1 15.6 %collective-permute-start.16 = (bf16[2,512,64]{1,2,0:T(8,128)(2,1)S(1)}, bf16[2,512,64]{1,2,0:T(8,128)(2,1)S(1)}, u32[]{:S(2)}, u32[]{:S(2)}) collective-permute-start(bf16[2,512,64]{1,2,0:T(8,128)(2,1)S(1)} %get-tuple-element.6), channel_id=1, source_target_pairs={{0,6},{1,7},{2,0},{3,1},{4,2},{5,3},{6,4},{7,5},{8,14},{9,15},{10,... | collective-permute-start | bytes 393224 | tf_op jit(solution)/shard_map/ppermute | solution.py:13
  77.6 13.7 %collective-permute-start.17 = (bf16[2,512,64]{1,2,0:T(8,128)(2,1)S(1)}, bf16[2,512,64]{1,2,0:T(8,128)(2,1)S(1)}, u32[]{:S(2)}, u32[]{:S(2)}) collective-permute-start(bf16[2,512,64]{1,2,0:T(8,128)(2,1)S(1)} %get-tuple-element.11), channel_id=1, source_target_pairs={{0,1},{1,2},{2,3},{3,4},{4,5},{5,6},{6,7},{7,0},{8,9},{9,10},{10,1... | collective-permute-start | bytes 393224 | tf_op jit(solution)/shard_map/ppermute | solution.py:13
  83.4 8.1 %collective-permute-start.18 = (bf16[2,512,64]{1,2,0:T(8,128)(2,1)S(1)}, bf16[2,512,64]{1,2,0:T(8,128)(2,1)}, u32[]{:S(2)}, u32[]{:S(2)}) collective-permute-start(bf16[2,512,64]{1,2,0:T(8,128)(2,1)S(1)} %get-tuple-element.10), channel_id=1, source_target_pairs={{0,7},{1,0},{2,1},{3,2},{4,3},{5,4},{6,5},{7,6},{8,15},{9,8},{10,9... | collective-permute-start | bytes 393224 | tf_op jit(solution)/shard_map/ppermute | solution.py:13

commit v16 on v15

--- a/solution.py
+++ b/solution.py
@@ -4,15 +4,14 @@
 from jax.sharding import PartitionSpec as P
 
 
-def scatter_sum(chunks, axis):
-    n = chunks.shape[0]
+def scatter_sum(make_chunk, n, axis):
     me = lax.axis_index(axis)
-    total = lax.dynamic_index_in_dim(chunks, me, 0, keepdims=False).astype(jnp.float32)
+    total = None
     for k in sorted(range(1, n), key=lambda k: (-min(k, n - k), k)):
-        send = lax.dynamic_index_in_dim(chunks, (me + k) % n, 0, keepdims=False)
+        send = make_chunk((me + k) % n)
         got = lax.ppermute(send, axis, [(j, (j + k) % n) for j in range(n)])
-        total = total + got.astype(jnp.float32)
-    return total
+        total = got.astype(jnp.float32) if total is None else total + got.astype(jnp.float32)
+    return total + make_chunk(me).astype(jnp.float32)
 
 
 def local(
@@ -122,11 +121,14 @@
     basis_rows = jnp.einsum(
         "jrm,jkm->jrk", scaled, right_eigenvector_matrix, preferred_element_type=jnp.float32
     ).astype(jnp.bfloat16)
-    basis_rows = basis_rows.reshape(local_blocks, width_two, pieces, cols)
-    spread = jnp.einsum(
-        "jab,jbkc->kjac", left_basis, basis_rows, preferred_element_type=jnp.float32
-    ).astype(jnp.bfloat16)
-    return scatter_sum(spread, "sub")
+
+    def make_chunk(idx):
+        piece = lax.dynamic_slice_in_dim(basis_rows, idx * cols, cols, axis=2)
+        return jnp.einsum(
+            "jab,jbc->jac", left_basis, piece, preferred_element_type=jnp.float32
+        ).astype(jnp.bfloat16)
+
+    return scatter_sum(make_chunk, pieces, "sub")
 
 
 def solution(mesh):

time: 93.9 us -> 92.8 us (0.988)
  waiting for transfers between devices: 27.7 us -> 23.3 us
  matrix products: 19.2 us -> 22.6 us
  starting transfers between devices: 34.7 us -> 36.5 us
  other arithmetic: 4.52 us -> 2.77 us
    ppermute x7, waiting for transfers between devices: 14.7 us -> 10.3 us  [scatter_sum(): got = lax.ppermute(send, axis, [(j, (j + k) % n) for j in range(n)])]
    dot_general x1 -> x8, matrix products: 0.74 us -> 4.21 us  [make_chunk(): jnp.einsum('jab,jbc->jac', left_basis, piece, preferred_element_type=jnp....]
    ppermute x7, starting transfers between devices: 14.7 us -> 16.5 us  [scatter_sum(): got = lax.ppermute(send, axis, [(j, (j + k) % n) for j in range(n)])]
    add x1 -> x0, other arithmetic: 1.75 us -> none  [scatter_sum(): total = total + got.astype(jnp.float32)]
  transfers between devices with their start and end apart: 20 -> 20, of which waited for: 12 -> 11; matrix products, arithmetic and copies ran while one was open for 15% -> 18% of each run, Pallas kernels for 0% -> 0%
where the time goes in v16:
time: 92.8 us; the launch traced here: 92.1 us
  starting transfers between devices  36.5 us (39%)
  waiting for transfers between devices  23.3 us (25%)
  matrix products  22.6 us (24%)
  local copies, waits for them, and re-layouts  6.59 us (7%)
  other arithmetic  2.77 us (3%)
    ppermute x7, starting transfers between devices, scatter_sum(): got = lax.ppermute(send, axis, [(j, (j + k) % n) for j in range(n)])  16.5 us
    ppermute x12, waiting for transfers between devices, move(): return lax.ppermute(piece, 'blk', pairs_list)  13 us
    ppermute x12, starting transfers between devices, move(): return lax.ppermute(piece, 'blk', pairs_list)  11.5 us
    ppermute x7, waiting for transfers between devices, scatter_sum(): got = lax.ppermute(send, axis, [(j, (j + k) % n) for j in range(n)])  10.3 us
    all_to_all x1, starting transfers between devices, local(): lax.all_to_all(jnp.broadcast_to(rates_run, (pieces,) + left_rates.shape),...  8.47 us
    dot_general x1, matrix products, local(): jnp.einsum('tab,ktbc->kac', left_part, right_done, preferred_element_type...  6.71 us
    dot_general x8, matrix products, pool(): jnp.einsum('kab,abrn->krn', w, piece, preferred_element_type=jnp.float32)  5.86 us
    dot_general x8, matrix products, make_chunk(): jnp.einsum('jab,jbc->jac', left_basis, piece, preferred_element_type=jnp....  4.21 us
  transfers between devices with their start and end apart: 20, of which 11 were waited for; matrix products, arithmetic and copies ran while one was open for 18% of the time, Pallas kernels for 0%

profile of v16, /device:TPU:24, one launch (start us, length us, event | category | flops | bytes accessed | tf_op | source)
XLA Modules:
  0.0 92.1 jit_solution(14959528565797430651)
XLA Ops:
  0.0 1.5 %collective-permute-start.1 = (bf16[2,64,512]{2,1,0:T(8,128)(2,1)}, bf16[2,64,512]{2,1,0:T(8,128)(2,1)S(1)}, u32[]{:S(2)}, u32[]{:S(2)}) collective-permute-start(bf16[2,64,512]{2,1,0:T(8,128)(2,1)} %param.11), channel_id=1, source_target_pairs={{0,64},{8,72},{16,80},{24,88},{32,96},{40,104},{48,112},{56,120},{... | collective-permute-start | bytes 393224 | tf_op jit(solution)/shard_map/ppermute | solution.py:70
  1.5 1.7 %collective-permute-start = (bf16[2,64,512]{2,1,0:T(8,128)(2,1)}, bf16[2,64,512]{2,1,0:T(8,128)(2,1)S(1)}, u32[]{:S(2)}, u32[]{:S(2)}) collective-permute-start(bf16[2,64,512]{2,1,0:T(8,128)(2,1)} %param.11), channel_id=1, source_target_pairs={{0,192},{8,200},{16,208},{24,216},{32,224},{40,232},{48,240},{56,2... | collective-permute-start | bytes 393224 | tf_op jit(solution)/shard_map/ppermute | solution.py:70
  3.2 0.7 broadcast_in_dim.2
  3.9 0.7 reshape.158
  4.6 8.5 %all-to-all-start = ((f32[8,1,128]{2,1,0:T(1,128)}), f32[8,1,128]{2,1,0:T(1,128)S(1)}, u32[]{:S(2)}, u32[]{:S(2)}) async-start(f32[8,1,128]{2,1,0:T(1,128)} %reshape.158), calls=%async_computation | async-start | bytes 8192 | tf_op jit(solution)/shard_map/all_to_all | solution.py:109
  13.4 1.1 %constant_dynamic-slice_fusion = s32[32,1,2,3]{1,2,3,0:T(2,128)S(1)} fusion(s32[32,32,2,3]{1,2,3,0:T(2,128)} %param.14, s32[]{:T(128)S(6)} %select_n.99), kind=kLoop, calls=%fused_computation.71 | loop fusion | bytes 1540 | tf_op jit(solution)/shard_map/jit(dynamic_index_in_dim)/dynamic_slice | solution.py:41
  14.6 0.9 dynamic-slice_reduce_fusion
  15.9 3.0 %collective-permute-start.3 = (bf16[1,64,512]{2,1,0:T(8,128)(2,1)S(1)}, bf16[1,64,512]{2,1,0:T(8,128)(2,1)S(1)}, u32[]{:S(2)}, u32[]{:S(2)}) collective-permute-start(bf16[1,64,512]{2,1,0:T(8,128)(2,1)S(1)} %slice.65), channel_id=1, source_target_pairs={{0,192},{8,200},{16,208},{24,216},{32,224},{40,232},{48,240},{56,2... | collective-permute-start | bytes 196616 | tf_op jit(solution)/shard_map/ppermute | solution.py:70
  19.1 1.1 %copy.98 = bf16[1,2,64,512]{3,0,1,2:T(2,128)(2,1)S(1)} copy(bf16[1,2,64,512]{3,2,1,0:T(8,128)(2,1)} %bitcast.177) | data formatting | bytes 262144 | tf_op jit(solution)/shard_map/stack | solution.py:78
  20.6 0.5 collective-permute-done.2
  21.3 1.2 %pad_maximum_fusion = bf16[4,2,64,512]{3,0,1,2:T(4,128)(2,1)S(1)} fusion(bf16[1,2,64,512]{3,0,1,2:T(2,128)(2,1)S(1)} %copy.101, bf16[1,2,64,512]{3,0,1,2:T(2,128)(2,1)S(1)} %copy.100, bf16[1,2,64,512]{3,0,1,2:T(2,128)(2,1)S(1)} %copy.99, bf16[1,2,64,512]{3,0,1,2:T(2,128)(2,1)S(1)} %copy.98), kind=kLoop, calls=%fused_computation.39 | loop fusion | flops 2097152 | bytes 1048576 | tf_op jit(solution)/shard_map/stack | solution.py:78
  22.9 1.8 %collective-permute-start.4 = (bf16[4,2,64,512]{3,0,1,2:T(4,128)(2,1)S(1)}, bf16[4,2,64,512]{3,0,1,2:T(4,128)(2,1)S(1)}, u32[]{:S(2)}, u32[]{:S(2)}) collective-permute-start(bf16[4,2,64,512]{3,0,1,2:T(4,128)(2,1)S(1)} %pad_maximum_fusion), channel_id=1, source_target_pairs={{0,48},{8,56},{16,0},{24,8},{32,16},{40,24},{48,32},{56,40},{64,11... | collective-permute-start | bytes 1572872 | tf_op jit(solution)/shard_map/ppermute | solution.py:70
  25.1 0.5 broadcast.166
  25.6 0.7 reduce.2
  26.5 0.6 fusion.66
  27.1 7.5 %collective-permute-done.5 = bf16[4,2,64,512]{3,0,1,2:T(4,128)(2,1)S(1)} collective-permute-done((bf16[4,2,64,512]{3,0,1,2:T(4,128)(2,1)S(1)}, bf16[4,2,64,512]{3,0,1,2:T(4,128)(2,1)S(1)}, u32[]{:S(2)}, u32[]{:S(2)}) %collective-permute-start.5) | collective-permute-done | bytes 524320 | tf_op jit(solution)/shard_map/ppermute | solution.py:70
  34.8 1.6 %collective-permute-start.6 = (bf16[2,2,64,512]{3,0,1,2:T(2,128)(2,1)S(1)}, bf16[2,2,64,512]{3,0,1,2:T(2,128)(2,1)S(1)}, u32[]{:S(2)}, u32[]{:S(2)}) collective-permute-start(bf16[2,2,64,512]{3,0,1,2:T(2,128)(2,1)S(1)} %slice.68), channel_id=1, source_target_pairs={{0,16},{8,24},{16,32},{24,40},{32,48},{40,56},{48,0},{56,8},{64,80... | collective-permute-start | bytes 786440 | tf_op jit(solution)/shard_map/ppermute | solution.py:70
  36.7 0.6 collective-permute-start.7
  37.3 0.5 collective-permute-start.11
  37.8 0.6 fusion.60
  38.4 0.6 fusion.64
  39.1 0.6 fusion.58
  39.7 1.6 %collective-permute-done.6 = bf16[2,2,64,512]{3,0,1,2:T(2,128)(2,1)S(1)} collective-permute-done((bf16[2,2,64,512]{3,0,1,2:T(2,128)(2,1)S(1)}, bf16[2,2,64,512]{3,0,1,2:T(2,128)(2,1)S(1)}, u32[]{:S(2)}, u32[]{:S(2)}) %collective-permute-start.6) | collective-permute-done | bytes 262176 | tf_op jit(solution)/shard_map/ppermute | solution.py:70
  41.2 3.1 %collective-permute-done.7 = bf16[2,2,64,512]{3,0,1,2:T(2,128)(2,1)S(1)} collective-permute-done((bf16[2,2,64,512]{3,0,1,2:T(2,128)(2,1)S(1)}, bf16[2,2,64,512]{3,0,1,2:T(2,128)(2,1)S(1)}, u32[]{:S(2)}, u32[]{:S(2)}) %collective-permute-start.7) | collective-permute-done | bytes 262176 | tf_op jit(solution)/shard_map/ppermute | solution.py:70
  44.3 0.5 pad_maximum_fusion.1
  45.0 1.0 %fusion.62 = f32[16,64,512,1]{2,0,3,1:T(8,128)S(1)} fusion(bf16[16,1,1,4,2]{0,4,3,2,1:T(2,128)(2,1)S(1)} %get-tuple-element.10, bf16[2,2,64,512]{3,0,1,2:T(2,128)(2,1)S(1)} %collective-permute-done.7, bf16[2,2,64,512]{3,0,1,2:T(2,128)(2,1)S(1)} %collective-permute-done.6), kind=kOutput, calls=%fused_computation.85 | convolution fusion | flops 9437184 | bytes 2621696 | tf_op jit(solution)/shard_map/kab,abrn->krn/dot_general | solution.py:91
  46.0 0.6 fusion.56
  46.9 0.6 fusion.54
  47.5 1.2 %fusion.9 = bf16[2,8,64,512]{3,1,0,2:T(8,128)(2,1)S(1)} fusion(bf16[4,2,64,512]{3,0,1,2:T(4,128)(2,1)S(1)} %collective-permute-done.11, f32[16,64,512,1]{2,0,3,1:T(8,128)S(1)} %fusion.54, f32[16,64,512,1]{2,0,3,1:T(8,128)S(1)} %fusion.56, f32[16,64,512,1]{2,0,3,1:T(8,128)S(1)} %fusion.58, f32[16,64,512,1]{2,0,3,1:T(8,128)S(1)} %fusion.60, ...), kind=kOutput, calls=%fused_computation.16 | convolution fusion | flops 12582912 | bytes 16253184 | tf_op jit(solution)/shard_map/kab,abrn->krn/dot_general | solution.py:91
  48.7 6.7 %bitcast_convert_fusion = bf16[2,512,512]{2,1,0:T(8,128)(2,1)} fusion(bf16[8,512,512]{2,1,0:T(8,128)(2,1)} %param.12, s32[]{:T(128)S(6)} %select_n.106, bf16[8,512,512]{2,1,0:T(8,128)(2,1)} %param.13, bf16[2,8,64,512]{3,1,0,2:T(8,128)(2,1)S(1)} %fusion.9), kind=kOutput, calls=%fused_computation.2 | convolution fusion | flops 1074790400 | bytes 7340036 | tf_op jit(solution)/shard_map/tab,ktbc->kac/dot_general | solution.py:113
  55.4 3.6 %divide_convert_fusion = bf16[2,512,512]{2,1,0:T(8,128)(2,1)} fusion(bf16[2,512,512]{2,1,0:T(8,128)(2,1)S(1)} %copy-done, bf16[2,512,512]{2,1,0:T(8,128)(2,1)} %bitcast_convert_fusion, bf16[2,512,512]{2,1,0:T(8,128)(2,1)S(1)} %copy-done.2, f32[2,512]{1,0:T(2,128)S(1)} %copy-done.4, f32[2,512]{1,0:T(2,128)S(1)} %add.280), kind=kOutput, calls=%fused_computation.11 | convolution fusion | flops 1075838976 | bytes 4202496 | tf_op jit(solution)/shard_map/jrn,jmn->jrm/dot_general | solution.py:119
  59.0 2.1 %convolution_convert_fusion = bf16[2,512,512]{1,2,0:T(8,128)(2,1)S(1)} fusion(bf16[2,512,512]{2,1,0:T(8,128)(2,1)} %divide_convert_fusion, bf16[2,512,512]{2,1,0:T(8,128)(2,1)S(1)} %copy-done.3), kind=kOutput, calls=%fused_computation.13 | convolution fusion | flops 537395200 | bytes 3145728 | tf_op jit(solution)/shard_map/jrm,jkm->jrk/dot_general | solution.py:121
  61.1 0.4 fusion.12
  61.5 5.5 %collective-permute-start.12 = (bf16[2,512,64]{1,2,0:T(8,128)(2,1)S(1)}, bf16[2,512,64]{1,2,0:T(8,128)(2,1)S(1)}, u32[]{:S(2)}, u32[]{:S(2)}) collective-permute-start(bf16[2,512,64]{1,2,0:T(8,128)(2,1)S(1)} %fusion.12), channel_id=1, source_target_pairs={{0,4},{1,5},{2,6},{3,7},{4,0},{5,1},{6,2},{7,3},{8,12},{9,13},{10,... | collective-permute-start | bytes 393224 | tf_op jit(solution)/shard_map/ppermute | solution.py:12
  67.1 0.4 fusion.13
  67.5 0.6 collective-permute-start.13
  68.6 4.8 %collective-permute-start.14 = (bf16[2,512,64]{1,2,0:T(8,128)(2,1)S(1)}, bf16[2,512,64]{1,2,0:T(8,128)(2,1)S(1)}, u32[]{:S(2)}, u32[]{:S(2)}) collective-permute-start(bf16[2,512,64]{1,2,0:T(8,128)(2,1)S(1)} %fusion.14), channel_id=1, source_target_pairs={{0,5},{1,6},{2,7},{3,0},{4,1},{5,2},{6,3},{7,4},{8,13},{9,14},{10,... | collective-permute-start | bytes 393224 | tf_op jit(solution)/shard_map/ppermute | solution.py:12
  73.8 0.6 collective-permute-start.15
  74.8 3.7 %collective-permute-start.16 = (bf16[2,512,64]{1,2,0:T(8,128)(2,1)S(1)}, bf16[2,512,64]{1,2,0:T(8,128)(2,1)S(1)}, u32[]{:S(2)}, u32[]{:S(2)}) collective-permute-start(bf16[2,512,64]{1,2,0:T(8,128)(2,1)S(1)} %fusion.16), channel_id=1, source_target_pairs={{0,6},{1,7},{2,0},{3,1},{4,2},{5,3},{6,4},{7,5},{8,14},{9,15},{10,... | collective-permute-start | bytes 393224 | tf_op jit(solution)/shard_map/ppermute | solution.py:12
  78.9 0.4 fusion.18
  79.4 0.6 collective-permute-start.17
  80.0 2.1 %collective-permute-done.13 = bf16[2,512,64]{1,2,0:T(8,128)(2,1)S(1)} collective-permute-done((bf16[2,512,64]{1,2,0:T(8,128)(2,1)S(1)}, bf16[2,512,64]{1,2,0:T(8,128)(2,1)S(1)}, u32[]{:S(2)}, u32[]{:S(2)}) %collective-permute-start.13) | collective-permute-done | bytes 131104 | tf_op jit(solution)/shard_map/ppermute | solution.py:12
  82.1 0.6 collective-permute-start.18
  82.7 2.4 %collective-permute-done.14 = bf16[2,512,64]{1,2,0:T(8,128)(2,1)S(1)} collective-permute-done((bf16[2,512,64]{1,2,0:T(8,128)(2,1)S(1)}, bf16[2,512,64]{1,2,0:T(8,128)(2,1)S(1)}, u32[]{:S(2)}, u32[]{:S(2)}) %collective-permute-start.14) | collective-permute-done | bytes 131104 | tf_op jit(solution)/shard_map/ppermute | solution.py:12
  85.1 2.5 %collective-permute-done.15 = bf16[2,512,64]{1,2,0:T(8,128)(2,1)S(1)} collective-permute-done((bf16[2,512,64]{1,2,0:T(8,128)(2,1)S(1)}, bf16[2,512,64]{1,2,0:T(8,128)(2,1)S(1)}, u32[]{:S(2)}, u32[]{:S(2)}) %collective-permute-start.15) | collective-permute-done | bytes 131104 | tf_op jit(solution)/shard_map/ppermute | solution.py:12
  87.6 0.6 collective-permute-done.16
  88.2 2.6 %collective-permute-done.17 = bf16[2,512,64]{1,2,0:T(8,128)(2,1)S(1)} collective-permute-done((bf16[2,512,64]{1,2,0:T(8,128)(2,1)S(1)}, bf16[2,512,64]{1,2,0:T(8,128)(2,1)S(1)}, u32[]{:S(2)}, u32[]{:S(2)}) %collective-permute-start.17) | collective-permute-done | bytes 131104 | tf_op jit(solution)/shard_map/ppermute | solution.py:12
  91.0 1.2 %add_add_fusion = f32[2,512,64]{1,2,0:T(8,128)} fusion(bf16[2,512,64]{1,2,0:T(8,128)(2,1)S(1)} %collective-permute-done.18, bf16[2,512,64]{1,2,0:T(8,128)(2,1)S(1)} %collective-permute-done.17, bf16[2,512,64]{1,2,0:T(8,128)(2,1)S(1)} %collective-permute-done.16, bf16[2,512,64]{1,2,0:T(8,128)(2,1)S(1)} %collective-permute-done.15, ...), kind=kOutput, calls=%fused_computation.41 | convolution fusion | flops 68157440 | bytes 2359300 | tf_op jit(solution)/shard_map/jab,jbc->jac/dot_general | solution.py:127
  (54 shorter events, 5.1 us)
Async XLA Ops:
  0.0 55.4 %copy-start = (bf16[2,512,512]{2,1,0:T(8,128)(2,1)S(1)}, bf16[2,512,512]{2,1,0:T(8,128)(2,1)}, u32[]{:S(2)}) copy-start(bf16[2,512,512]{2,1,0:T(8,128)(2,1)} %param.19) | copy-start | bytes 3145732
  0.0 15.5 %collective-permute-start.1 = (bf16[2,64,512]{2,1,0:T(8,128)(2,1)}, bf16[2,64,512]{2,1,0:T(8,128)(2,1)S(1)}, u32[]{:S(2)}, u32[]{:S(2)}) collective-permute-start(bf16[2,64,512]{2,1,0:T(8,128)(2,1)} %param.11), channel_id=1, source_target_pairs={{0,64},{8,72},{16,80},{24,88},{32,96},{40,104},{48,112},{56,120},{... | collective-permute-start | bytes 393224 | tf_op jit(solution)/shard_map/ppermute | solution.py:70
  1.5 14.4 %collective-permute-start = (bf16[2,64,512]{2,1,0:T(8,128)(2,1)}, bf16[2,64,512]{2,1,0:T(8,128)(2,1)S(1)}, u32[]{:S(2)}, u32[]{:S(2)}) collective-permute-start(bf16[2,64,512]{2,1,0:T(8,128)(2,1)} %param.11), channel_id=1, source_target_pairs={{0,192},{8,200},{16,208},{24,216},{32,224},{40,232},{48,240},{56,2... | collective-permute-start | bytes 393224 | tf_op jit(solution)/shard_map/ppermute | solution.py:70
  4.6 20.5 %all-to-all-start = ((f32[8,1,128]{2,1,0:T(1,128)}), f32[8,1,128]{2,1,0:T(1,128)S(1)}, u32[]{:S(2)}, u32[]{:S(2)}) async-start(f32[8,1,128]{2,1,0:T(1,128)} %reshape.158), calls=%async_computation | async-start | bytes 8192 | tf_op jit(solution)/shard_map/all_to_all | solution.py:109
  15.5 5.6 %collective-permute-start.2 = (bf16[1,64,512]{2,1,0:T(8,128)(2,1)S(1)}, bf16[1,64,512]{2,1,0:T(8,128)(2,1)S(1)}, u32[]{:S(2)}, u32[]{:S(2)}) collective-permute-start(bf16[1,64,512]{2,1,0:T(8,128)(2,1)S(1)} %slice.64), channel_id=1, source_target_pairs={{0,64},{8,72},{16,80},{24,88},{32,96},{40,104},{48,112},{56,120},{... | collective-permute-start | bytes 196616 | tf_op jit(solution)/shard_map/ppermute | solution.py:70
  15.9 5.2 %collective-permute-start.3 = (bf16[1,64,512]{2,1,0:T(8,128)(2,1)S(1)}, bf16[1,64,512]{2,1,0:T(8,128)(2,1)S(1)}, u32[]{:S(2)}, u32[]{:S(2)}) collective-permute-start(bf16[1,64,512]{2,1,0:T(8,128)(2,1)S(1)} %slice.65), channel_id=1, source_target_pairs={{0,192},{8,200},{16,208},{24,216},{32,224},{40,232},{48,240},{56,2... | collective-permute-start | bytes 196616 | tf_op jit(solution)/shard_map/ppermute | solution.py:70
  22.6 12.0 %collective-permute-start.5 = (bf16[4,2,64,512]{3,0,1,2:T(4,128)(2,1)S(1)}, bf16[4,2,64,512]{3,0,1,2:T(4,128)(2,1)S(1)}, u32[]{:S(2)}, u32[]{:S(2)}) collective-permute-start(bf16[4,2,64,512]{3,0,1,2:T(4,128)(2,1)S(1)} %pad_maximum_fusion), channel_id=1, source_target_pairs={{0,16},{8,24},{16,32},{24,40},{32,48},{40,56},{48,0},{56,8},{64,80... | collective-permute-start | bytes 1572872 | tf_op jit(solution)/shard_map/ppermute | solution.py:70
  22.9 13.5 %collective-permute-start.4 = (bf16[4,2,64,512]{3,0,1,2:T(4,128)(2,1)S(1)}, bf16[4,2,64,512]{3,0,1,2:T(4,128)(2,1)S(1)}, u32[]{:S(2)}, u32[]{:S(2)}) collective-permute-start(bf16[4,2,64,512]{3,0,1,2:T(4,128)(2,1)S(1)} %pad_maximum_fusion), channel_id=1, source_target_pairs={{0,48},{8,56},{16,0},{24,8},{32,16},{40,24},{48,32},{56,40},{64,11... | collective-permute-start | bytes 1572872 | tf_op jit(solution)/shard_map/ppermute | solution.py:70
  26.4 12.6 %collective-permute-start.8 = (bf16[4,2,64,512]{3,0,1,2:T(4,128)(2,1)S(1)}, bf16[4,2,64,512]{3,0,1,2:T(4,128)(2,1)S(1)}, u32[]{:S(2)}, u32[]{:S(2)}) collective-permute-start(bf16[4,2,64,512]{3,0,1,2:T(4,128)(2,1)S(1)} %pad_maximum_fusion), channel_id=1, source_target_pairs={{0,8},{8,0},{16,24},{24,16},{32,40},{40,32},{48,56},{56,48},{64,72... | collective-permute-start | bytes 1572872 | tf_op jit(solution)/shard_map/ppermute | solution.py:70
  34.8 6.4 %collective-permute-start.6 = (bf16[2,2,64,512]{3,0,1,2:T(2,128)(2,1)S(1)}, bf16[2,2,64,512]{3,0,1,2:T(2,128)(2,1)S(1)}, u32[]{:S(2)}, u32[]{:S(2)}) collective-permute-start(bf16[2,2,64,512]{3,0,1,2:T(2,128)(2,1)S(1)} %slice.68), channel_id=1, source_target_pairs={{0,16},{8,24},{16,32},{24,40},{32,48},{40,56},{48,0},{56,8},{64,80... | collective-permute-start | bytes 786440 | tf_op jit(solution)/shard_map/ppermute | solution.py:70
  36.7 7.7 %collective-permute-start.7 = (bf16[2,2,64,512]{3,0,1,2:T(2,128)(2,1)S(1)}, bf16[2,2,64,512]{3,0,1,2:T(2,128)(2,1)S(1)}, u32[]{:S(2)}, u32[]{:S(2)}) collective-permute-start(bf16[2,2,64,512]{3,0,1,2:T(2,128)(2,1)S(1)} %slice.69), channel_id=1, source_target_pairs={{0,48},{8,56},{16,0},{24,8},{32,16},{40,24},{48,32},{56,40},{64,11... | collective-permute-start | bytes 786440 | tf_op jit(solution)/shard_map/ppermute | solution.py:70
  37.3 8.7 %collective-permute-start.9 = (bf16[4,2,64,512]{3,0,1,2:T(4,128)(2,1)S(1)}, bf16[4,2,64,512]{3,0,1,2:T(4,128)(2,1)S(1)}, u32[]{:S(2)}, u32[]{:S(2)}) collective-permute-start(bf16[4,2,64,512]{3,0,1,2:T(4,128)(2,1)S(1)} %collective-permute-done.4), channel_id=1, source_target_pairs={{0,8},{8,0},{16,24},{24,16},{32,40},{40,32},{48,56},{56,48},{64,72... | collective-permute-start | bytes 1572872 | tf_op jit(solution)/shard_map/ppermute | solution.py:70
  37.3 10.2 %collective-permute-start.11 = (bf16[4,2,64,512]{3,0,1,2:T(4,128)(2,1)S(1)}, bf16[4,2,64,512]{3,0,1,2:T(4,128)(2,1)S(1)}, u32[]{:S(2)}, u32[]{:S(2)}) collective-permute-start(bf16[4,2,64,512]{3,0,1,2:T(4,128)(2,1)S(1)} %collective-permute-done.5), channel_id=1, source_target_pairs={{0,8},{8,0},{16,24},{24,16},{32,40},{40,32},{48,56},{56,48},{64,72... | collective-permute-start | bytes 1572872 | tf_op jit(solution)/shard_map/ppermute | solution.py:70
  44.9 2.0 %collective-permute-start.10 = (bf16[4,2,64,512]{3,0,1,2:T(4,128)(2,1)S(1)}, bf16[4,2,64,512]{3,0,1,2:T(4,128)(2,1)S(1)}, u32[]{:S(2)}, u32[]{:S(2)}) collective-permute-start(bf16[4,2,64,512]{3,0,1,2:T(4,128)(2,1)S(1)} %pad_maximum_fusion.1), channel_id=1, source_target_pairs={{0,8},{8,0},{16,24},{24,16},{32,40},{40,32},{48,56},{56,48},{64,72... | collective-permute-start | bytes 1572872 | tf_op jit(solution)/shard_map/ppermute | solution.py:70
  48.7 6.7 %copy-start.2 = (bf16[2,512,512]{2,1,0:T(8,128)(2,1)S(1)}, bf16[2,512,512]{2,1,0:T(8,128)(2,1)}, u32[]{:S(2)}) copy-start(bf16[2,512,512]{2,1,0:T(8,128)(2,1)} %param.17) | copy-start | bytes 3145732
  48.7 6.7 %copy-start.4 = (f32[2,512]{1,0:T(2,128)S(1)}, f32[2,512]{1,0:T(2,128)}, u32[]{:S(2)}) copy-start(f32[2,512]{1,0:T(2,128)} %param.21) | copy-start | bytes 12292
  55.4 3.6 %copy-start.3 = (bf16[2,512,512]{2,1,0:T(8,128)(2,1)S(1)}, bf16[2,512,512]{2,1,0:T(8,128)(2,1)}, u32[]{:S(2)}) copy-start(bf16[2,512,512]{2,1,0:T(8,128)(2,1)} %param.18) | copy-start | bytes 3145732
  59.0 2.1 %copy-start.1 = (bf16[2,512,512]{2,1,0:T(8,128)(2,1)S(1)}, bf16[2,512,512]{2,1,0:T(8,128)(2,1)}, u32[]{:S(2)}) copy-start(bf16[2,512,512]{2,1,0:T(8,128)(2,1)} %param.16) | copy-start | bytes 3145732
  61.5 17.8 %collective-permute-start.12 = (bf16[2,512,64]{1,2,0:T(8,128)(2,1)S(1)}, bf16[2,512,64]{1,2,0:T(8,128)(2,1)S(1)}, u32[]{:S(2)}, u32[]{:S(2)}) collective-permute-start(bf16[2,512,64]{1,2,0:T(8,128)(2,1)S(1)} %fusion.12), channel_id=1, source_target_pairs={{0,4},{1,5},{2,6},{3,7},{4,0},{5,1},{6,2},{7,3},{8,12},{9,13},{10,... | collective-permute-start | bytes 393224 | tf_op jit(solution)/shard_map/ppermute | solution.py:12
  67.5 14.6 %collective-permute-start.13 = (bf16[2,512,64]{1,2,0:T(8,128)(2,1)S(1)}, bf16[2,512,64]{1,2,0:T(8,128)(2,1)S(1)}, u32[]{:S(2)}, u32[]{:S(2)}) collective-permute-start(bf16[2,512,64]{1,2,0:T(8,128)(2,1)S(1)} %fusion.13), channel_id=1, source_target_pairs={{0,3},{1,4},{2,5},{3,6},{4,7},{5,0},{6,1},{7,2},{8,11},{9,12},{10,... | collective-permute-start | bytes 393224 | tf_op jit(solution)/shard_map/ppermute | solution.py:12
  68.6 16.6 %collective-permute-start.14 = (bf16[2,512,64]{1,2,0:T(8,128)(2,1)S(1)}, bf16[2,512,64]{1,2,0:T(8,128)(2,1)S(1)}, u32[]{:S(2)}, u32[]{:S(2)}) collective-permute-start(bf16[2,512,64]{1,2,0:T(8,128)(2,1)S(1)} %fusion.14), channel_id=1, source_target_pairs={{0,5},{1,6},{2,7},{3,0},{4,1},{5,2},{6,3},{7,4},{8,13},{9,14},{10,... | collective-permute-start | bytes 393224 | tf_op jit(solution)/shard_map/ppermute | solution.py:12
  73.8 13.9 %collective-permute-start.15 = (bf16[2,512,64]{1,2,0:T(8,128)(2,1)S(1)}, bf16[2,512,64]{1,2,0:T(8,128)(2,1)S(1)}, u32[]{:S(2)}, u32[]{:S(2)}) collective-permute-start(bf16[2,512,64]{1,2,0:T(8,128)(2,1)S(1)} %fusion.15), channel_id=1, source_target_pairs={{0,2},{1,3},{2,4},{3,5},{4,6},{5,7},{6,0},{7,1},{8,10},{9,11},{10,... | collective-permute-start | bytes 393224 | tf_op jit(solution)/shard_map/ppermute | solution.py:12
  74.8 13.4 %collective-permute-start.16 = (bf16[2,512,64]{1,2,0:T(8,128)(2,1)S(1)}, bf16[2,512,64]{1,2,0:T(8,128)(2,1)S(1)}, u32[]{:S(2)}, u32[]{:S(2)}) collective-permute-start(bf16[2,512,64]{1,2,0:T(8,128)(2,1)S(1)} %fusion.16), channel_id=1, source_target_pairs={{0,6},{1,7},{2,0},{3,1},{4,2},{5,3},{6,4},{7,5},{8,14},{9,15},{10,... | collective-permute-start | bytes 393224 | tf_op jit(solution)/shard_map/ppermute | solution.py:12
  79.4 11.5 %collective-permute-start.17 = (bf16[2,512,64]{1,2,0:T(8,128)(2,1)S(1)}, bf16[2,512,64]{1,2,0:T(8,128)(2,1)S(1)}, u32[]{:S(2)}, u32[]{:S(2)}) collective-permute-start(bf16[2,512,64]{1,2,0:T(8,128)(2,1)S(1)} %fusion.17), channel_id=1, source_target_pairs={{0,1},{1,2},{2,3},{3,4},{4,5},{5,6},{6,7},{7,0},{8,9},{9,10},{10,1... | collective-permute-start | bytes 393224 | tf_op jit(solution)/shard_map/ppermute | solution.py:12
  82.1 8.9 %collective-permute-start.18 = (bf16[2,512,64]{1,2,0:T(8,128)(2,1)S(1)}, bf16[2,512,64]{1,2,0:T(8,128)(2,1)S(1)}, u32[]{:S(2)}, u32[]{:S(2)}) collective-permute-start(bf16[2,512,64]{1,2,0:T(8,128)(2,1)S(1)} %fusion.18), channel_id=1, source_target_pairs={{0,7},{1,0},{2,1},{3,2},{4,3},{5,4},{6,5},{7,6},{8,15},{9,8},{10,9... | collective-permute-start | bytes 393224 | tf_op jit(solution)/shard_map/ppermute | solution.py:12

commit v17 on v16

--- a/solution.py
+++ b/solution.py
@@ -82,10 +82,10 @@
     side_above = move(from_above, 0, 0, sibling=True)
     side_below = move(from_below, 0, 0, sibling=True)
     half_ring = ring // 2
-    far_y = jnp.concatenate(
-        [move(from_below[:half_ring], 0, 1), move(from_above[half_ring:], 0, -1)], axis=0
-    )
-    side_far = move(far_y, 0, 0, sibling=True)
+    far_low = move(from_below[:half_ring], 0, 1)
+    far_high = move(from_above[half_ring:], 0, -1)
+    side_low = move(far_low, 0, 0, sibling=True)
+    side_high = move(far_high, 0, 0, sibling=True)
 
     def pool(w, piece):
         return jnp.einsum("kab,abrn->krn", w, piece, preferred_element_type=jnp.float32)
@@ -93,11 +93,13 @@
     pooled = (
         pool(weights[:, 0, 0], x_row)
         + pool(weights[:, 0, 1], from_above)
-        + pool(weights[:, 0, 2], far_y)
+        + pool(weights[:, 0, 2, :half_ring], far_low)
+        + pool(weights[:, 0, 2, half_ring:], far_high)
         + pool(weights[:, 0, 3], from_below)
         + pool(weights[:, 1, 0], side_x)
         + pool(weights[:, 1, 1], side_above)
-        + pool(weights[:, 1, 2], side_far)
+        + pool(weights[:, 1, 2, :half_ring], side_low)
+        + pool(weights[:, 1, 2, half_ring:], side_high)
         + pool(weights[:, 1, 3], side_below)
     ).astype(jnp.bfloat16)
     pooled = pooled.reshape(local_blocks, term_total, row_count, width_two)

time: 92.8 us -> 94.5 us (1.018)
  matrix products: 22.6 us -> 23.9 us
    dot_general x8 -> x10, matrix products: 5.86 us -> 6.94 us  [pool(): jnp.einsum('kab,abrn->krn', w, piece, preferred_element_type=jnp.float32)]
    ppermute x12 -> x13, starting transfers between devices: 11.5 us -> 12 us  [move(): return lax.ppermute(piece, 'blk', pairs_list)]
    ppermute x12 -> x13, waiting for transfers between devices: 13 us -> 13.2 us  [move(): return lax.ppermute(piece, 'blk', pairs_list)]
  transfers between devices with their start and end apart: 20 -> 21, of which waited for: 11 -> 10; matrix products, arithmetic and copies ran while one was open for 18% -> 18% of each run, Pallas kernels for 0% -> 0%
where the time goes in v17:
time: 94.5 us; the launch traced here: 93.8 us
  starting transfers between devices  37 us (39%)
  matrix products  23.9 us (25%)
  waiting for transfers between devices  23.7 us (25%)
  local copies, waits for them, and re-layouts  6.58 us (7%)
  other arithmetic  2.22 us (2%)
    ppermute x7, starting transfers between devices, scatter_sum(): got = lax.ppermute(send, axis, [(j, (j + k) % n) for j in range(n)])  16.5 us
    ppermute x13, waiting for transfers between devices, move(): return lax.ppermute(piece, 'blk', pairs_list)  13.2 us
    ppermute x13, starting transfers between devices, move(): return lax.ppermute(piece, 'blk', pairs_list)  12 us
    ppermute x7, waiting for transfers between devices, scatter_sum(): got = lax.ppermute(send, axis, [(j, (j + k) % n) for j in range(n)])  10.4 us
    all_to_all x1, starting transfers between devices, local(): lax.all_to_all(jnp.broadcast_to(rates_run, (pieces,) + left_rates.shape),...  8.47 us
    dot_general x10, matrix products, pool(): jnp.einsum('kab,abrn->krn', w, piece, preferred_element_type=jnp.float32)  6.94 us
    dot_general x1, matrix products, local(): jnp.einsum('tab,ktbc->kac', left_part, right_done, preferred_element_type...  6.7 us
    dot_general x8, matrix products, make_chunk(): jnp.einsum('jab,jbc->jac', left_basis, piece, preferred_element_type=jnp....  4.22 us
  transfers between devices with their start and end apart: 21, of which 10 were waited for; matrix products, arithmetic and copies ran while one was open for 18% of the time, Pallas kernels for 0%

profile of v17, /device:TPU:24, one launch (start us, length us, event | category | flops | bytes accessed | tf_op | source)
XLA Modules:
  0.0 93.8 jit_solution(9559122146963604045)
XLA Ops:
  0.0 1.5 %collective-permute-start.1 = (bf16[2,64,512]{2,1,0:T(8,128)(2,1)}, bf16[2,64,512]{2,1,0:T(8,128)(2,1)S(1)}, u32[]{:S(2)}, u32[]{:S(2)}) collective-permute-start(bf16[2,64,512]{2,1,0:T(8,128)(2,1)} %param.11), channel_id=1, source_target_pairs={{0,64},{8,72},{16,80},{24,88},{32,96},{40,104},{48,112},{56,120},{... | collective-permute-start | bytes 393224 | tf_op jit(solution)/shard_map/ppermute | solution.py:70
  1.5 1.7 %collective-permute-start = (bf16[2,64,512]{2,1,0:T(8,128)(2,1)}, bf16[2,64,512]{2,1,0:T(8,128)(2,1)S(1)}, u32[]{:S(2)}, u32[]{:S(2)}) collective-permute-start(bf16[2,64,512]{2,1,0:T(8,128)(2,1)} %param.11), channel_id=1, source_target_pairs={{0,192},{8,200},{16,208},{24,216},{32,224},{40,232},{48,240},{56,2... | collective-permute-start | bytes 393224 | tf_op jit(solution)/shard_map/ppermute | solution.py:70
  3.2 0.7 broadcast_in_dim.2
  3.9 0.7 reshape.162
  4.6 8.5 %all-to-all-start = ((f32[8,1,128]{2,1,0:T(1,128)}), f32[8,1,128]{2,1,0:T(1,128)S(1)}, u32[]{:S(2)}, u32[]{:S(2)}) async-start(f32[8,1,128]{2,1,0:T(1,128)} %reshape.162), calls=%async_computation | async-start | bytes 8192 | tf_op jit(solution)/shard_map/all_to_all | solution.py:111
  13.4 1.1 %constant_dynamic-slice_fusion = s32[32,1,2,3]{1,2,3,0:T(2,128)S(1)} fusion(s32[32,32,2,3]{1,2,3,0:T(2,128)} %param.14, s32[]{:T(128)S(6)} %select_n.99), kind=kLoop, calls=%fused_computation.80 | loop fusion | bytes 1540 | tf_op jit(solution)/shard_map/jit(dynamic_index_in_dim)/dynamic_slice | solution.py:41
  14.6 0.9 dynamic-slice_reduce_fusion
  15.9 3.0 %collective-permute-start.3 = (bf16[1,64,512]{2,1,0:T(8,128)(2,1)S(1)}, bf16[1,64,512]{2,1,0:T(8,128)(2,1)S(1)}, u32[]{:S(2)}, u32[]{:S(2)}) collective-permute-start(bf16[1,64,512]{2,1,0:T(8,128)(2,1)S(1)} %slice.73), channel_id=1, source_target_pairs={{0,192},{8,200},{16,208},{24,216},{32,224},{40,232},{48,240},{56,2... | collective-permute-start | bytes 196616 | tf_op jit(solution)/shard_map/ppermute | solution.py:70
  19.1 1.1 %copy.112 = bf16[1,2,64,512]{3,0,1,2:T(2,128)(2,1)S(1)} copy(bf16[1,2,64,512]{3,2,1,0:T(8,128)(2,1)} %bitcast.200) | data formatting | bytes 262144 | tf_op jit(solution)/shard_map/stack | solution.py:78
  20.6 0.5 collective-permute-done.2
  21.3 1.2 %pad_maximum_fusion = bf16[4,2,64,512]{3,0,1,2:T(4,128)(2,1)S(1)} fusion(bf16[1,2,64,512]{3,0,1,2:T(2,128)(2,1)S(1)} %copy.115, bf16[1,2,64,512]{3,0,1,2:T(2,128)(2,1)S(1)} %copy.114, bf16[1,2,64,512]{3,0,1,2:T(2,128)(2,1)S(1)} %copy.113, bf16[1,2,64,512]{3,0,1,2:T(2,128)(2,1)S(1)} %copy.112), kind=kLoop, calls=%fused_computation.41 | loop fusion | flops 2097152 | bytes 1048576 | tf_op jit(solution)/shard_map/stack | solution.py:78
  22.9 1.8 %collective-permute-start.4 = (bf16[4,2,64,512]{3,0,1,2:T(4,128)(2,1)S(1)}, bf16[4,2,64,512]{3,0,1,2:T(4,128)(2,1)S(1)}, u32[]{:S(2)}, u32[]{:S(2)}) collective-permute-start(bf16[4,2,64,512]{3,0,1,2:T(4,128)(2,1)S(1)} %pad_maximum_fusion), channel_id=1, source_target_pairs={{0,48},{8,56},{16,0},{24,8},{32,16},{40,24},{48,32},{56,40},{64,11... | collective-permute-start | bytes 1572872 | tf_op jit(solution)/shard_map/ppermute | solution.py:70
  25.1 0.5 broadcast.166
  25.6 0.7 reduce.2
  26.5 0.6 fusion.70
  27.1 7.5 %collective-permute-done.5 = bf16[4,2,64,512]{3,0,1,2:T(4,128)(2,1)S(1)} collective-permute-done((bf16[4,2,64,512]{3,0,1,2:T(4,128)(2,1)S(1)}, bf16[4,2,64,512]{3,0,1,2:T(4,128)(2,1)S(1)}, u32[]{:S(2)}, u32[]{:S(2)}) %collective-permute-start.5) | collective-permute-done | bytes 524320 | tf_op jit(solution)/shard_map/ppermute | solution.py:70
  34.8 1.6 %collective-permute-start.6 = (bf16[2,2,64,512]{3,0,1,2:T(2,128)(2,1)S(1)}, bf16[2,2,64,512]{3,0,1,2:T(2,128)(2,1)S(1)}, u32[]{:S(2)}, u32[]{:S(2)}) collective-permute-start(bf16[2,2,64,512]{3,0,1,2:T(2,128)(2,1)S(1)} %slice.76), channel_id=1, source_target_pairs={{0,16},{8,24},{16,32},{24,40},{32,48},{40,56},{48,0},{56,8},{64,80... | collective-permute-start | bytes 786440 | tf_op jit(solution)/shard_map/ppermute | solution.py:70
  36.7 0.6 collective-permute-start.7
  37.3 0.5 collective-permute-start.12
  37.8 0.6 fusion.66
  38.4 0.6 fusion.68
  39.1 0.6 fusion.64
  39.7 4.7 %collective-permute-done.7 = bf16[2,2,64,512]{3,0,1,2:T(2,128)(2,1)S(1)} collective-permute-done((bf16[2,2,64,512]{3,0,1,2:T(2,128)(2,1)S(1)}, bf16[2,2,64,512]{3,0,1,2:T(2,128)(2,1)S(1)}, u32[]{:S(2)}, u32[]{:S(2)}) %collective-permute-start.7) | collective-permute-done | bytes 262176 | tf_op jit(solution)/shard_map/ppermute | solution.py:70
  44.3 0.6 fusion.31
  45.0 0.6 collective-permute-start.10
  45.6 0.6 fusion.33
  46.2 0.5 collective-permute-done.10
  46.7 0.6 fusion.29
  47.4 0.6 fusion.27
  48.0 0.6 fusion.62
  48.6 1.3 %fusion.9 = bf16[2,8,64,512]{3,1,0,2:T(8,128)(2,1)S(1)} fusion(bf16[4,2,64,512]{3,0,1,2:T(4,128)(2,1)S(1)} %collective-permute-done.12, f32[16,64,512,1]{2,0,3,1:T(8,128)S(1)} %fusion.27, f32[16,64,512,1]{2,0,3,1:T(8,128)S(1)} %fusion.29, f32[16,64,512,1]{2,0,3,1:T(8,128)S(1)} %fusion.62, f32[16,64,512,1]{2,0,3,1:T(8,128)S(1)} %fusion.64, ...), kind=kOutput, calls=%fused_computation.18 | convolution fusion | flops 13631488 | bytes 20447488 | tf_op jit(solution)/shard_map/kab,abrn->krn/dot_general | solution.py:91
  50.0 6.7 %bitcast_convert_fusion = bf16[2,512,512]{2,1,0:T(8,128)(2,1)} fusion(bf16[8,512,512]{2,1,0:T(8,128)(2,1)} %param.12, s32[]{:T(128)S(6)} %select_n.106, bf16[8,512,512]{2,1,0:T(8,128)(2,1)} %param.13, bf16[2,8,64,512]{3,1,0,2:T(8,128)(2,1)S(1)} %fusion.9), kind=kOutput, calls=%fused_computation.2 | convolution fusion | flops 1074790400 | bytes 7340036 | tf_op jit(solution)/shard_map/tab,ktbc->kac/dot_general | solution.py:115
  56.7 3.5 %divide_convert_fusion = bf16[2,512,512]{2,1,0:T(8,128)(2,1)} fusion(bf16[2,512,512]{2,1,0:T(8,128)(2,1)S(1)} %copy-done, bf16[2,512,512]{2,1,0:T(8,128)(2,1)} %bitcast_convert_fusion, bf16[2,512,512]{2,1,0:T(8,128)(2,1)S(1)} %copy-done.2, f32[2,512]{1,0:T(2,128)S(1)} %copy-done.3, f32[2,512]{1,0:T(2,128)S(1)} %add.288), kind=kOutput, calls=%fused_computation.13 | convolution fusion | flops 1075838976 | bytes 4202496 | tf_op jit(solution)/shard_map/jrn,jmn->jrm/dot_general | solution.py:121
  60.2 2.4 %convolution_convert_fusion = bf16[2,512,512]{1,2,0:T(8,128)(2,1)S(1)} fusion(bf16[2,512,512]{2,1,0:T(8,128)(2,1)} %divide_convert_fusion, bf16[2,512,512]{2,1,0:T(8,128)(2,1)} %param.18), kind=kOutput, calls=%fused_computation.15 | convolution fusion | flops 537395200 | bytes 3145728 | tf_op jit(solution)/shard_map/jrm,jkm->jrk/dot_general | solution.py:123
  63.1 5.5 %collective-permute-start.13 = (bf16[2,512,64]{1,2,0:T(8,128)(2,1)S(1)}, bf16[2,512,64]{1,2,0:T(8,128)(2,1)S(1)}, u32[]{:S(2)}, u32[]{:S(2)}) collective-permute-start(bf16[2,512,64]{1,2,0:T(8,128)(2,1)S(1)} %fusion.12), channel_id=1, source_target_pairs={{0,4},{1,5},{2,6},{3,7},{4,0},{5,1},{6,2},{7,3},{8,12},{9,13},{10,... | collective-permute-start | bytes 393224 | tf_op jit(solution)/shard_map/ppermute | solution.py:12
  69.0 0.9 collective-permute-start.14
  70.3 4.5 %collective-permute-start.15 = (bf16[2,512,64]{1,2,0:T(8,128)(2,1)S(1)}, bf16[2,512,64]{1,2,0:T(8,128)(2,1)S(1)}, u32[]{:S(2)}, u32[]{:S(2)}) collective-permute-start(bf16[2,512,64]{1,2,0:T(8,128)(2,1)S(1)} %fusion.14), channel_id=1, source_target_pairs={{0,5},{1,6},{2,7},{3,0},{4,1},{5,2},{6,3},{7,4},{8,13},{9,14},{10,... | collective-permute-start | bytes 393224 | tf_op jit(solution)/shard_map/ppermute | solution.py:12
  75.3 0.6 collective-permute-start.16
  76.4 3.6 %collective-permute-start.17 = (bf16[2,512,64]{1,2,0:T(8,128)(2,1)S(1)}, bf16[2,512,64]{1,2,0:T(8,128)(2,1)S(1)}, u32[]{:S(2)}, u32[]{:S(2)}) collective-permute-start(bf16[2,512,64]{1,2,0:T(8,128)(2,1)S(1)} %fusion.16), channel_id=1, source_target_pairs={{0,6},{1,7},{2,0},{3,1},{4,2},{5,3},{6,4},{7,5},{8,14},{9,15},{10,... | collective-permute-start | bytes 393224 | tf_op jit(solution)/shard_map/ppermute | solution.py:12
  80.5 0.4 fusion.18
  80.9 0.6 collective-permute-start.18
  81.6 2.1 %collective-permute-done.14 = bf16[2,512,64]{1,2,0:T(8,128)(2,1)S(1)} collective-permute-done((bf16[2,512,64]{1,2,0:T(8,128)(2,1)S(1)}, bf16[2,512,64]{1,2,0:T(8,128)(2,1)S(1)}, u32[]{:S(2)}, u32[]{:S(2)}) %collective-permute-start.14) | collective-permute-done | bytes 131104 | tf_op jit(solution)/shard_map/ppermute | solution.py:12
  83.6 0.6 collective-permute-start.19
  84.3 2.6 %collective-permute-done.15 = bf16[2,512,64]{1,2,0:T(8,128)(2,1)S(1)} collective-permute-done((bf16[2,512,64]{1,2,0:T(8,128)(2,1)S(1)}, bf16[2,512,64]{1,2,0:T(8,128)(2,1)S(1)}, u32[]{:S(2)}, u32[]{:S(2)}) %collective-permute-start.15) | collective-permute-done | bytes 131104 | tf_op jit(solution)/shard_map/ppermute | solution.py:12
  86.8 2.4 %collective-permute-done.16 = bf16[2,512,64]{1,2,0:T(8,128)(2,1)S(1)} collective-permute-done((bf16[2,512,64]{1,2,0:T(8,128)(2,1)S(1)}, bf16[2,512,64]{1,2,0:T(8,128)(2,1)S(1)}, u32[]{:S(2)}, u32[]{:S(2)}) %collective-permute-start.16) | collective-permute-done | bytes 131104 | tf_op jit(solution)/shard_map/ppermute | solution.py:12
  89.2 0.7 collective-permute-done.17
  89.9 2.7 %collective-permute-done.18 = bf16[2,512,64]{1,2,0:T(8,128)(2,1)S(1)} collective-permute-done((bf16[2,512,64]{1,2,0:T(8,128)(2,1)S(1)}, bf16[2,512,64]{1,2,0:T(8,128)(2,1)S(1)}, u32[]{:S(2)}, u32[]{:S(2)}) %collective-permute-start.18) | collective-permute-done | bytes 131104 | tf_op jit(solution)/shard_map/ppermute | solution.py:12
  92.6 1.2 %add_add_fusion = f32[2,512,64]{1,2,0:T(8,128)} fusion(bf16[2,512,64]{1,2,0:T(8,128)(2,1)S(1)} %collective-permute-done.19, bf16[2,512,64]{1,2,0:T(8,128)(2,1)S(1)} %collective-permute-done.18, bf16[2,512,64]{1,2,0:T(8,128)(2,1)S(1)} %collective-permute-done.17, bf16[2,512,64]{1,2,0:T(8,128)(2,1)S(1)} %collective-permute-done.16, ...), kind=kOutput, calls=%fused_computation.50 | convolution fusion | flops 68157440 | bytes 2359300 | tf_op jit(solution)/shard_map/jab,jbc->jac/dot_general | solution.py:129
  (55 shorter events, 5.5 us)
Async XLA Ops:
  0.0 56.7 %copy-start = (bf16[2,512,512]{2,1,0:T(8,128)(2,1)S(1)}, bf16[2,512,512]{2,1,0:T(8,128)(2,1)}, u32[]{:S(2)}) copy-start(bf16[2,512,512]{2,1,0:T(8,128)(2,1)} %param.19) | copy-start | bytes 3145732
  0.0 15.5 %collective-permute-start.1 = (bf16[2,64,512]{2,1,0:T(8,128)(2,1)}, bf16[2,64,512]{2,1,0:T(8,128)(2,1)S(1)}, u32[]{:S(2)}, u32[]{:S(2)}) collective-permute-start(bf16[2,64,512]{2,1,0:T(8,128)(2,1)} %param.11), channel_id=1, source_target_pairs={{0,64},{8,72},{16,80},{24,88},{32,96},{40,104},{48,112},{56,120},{... | collective-permute-start | bytes 393224 | tf_op jit(solution)/shard_map/ppermute | solution.py:70
  1.5 14.4 %collective-permute-start = (bf16[2,64,512]{2,1,0:T(8,128)(2,1)}, bf16[2,64,512]{2,1,0:T(8,128)(2,1)S(1)}, u32[]{:S(2)}, u32[]{:S(2)}) collective-permute-start(bf16[2,64,512]{2,1,0:T(8,128)(2,1)} %param.11), channel_id=1, source_target_pairs={{0,192},{8,200},{16,208},{24,216},{32,224},{40,232},{48,240},{56,2... | collective-permute-start | bytes 393224 | tf_op jit(solution)/shard_map/ppermute | solution.py:70
  4.6 20.5 %all-to-all-start = ((f32[8,1,128]{2,1,0:T(1,128)}), f32[8,1,128]{2,1,0:T(1,128)S(1)}, u32[]{:S(2)}, u32[]{:S(2)}) async-start(f32[8,1,128]{2,1,0:T(1,128)} %reshape.162), calls=%async_computation | async-start | bytes 8192 | tf_op jit(solution)/shard_map/all_to_all | solution.py:111
  15.5 5.6 %collective-permute-start.2 = (bf16[1,64,512]{2,1,0:T(8,128)(2,1)S(1)}, bf16[1,64,512]{2,1,0:T(8,128)(2,1)S(1)}, u32[]{:S(2)}, u32[]{:S(2)}) collective-permute-start(bf16[1,64,512]{2,1,0:T(8,128)(2,1)S(1)} %slice.72), channel_id=1, source_target_pairs={{0,64},{8,72},{16,80},{24,88},{32,96},{40,104},{48,112},{56,120},{... | collective-permute-start | bytes 196616 | tf_op jit(solution)/shard_map/ppermute | solution.py:70
  15.9 5.2 %collective-permute-start.3 = (bf16[1,64,512]{2,1,0:T(8,128)(2,1)S(1)}, bf16[1,64,512]{2,1,0:T(8,128)(2,1)S(1)}, u32[]{:S(2)}, u32[]{:S(2)}) collective-permute-start(bf16[1,64,512]{2,1,0:T(8,128)(2,1)S(1)} %slice.73), channel_id=1, source_target_pairs={{0,192},{8,200},{16,208},{24,216},{32,224},{40,232},{48,240},{56,2... | collective-permute-start | bytes 196616 | tf_op jit(solution)/shard_map/ppermute | solution.py:70
  22.6 12.0 %collective-permute-start.5 = (bf16[4,2,64,512]{3,0,1,2:T(4,128)(2,1)S(1)}, bf16[4,2,64,512]{3,0,1,2:T(4,128)(2,1)S(1)}, u32[]{:S(2)}, u32[]{:S(2)}) collective-permute-start(bf16[4,2,64,512]{3,0,1,2:T(4,128)(2,1)S(1)} %pad_maximum_fusion), channel_id=1, source_target_pairs={{0,16},{8,24},{16,32},{24,40},{32,48},{40,56},{48,0},{56,8},{64,80... | collective-permute-start | bytes 1572872 | tf_op jit(solution)/shard_map/ppermute | solution.py:70
  22.9 13.5 %collective-permute-start.4 = (bf16[4,2,64,512]{3,0,1,2:T(4,128)(2,1)S(1)}, bf16[4,2,64,512]{3,0,1,2:T(4,128)(2,1)S(1)}, u32[]{:S(2)}, u32[]{:S(2)}) collective-permute-start(bf16[4,2,64,512]{3,0,1,2:T(4,128)(2,1)S(1)} %pad_maximum_fusion), channel_id=1, source_target_pairs={{0,48},{8,56},{16,0},{24,8},{32,16},{40,24},{48,32},{56,40},{64,11... | collective-permute-start | bytes 1572872 | tf_op jit(solution)/shard_map/ppermute | solution.py:70
  26.4 12.6 %collective-permute-start.8 = (bf16[4,2,64,512]{3,0,1,2:T(4,128)(2,1)S(1)}, bf16[4,2,64,512]{3,0,1,2:T(4,128)(2,1)S(1)}, u32[]{:S(2)}, u32[]{:S(2)}) collective-permute-start(bf16[4,2,64,512]{3,0,1,2:T(4,128)(2,1)S(1)} %pad_maximum_fusion), channel_id=1, source_target_pairs={{0,8},{8,0},{16,24},{24,16},{32,40},{40,32},{48,56},{56,48},{64,72... | collective-permute-start | bytes 1572872 | tf_op jit(solution)/shard_map/ppermute | solution.py:70
  34.8 10.2 %collective-permute-start.6 = (bf16[2,2,64,512]{3,0,1,2:T(2,128)(2,1)S(1)}, bf16[2,2,64,512]{3,0,1,2:T(2,128)(2,1)S(1)}, u32[]{:S(2)}, u32[]{:S(2)}) collective-permute-start(bf16[2,2,64,512]{3,0,1,2:T(2,128)(2,1)S(1)} %slice.76), channel_id=1, source_target_pairs={{0,16},{8,24},{16,32},{24,40},{32,48},{40,56},{48,0},{56,8},{64,80... | collective-permute-start | bytes 786440 | tf_op jit(solution)/shard_map/ppermute | solution.py:70
  36.7 7.7 %collective-permute-start.7 = (bf16[2,2,64,512]{3,0,1,2:T(2,128)(2,1)S(1)}, bf16[2,2,64,512]{3,0,1,2:T(2,128)(2,1)S(1)}, u32[]{:S(2)}, u32[]{:S(2)}) collective-permute-start(bf16[2,2,64,512]{3,0,1,2:T(2,128)(2,1)S(1)} %slice.78), channel_id=1, source_target_pairs={{0,48},{8,56},{16,0},{24,8},{32,16},{40,24},{48,32},{56,40},{64,11... | collective-permute-start | bytes 786440 | tf_op jit(solution)/shard_map/ppermute | solution.py:70
  37.3 10.7 %collective-permute-start.9 = (bf16[4,2,64,512]{3,0,1,2:T(4,128)(2,1)S(1)}, bf16[4,2,64,512]{3,0,1,2:T(4,128)(2,1)S(1)}, u32[]{:S(2)}, u32[]{:S(2)}) collective-permute-start(bf16[4,2,64,512]{3,0,1,2:T(4,128)(2,1)S(1)} %collective-permute-done.4), channel_id=1, source_target_pairs={{0,8},{8,0},{16,24},{24,16},{32,40},{40,32},{48,56},{56,48},{64,72... | collective-permute-start | bytes 1572872 | tf_op jit(solution)/shard_map/ppermute | solution.py:70
  37.3 11.4 %collective-permute-start.12 = (bf16[4,2,64,512]{3,0,1,2:T(4,128)(2,1)S(1)}, bf16[4,2,64,512]{3,0,1,2:T(4,128)(2,1)S(1)}, u32[]{:S(2)}, u32[]{:S(2)}) collective-permute-start(bf16[4,2,64,512]{3,0,1,2:T(4,128)(2,1)S(1)} %collective-permute-done.5), channel_id=1, source_target_pairs={{0,8},{8,0},{16,24},{24,16},{32,40},{40,32},{48,56},{56,48},{64,72... | collective-permute-start | bytes 1572872 | tf_op jit(solution)/shard_map/ppermute | solution.py:70
  44.3 3.0 %collective-permute-start.11 = (bf16[2,2,64,512]{3,0,1,2:T(2,128)(2,1)S(1)}, bf16[2,2,64,512]{3,0,1,2:T(2,128)(2,1)S(1)}, u32[]{:S(2)}, u32[]{:S(2)}) collective-permute-start(bf16[2,2,64,512]{3,0,1,2:T(2,128)(2,1)S(1)} %collective-permute-done.7), channel_id=1, source_target_pairs={{0,8},{8,0},{16,24},{24,16},{32,40},{40,32},{48,56},{56,48},{64,72... | collective-permute-start | bytes 786440 | tf_op jit(solution)/shard_map/ppermute | solution.py:70
  45.0 1.8 %collective-permute-start.10 = (bf16[2,2,64,512]{3,0,1,2:T(2,128)(2,1)S(1)}, bf16[2,2,64,512]{3,0,1,2:T(2,128)(2,1)S(1)}, u32[]{:S(2)}, u32[]{:S(2)}) collective-permute-start(bf16[2,2,64,512]{3,0,1,2:T(2,128)(2,1)S(1)} %collective-permute-done.6), channel_id=1, source_target_pairs={{0,8},{8,0},{16,24},{24,16},{32,40},{40,32},{48,56},{56,48},{64,72... | collective-permute-start | bytes 786440 | tf_op jit(solution)/shard_map/ppermute | solution.py:70
  50.0 6.7 %copy-start.2 = (bf16[2,512,512]{2,1,0:T(8,128)(2,1)S(1)}, bf16[2,512,512]{2,1,0:T(8,128)(2,1)}, u32[]{:S(2)}) copy-start(bf16[2,512,512]{2,1,0:T(8,128)(2,1)} %param.17) | copy-start | bytes 3145732
  50.0 6.7 %copy-start.3 = (f32[2,512]{1,0:T(2,128)S(1)}, f32[2,512]{1,0:T(2,128)}, u32[]{:S(2)}) copy-start(f32[2,512]{1,0:T(2,128)} %param.21) | copy-start | bytes 12292
  60.2 2.4 %copy-start.1 = (bf16[2,512,512]{2,1,0:T(8,128)(2,1)S(1)}, bf16[2,512,512]{2,1,0:T(8,128)(2,1)}, u32[]{:S(2)}) copy-start(bf16[2,512,512]{2,1,0:T(8,128)(2,1)} %param.16) | copy-start | bytes 3145732
  63.1 17.9 %collective-permute-start.13 = (bf16[2,512,64]{1,2,0:T(8,128)(2,1)S(1)}, bf16[2,512,64]{1,2,0:T(8,128)(2,1)S(1)}, u32[]{:S(2)}, u32[]{:S(2)}) collective-permute-start(bf16[2,512,64]{1,2,0:T(8,128)(2,1)S(1)} %fusion.12), channel_id=1, source_target_pairs={{0,4},{1,5},{2,6},{3,7},{4,0},{5,1},{6,2},{7,3},{8,12},{9,13},{10,... | collective-permute-start | bytes 393224 | tf_op jit(solution)/shard_map/ppermute | solution.py:12
  69.0 14.6 %collective-permute-start.14 = (bf16[2,512,64]{1,2,0:T(8,128)(2,1)S(1)}, bf16[2,512,64]{1,2,0:T(8,128)(2,1)S(1)}, u32[]{:S(2)}, u32[]{:S(2)}) collective-permute-start(bf16[2,512,64]{1,2,0:T(8,128)(2,1)S(1)} %fusion.13), channel_id=1, source_target_pairs={{0,3},{1,4},{2,5},{3,6},{4,7},{5,0},{6,1},{7,2},{8,11},{9,12},{10,... | collective-permute-start | bytes 393224 | tf_op jit(solution)/shard_map/ppermute | solution.py:12
  70.3 16.5 %collective-permute-start.15 = (bf16[2,512,64]{1,2,0:T(8,128)(2,1)S(1)}, bf16[2,512,64]{1,2,0:T(8,128)(2,1)S(1)}, u32[]{:S(2)}, u32[]{:S(2)}) collective-permute-start(bf16[2,512,64]{1,2,0:T(8,128)(2,1)S(1)} %fusion.14), channel_id=1, source_target_pairs={{0,5},{1,6},{2,7},{3,0},{4,1},{5,2},{6,3},{7,4},{8,13},{9,14},{10,... | collective-permute-start | bytes 393224 | tf_op jit(solution)/shard_map/ppermute | solution.py:12
  75.3 13.9 %collective-permute-start.16 = (bf16[2,512,64]{1,2,0:T(8,128)(2,1)S(1)}, bf16[2,512,64]{1,2,0:T(8,128)(2,1)S(1)}, u32[]{:S(2)}, u32[]{:S(2)}) collective-permute-start(bf16[2,512,64]{1,2,0:T(8,128)(2,1)S(1)} %fusion.15), channel_id=1, source_target_pairs={{0,2},{1,3},{2,4},{3,5},{4,6},{5,7},{6,0},{7,1},{8,10},{9,11},{10,... | collective-permute-start | bytes 393224 | tf_op jit(solution)/shard_map/ppermute | solution.py:12
  76.4 13.5 %collective-permute-start.17 = (bf16[2,512,64]{1,2,0:T(8,128)(2,1)S(1)}, bf16[2,512,64]{1,2,0:T(8,128)(2,1)S(1)}, u32[]{:S(2)}, u32[]{:S(2)}) collective-permute-start(bf16[2,512,64]{1,2,0:T(8,128)(2,1)S(1)} %fusion.16), channel_id=1, source_target_pairs={{0,6},{1,7},{2,0},{3,1},{4,2},{5,3},{6,4},{7,5},{8,14},{9,15},{10,... | collective-permute-start | bytes 393224 | tf_op jit(solution)/shard_map/ppermute | solution.py:12
  80.9 11.6 %collective-permute-start.18 = (bf16[2,512,64]{1,2,0:T(8,128)(2,1)S(1)}, bf16[2,512,64]{1,2,0:T(8,128)(2,1)S(1)}, u32[]{:S(2)}, u32[]{:S(2)}) collective-permute-start(bf16[2,512,64]{1,2,0:T(8,128)(2,1)S(1)} %fusion.17), channel_id=1, source_target_pairs={{0,1},{1,2},{2,3},{3,4},{4,5},{5,6},{6,7},{7,0},{8,9},{9,10},{10,1... | collective-permute-start | bytes 393224 | tf_op jit(solution)/shard_map/ppermute | solution.py:12
  83.6 9.0 %collective-permute-start.19 = (bf16[2,512,64]{1,2,0:T(8,128)(2,1)S(1)}, bf16[2,512,64]{1,2,0:T(8,128)(2,1)S(1)}, u32[]{:S(2)}, u32[]{:S(2)}) collective-permute-start(bf16[2,512,64]{1,2,0:T(8,128)(2,1)S(1)} %fusion.18), channel_id=1, source_target_pairs={{0,7},{1,0},{2,1},{3,2},{4,3},{5,4},{6,5},{7,6},{8,15},{9,8},{10,9... | collective-permute-start | bytes 393224 | tf_op jit(solution)/shard_map/ppermute | solution.py:12

commit v18 on v16

--- a/solution.py
+++ b/solution.py
@@ -7,7 +7,7 @@
 def scatter_sum(make_chunk, n, axis):
     me = lax.axis_index(axis)
     total = None
-    for k in sorted(range(1, n), key=lambda k: (-min(k, n - k), k)):
+    for k in [n // 2] + list(range(n // 2 - 1, 0, -1)) + list(range(n // 2 + 1, n)):
         send = make_chunk((me + k) % n)
         got = lax.ppermute(send, axis, [(j, (j + k) % n) for j in range(n)])
         total = got.astype(jnp.float32) if total is None else total + got.astype(jnp.float32)

time: 92.8 us -> 94.3 us (1.016)
  waiting for transfers between devices: 23.3 us -> 25.7 us
    ppermute x7, waiting for transfers between devices: 10.3 us -> 12.7 us  [scatter_sum(): got = lax.ppermute(send, axis, [(j, (j + k) % n) for j in range(n)])]
  transfers between devices with their start and end apart: 20 -> 20, of which waited for: 11 -> 10; matrix products, arithmetic and copies ran while one was open for 18% -> 18% of each run, Pallas kernels for 0% -> 0%
where the time goes in v18:
time: 94.3 us; the launch traced here: 93.7 us
  starting transfers between devices  35.6 us (38%)
  waiting for transfers between devices  25.7 us (27%)
  matrix products  22.6 us (24%)
  local copies, waits for them, and re-layouts  6.59 us (7%)
  other arithmetic  2.77 us (3%)
    ppermute x7, starting transfers between devices, scatter_sum(): got = lax.ppermute(send, axis, [(j, (j + k) % n) for j in range(n)])  15.6 us
    ppermute x12, waiting for transfers between devices, move(): return lax.ppermute(piece, 'blk', pairs_list)  13 us
    ppermute x7, waiting for transfers between devices, scatter_sum(): got = lax.ppermute(send, axis, [(j, (j + k) % n) for j in range(n)])  12.7 us
    ppermute x12, starting transfers between devices, move(): return lax.ppermute(piece, 'blk', pairs_list)  11.5 us
    all_to_all x1, starting transfers between devices, local(): lax.all_to_all(jnp.broadcast_to(rates_run, (pieces,) + left_rates.shape),...  8.47 us
    dot_general x1, matrix products, local(): jnp.einsum('tab,ktbc->kac', left_part, right_done, preferred_element_type...  6.71 us
    dot_general x8, matrix products, pool(): jnp.einsum('kab,abrn->krn', w, piece, preferred_element_type=jnp.float32)  5.86 us
    dot_general x8, matrix products, make_chunk(): jnp.einsum('jab,jbc->jac', left_basis, piece, preferred_element_type=jnp....  4.21 us
  transfers between devices with their start and end apart: 20, of which 10 were waited for; matrix products, arithmetic and copies ran while one was open for 18% of the time, Pallas kernels for 0%

profile of v18, /device:TPU:24, one launch (start us, length us, event | category | flops | bytes accessed | tf_op | source)
XLA Modules:
  0.0 93.7 jit_solution(6052584448189919801)
XLA Ops:
  0.0 1.5 %collective-permute-start.1 = (bf16[2,64,512]{2,1,0:T(8,128)(2,1)}, bf16[2,64,512]{2,1,0:T(8,128)(2,1)S(1)}, u32[]{:S(2)}, u32[]{:S(2)}) collective-permute-start(bf16[2,64,512]{2,1,0:T(8,128)(2,1)} %param.11), channel_id=1, source_target_pairs={{0,64},{8,72},{16,80},{24,88},{32,96},{40,104},{48,112},{56,120},{... | collective-permute-start | bytes 393224 | tf_op jit(solution)/shard_map/ppermute | solution.py:70
  1.5 1.7 %collective-permute-start = (bf16[2,64,512]{2,1,0:T(8,128)(2,1)}, bf16[2,64,512]{2,1,0:T(8,128)(2,1)S(1)}, u32[]{:S(2)}, u32[]{:S(2)}) collective-permute-start(bf16[2,64,512]{2,1,0:T(8,128)(2,1)} %param.11), channel_id=1, source_target_pairs={{0,192},{8,200},{16,208},{24,216},{32,224},{40,232},{48,240},{56,2... | collective-permute-start | bytes 393224 | tf_op jit(solution)/shard_map/ppermute | solution.py:70
  3.2 0.7 broadcast_in_dim.2
  3.9 0.7 reshape.158
  4.6 8.5 %all-to-all-start = ((f32[8,1,128]{2,1,0:T(1,128)}), f32[8,1,128]{2,1,0:T(1,128)S(1)}, u32[]{:S(2)}, u32[]{:S(2)}) async-start(f32[8,1,128]{2,1,0:T(1,128)} %reshape.158), calls=%async_computation | async-start | bytes 8192 | tf_op jit(solution)/shard_map/all_to_all | solution.py:109
  13.4 1.1 %constant_dynamic-slice_fusion = s32[32,1,2,3]{1,2,3,0:T(2,128)S(1)} fusion(s32[32,32,2,3]{1,2,3,0:T(2,128)} %param.14, s32[]{:T(128)S(6)} %select_n.99), kind=kLoop, calls=%fused_computation.71 | loop fusion | bytes 1540 | tf_op jit(solution)/shard_map/jit(dynamic_index_in_dim)/dynamic_slice | solution.py:41
  14.6 0.9 dynamic-slice_reduce_fusion
  15.9 3.0 %collective-permute-start.3 = (bf16[1,64,512]{2,1,0:T(8,128)(2,1)S(1)}, bf16[1,64,512]{2,1,0:T(8,128)(2,1)S(1)}, u32[]{:S(2)}, u32[]{:S(2)}) collective-permute-start(bf16[1,64,512]{2,1,0:T(8,128)(2,1)S(1)} %slice.65), channel_id=1, source_target_pairs={{0,192},{8,200},{16,208},{24,216},{32,224},{40,232},{48,240},{56,2... | collective-permute-start | bytes 196616 | tf_op jit(solution)/shard_map/ppermute | solution.py:70
  19.1 1.1 %copy.98 = bf16[1,2,64,512]{3,0,1,2:T(2,128)(2,1)S(1)} copy(bf16[1,2,64,512]{3,2,1,0:T(8,128)(2,1)} %bitcast.177) | data formatting | bytes 262144 | tf_op jit(solution)/shard_map/stack | solution.py:78
  20.6 0.5 collective-permute-done.2
  21.3 1.2 %pad_maximum_fusion = bf16[4,2,64,512]{3,0,1,2:T(4,128)(2,1)S(1)} fusion(bf16[1,2,64,512]{3,0,1,2:T(2,128)(2,1)S(1)} %copy.101, bf16[1,2,64,512]{3,0,1,2:T(2,128)(2,1)S(1)} %copy.100, bf16[1,2,64,512]{3,0,1,2:T(2,128)(2,1)S(1)} %copy.99, bf16[1,2,64,512]{3,0,1,2:T(2,128)(2,1)S(1)} %copy.98), kind=kLoop, calls=%fused_computation.39 | loop fusion | flops 2097152 | bytes 1048576 | tf_op jit(solution)/shard_map/stack | solution.py:78
  22.9 1.8 %collective-permute-start.4 = (bf16[4,2,64,512]{3,0,1,2:T(4,128)(2,1)S(1)}, bf16[4,2,64,512]{3,0,1,2:T(4,128)(2,1)S(1)}, u32[]{:S(2)}, u32[]{:S(2)}) collective-permute-start(bf16[4,2,64,512]{3,0,1,2:T(4,128)(2,1)S(1)} %pad_maximum_fusion), channel_id=1, source_target_pairs={{0,48},{8,56},{16,0},{24,8},{32,16},{40,24},{48,32},{56,40},{64,11... | collective-permute-start | bytes 1572872 | tf_op jit(solution)/shard_map/ppermute | solution.py:70
  25.1 0.5 broadcast.166
  25.6 0.7 reduce.2
  26.5 0.6 fusion.66
  27.1 7.5 %collective-permute-done.5 = bf16[4,2,64,512]{3,0,1,2:T(4,128)(2,1)S(1)} collective-permute-done((bf16[4,2,64,512]{3,0,1,2:T(4,128)(2,1)S(1)}, bf16[4,2,64,512]{3,0,1,2:T(4,128)(2,1)S(1)}, u32[]{:S(2)}, u32[]{:S(2)}) %collective-permute-start.5) | collective-permute-done | bytes 524320 | tf_op jit(solution)/shard_map/ppermute | solution.py:70
  34.8 1.6 %collective-permute-start.6 = (bf16[2,2,64,512]{3,0,1,2:T(2,128)(2,1)S(1)}, bf16[2,2,64,512]{3,0,1,2:T(2,128)(2,1)S(1)}, u32[]{:S(2)}, u32[]{:S(2)}) collective-permute-start(bf16[2,2,64,512]{3,0,1,2:T(2,128)(2,1)S(1)} %slice.68), channel_id=1, source_target_pairs={{0,16},{8,24},{16,32},{24,40},{32,48},{40,56},{48,0},{56,8},{64,80... | collective-permute-start | bytes 786440 | tf_op jit(solution)/shard_map/ppermute | solution.py:70
  36.7 0.6 collective-permute-start.7
  37.3 0.5 collective-permute-start.11
  37.8 0.6 fusion.60
  38.4 0.6 fusion.64
  39.1 0.6 fusion.58
  39.7 1.6 %collective-permute-done.6 = bf16[2,2,64,512]{3,0,1,2:T(2,128)(2,1)S(1)} collective-permute-done((bf16[2,2,64,512]{3,0,1,2:T(2,128)(2,1)S(1)}, bf16[2,2,64,512]{3,0,1,2:T(2,128)(2,1)S(1)}, u32[]{:S(2)}, u32[]{:S(2)}) %collective-permute-start.6) | collective-permute-done | bytes 262176 | tf_op jit(solution)/shard_map/ppermute | solution.py:70
  41.2 3.1 %collective-permute-done.7 = bf16[2,2,64,512]{3,0,1,2:T(2,128)(2,1)S(1)} collective-permute-done((bf16[2,2,64,512]{3,0,1,2:T(2,128)(2,1)S(1)}, bf16[2,2,64,512]{3,0,1,2:T(2,128)(2,1)S(1)}, u32[]{:S(2)}, u32[]{:S(2)}) %collective-permute-start.7) | collective-permute-done | bytes 262176 | tf_op jit(solution)/shard_map/ppermute | solution.py:70
  44.3 0.5 pad_maximum_fusion.1
  45.0 1.0 %fusion.62 = f32[16,64,512,1]{2,0,3,1:T(8,128)S(1)} fusion(bf16[16,1,1,4,2]{0,4,3,2,1:T(2,128)(2,1)S(1)} %get-tuple-element.10, bf16[2,2,64,512]{3,0,1,2:T(2,128)(2,1)S(1)} %collective-permute-done.7, bf16[2,2,64,512]{3,0,1,2:T(2,128)(2,1)S(1)} %collective-permute-done.6), kind=kOutput, calls=%fused_computation.85 | convolution fusion | flops 9437184 | bytes 2621696 | tf_op jit(solution)/shard_map/kab,abrn->krn/dot_general | solution.py:91
  46.0 0.6 fusion.56
  46.9 0.6 fusion.54
  47.5 1.2 %fusion.9 = bf16[2,8,64,512]{3,1,0,2:T(8,128)(2,1)S(1)} fusion(bf16[4,2,64,512]{3,0,1,2:T(4,128)(2,1)S(1)} %collective-permute-done.11, f32[16,64,512,1]{2,0,3,1:T(8,128)S(1)} %fusion.54, f32[16,64,512,1]{2,0,3,1:T(8,128)S(1)} %fusion.56, f32[16,64,512,1]{2,0,3,1:T(8,128)S(1)} %fusion.58, f32[16,64,512,1]{2,0,3,1:T(8,128)S(1)} %fusion.60, ...), kind=kOutput, calls=%fused_computation.16 | convolution fusion | flops 12582912 | bytes 16253184 | tf_op jit(solution)/shard_map/kab,abrn->krn/dot_general | solution.py:91
  48.7 6.7 %bitcast_convert_fusion = bf16[2,512,512]{2,1,0:T(8,128)(2,1)} fusion(bf16[8,512,512]{2,1,0:T(8,128)(2,1)} %param.12, s32[]{:T(128)S(6)} %select_n.106, bf16[8,512,512]{2,1,0:T(8,128)(2,1)} %param.13, bf16[2,8,64,512]{3,1,0,2:T(8,128)(2,1)S(1)} %fusion.9), kind=kOutput, calls=%fused_computation.2 | convolution fusion | flops 1074790400 | bytes 7340036 | tf_op jit(solution)/shard_map/tab,ktbc->kac/dot_general | solution.py:113
  55.4 3.6 %divide_convert_fusion = bf16[2,512,512]{2,1,0:T(8,128)(2,1)} fusion(bf16[2,512,512]{2,1,0:T(8,128)(2,1)S(1)} %copy-done, bf16[2,512,512]{2,1,0:T(8,128)(2,1)} %bitcast_convert_fusion, bf16[2,512,512]{2,1,0:T(8,128)(2,1)S(1)} %copy-done.2, f32[2,512]{1,0:T(2,128)S(1)} %copy-done.4, f32[2,512]{1,0:T(2,128)S(1)} %add.280), kind=kOutput, calls=%fused_computation.11 | convolution fusion | flops 1075838976 | bytes 4202496 | tf_op jit(solution)/shard_map/jrn,jmn->jrm/dot_general | solution.py:119
  59.0 2.1 %convolution_convert_fusion = bf16[2,512,512]{1,2,0:T(8,128)(2,1)S(1)} fusion(bf16[2,512,512]{2,1,0:T(8,128)(2,1)} %divide_convert_fusion, bf16[2,512,512]{2,1,0:T(8,128)(2,1)S(1)} %copy-done.3), kind=kOutput, calls=%fused_computation.13 | convolution fusion | flops 537395200 | bytes 3145728 | tf_op jit(solution)/shard_map/jrm,jkm->jrk/dot_general | solution.py:121
  61.1 0.4 fusion.12
  61.5 5.5 %collective-permute-start.12 = (bf16[2,512,64]{1,2,0:T(8,128)(2,1)S(1)}, bf16[2,512,64]{1,2,0:T(8,128)(2,1)S(1)}, u32[]{:S(2)}, u32[]{:S(2)}) collective-permute-start(bf16[2,512,64]{1,2,0:T(8,128)(2,1)S(1)} %fusion.12), channel_id=1, source_target_pairs={{0,4},{1,5},{2,6},{3,7},{4,0},{5,1},{6,2},{7,3},{8,12},{9,13},{10,... | collective-permute-start | bytes 393224 | tf_op jit(solution)/shard_map/ppermute | solution.py:12
  67.1 0.4 fusion.13
  67.5 0.6 collective-permute-start.13
  68.1 0.4 fusion.14
  68.6 1.9 %collective-permute-start.14 = (bf16[2,512,64]{1,2,0:T(8,128)(2,1)S(1)}, bf16[2,512,64]{1,2,0:T(8,128)(2,1)S(1)}, u32[]{:S(2)}, u32[]{:S(2)}) collective-permute-start(bf16[2,512,64]{1,2,0:T(8,128)(2,1)S(1)} %fusion.14), channel_id=1, source_target_pairs={{0,2},{1,3},{2,4},{3,5},{4,6},{5,7},{6,0},{7,1},{8,10},{9,11},{10,... | collective-permute-start | bytes 393224 | tf_op jit(solution)/shard_map/ppermute | solution.py:12
  70.9 1.4 %collective-permute-start.15 = (bf16[2,512,64]{1,2,0:T(8,128)(2,1)S(1)}, bf16[2,512,64]{1,2,0:T(8,128)(2,1)S(1)}, u32[]{:S(2)}, u32[]{:S(2)}) collective-permute-start(bf16[2,512,64]{1,2,0:T(8,128)(2,1)S(1)} %fusion.15), channel_id=1, source_target_pairs={{0,1},{1,2},{2,3},{3,4},{4,5},{5,6},{6,7},{7,0},{8,9},{9,10},{10,1... | collective-permute-start | bytes 393224 | tf_op jit(solution)/shard_map/ppermute | solution.py:12
  72.7 2.8 %collective-permute-start.16 = (bf16[2,512,64]{1,2,0:T(8,128)(2,1)S(1)}, bf16[2,512,64]{1,2,0:T(8,128)(2,1)S(1)}, u32[]{:S(2)}, u32[]{:S(2)}) collective-permute-start(bf16[2,512,64]{1,2,0:T(8,128)(2,1)S(1)} %fusion.16), channel_id=1, source_target_pairs={{0,5},{1,6},{2,7},{3,0},{4,1},{5,2},{6,3},{7,4},{8,13},{9,14},{10,... | collective-permute-start | bytes 393224 | tf_op jit(solution)/shard_map/ppermute | solution.py:12
  75.5 0.4 fusion.17
  75.9 0.4 fusion.18
  76.6 3.4 %collective-permute-start.17 = (bf16[2,512,64]{1,2,0:T(8,128)(2,1)S(1)}, bf16[2,512,64]{1,2,0:T(8,128)(2,1)S(1)}, u32[]{:S(2)}, u32[]{:S(2)}) collective-permute-start(bf16[2,512,64]{1,2,0:T(8,128)(2,1)S(1)} %fusion.17), channel_id=1, source_target_pairs={{0,6},{1,7},{2,0},{3,1},{4,2},{5,3},{6,4},{7,5},{8,14},{9,15},{10,... | collective-permute-start | bytes 393224 | tf_op jit(solution)/shard_map/ppermute | solution.py:12
  80.0 2.1 %collective-permute-done.13 = bf16[2,512,64]{1,2,0:T(8,128)(2,1)S(1)} collective-permute-done((bf16[2,512,64]{1,2,0:T(8,128)(2,1)S(1)}, bf16[2,512,64]{1,2,0:T(8,128)(2,1)S(1)}, u32[]{:S(2)}, u32[]{:S(2)}) %collective-permute-start.13) | collective-permute-done | bytes 131104 | tf_op jit(solution)/shard_map/ppermute | solution.py:12
  82.1 5.5 %collective-permute-done.14 = bf16[2,512,64]{1,2,0:T(8,128)(2,1)S(1)} collective-permute-done((bf16[2,512,64]{1,2,0:T(8,128)(2,1)S(1)}, bf16[2,512,64]{1,2,0:T(8,128)(2,1)S(1)}, u32[]{:S(2)}, u32[]{:S(2)}) %collective-permute-start.14) | collective-permute-done | bytes 131104 | tf_op jit(solution)/shard_map/ppermute | solution.py:12
  87.6 3.2 %collective-permute-done.15 = bf16[2,512,64]{1,2,0:T(8,128)(2,1)S(1)} collective-permute-done((bf16[2,512,64]{1,2,0:T(8,128)(2,1)S(1)}, bf16[2,512,64]{1,2,0:T(8,128)(2,1)S(1)}, u32[]{:S(2)}, u32[]{:S(2)}) %collective-permute-start.15) | collective-permute-done | bytes 131104 | tf_op jit(solution)/shard_map/ppermute | solution.py:12
  90.9 1.6 %collective-permute-done.18 = bf16[2,512,64]{1,2,0:T(8,128)(2,1)S(1)} collective-permute-done((bf16[2,512,64]{1,2,0:T(8,128)(2,1)S(1)}, bf16[2,512,64]{1,2,0:T(8,128)(2,1)S(1)}, u32[]{:S(2)}, u32[]{:S(2)}) %collective-permute-start.18) | collective-permute-done | bytes 131104 | tf_op jit(solution)/shard_map/ppermute | solution.py:12
  92.5 1.2 %add_add_fusion = f32[2,512,64]{1,2,0:T(8,128)} fusion(bf16[2,512,64]{1,2,0:T(8,128)(2,1)S(1)} %collective-permute-done.18, bf16[2,512,64]{1,2,0:T(8,128)(2,1)S(1)} %collective-permute-done.17, bf16[2,512,64]{1,2,0:T(8,128)(2,1)S(1)} %collective-permute-done.16, bf16[2,512,64]{1,2,0:T(8,128)(2,1)S(1)} %collective-permute-done.15, ...), kind=kOutput, calls=%fused_computation.41 | convolution fusion | flops 68157440 | bytes 2359300 | tf_op jit(solution)/shard_map/jab,jbc->jac/dot_general | solution.py:127
  (54 shorter events, 4.4 us)
Async XLA Ops:
  0.0 55.4 %copy-start = (bf16[2,512,512]{2,1,0:T(8,128)(2,1)S(1)}, bf16[2,512,512]{2,1,0:T(8,128)(2,1)}, u32[]{:S(2)}) copy-start(bf16[2,512,512]{2,1,0:T(8,128)(2,1)} %param.19) | copy-start | bytes 3145732
  0.0 15.5 %collective-permute-start.1 = (bf16[2,64,512]{2,1,0:T(8,128)(2,1)}, bf16[2,64,512]{2,1,0:T(8,128)(2,1)S(1)}, u32[]{:S(2)}, u32[]{:S(2)}) collective-permute-start(bf16[2,64,512]{2,1,0:T(8,128)(2,1)} %param.11), channel_id=1, source_target_pairs={{0,64},{8,72},{16,80},{24,88},{32,96},{40,104},{48,112},{56,120},{... | collective-permute-start | bytes 393224 | tf_op jit(solution)/shard_map/ppermute | solution.py:70
  1.5 14.4 %collective-permute-start = (bf16[2,64,512]{2,1,0:T(8,128)(2,1)}, bf16[2,64,512]{2,1,0:T(8,128)(2,1)S(1)}, u32[]{:S(2)}, u32[]{:S(2)}) collective-permute-start(bf16[2,64,512]{2,1,0:T(8,128)(2,1)} %param.11), channel_id=1, source_target_pairs={{0,192},{8,200},{16,208},{24,216},{32,224},{40,232},{48,240},{56,2... | collective-permute-start | bytes 393224 | tf_op jit(solution)/shard_map/ppermute | solution.py:70
  4.6 20.5 %all-to-all-start = ((f32[8,1,128]{2,1,0:T(1,128)}), f32[8,1,128]{2,1,0:T(1,128)S(1)}, u32[]{:S(2)}, u32[]{:S(2)}) async-start(f32[8,1,128]{2,1,0:T(1,128)} %reshape.158), calls=%async_computation | async-start | bytes 8192 | tf_op jit(solution)/shard_map/all_to_all | solution.py:109
  15.5 5.6 %collective-permute-start.2 = (bf16[1,64,512]{2,1,0:T(8,128)(2,1)S(1)}, bf16[1,64,512]{2,1,0:T(8,128)(2,1)S(1)}, u32[]{:S(2)}, u32[]{:S(2)}) collective-permute-start(bf16[1,64,512]{2,1,0:T(8,128)(2,1)S(1)} %slice.64), channel_id=1, source_target_pairs={{0,64},{8,72},{16,80},{24,88},{32,96},{40,104},{48,112},{56,120},{... | collective-permute-start | bytes 196616 | tf_op jit(solution)/shard_map/ppermute | solution.py:70
  15.9 5.2 %collective-permute-start.3 = (bf16[1,64,512]{2,1,0:T(8,128)(2,1)S(1)}, bf16[1,64,512]{2,1,0:T(8,128)(2,1)S(1)}, u32[]{:S(2)}, u32[]{:S(2)}) collective-permute-start(bf16[1,64,512]{2,1,0:T(8,128)(2,1)S(1)} %slice.65), channel_id=1, source_target_pairs={{0,192},{8,200},{16,208},{24,216},{32,224},{40,232},{48,240},{56,2... | collective-permute-start | bytes 196616 | tf_op jit(solution)/shard_map/ppermute | solution.py:70
  22.6 12.0 %collective-permute-start.5 = (bf16[4,2,64,512]{3,0,1,2:T(4,128)(2,1)S(1)}, bf16[4,2,64,512]{3,0,1,2:T(4,128)(2,1)S(1)}, u32[]{:S(2)}, u32[]{:S(2)}) collective-permute-start(bf16[4,2,64,512]{3,0,1,2:T(4,128)(2,1)S(1)} %pad_maximum_fusion), channel_id=1, source_target_pairs={{0,16},{8,24},{16,32},{24,40},{32,48},{40,56},{48,0},{56,8},{64,80... | collective-permute-start | bytes 1572872 | tf_op jit(solution)/shard_map/ppermute | solution.py:70
  22.9 13.5 %collective-permute-start.4 = (bf16[4,2,64,512]{3,0,1,2:T(4,128)(2,1)S(1)}, bf16[4,2,64,512]{3,0,1,2:T(4,128)(2,1)S(1)}, u32[]{:S(2)}, u32[]{:S(2)}) collective-permute-start(bf16[4,2,64,512]{3,0,1,2:T(4,128)(2,1)S(1)} %pad_maximum_fusion), channel_id=1, source_target_pairs={{0,48},{8,56},{16,0},{24,8},{32,16},{40,24},{48,32},{56,40},{64,11... | collective-permute-start | bytes 1572872 | tf_op jit(solution)/shard_map/ppermute | solution.py:70
  26.4 12.6 %collective-permute-start.8 = (bf16[4,2,64,512]{3,0,1,2:T(4,128)(2,1)S(1)}, bf16[4,2,64,512]{3,0,1,2:T(4,128)(2,1)S(1)}, u32[]{:S(2)}, u32[]{:S(2)}) collective-permute-start(bf16[4,2,64,512]{3,0,1,2:T(4,128)(2,1)S(1)} %pad_maximum_fusion), channel_id=1, source_target_pairs={{0,8},{8,0},{16,24},{24,16},{32,40},{40,32},{48,56},{56,48},{64,72... | collective-permute-start | bytes 1572872 | tf_op jit(solution)/shard_map/ppermute | solution.py:70
  34.8 6.4 %collective-permute-start.6 = (bf16[2,2,64,512]{3,0,1,2:T(2,128)(2,1)S(1)}, bf16[2,2,64,512]{3,0,1,2:T(2,128)(2,1)S(1)}, u32[]{:S(2)}, u32[]{:S(2)}) collective-permute-start(bf16[2,2,64,512]{3,0,1,2:T(2,128)(2,1)S(1)} %slice.68), channel_id=1, source_target_pairs={{0,16},{8,24},{16,32},{24,40},{32,48},{40,56},{48,0},{56,8},{64,80... | collective-permute-start | bytes 786440 | tf_op jit(solution)/shard_map/ppermute | solution.py:70
  36.7 7.7 %collective-permute-start.7 = (bf16[2,2,64,512]{3,0,1,2:T(2,128)(2,1)S(1)}, bf16[2,2,64,512]{3,0,1,2:T(2,128)(2,1)S(1)}, u32[]{:S(2)}, u32[]{:S(2)}) collective-permute-start(bf16[2,2,64,512]{3,0,1,2:T(2,128)(2,1)S(1)} %slice.69), channel_id=1, source_target_pairs={{0,48},{8,56},{16,0},{24,8},{32,16},{40,24},{48,32},{56,40},{64,11... | collective-permute-start | bytes 786440 | tf_op jit(solution)/shard_map/ppermute | solution.py:70
  37.3 8.7 %collective-permute-start.9 = (bf16[4,2,64,512]{3,0,1,2:T(4,128)(2,1)S(1)}, bf16[4,2,64,512]{3,0,1,2:T(4,128)(2,1)S(1)}, u32[]{:S(2)}, u32[]{:S(2)}) collective-permute-start(bf16[4,2,64,512]{3,0,1,2:T(4,128)(2,1)S(1)} %collective-permute-done.4), channel_id=1, source_target_pairs={{0,8},{8,0},{16,24},{24,16},{32,40},{40,32},{48,56},{56,48},{64,72... | collective-permute-start | bytes 1572872 | tf_op jit(solution)/shard_map/ppermute | solution.py:70
  37.3 10.2 %collective-permute-start.11 = (bf16[4,2,64,512]{3,0,1,2:T(4,128)(2,1)S(1)}, bf16[4,2,64,512]{3,0,1,2:T(4,128)(2,1)S(1)}, u32[]{:S(2)}, u32[]{:S(2)}) collective-permute-start(bf16[4,2,64,512]{3,0,1,2:T(4,128)(2,1)S(1)} %collective-permute-done.5), channel_id=1, source_target_pairs={{0,8},{8,0},{16,24},{24,16},{32,40},{40,32},{48,56},{56,48},{64,72... | collective-permute-start | bytes 1572872 | tf_op jit(solution)/shard_map/ppermute | solution.py:70
  44.9 2.0 %collective-permute-start.10 = (bf16[4,2,64,512]{3,0,1,2:T(4,128)(2,1)S(1)}, bf16[4,2,64,512]{3,0,1,2:T(4,128)(2,1)S(1)}, u32[]{:S(2)}, u32[]{:S(2)}) collective-permute-start(bf16[4,2,64,512]{3,0,1,2:T(4,128)(2,1)S(1)} %pad_maximum_fusion.1), channel_id=1, source_target_pairs={{0,8},{8,0},{16,24},{24,16},{32,40},{40,32},{48,56},{56,48},{64,72... | collective-permute-start | bytes 1572872 | tf_op jit(solution)/shard_map/ppermute | solution.py:70
  48.7 6.7 %copy-start.2 = (bf16[2,512,512]{2,1,0:T(8,128)(2,1)S(1)}, bf16[2,512,512]{2,1,0:T(8,128)(2,1)}, u32[]{:S(2)}) copy-start(bf16[2,512,512]{2,1,0:T(8,128)(2,1)} %param.17) | copy-start | bytes 3145732
  48.7 6.7 %copy-start.4 = (f32[2,512]{1,0:T(2,128)S(1)}, f32[2,512]{1,0:T(2,128)}, u32[]{:S(2)}) copy-start(f32[2,512]{1,0:T(2,128)} %param.21) | copy-start | bytes 12292
  55.4 3.6 %copy-start.3 = (bf16[2,512,512]{2,1,0:T(8,128)(2,1)S(1)}, bf16[2,512,512]{2,1,0:T(8,128)(2,1)}, u32[]{:S(2)}) copy-start(bf16[2,512,512]{2,1,0:T(8,128)(2,1)} %param.18) | copy-start | bytes 3145732
  59.0 2.1 %copy-start.1 = (bf16[2,512,512]{2,1,0:T(8,128)(2,1)S(1)}, bf16[2,512,512]{2,1,0:T(8,128)(2,1)}, u32[]{:S(2)}) copy-start(bf16[2,512,512]{2,1,0:T(8,128)(2,1)} %param.16) | copy-start | bytes 3145732
  61.5 15.1 %collective-permute-start.12 = (bf16[2,512,64]{1,2,0:T(8,128)(2,1)S(1)}, bf16[2,512,64]{1,2,0:T(8,128)(2,1)S(1)}, u32[]{:S(2)}, u32[]{:S(2)}) collective-permute-start(bf16[2,512,64]{1,2,0:T(8,128)(2,1)S(1)} %fusion.12), channel_id=1, source_target_pairs={{0,4},{1,5},{2,6},{3,7},{4,0},{5,1},{6,2},{7,3},{8,12},{9,13},{10,... | collective-permute-start | bytes 393224 | tf_op jit(solution)/shard_map/ppermute | solution.py:12
  67.5 14.6 %collective-permute-start.13 = (bf16[2,512,64]{1,2,0:T(8,128)(2,1)S(1)}, bf16[2,512,64]{1,2,0:T(8,128)(2,1)S(1)}, u32[]{:S(2)}, u32[]{:S(2)}) collective-permute-start(bf16[2,512,64]{1,2,0:T(8,128)(2,1)S(1)} %fusion.13), channel_id=1, source_target_pairs={{0,3},{1,4},{2,5},{3,6},{4,7},{5,0},{6,1},{7,2},{8,11},{9,12},{10,... | collective-permute-start | bytes 393224 | tf_op jit(solution)/shard_map/ppermute | solution.py:12
  68.6 19.1 %collective-permute-start.14 = (bf16[2,512,64]{1,2,0:T(8,128)(2,1)S(1)}, bf16[2,512,64]{1,2,0:T(8,128)(2,1)S(1)}, u32[]{:S(2)}, u32[]{:S(2)}) collective-permute-start(bf16[2,512,64]{1,2,0:T(8,128)(2,1)S(1)} %fusion.14), channel_id=1, source_target_pairs={{0,2},{1,3},{2,4},{3,5},{4,6},{5,7},{6,0},{7,1},{8,10},{9,11},{10,... | collective-permute-start | bytes 393224 | tf_op jit(solution)/shard_map/ppermute | solution.py:12
  70.9 19.9 %collective-permute-start.15 = (bf16[2,512,64]{1,2,0:T(8,128)(2,1)S(1)}, bf16[2,512,64]{1,2,0:T(8,128)(2,1)S(1)}, u32[]{:S(2)}, u32[]{:S(2)}) collective-permute-start(bf16[2,512,64]{1,2,0:T(8,128)(2,1)S(1)} %fusion.15), channel_id=1, source_target_pairs={{0,1},{1,2},{2,3},{3,4},{4,5},{5,6},{6,7},{7,0},{8,9},{9,10},{10,1... | collective-permute-start | bytes 393224 | tf_op jit(solution)/shard_map/ppermute | solution.py:12
  72.7 18.1 %collective-permute-start.16 = (bf16[2,512,64]{1,2,0:T(8,128)(2,1)S(1)}, bf16[2,512,64]{1,2,0:T(8,128)(2,1)S(1)}, u32[]{:S(2)}, u32[]{:S(2)}) collective-permute-start(bf16[2,512,64]{1,2,0:T(8,128)(2,1)S(1)} %fusion.16), channel_id=1, source_target_pairs={{0,5},{1,6},{2,7},{3,0},{4,1},{5,2},{6,3},{7,4},{8,13},{9,14},{10,... | collective-permute-start | bytes 393224 | tf_op jit(solution)/shard_map/ppermute | solution.py:12
  76.6 14.2 %collective-permute-start.17 = (bf16[2,512,64]{1,2,0:T(8,128)(2,1)S(1)}, bf16[2,512,64]{1,2,0:T(8,128)(2,1)S(1)}, u32[]{:S(2)}, u32[]{:S(2)}) collective-permute-start(bf16[2,512,64]{1,2,0:T(8,128)(2,1)S(1)} %fusion.17), channel_id=1, source_target_pairs={{0,6},{1,7},{2,0},{3,1},{4,2},{5,3},{6,4},{7,5},{8,14},{9,15},{10,... | collective-permute-start | bytes 393224 | tf_op jit(solution)/shard_map/ppermute | solution.py:12
  82.1 10.4 %collective-permute-start.18 = (bf16[2,512,64]{1,2,0:T(8,128)(2,1)S(1)}, bf16[2,512,64]{1,2,0:T(8,128)(2,1)S(1)}, u32[]{:S(2)}, u32[]{:S(2)}) collective-permute-start(bf16[2,512,64]{1,2,0:T(8,128)(2,1)S(1)} %fusion.18), channel_id=1, source_target_pairs={{0,7},{1,0},{2,1},{3,2},{4,3},{5,4},{6,5},{7,6},{8,15},{9,8},{10,9... | collective-permute-start | bytes 393224 | tf_op jit(solution)/shard_map/ppermute | solution.py:12

commit v19 on v16

--- a/solution.py
+++ b/solution.py
@@ -11,6 +11,7 @@
         send = make_chunk((me + k) % n)
         got = lax.ppermute(send, axis, [(j, (j + k) % n) for j in range(n)])
         total = got.astype(jnp.float32) if total is None else total + got.astype(jnp.float32)
+        total = lax.optimization_barrier(total)
     return total + make_chunk(me).astype(jnp.float32)
 
 

time: 92.8 us -> 93.1 us (level)
  other arithmetic: 2.77 us -> 3.72 us
    add x0 -> x7, other arithmetic: none -> 0.93 us  [the longest x1 0.74 us: scatter_sum(): return total + make_chunk(me).astype(jnp.float32)]
where the time goes in v19:
time: 93.1 us; the launch traced here: 92.4 us
  starting transfers between devices  36.6 us (39%)
  waiting for transfers between devices  23 us (25%)
  matrix products  22.1 us (24%)
  local copies, waits for them, and re-layouts  6.58 us (7%)
  other arithmetic  3.72 us (4%)
    ppermute x7, starting transfers between devices, scatter_sum(): got = lax.ppermute(send, axis, [(j, (j + k) % n) for j in range(n)])  16.6 us
    ppermute x12, waiting for transfers between devices, move(): return lax.ppermute(piece, 'blk', pairs_list)  13 us
    ppermute x12, starting transfers between devices, move(): return lax.ppermute(piece, 'blk', pairs_list)  11.5 us
    ppermute x7, waiting for transfers between devices, scatter_sum(): got = lax.ppermute(send, axis, [(j, (j + k) % n) for j in range(n)])  10 us
    all_to_all x1, starting transfers between devices, local(): lax.all_to_all(jnp.broadcast_to(rates_run, (pieces,) + left_rates.shape),...  8.47 us
    dot_general x1, matrix products, local(): jnp.einsum('tab,ktbc->kac', left_part, right_done, preferred_element_type...  6.6 us
    dot_general x8, matrix products, pool(): jnp.einsum('kab,abrn->krn', w, piece, preferred_element_type=jnp.float32)  5.87 us
    dot_general x1, matrix products, local(): jnp.einsum('jrn,jmn->jrm', dual_cols, right_dual, preferred_element_type=...  3.91 us
  transfers between devices with their start and end apart: 20, of which 11 were waited for; matrix products, arithmetic and copies ran while one was open for 18% of the time, Pallas kernels for 0%

profile of v19, /device:TPU:24, one launch (start us, length us, event | category | flops | bytes accessed | tf_op | source)
XLA Modules:
  0.0 92.4 jit_solution(11245659556007706045)
XLA Ops:
  0.0 1.5 %collective-permute-start.1 = (bf16[2,64,512]{2,1,0:T(8,128)(2,1)}, bf16[2,64,512]{2,1,0:T(8,128)(2,1)S(1)}, u32[]{:S(2)}, u32[]{:S(2)}) collective-permute-start(bf16[2,64,512]{2,1,0:T(8,128)(2,1)} %param.11), channel_id=1, source_target_pairs={{0,64},{8,72},{16,80},{24,88},{32,96},{40,104},{48,112},{56,120},{... | collective-permute-start | bytes 393224 | tf_op jit(solution)/shard_map/ppermute | solution.py:71
  1.5 1.7 %collective-permute-start = (bf16[2,64,512]{2,1,0:T(8,128)(2,1)}, bf16[2,64,512]{2,1,0:T(8,128)(2,1)S(1)}, u32[]{:S(2)}, u32[]{:S(2)}) collective-permute-start(bf16[2,64,512]{2,1,0:T(8,128)(2,1)} %param.11), channel_id=1, source_target_pairs={{0,192},{8,200},{16,208},{24,216},{32,224},{40,232},{48,240},{56,2... | collective-permute-start | bytes 393224 | tf_op jit(solution)/shard_map/ppermute | solution.py:71
  3.2 0.7 broadcast_in_dim.2
  3.9 0.7 reshape.158
  4.6 8.5 %all-to-all-start = ((f32[8,1,128]{2,1,0:T(1,128)}), f32[8,1,128]{2,1,0:T(1,128)S(1)}, u32[]{:S(2)}, u32[]{:S(2)}) async-start(f32[8,1,128]{2,1,0:T(1,128)} %reshape.158), calls=%async_computation | async-start | bytes 8192 | tf_op jit(solution)/shard_map/all_to_all | solution.py:110
  13.4 1.1 %constant_dynamic-slice_fusion = s32[32,1,2,3]{1,2,3,0:T(2,128)S(1)} fusion(s32[32,32,2,3]{1,2,3,0:T(2,128)} %param.14, s32[]{:T(128)S(6)} %select_n.99), kind=kLoop, calls=%fused_computation.76 | loop fusion | bytes 1540 | tf_op jit(solution)/shard_map/jit(dynamic_index_in_dim)/dynamic_slice | solution.py:42
  14.6 0.9 dynamic-slice_reduce_fusion
  15.9 3.0 %collective-permute-start.3 = (bf16[1,64,512]{2,1,0:T(8,128)(2,1)S(1)}, bf16[1,64,512]{2,1,0:T(8,128)(2,1)S(1)}, u32[]{:S(2)}, u32[]{:S(2)}) collective-permute-start(bf16[1,64,512]{2,1,0:T(8,128)(2,1)S(1)} %slice.65), channel_id=1, source_target_pairs={{0,192},{8,200},{16,208},{24,216},{32,224},{40,232},{48,240},{56,2... | collective-permute-start | bytes 196616 | tf_op jit(solution)/shard_map/ppermute | solution.py:71
  19.1 1.1 %copy.98 = bf16[1,2,64,512]{3,0,1,2:T(2,128)(2,1)S(1)} copy(bf16[1,2,64,512]{3,2,1,0:T(8,128)(2,1)} %bitcast.175) | data formatting | bytes 262144 | tf_op jit(solution)/shard_map/stack | solution.py:79
  20.6 0.5 collective-permute-done.2
  21.3 1.2 %pad_maximum_fusion = bf16[4,2,64,512]{3,0,1,2:T(4,128)(2,1)S(1)} fusion(bf16[1,2,64,512]{3,0,1,2:T(2,128)(2,1)S(1)} %copy.101, bf16[1,2,64,512]{3,0,1,2:T(2,128)(2,1)S(1)} %copy.100, bf16[1,2,64,512]{3,0,1,2:T(2,128)(2,1)S(1)} %copy.99, bf16[1,2,64,512]{3,0,1,2:T(2,128)(2,1)S(1)} %copy.98), kind=kLoop, calls=%fused_computation.39 | loop fusion | flops 2097152 | bytes 1048576 | tf_op jit(solution)/shard_map/stack | solution.py:79
  22.9 1.8 %collective-permute-start.4 = (bf16[4,2,64,512]{3,0,1,2:T(4,128)(2,1)S(1)}, bf16[4,2,64,512]{3,0,1,2:T(4,128)(2,1)S(1)}, u32[]{:S(2)}, u32[]{:S(2)}) collective-permute-start(bf16[4,2,64,512]{3,0,1,2:T(4,128)(2,1)S(1)} %pad_maximum_fusion), channel_id=1, source_target_pairs={{0,48},{8,56},{16,0},{24,8},{32,16},{40,24},{48,32},{56,40},{64,11... | collective-permute-start | bytes 1572872 | tf_op jit(solution)/shard_map/ppermute | solution.py:71
  25.1 0.5 broadcast.166
  25.6 0.7 reduce.2
  26.5 0.6 fusion.64
  27.1 7.5 %collective-permute-done.5 = bf16[4,2,64,512]{3,0,1,2:T(4,128)(2,1)S(1)} collective-permute-done((bf16[4,2,64,512]{3,0,1,2:T(4,128)(2,1)S(1)}, bf16[4,2,64,512]{3,0,1,2:T(4,128)(2,1)S(1)}, u32[]{:S(2)}, u32[]{:S(2)}) %collective-permute-start.5) | collective-permute-done | bytes 524320 | tf_op jit(solution)/shard_map/ppermute | solution.py:71
  34.8 1.6 %collective-permute-start.6 = (bf16[2,2,64,512]{3,0,1,2:T(2,128)(2,1)S(1)}, bf16[2,2,64,512]{3,0,1,2:T(2,128)(2,1)S(1)}, u32[]{:S(2)}, u32[]{:S(2)}) collective-permute-start(bf16[2,2,64,512]{3,0,1,2:T(2,128)(2,1)S(1)} %slice.68), channel_id=1, source_target_pairs={{0,16},{8,24},{16,32},{24,40},{32,48},{40,56},{48,0},{56,8},{64,80... | collective-permute-start | bytes 786440 | tf_op jit(solution)/shard_map/ppermute | solution.py:71
  36.7 0.6 collective-permute-start.7
  37.3 0.5 collective-permute-start.11
  37.8 0.6 fusion.58
  38.4 0.6 fusion.62
  39.1 0.6 fusion.56
  39.7 1.6 %collective-permute-done.6 = bf16[2,2,64,512]{3,0,1,2:T(2,128)(2,1)S(1)} collective-permute-done((bf16[2,2,64,512]{3,0,1,2:T(2,128)(2,1)S(1)}, bf16[2,2,64,512]{3,0,1,2:T(2,128)(2,1)S(1)}, u32[]{:S(2)}, u32[]{:S(2)}) %collective-permute-start.6) | collective-permute-done | bytes 262176 | tf_op jit(solution)/shard_map/ppermute | solution.py:71
  41.2 3.1 %collective-permute-done.7 = bf16[2,2,64,512]{3,0,1,2:T(2,128)(2,1)S(1)} collective-permute-done((bf16[2,2,64,512]{3,0,1,2:T(2,128)(2,1)S(1)}, bf16[2,2,64,512]{3,0,1,2:T(2,128)(2,1)S(1)}, u32[]{:S(2)}, u32[]{:S(2)}) %collective-permute-start.7) | collective-permute-done | bytes 262176 | tf_op jit(solution)/shard_map/ppermute | solution.py:71
  44.3 0.5 pad_maximum_fusion.1
  45.0 1.0 %fusion.60 = f32[16,64,512,1]{2,0,3,1:T(8,128)S(1)} fusion(bf16[16,1,1,4,2]{0,4,3,2,1:T(2,128)(2,1)S(1)} %get-tuple-element.10, bf16[2,2,64,512]{3,0,1,2:T(2,128)(2,1)S(1)} %collective-permute-done.7, bf16[2,2,64,512]{3,0,1,2:T(2,128)(2,1)S(1)} %collective-permute-done.6), kind=kOutput, calls=%fused_computation.90 | convolution fusion | flops 9437184 | bytes 2621696 | tf_op jit(solution)/shard_map/kab,abrn->krn/dot_general | solution.py:92
  46.0 0.6 fusion.54
  46.9 0.6 fusion.52
  47.5 1.2 %fusion.9 = bf16[2,8,64,512]{3,1,0,2:T(8,128)(2,1)S(1)} fusion(bf16[4,2,64,512]{3,0,1,2:T(4,128)(2,1)S(1)} %collective-permute-done.11, f32[16,64,512,1]{2,0,3,1:T(8,128)S(1)} %fusion.52, f32[16,64,512,1]{2,0,3,1:T(8,128)S(1)} %fusion.54, f32[16,64,512,1]{2,0,3,1:T(8,128)S(1)} %fusion.56, f32[16,64,512,1]{2,0,3,1:T(8,128)S(1)} %fusion.58, ...), kind=kOutput, calls=%fused_computation.16 | convolution fusion | flops 12582912 | bytes 16253184 | tf_op jit(solution)/shard_map/kab,abrn->krn/dot_general | solution.py:92
  48.7 6.6 %bitcast_convert_fusion = bf16[2,512,512]{2,1,0:T(8,128)(2,1)} fusion(bf16[8,512,512]{2,1,0:T(8,128)(2,1)} %param.12, s32[]{:T(128)S(6)} %select_n.106, bf16[8,512,512]{2,1,0:T(8,128)(2,1)} %param.13, bf16[2,8,64,512]{3,1,0,2:T(8,128)(2,1)S(1)} %fusion.9), kind=kOutput, calls=%fused_computation.2 | convolution fusion | flops 1074790400 | bytes 7340036 | tf_op jit(solution)/shard_map/tab,ktbc->kac/dot_general | solution.py:114
  55.3 3.9 %divide_convert_fusion = bf16[2,512,512]{2,1,0:T(8,128)(2,1)} fusion(bf16[2,512,512]{2,1,0:T(8,128)(2,1)S(1)} %copy-done, bf16[2,512,512]{2,1,0:T(8,128)(2,1)} %bitcast_convert_fusion, bf16[2,512,512]{2,1,0:T(8,128)(2,1)} %param.17, f32[2,512]{1,0:T(2,128)S(1)} %copy-done.3, f32[2,512]{1,0:T(2,128)S(1)} %add.280), kind=kOutput, calls=%fused_computation.11 | convolution fusion | flops 1075838976 | bytes 4202496 | tf_op jit(solution)/shard_map/jrn,jmn->jrm/dot_general | solution.py:120
  59.2 2.0 %convolution_convert_fusion = bf16[2,512,512]{1,2,0:T(8,128)(2,1)S(1)} fusion(bf16[2,512,512]{2,1,0:T(8,128)(2,1)} %divide_convert_fusion, bf16[2,512,512]{2,1,0:T(8,128)(2,1)S(1)} %copy-done.2), kind=kOutput, calls=%fused_computation.13 | convolution fusion | flops 537395200 | bytes 3145728 | tf_op jit(solution)/shard_map/jrm,jkm->jrk/dot_general | solution.py:122
  61.7 0.4 fusion.12
  62.2 5.5 %collective-permute-start.12 = (bf16[2,512,64]{1,2,0:T(8,128)(2,1)S(1)}, bf16[2,512,64]{1,2,0:T(8,128)(2,1)S(1)}, u32[]{:S(2)}, u32[]{:S(2)}) collective-permute-start(bf16[2,512,64]{1,2,0:T(8,128)(2,1)S(1)} %fusion.12), channel_id=1, source_target_pairs={{0,4},{1,5},{2,6},{3,7},{4,0},{5,1},{6,2},{7,3},{8,12},{9,13},{10,... | collective-permute-start | bytes 393224 | tf_op jit(solution)/shard_map/ppermute | solution.py:12
  68.1 0.6 collective-permute-start.13
  69.2 4.8 %collective-permute-start.14 = (bf16[2,512,64]{1,2,0:T(8,128)(2,1)S(1)}, bf16[2,512,64]{1,2,0:T(8,128)(2,1)S(1)}, u32[]{:S(2)}, u32[]{:S(2)}) collective-permute-start(bf16[2,512,64]{1,2,0:T(8,128)(2,1)S(1)} %fusion.14), channel_id=1, source_target_pairs={{0,5},{1,6},{2,7},{3,0},{4,1},{5,2},{6,3},{7,4},{8,13},{9,14},{10,... | collective-permute-start | bytes 393224 | tf_op jit(solution)/shard_map/ppermute | solution.py:12
  74.4 0.6 collective-permute-start.15
  75.0 0.4 fusion.16
  75.5 3.6 %collective-permute-start.16 = (bf16[2,512,64]{1,2,0:T(8,128)(2,1)S(1)}, bf16[2,512,64]{1,2,0:T(8,128)(2,1)S(1)}, u32[]{:S(2)}, u32[]{:S(2)}) collective-permute-start(bf16[2,512,64]{1,2,0:T(8,128)(2,1)S(1)} %fusion.16), channel_id=1, source_target_pairs={{0,6},{1,7},{2,0},{3,1},{4,2},{5,3},{6,4},{7,5},{8,14},{9,15},{10,... | collective-permute-start | bytes 393224 | tf_op jit(solution)/shard_map/ppermute | solution.py:12
  79.6 0.4 fusion.18
  80.0 0.6 collective-permute-start.17
  80.7 2.1 %collective-permute-done.13 = bf16[2,512,64]{1,2,0:T(8,128)(2,1)S(1)} collective-permute-done((bf16[2,512,64]{1,2,0:T(8,128)(2,1)S(1)}, bf16[2,512,64]{1,2,0:T(8,128)(2,1)S(1)}, u32[]{:S(2)}, u32[]{:S(2)}) %collective-permute-start.13) | collective-permute-done | bytes 131104 | tf_op jit(solution)/shard_map/ppermute | solution.py:12
  82.7 0.7 collective-permute-start.18
  83.5 2.2 %collective-permute-done.14 = bf16[2,512,64]{1,2,0:T(8,128)(2,1)S(1)} collective-permute-done((bf16[2,512,64]{1,2,0:T(8,128)(2,1)S(1)}, bf16[2,512,64]{1,2,0:T(8,128)(2,1)S(1)}, u32[]{:S(2)}, u32[]{:S(2)}) %collective-permute-start.14) | collective-permute-done | bytes 131104 | tf_op jit(solution)/shard_map/ppermute | solution.py:12
  85.8 2.5 %collective-permute-done.15 = bf16[2,512,64]{1,2,0:T(8,128)(2,1)S(1)} collective-permute-done((bf16[2,512,64]{1,2,0:T(8,128)(2,1)S(1)}, bf16[2,512,64]{1,2,0:T(8,128)(2,1)S(1)}, u32[]{:S(2)}, u32[]{:S(2)}) %collective-permute-start.15) | collective-permute-done | bytes 131104 | tf_op jit(solution)/shard_map/ppermute | solution.py:12
  88.3 0.5 collective-permute-done.16
  88.9 2.5 %collective-permute-done.17 = bf16[2,512,64]{1,2,0:T(8,128)(2,1)S(1)} collective-permute-done((bf16[2,512,64]{1,2,0:T(8,128)(2,1)S(1)}, bf16[2,512,64]{1,2,0:T(8,128)(2,1)S(1)}, u32[]{:S(2)}, u32[]{:S(2)}) %collective-permute-start.17) | collective-permute-done | bytes 131104 | tf_op jit(solution)/shard_map/ppermute | solution.py:12
  91.6 0.7 add.311
  (60 shorter events, 5.8 us)
Async XLA Ops:
  0.0 55.3 %copy-start = (bf16[2,512,512]{2,1,0:T(8,128)(2,1)S(1)}, bf16[2,512,512]{2,1,0:T(8,128)(2,1)}, u32[]{:S(2)}) copy-start(bf16[2,512,512]{2,1,0:T(8,128)(2,1)} %param.19) | copy-start | bytes 3145732
  0.0 15.5 %collective-permute-start.1 = (bf16[2,64,512]{2,1,0:T(8,128)(2,1)}, bf16[2,64,512]{2,1,0:T(8,128)(2,1)S(1)}, u32[]{:S(2)}, u32[]{:S(2)}) collective-permute-start(bf16[2,64,512]{2,1,0:T(8,128)(2,1)} %param.11), channel_id=1, source_target_pairs={{0,64},{8,72},{16,80},{24,88},{32,96},{40,104},{48,112},{56,120},{... | collective-permute-start | bytes 393224 | tf_op jit(solution)/shard_map/ppermute | solution.py:71
  1.5 14.4 %collective-permute-start = (bf16[2,64,512]{2,1,0:T(8,128)(2,1)}, bf16[2,64,512]{2,1,0:T(8,128)(2,1)S(1)}, u32[]{:S(2)}, u32[]{:S(2)}) collective-permute-start(bf16[2,64,512]{2,1,0:T(8,128)(2,1)} %param.11), channel_id=1, source_target_pairs={{0,192},{8,200},{16,208},{24,216},{32,224},{40,232},{48,240},{56,2... | collective-permute-start | bytes 393224 | tf_op jit(solution)/shard_map/ppermute | solution.py:71
  4.6 20.5 %all-to-all-start = ((f32[8,1,128]{2,1,0:T(1,128)}), f32[8,1,128]{2,1,0:T(1,128)S(1)}, u32[]{:S(2)}, u32[]{:S(2)}) async-start(f32[8,1,128]{2,1,0:T(1,128)} %reshape.158), calls=%async_computation | async-start | bytes 8192 | tf_op jit(solution)/shard_map/all_to_all | solution.py:110
  15.5 5.6 %collective-permute-start.2 = (bf16[1,64,512]{2,1,0:T(8,128)(2,1)S(1)}, bf16[1,64,512]{2,1,0:T(8,128)(2,1)S(1)}, u32[]{:S(2)}, u32[]{:S(2)}) collective-permute-start(bf16[1,64,512]{2,1,0:T(8,128)(2,1)S(1)} %slice.64), channel_id=1, source_target_pairs={{0,64},{8,72},{16,80},{24,88},{32,96},{40,104},{48,112},{56,120},{... | collective-permute-start | bytes 196616 | tf_op jit(solution)/shard_map/ppermute | solution.py:71
  15.9 5.2 %collective-permute-start.3 = (bf16[1,64,512]{2,1,0:T(8,128)(2,1)S(1)}, bf16[1,64,512]{2,1,0:T(8,128)(2,1)S(1)}, u32[]{:S(2)}, u32[]{:S(2)}) collective-permute-start(bf16[1,64,512]{2,1,0:T(8,128)(2,1)S(1)} %slice.65), channel_id=1, source_target_pairs={{0,192},{8,200},{16,208},{24,216},{32,224},{40,232},{48,240},{56,2... | collective-permute-start | bytes 196616 | tf_op jit(solution)/shard_map/ppermute | solution.py:71
  22.6 12.0 %collective-permute-start.5 = (bf16[4,2,64,512]{3,0,1,2:T(4,128)(2,1)S(1)}, bf16[4,2,64,512]{3,0,1,2:T(4,128)(2,1)S(1)}, u32[]{:S(2)}, u32[]{:S(2)}) collective-permute-start(bf16[4,2,64,512]{3,0,1,2:T(4,128)(2,1)S(1)} %pad_maximum_fusion), channel_id=1, source_target_pairs={{0,16},{8,24},{16,32},{24,40},{32,48},{40,56},{48,0},{56,8},{64,80... | collective-permute-start | bytes 1572872 | tf_op jit(solution)/shard_map/ppermute | solution.py:71
  22.9 13.5 %collective-permute-start.4 = (bf16[4,2,64,512]{3,0,1,2:T(4,128)(2,1)S(1)}, bf16[4,2,64,512]{3,0,1,2:T(4,128)(2,1)S(1)}, u32[]{:S(2)}, u32[]{:S(2)}) collective-permute-start(bf16[4,2,64,512]{3,0,1,2:T(4,128)(2,1)S(1)} %pad_maximum_fusion), channel_id=1, source_target_pairs={{0,48},{8,56},{16,0},{24,8},{32,16},{40,24},{48,32},{56,40},{64,11... | collective-permute-start | bytes 1572872 | tf_op jit(solution)/shard_map/ppermute | solution.py:71
  26.4 12.6 %collective-permute-start.8 = (bf16[4,2,64,512]{3,0,1,2:T(4,128)(2,1)S(1)}, bf16[4,2,64,512]{3,0,1,2:T(4,128)(2,1)S(1)}, u32[]{:S(2)}, u32[]{:S(2)}) collective-permute-start(bf16[4,2,64,512]{3,0,1,2:T(4,128)(2,1)S(1)} %pad_maximum_fusion), channel_id=1, source_target_pairs={{0,8},{8,0},{16,24},{24,16},{32,40},{40,32},{48,56},{56,48},{64,72... | collective-permute-start | bytes 1572872 | tf_op jit(solution)/shard_map/ppermute | solution.py:71
  34.8 6.4 %collective-permute-start.6 = (bf16[2,2,64,512]{3,0,1,2:T(2,128)(2,1)S(1)}, bf16[2,2,64,512]{3,0,1,2:T(2,128)(2,1)S(1)}, u32[]{:S(2)}, u32[]{:S(2)}) collective-permute-start(bf16[2,2,64,512]{3,0,1,2:T(2,128)(2,1)S(1)} %slice.68), channel_id=1, source_target_pairs={{0,16},{8,24},{16,32},{24,40},{32,48},{40,56},{48,0},{56,8},{64,80... | collective-permute-start | bytes 786440 | tf_op jit(solution)/shard_map/ppermute | solution.py:71
  36.7 7.7 %collective-permute-start.7 = (bf16[2,2,64,512]{3,0,1,2:T(2,128)(2,1)S(1)}, bf16[2,2,64,512]{3,0,1,2:T(2,128)(2,1)S(1)}, u32[]{:S(2)}, u32[]{:S(2)}) collective-permute-start(bf16[2,2,64,512]{3,0,1,2:T(2,128)(2,1)S(1)} %slice.69), channel_id=1, source_target_pairs={{0,48},{8,56},{16,0},{24,8},{32,16},{40,24},{48,32},{56,40},{64,11... | collective-permute-start | bytes 786440 | tf_op jit(solution)/shard_map/ppermute | solution.py:71
  37.3 8.7 %collective-permute-start.9 = (bf16[4,2,64,512]{3,0,1,2:T(4,128)(2,1)S(1)}, bf16[4,2,64,512]{3,0,1,2:T(4,128)(2,1)S(1)}, u32[]{:S(2)}, u32[]{:S(2)}) collective-permute-start(bf16[4,2,64,512]{3,0,1,2:T(4,128)(2,1)S(1)} %collective-permute-done.4), channel_id=1, source_target_pairs={{0,8},{8,0},{16,24},{24,16},{32,40},{40,32},{48,56},{56,48},{64,72... | collective-permute-start | bytes 1572872 | tf_op jit(solution)/shard_map/ppermute | solution.py:71
  37.3 10.2 %collective-permute-start.11 = (bf16[4,2,64,512]{3,0,1,2:T(4,128)(2,1)S(1)}, bf16[4,2,64,512]{3,0,1,2:T(4,128)(2,1)S(1)}, u32[]{:S(2)}, u32[]{:S(2)}) collective-permute-start(bf16[4,2,64,512]{3,0,1,2:T(4,128)(2,1)S(1)} %collective-permute-done.5), channel_id=1, source_target_pairs={{0,8},{8,0},{16,24},{24,16},{32,40},{40,32},{48,56},{56,48},{64,72... | collective-permute-start | bytes 1572872 | tf_op jit(solution)/shard_map/ppermute | solution.py:71
  44.9 2.0 %collective-permute-start.10 = (bf16[4,2,64,512]{3,0,1,2:T(4,128)(2,1)S(1)}, bf16[4,2,64,512]{3,0,1,2:T(4,128)(2,1)S(1)}, u32[]{:S(2)}, u32[]{:S(2)}) collective-permute-start(bf16[4,2,64,512]{3,0,1,2:T(4,128)(2,1)S(1)} %pad_maximum_fusion.1), channel_id=1, source_target_pairs={{0,8},{8,0},{16,24},{24,16},{32,40},{40,32},{48,56},{56,48},{64,72... | collective-permute-start | bytes 1572872 | tf_op jit(solution)/shard_map/ppermute | solution.py:71
  48.7 6.6 %copy-start.3 = (f32[2,512]{1,0:T(2,128)S(1)}, f32[2,512]{1,0:T(2,128)}, u32[]{:S(2)}) copy-start(f32[2,512]{1,0:T(2,128)} %param.21) | copy-start | bytes 12292
  55.3 3.9 %copy-start.2 = (bf16[2,512,512]{2,1,0:T(8,128)(2,1)S(1)}, bf16[2,512,512]{2,1,0:T(8,128)(2,1)}, u32[]{:S(2)}) copy-start(bf16[2,512,512]{2,1,0:T(8,128)(2,1)} %param.18) | copy-start | bytes 3145732
  59.2 2.1 %copy-start.1 = (bf16[2,512,512]{2,1,0:T(8,128)(2,1)S(1)}, bf16[2,512,512]{2,1,0:T(8,128)(2,1)}, u32[]{:S(2)}) copy-start(bf16[2,512,512]{2,1,0:T(8,128)(2,1)} %param.16) | copy-start | bytes 3145732
  62.2 17.8 %collective-permute-start.12 = (bf16[2,512,64]{1,2,0:T(8,128)(2,1)S(1)}, bf16[2,512,64]{1,2,0:T(8,128)(2,1)S(1)}, u32[]{:S(2)}, u32[]{:S(2)}) collective-permute-start(bf16[2,512,64]{1,2,0:T(8,128)(2,1)S(1)} %fusion.12), channel_id=1, source_target_pairs={{0,4},{1,5},{2,6},{3,7},{4,0},{5,1},{6,2},{7,3},{8,12},{9,13},{10,... | collective-permute-start | bytes 393224 | tf_op jit(solution)/shard_map/ppermute | solution.py:12
  68.1 14.6 %collective-permute-start.13 = (bf16[2,512,64]{1,2,0:T(8,128)(2,1)S(1)}, bf16[2,512,64]{1,2,0:T(8,128)(2,1)S(1)}, u32[]{:S(2)}, u32[]{:S(2)}) collective-permute-start(bf16[2,512,64]{1,2,0:T(8,128)(2,1)S(1)} %fusion.13), channel_id=1, source_target_pairs={{0,3},{1,4},{2,5},{3,6},{4,7},{5,0},{6,1},{7,2},{8,11},{9,12},{10,... | collective-permute-start | bytes 393224 | tf_op jit(solution)/shard_map/ppermute | solution.py:12
  69.2 16.5 %collective-permute-start.14 = (bf16[2,512,64]{1,2,0:T(8,128)(2,1)S(1)}, bf16[2,512,64]{1,2,0:T(8,128)(2,1)S(1)}, u32[]{:S(2)}, u32[]{:S(2)}) collective-permute-start(bf16[2,512,64]{1,2,0:T(8,128)(2,1)S(1)} %fusion.14), channel_id=1, source_target_pairs={{0,5},{1,6},{2,7},{3,0},{4,1},{5,2},{6,3},{7,4},{8,13},{9,14},{10,... | collective-permute-start | bytes 393224 | tf_op jit(solution)/shard_map/ppermute | solution.py:12
  74.4 13.9 %collective-permute-start.15 = (bf16[2,512,64]{1,2,0:T(8,128)(2,1)S(1)}, bf16[2,512,64]{1,2,0:T(8,128)(2,1)S(1)}, u32[]{:S(2)}, u32[]{:S(2)}) collective-permute-start(bf16[2,512,64]{1,2,0:T(8,128)(2,1)S(1)} %fusion.15), channel_id=1, source_target_pairs={{0,2},{1,3},{2,4},{3,5},{4,6},{5,7},{6,0},{7,1},{8,10},{9,11},{10,... | collective-permute-start | bytes 393224 | tf_op jit(solution)/shard_map/ppermute | solution.py:12
  75.5 13.4 %collective-permute-start.16 = (bf16[2,512,64]{1,2,0:T(8,128)(2,1)S(1)}, bf16[2,512,64]{1,2,0:T(8,128)(2,1)S(1)}, u32[]{:S(2)}, u32[]{:S(2)}) collective-permute-start(bf16[2,512,64]{1,2,0:T(8,128)(2,1)S(1)} %fusion.16), channel_id=1, source_target_pairs={{0,6},{1,7},{2,0},{3,1},{4,2},{5,3},{6,4},{7,5},{8,14},{9,15},{10,... | collective-permute-start | bytes 393224 | tf_op jit(solution)/shard_map/ppermute | solution.py:12
  80.0 11.4 %collective-permute-start.17 = (bf16[2,512,64]{1,2,0:T(8,128)(2,1)S(1)}, bf16[2,512,64]{1,2,0:T(8,128)(2,1)S(1)}, u32[]{:S(2)}, u32[]{:S(2)}) collective-permute-start(bf16[2,512,64]{1,2,0:T(8,128)(2,1)S(1)} %fusion.17), channel_id=1, source_target_pairs={{0,1},{1,2},{2,3},{3,4},{4,5},{5,6},{6,7},{7,0},{8,9},{9,10},{10,1... | collective-permute-start | bytes 393224 | tf_op jit(solution)/shard_map/ppermute | solution.py:12
  82.7 8.9 %collective-permute-start.18 = (bf16[2,512,64]{1,2,0:T(8,128)(2,1)S(1)}, bf16[2,512,64]{1,2,0:T(8,128)(2,1)S(1)}, u32[]{:S(2)}, u32[]{:S(2)}) collective-permute-start(bf16[2,512,64]{1,2,0:T(8,128)(2,1)S(1)} %fusion.18), channel_id=1, source_target_pairs={{0,7},{1,0},{2,1},{3,2},{4,3},{5,4},{6,5},{7,6},{8,15},{9,8},{10,9... | collective-permute-start | bytes 393224 | tf_op jit(solution)/shard_map/ppermute | solution.py:12
